TPU v7x, 32 devices: a whole 2x2x4 slice. The times are simulated.
32 devices in a mesh: dp: 16 (over z, x, core), tensor: 2 (over y).
Axes of the slice: x: 2, y: 2, z: 4, core: 2. Of those that a mesh axis runs over, the one named last changes fastest.
Arguments:
- context: bfloat16 [4096, 4096], P('dp', 'tensor'), may hold values from -6 to 6
- w_out: bfloat16 [4096, 4096], P('tensor'), may hold values from -1 to 1
- teacher_input: bfloat16 [4096, 4096], P(('dp', 'tensor')), may hold values from -6 to 6
- teacher_gain: bfloat16 [4096], replicated, may hold values from 0.5 to 1.5
- layer_weights: float32 [2], replicated, may hold values from 0.3 to 1.5
- teacher_head: bfloat16 [4096, 4], replicated, may hold values from -16 to 16
- student_hidden: bfloat16 [4096, 3072], P(('dp', 'tensor')), may hold values from -6 to 6
- student_input: bfloat16 [4096, 768], P(('dp', 'tensor')), may hold values from -10 to 10
- down_weight: bfloat16 [3072, 768], P(('dp', 'tensor')), may hold values from -0.109375 to 0.109375
- student_gain: bfloat16 [768], replicated, may hold values from 0.5 to 1.5
- student_head: bfloat16 [768, 4], replicated, may hold values from -32 to 32
- labels: int32 [4096], P(('dp', 'tensor')), may hold values from 0 to 3
- lengths: int32 [8], replicated, may hold values from 64 to 512
Outputs:
- grad_down: float32 [3072, 768], P(('dp', 'tensor'))
- grad_head: float32 [768, 4], replicated
- loss: float32 [], replicated
All inputs are finite; a program needn't handle non-finite values.
Results may differ from a plain program's by a relative error of at most 0.0075.
Values may be sent and summed in bfloat16 or wider, within the bound.
No kernel may reach another device: no remote copies, remote signals or barrier semaphores. Data moves between devices by JAX's collectives and lax.ppermute only.
A program may use at most 128 MiB of HBM per device.

v0:
```python
import jax
import jax.numpy as jnp
from jax import lax
from jax.sharding import PartitionSpec as P

SEQ = 512


label_weight = 0.5
teacher_eps = 1e-05
student_eps = 1e-07


def norm_rows(values, gain_vec, epsilon):
    center = values - jnp.mean(values, axis=-1, keepdims=True)
    spread = jnp.mean(center * center, axis=-1, keepdims=True)
    inverse = lax.rsqrt(spread + epsilon)
    scaled = center * inverse
    return (scaled * gain_vec, scaled, inverse)


def folder(ordered, row_piece):
    return jnp.dot(ordered, row_piece, preferred_element_type=jnp.float32)


def local(
    context,
    w_out,
    teacher_input,
    teacher_gain,
    layer_weights,
    teacher_head,
    student_hidden,
    student_input,
    down_weight,
    student_gain,
    student_head,
    labels,
    lengths,
):
    tok_rows = teacher_input.shape[0]
    tensor_size = lax.axis_size("tensor")
    attention = lax.psum_scatter(
        jnp.dot(context, w_out, preferred_element_type=jnp.float32).astype(jnp.bfloat16),
        "tensor",
        scatter_dimension=0,
        tiled=True,
    ).astype(jnp.float32)
    residual = teacher_input.astype(jnp.float32)
    layer_out = norm_rows(residual + attention, teacher_gain.astype(jnp.float32), teacher_eps)[0]
    blended = (layer_weights[0] * residual + layer_weights[1] * layer_out).astype(jnp.bfloat16)
    teacher_logits = jnp.dot(blended, teacher_head, preferred_element_type=jnp.float32)
    teacher_logp = jax.nn.log_softmax(teacher_logits, axis=-1)
    teacher_prob = jnp.exp(teacher_logp)
    ffn_out = folder(
        student_hidden, lax.all_gather(down_weight, ("dp", "tensor"), axis=0, tiled=True)
    )
    student_scale = student_gain.astype(jnp.float32)
    normed, scaled, inverse = norm_rows(
        student_input.astype(jnp.float32) + ffn_out, student_scale, student_eps
    )
    features = normed.astype(jnp.bfloat16)
    student_logits = jnp.dot(features, student_head, preferred_element_type=jnp.float32)
    student_logp = jax.nn.log_softmax(student_logits, axis=-1)
    student_prob = jnp.exp(student_logp)
    first_token = (lax.axis_index("dp") * tensor_size + lax.axis_index("tensor")) * tok_rows
    positions = first_token + jnp.arange(tok_rows, dtype=jnp.int32)
    sentence = positions // SEQ
    matches = sentence[:, None] == jnp.arange(lengths.shape[0], dtype=jnp.int32)[None, :]
    lengths_tok = jnp.sum(jnp.where(matches, lengths[None, :], 0), axis=1)
    validity = (positions % SEQ < lengths_tok).astype(jnp.float32)
    onehot = (
        labels[:, None] == jnp.arange(teacher_logits.shape[1], dtype=jnp.int32)[None, :]
    ).astype(jnp.float32)
    token_loss = jnp.sum(
        teacher_prob * (teacher_logp - student_logp), axis=1
    ) - label_weight * jnp.sum(onehot * student_logp, axis=1)
    loss_part = jnp.sum(validity * token_loss)
    logit_grad = (
        validity[:, None]
        * ((1.0 + label_weight) * student_prob - teacher_prob - label_weight * onehot)
    ).astype(jnp.bfloat16)
    head_term = lax.dot_general(
        features, logit_grad, (((0,), (0,)), ((), ())), preferred_element_type=jnp.float32
    )
    norm_grad = (
        jnp.dot(logit_grad, student_head.T, preferred_element_type=jnp.float32) * student_scale
    )
    grad_out = (
        (
            norm_grad
            - jnp.mean(norm_grad, axis=-1, keepdims=True)
            - scaled * jnp.mean(norm_grad * scaled, axis=-1, keepdims=True)
        )
        * inverse
    ).astype(jnp.bfloat16)
    grad_down = lax.psum_scatter(
        lax.dot_general(
            student_hidden, grad_out, (((0,), (0,)), ((), ())), preferred_element_type=jnp.float32
        ),
        ("dp", "tensor"),
        scatter_dimension=0,
        tiled=True,
    )
    head_total, loss_total, count_total = lax.psum(
        (head_term, loss_part, jnp.sum(validity)), ("dp", "tensor")
    )
    return (grad_down, head_total, loss_total / count_total)


def solution(mesh):
    return jax.shard_map(
        local,
        mesh=mesh,
        in_specs=(
            P("dp", "tensor"),
            P("tensor", None),
            P(("dp", "tensor"), None),
            P(),
            P(),
            P(),
            P(("dp", "tensor"), None),
            P(("dp", "tensor"), None),
            P(("dp", "tensor"), None),
            P(),
            P(),
            P(("dp", "tensor")),
            P(),
        ),
        out_specs=(P(("dp", "tensor"), None), P(), P()),
        check_vma=False,
    )
```

profile of v0, /device:TPU:0, one launch (start us, length us, event | category | flops | bytes accessed | tf_op | source)
XLA Modules:
  0.0 268.8 jit_solution(7776146395088304549)
XLA Ops:
  8.1 1.2 copy-done
  9.2 11.5 %convolution_convert_fusion = bf16[256,4096]{1,0:T(8,128)(2,1)} fusion(bf16[256,2048]{1,0:T(8,128)(2,1)S(1)} %copy-done, bf16[2048,4096]{1,0:T(8,128)(2,1)} %param.15), kind=kOutput, calls=%fused_computation.1 | convolution fusion | flops 4296015872 | bytes 19922944 | tf_op jit(solution)/shard_map/dot_general | solution.py:44
  20.7 0.0 all-gather.2.cloned.1.call-start
  20.8 0.5 all-gather.2.cloned.1.call-update
  21.3 0.0 reduce-scatter.7.cloned.1.call-start
  21.4 0.6 fusion.13
  22.0 0.1 select_reduce_fusion
  22.1 33.5 %reduce-scatter.5.cloned.1.call-done = bf16[128,4096]{1,0:T(8,128)(2,1)} async-done(((bf16[256,4096]{1,0:T(8,128)(2,1)}), bf16[128,4096]{1,0:T(8,128)(2,1)}) %reduce-scatter.5.cloned.1.call-update) | async-done | bytes 1048592 | tf_op jit(solution)/shard_map/reduce_scatter | solution.py:43
  55.7 1.7 fusion.3
  57.3 0.5 multiply_reduce_fusion
  57.9 2.2 fusion.15
  60.1 46.4 %all-gather.2.cloned.1.call-done = bf16[3072,768]{1,0:T(8,128)(2,1)} async-done(((bf16[96,768]{1,0:T(8,128)(2,1)}), bf16[3072,768]{1,0:T(8,128)(2,1)}) %all-gather.2.cloned.1.call-update) | async-done | bytes 4718608 | tf_op jit(solution)/shard_map/all_gather | solution.py:56
  106.5 3.2 %fusion.14 = (f32[128]{0:T(128)S(1)}, f32[128,768]{1,0:T(8,128)S(1)}) fusion(bf16[128,3072]{1,0:T(8,128)(2,1)S(1)} %copy-done.3, bf16[3072,768]{1,0:T(8,128)(2,1)} %all-gather.2.cloned.1.call-done, bf16[128,768]{1,0:T(8,128)(2,1)S(1)} %copy-done.4), kind=kOutput, calls=%fused_computation.48 | convolution fusion | flops 604274560 | bytes 6095360 | tf_op jit(solution)/shard_map/dot_general | solution.py:23
  109.8 0.2 multiply_reduce_fusion.2
  110.0 0.1 multiply_convert_fusion.1
  110.1 0.1 fusion.16
  110.2 0.1 exponential_reduce_fusion.1
  110.4 0.6 convert_reduce_fusion
  111.0 0.4 fusion.11
  111.4 5.2 %convolution_bitcast_fusion = f32[3072,768]{0,1:T(8,128)} fusion(bf16[128,3072]{1,0:T(8,128)(2,1)S(1)} %copy-done.3, f32[128,768]{1,0:T(8,128)S(1)} %get-tuple-element.31, f32[128,768]{1,0:T(8,128)S(1)} %get-tuple-element.26, f32[128]{0:T(128)S(1)} %get-tuple-element.32, f32[128]{0:T(128)S(1)} %get-tuple-element.33, f32[128]{0:T(128)S(1)} %add_rsqrt_fusion.1, ...), kind=kOutput, calls=%fused_computation | convolution fusion | flops 604667904 | bytes 11012096 | tf_op jit(solution)/shard_map/dot_general | solution.py:98
  116.6 9.6 %copy.19 = f32[3072,768]{1,0:T(8,128)} copy(f32[3072,768]{0,1:T(8,128)} %convolution_bitcast_fusion) | data formatting | bytes 18874368
  126.3 0.1 fusion.17
  126.4 39.3 %all-reduce = (f32[768,4]{0,1:T(4,128)}, f32[]{:T(128)}, f32[]{:T(128)}) all-reduce(f32[768,4]{0,1:T(4,128)S(1)} %fusion.17, f32[]{:T(128)} %get-tuple-element.18, f32[]{:T(128)} %get-tuple-element.17), channel_id=1, replica_groups=mesh['dp'=16,'tensor'=2] {'dp','tensor'}, use_global_device_ids=true, to_apply=%region_11.13 | all-reduce | flops 3074 | bytes 24592 | tf_op jit(solution)/shard_map/psum | solution.py:105
  167.0 93.2 %reduce-scatter.7.cloned.1.call-done = f32[96,768]{1,0:T(8,128)} async-done(((f32[3072,768]{1,0:T(8,128)}), f32[96,768]{1,0:T(8,128)}) %reduce-scatter.7.cloned.1.call-update) | async-done | bytes 294928
  (39 shorter events, 0.3 us)
Async XLA Ops:
  8.0 1.2 copy-start
  8.0 47.6 %reduce-scatter.5.cloned.1.call-start = ((), (), s32[]{:S(2)}) async-start(), calls=%async_computation.3 | async-start | bytes 3145728 | tf_op jit(solution)/shard_map/reduce_scatter | solution.py:43
  20.7 0.7 copy-start.8
  20.7 0.7 copy-start.6
  20.7 0.8 copy-start.9
  20.7 1.3 copy-start.11
  20.7 35.0 %copy-start.1 = (bf16[128,4096]{1,0:T(8,128)(2,1)S(1)}, bf16[128,4096]{1,0:T(8,128)(2,1)}, u32[]{:S(2)}) copy-start(bf16[128,4096]{1,0:T(8,128)(2,1)} %param.16) | copy-start | bytes 3145732
  20.7 85.8 %all-gather.2.cloned.1.call-start = ((), (), s32[]{:S(2)}) async-start(), calls=%async_computation.2 | async-start | bytes 4866048 | tf_op jit(solution)/shard_map/all_gather | solution.py:56
  21.3 238.9 %reduce-scatter.7.cloned.1.call-start = ((), (), s32[]{:S(2)}) async-start(), calls=%async_computation.4 | async-start | bytes 9732096
  22.1 35.8 %copy-start.10 = (bf16[4096,4]{0,1:T(4,128)(2,1)S(1)}, bf16[4096,4]{0,1:T(4,128)(2,1)}, u32[]{:S(2)}) copy-start(bf16[4096,4]{0,1:T(4,128)(2,1)} %param.19) | copy-start | bytes 98308
  55.7 1.7 copy-start.2
  57.9 48.6 %copy-start.3 = (bf16[128,3072]{1,0:T(8,128)(2,1)S(1)}, bf16[128,3072]{1,0:T(8,128)(2,1)}, u32[]{:S(2)}) copy-start(bf16[128,3072]{1,0:T(8,128)(2,1)} %param.20) | copy-start | bytes 2359300
  57.9 48.6 %copy-start.4 = (bf16[128,768]{1,0:T(8,128)(2,1)S(1)}, bf16[128,768]{1,0:T(8,128)(2,1)}, u32[]{:S(2)}) copy-start(bf16[128,768]{1,0:T(8,128)(2,1)} %param.21) | copy-start | bytes 589828
  60.1 50.0 %copy-start.5 = (bf16[768,4]{0,1:T(4,128)(2,1)S(1)}, bf16[768,4]{0,1:T(4,128)(2,1)}, u32[]{:S(2)}) copy-start(bf16[768,4]{0,1:T(4,128)(2,1)} %param.24) | copy-start | bytes 18436
  60.1 50.2 %copy-start.7 = (s32[128]{0:T(128)S(1)}, s32[128]{0:T(128)}, u32[]{:S(2)}) copy-start(s32[128]{0:T(128)} %param.25) | copy-start | bytes 1540
Sparse Core Ops, SparseCore 0:
  20.9 34.7 reduce-scatter.4
Sparse Core Ops, SparseCore 1:
  24.1 82.3 all-gather.1
  126.4 133.8 reduce-scatter.6
where the time goes:
time: 269 us
  waiting for transfers between devices  174 us (65%)
  blocking collectives  39.3 us (15%)
  matrix products  22.7 us (8%)
  between operations  18.1 us (7%)
  local copies, waits for them, and re-layouts  11.5 us (4%)
  other arithmetic  3.44 us (1%)
    unnamed x4, waiting for transfers between devices  93.8 us
    all_gather x1, waiting for transfers between devices, local(): lax.all_gather(down_weight, ('dp', 'tensor'), axis=0, tiled=True)  46.4 us
    psum x1, blocking collectives, local(): lax.psum((head_term, loss_part, jnp.sum(validity)), ('dp', 'tensor'))  39.3 us
    reduce_scatter x1, waiting for transfers between devices, local(): lax.psum_scatter(jnp.dot(context, w_out, preferred_element_type=jnp.float...  33.5 us
    dot_general x1, matrix products, local(): jnp.dot(context, w_out, preferred_element_type=jnp.float32)  11.5 us
    unnamed x25, local copies, waits for them, and re-layouts  10.9 us
  transfers between devices with their start and end apart: 3, of which 3 were waited for; matrix products, arithmetic and copies ran while one was open for 2% of the time, Pallas kernels for 0%

commit v1 on v0

--- a/solution.py
+++ b/solution.py
@@ -1,6 +1,8 @@
 import jax
 import jax.numpy as jnp
+import numpy as np
 from jax import lax
+from jax.sharding import Mesh
 from jax.sharding import PartitionSpec as P
 
 SEQ = 512
@@ -9,6 +11,8 @@
 label_weight = 0.5
 teacher_eps = 1e-05
 student_eps = 1e-07
+
+TOKS = ("g", "c", "tensor")
 
 
 def norm_rows(values, gain_vec, epsilon):
@@ -21,6 +25,21 @@
 
 def folder(ordered, row_piece):
     return jnp.dot(ordered, row_piece, preferred_element_type=jnp.float32)
+
+
+def teacher_attention(context, w_out, tok_rows):
+    tensor_size = lax.axis_size("tensor")
+    partial = jnp.dot(context, w_out, preferred_element_type=jnp.float32).astype(jnp.bfloat16)
+    if tensor_size != 2:
+        return lax.psum_scatter(
+            partial, "tensor", scatter_dimension=0, tiled=True
+        ).astype(jnp.float32)
+    me = lax.axis_index("tensor")
+    halves = partial.reshape(2, tok_rows, partial.shape[1])
+    mine = jnp.where(me == 0, halves[0], halves[1])
+    theirs = jnp.where(me == 0, halves[1], halves[0])
+    got = lax.ppermute(theirs, "tensor", perm=[(0, 1), (1, 0)])
+    return mine.astype(jnp.float32) + got.astype(jnp.float32)
 
 
 def local(
@@ -39,22 +58,14 @@
     lengths,
 ):
     tok_rows = teacher_input.shape[0]
-    tensor_size = lax.axis_size("tensor")
-    attention = lax.psum_scatter(
-        jnp.dot(context, w_out, preferred_element_type=jnp.float32).astype(jnp.bfloat16),
-        "tensor",
-        scatter_dimension=0,
-        tiled=True,
-    ).astype(jnp.float32)
+    attention = teacher_attention(context, w_out, tok_rows)
     residual = teacher_input.astype(jnp.float32)
     layer_out = norm_rows(residual + attention, teacher_gain.astype(jnp.float32), teacher_eps)[0]
     blended = (layer_weights[0] * residual + layer_weights[1] * layer_out).astype(jnp.bfloat16)
     teacher_logits = jnp.dot(blended, teacher_head, preferred_element_type=jnp.float32)
     teacher_logp = jax.nn.log_softmax(teacher_logits, axis=-1)
     teacher_prob = jnp.exp(teacher_logp)
-    ffn_out = folder(
-        student_hidden, lax.all_gather(down_weight, ("dp", "tensor"), axis=0, tiled=True)
-    )
+    ffn_out = folder(student_hidden, lax.all_gather(down_weight, TOKS, axis=0, tiled=True))
     student_scale = student_gain.astype(jnp.float32)
     normed, scaled, inverse = norm_rows(
         student_input.astype(jnp.float32) + ffn_out, student_scale, student_eps
@@ -63,7 +74,7 @@
     student_logits = jnp.dot(features, student_head, preferred_element_type=jnp.float32)
     student_logp = jax.nn.log_softmax(student_logits, axis=-1)
     student_prob = jnp.exp(student_logp)
-    first_token = (lax.axis_index("dp") * tensor_size + lax.axis_index("tensor")) * tok_rows
+    first_token = lax.axis_index(TOKS) * tok_rows
     positions = first_token + jnp.arange(tok_rows, dtype=jnp.int32)
     sentence = positions // SEQ
     matches = sentence[:, None] == jnp.arange(lengths.shape[0], dtype=jnp.int32)[None, :]
@@ -94,39 +105,52 @@
         )
         * inverse
     ).astype(jnp.bfloat16)
+    group = lax.axis_size("g")
+    hidden_cols = student_hidden.shape[1]
+    hidden_split = student_hidden.reshape(tok_rows, group, hidden_cols // group)
+    hidden_split = jnp.transpose(hidden_split, (1, 0, 2))
+    hidden_mine = lax.all_to_all(hidden_split, "g", 0, 0, tiled=True)
+    hidden_mine = hidden_mine.reshape(group * tok_rows, hidden_cols // group)
+    grad_out_group = lax.all_gather(grad_out, "g", axis=0, tiled=True)
+    grad_block = lax.dot_general(
+        hidden_mine, grad_out_group, (((0,), (0,)), ((), ())), preferred_element_type=jnp.float32
+    )
     grad_down = lax.psum_scatter(
-        lax.dot_general(
-            student_hidden, grad_out, (((0,), (0,)), ((), ())), preferred_element_type=jnp.float32
-        ),
-        ("dp", "tensor"),
-        scatter_dimension=0,
-        tiled=True,
+        grad_block, ("c", "tensor"), scatter_dimension=0, tiled=True
     )
-    head_total, loss_total, count_total = lax.psum(
-        (head_term, loss_part, jnp.sum(validity)), ("dp", "tensor")
+    classes = head_term.shape[1]
+    packed = jnp.concatenate(
+        [head_term.reshape(-1), jnp.stack([loss_part, jnp.sum(validity)])]
     )
-    return (grad_down, head_total, loss_total / count_total)
+    packed = lax.psum(packed, TOKS)
+    head_total = packed[: head_term.size].reshape(-1, classes)
+    return (grad_down, head_total, packed[head_term.size] / packed[head_term.size + 1])
 
 
 def solution(mesh):
+    dp = mesh.shape["dp"]
+    tensor = mesh.shape["tensor"]
+    devices = np.asarray(mesh.devices).reshape(dp // 2, 2, tensor)
+    fine = Mesh(devices, TOKS)
+    rows = P(TOKS, None)
     return jax.shard_map(
         local,
-        mesh=mesh,
+        mesh=fine,
         in_specs=(
-            P("dp", "tensor"),
+            P(("g", "c"), "tensor"),
             P("tensor", None),
-            P(("dp", "tensor"), None),
+            rows,
             P(),
             P(),
             P(),
-            P(("dp", "tensor"), None),
-            P(("dp", "tensor"), None),
-            P(("dp", "tensor"), None),
+            rows,
+            rows,
+            rows,
             P(),
             P(),
-            P(("dp", "tensor")),
+            P(TOKS),
             P(),
         ),
-        out_specs=(P(("dp", "tensor"), None), P(), P()),
+        out_specs=(rows, P(), P()),
         check_vma=False,
     )

time: 269 us -> 189 us (0.70)
  waiting for transfers between devices: 174 us -> 66.7 us
  blocking collectives: 39.3 us -> 70.6 us
  local copies, waits for them, and re-layouts: 11.5 us -> 6.52 us
  matrix products: 22.7 us -> 18.3 us
  other arithmetic: 3.44 us -> 7.26 us
  starting transfers between devices: 0.12 us -> 3.08 us
    unnamed x4, waiting for transfers between devices: 93.8 us -> 0.73 us
    reduce_scatter x1 -> x0, waiting for transfers between devices: 33.5 us -> none  [local(): lax.psum_scatter(jnp.dot(context, w_out, preferred_element_type=jnp.float...]
    all_to_all x0 -> x1, blocking collectives: none -> 30.9 us  [local(): hidden_mine = lax.all_to_all(hidden_split, 'g', 0, 0, tiled=True)]
    ppermute x0 -> x1, waiting for transfers between devices: none -> 25.9 us  [teacher_attention(): got = lax.ppermute(theirs, 'tensor', perm=[(0, 1), (1, 0)])]
    unnamed x25, local copies, waits for them, and re-layouts: 10.9 us -> 3 us
    all_gather x1 -> x2, waiting for transfers between devices: 46.4 us -> 40.1 us  [the longest x1 22.5 us: local(): lax.all_gather(down_weight, TOKS, axis=0, tiled=True)]
    dot_general x2, matrix products: 16.7 us -> 10.8 us  [the longest x1 8.41 us: teacher_attention(): jnp.dot(context, w_out, preferred_element_type=jnp.float32)]
    ppermute x0 -> x1, starting transfers between devices: none -> 2.97 us  [teacher_attention(): got = lax.ppermute(theirs, 'tensor', perm=[(0, 1), (1, 0)])]
  transfers between devices with their start and end apart: 3 -> 4, of which waited for: 3 -> 3; matrix products, arithmetic and copies ran while one was open for 2% -> 12% of each run, Pallas kernels for 0% -> 0%
where the time goes in v1:
time: 189 us
  blocking collectives  70.6 us (37%)
  waiting for transfers between devices  66.7 us (35%)
  matrix products  18.3 us (10%)
  between operations  16.4 us (9%)
  other arithmetic  7.26 us (4%)
  local copies, waits for them, and re-layouts  6.52 us (3%)
  starting transfers between devices  3.08 us (2%)
    psum x1, blocking collectives, local(): packed = lax.psum(packed, TOKS)  39.7 us
    all_to_all x1, blocking collectives, local(): hidden_mine = lax.all_to_all(hidden_split, 'g', 0, 0, tiled=True)  30.9 us
    ppermute x1, waiting for transfers between devices, teacher_attention(): got = lax.ppermute(theirs, 'tensor', perm=[(0, 1), (1, 0)])  25.9 us
    all_gather x1, waiting for transfers between devices, local(): lax.all_gather(down_weight, TOKS, axis=0, tiled=True)  22.5 us
    all_gather x1, waiting for transfers between devices, local(): grad_out_group = lax.all_gather(grad_out, 'g', axis=0, tiled=True)  17.6 us
    dot_general x1, matrix products, teacher_attention(): jnp.dot(context, w_out, preferred_element_type=jnp.float32)  8.41 us
  transfers between devices with their start and end apart: 4, of which 3 were waited for; matrix products, arithmetic and copies ran while one was open for 12% of the time, Pallas kernels for 0%

profile of v1, /device:TPU:0, one launch (start us, length us, event | category | flops | bytes accessed | tf_op | source)
XLA Modules:
  0.0 189.0 jit_solution(11257666888015991523)
XLA Ops:
  7.2 0.7 all-gather.3.cloned.1.call-update
  8.0 0.4 copy-done
  8.4 8.4 %convolution_convert_fusion = bf16[256,4096]{1,0:T(8,128)(2,1)S(1)} fusion(bf16[256,2048]{1,0:T(8,128)(2,1)S(1)} %copy-done, bf16[2048,4096]{1,0:T(8,128)(2,1)} %param.15), kind=kOutput, calls=%fused_computation | convolution fusion | flops 4296015872 | bytes 19922944 | tf_op jit(solution)/shard_map/dot_general | solution.py:32
  16.9 1.1 broadcast_select_fusion
  18.0 3.0 %collective-permute-start = (bf16[128,4096]{1,0:T(8,128)(2,1)}, bf16[128,4096]{1,0:T(8,128)(2,1)}, u32[]{:S(2)}, u32[]{:S(2)}) collective-permute-start(bf16[128,4096]{1,0:T(8,128)(2,1)} %broadcast_select_fusion), channel_id=1, source_target_pairs={{0,1},{1,0},{2,3},{3,2},{4,5},{5,4},{6,7},{7,6},{8,9},{9,8},{10,11... | collective-permute-start | bytes 3145736 | tf_op jit(solution)/shard_map/ppermute | solution.py:41
  21.0 0.6 fusion.9
  21.7 25.9 %collective-permute-done = bf16[128,4096]{1,0:T(8,128)(2,1)} collective-permute-done((bf16[128,4096]{1,0:T(8,128)(2,1)}, bf16[128,4096]{1,0:T(8,128)(2,1)}, u32[]{:S(2)}, u32[]{:S(2)}) %collective-permute-start) | collective-permute-done | bytes 1048608 | tf_op jit(solution)/shard_map/ppermute | solution.py:41
  47.6 2.2 %fusion.2 = (f32[128]{0:T(128)S(1)}, bf16[128,4096]{1,0:T(8,128)(2,1)S(1)}) fusion(bf16[128,4096]{1,0:T(8,128)(2,1)} %collective-permute-done, bf16[128,4096]{1,0:T(8,128)(2,1)} %param.16, bf16[256,4096]{1,0:T(8,128)(2,1)S(1)} %convolution_convert_fusion, pred[]{:T(512)S(6)} %eq.35), kind=kLoop, calls=%fused_computation.9 | loop fusion | flops 3669888 | bytes 5243393 | tf_op jit(solution)/shard_map/reduce_sum | solution.py:19
  49.8 1.9 multiply_reduce_fusion
  51.7 3.6 %fusion.11 = (f32[128]{0:T(128)S(1)}, f32[128,4]{0,1:T(4,128)S(1)}) fusion(bf16[4096,4]{0,1:T(4,128)(2,1)S(1)} %copy-done.9, bf16[128,4096]{1,0:T(8,128)(2,1)S(1)} %copy-done.1, bf16[128,4096]{1,0:T(8,128)(2,1)} %collective-permute-done, bf16[128,4096]{1,0:T(8,128)(2,1)S(1)} %get-tuple-element.27, f32[4096]{0:T(1024)S(1)} %convert_element_type.49, ...), kind=kOutput, calls=%fused_computation.47 | convolution fusion | flops 10486144 | bytes 3198472 | tf_op jit(solution)/shard_map/dot_general | solution.py:65
  55.4 22.5 %all-gather.3.cloned.1.call-done = bf16[3072,768]{1,0:T(8,128)(2,1)} async-done(((bf16[96,768]{1,0:T(8,128)(2,1)}), bf16[3072,768]{1,0:T(8,128)(2,1)}) %all-gather.3.cloned.1.call-update) | async-done | bytes 4718608 | tf_op jit(solution)/shard_map/all_gather | solution.py:68
  77.9 3.2 %fusion.10 = (f32[128]{0:T(128)S(1)}, f32[128,768]{1,0:T(8,128)S(1)}) fusion(bf16[128,3072]{1,0:T(8,128)(2,1)S(1)} %copy-done.2, bf16[3072,768]{1,0:T(8,128)(2,1)} %all-gather.3.cloned.1.call-done, bf16[128,768]{1,0:T(8,128)(2,1)S(1)} %copy-done.3), kind=kOutput, calls=%fused_computation.46 | convolution fusion | flops 604274560 | bytes 6095360 | tf_op jit(solution)/shard_map/dot_general | solution.py:27
  81.7 0.6 convert_reduce_fusion
  82.7 0.8 multiply_convert_fusion
  83.7 0.4 copy.30
  84.0 30.9 %all_to_all.5 = bf16[8,128,384]{1,2,0:T(8,128)(2,1)S(1)} all-to-all(bf16[8,128,384]{1,2,0:T(8,128)(2,1)S(1)} %bitcast.23), channel_id=1, replica_groups=mesh['g'=8,'c'=2,'tensor'=2] {'g'}, dimensions={0} | all-to-all | bytes 1572864 | tf_op jit(solution)/shard_map/all_to_all | solution.py:112
  115.3 17.6 %all-gather.5.cloned.1.call-done = bf16[1024,768]{1,0:T(8,128)(2,1)} async-done(((bf16[128,768]{1,0:T(8,128)(2,1)}), bf16[1024,768]{1,0:T(8,128)(2,1)}) %all-gather.5.cloned.1.call-update) | async-done | bytes 1572880 | tf_op jit(solution)/shard_map/all_gather | solution.py:114
  132.9 2.4 %convolution_bitcast_fusion = f32[384,768]{0,1:T(8,128)S(1)} fusion(bf16[1024,768]{1,0:T(8,128)(2,1)} %all-gather.5.cloned.1.call-done, bf16[1024,384]{1,0:T(8,128)(2,1)S(1)} %bitcast.24), kind=kOutput, calls=%fused_computation.6 | convolution fusion | flops 603979776 | bytes 3538944 | tf_op jit(solution)/shard_map/dot_general | solution.py:115
  135.3 1.4 copy.36
  137.2 1.4 concatenate.3
  138.6 39.7 %psum.7 = f32[3074]{0:T(1024)S(1)} all-reduce(f32[3074]{0:T(1024)S(1)} %concatenate.3), channel_id=1, replica_groups=mesh['g'=8,'c'=2,'tensor'=2] {'g','c','tensor'}, use_global_device_ids=true, to_apply=%region_14.16 | all-reduce | flops 3074 | bytes 24592 | tf_op jit(solution)/shard_map/psum | solution.py:125
  178.2 0.4 reshape.104
  178.6 0.8 copy.34
  179.4 0.6 fusion.8
  (50 shorter events, 2.2 us)
Async XLA Ops:
  7.2 1.2 copy-start
  7.2 70.7 %all-gather.3.cloned.1.call-start = ((), (), s32[]{:S(2)}) async-start(), calls=%async_computation.2 | async-start | bytes 4866048 | tf_op jit(solution)/shard_map/all_gather | solution.py:68
  7.9 125.0 %all-gather.5.cloned.1.call-start = ((), (), s32[]{:S(2)}) async-start(), calls=%async_computation.3 | async-start | bytes 1769472 | tf_op jit(solution)/shard_map/all_gather | solution.py:114
  16.8 4.1 %copy-start.7 = (bf16[768]{0:T(1024)(128)(2,1)S(1)}, bf16[768]{0:T(1024)(128)(2,1)}, u32[]{:S(2)}) copy-start(bf16[768]{0:T(1024)(128)(2,1)} %param.23) | copy-start | bytes 4612
  16.8 4.1 %copy-start.5 = (bf16[4096]{0:T(1024)(128)(2,1)S(1)}, bf16[4096]{0:T(1024)(128)(2,1)}, u32[]{:S(2)}) copy-start(bf16[4096]{0:T(1024)(128)(2,1)} %param.17) | copy-start | bytes 24580
  16.8 4.2 %copy-start.8 = (f32[2]{0:T(128)S(1)}, f32[2]{0:T(128)}, u32[]{:S(2)}) copy-start(f32[2]{0:T(128)} %param.18) | copy-start | bytes 28
  16.8 4.7 %copy-start.10 = (s32[8]{0:T(128)S(1)}, s32[8]{0:T(128)}, u32[]{:S(2)}) copy-start(s32[8]{0:T(128)} %param.26) | copy-start | bytes 100
  18.0 29.6 %collective-permute-start = (bf16[128,4096]{1,0:T(8,128)(2,1)}, bf16[128,4096]{1,0:T(8,128)(2,1)}, u32[]{:S(2)}, u32[]{:S(2)}) collective-permute-start(bf16[128,4096]{1,0:T(8,128)(2,1)} %broadcast_select_fusion), channel_id=1, source_target_pairs={{0,1},{1,0},{2,3},{3,2},{4,5},{5,4},{6,7},{7,6},{8,9},{9,8},{10,11... | collective-permute-start | bytes 3145736 | tf_op jit(solution)/shard_map/ppermute | solution.py:41
  21.7 28.2 %copy-start.1 = (bf16[128,4096]{1,0:T(8,128)(2,1)S(1)}, bf16[128,4096]{1,0:T(8,128)(2,1)}, u32[]{:S(2)}) copy-start(bf16[128,4096]{1,0:T(8,128)(2,1)} %param.16) | copy-start | bytes 3145732
  49.8 1.9 %copy-start.9 = (bf16[4096,4]{0,1:T(4,128)(2,1)S(1)}, bf16[4096,4]{0,1:T(4,128)(2,1)}, u32[]{:S(2)}) copy-start(bf16[4096,4]{0,1:T(4,128)(2,1)} %param.19) | copy-start | bytes 98308
  51.7 26.2 %copy-start.2 = (bf16[128,3072]{1,0:T(8,128)(2,1)S(1)}, bf16[128,3072]{1,0:T(8,128)(2,1)}, u32[]{:S(2)}) copy-start(bf16[128,3072]{1,0:T(8,128)(2,1)} %param.20) | copy-start | bytes 2359300
  51.7 26.2 %copy-start.3 = (bf16[128,768]{1,0:T(8,128)(2,1)S(1)}, bf16[128,768]{1,0:T(8,128)(2,1)}, u32[]{:S(2)}) copy-start(bf16[128,768]{1,0:T(8,128)(2,1)} %param.21) | copy-start | bytes 589828
  55.4 26.1 %copy-start.4 = (bf16[768,4]{0,1:T(4,128)(2,1)S(1)}, bf16[768,4]{0,1:T(4,128)(2,1)}, u32[]{:S(2)}) copy-start(bf16[768,4]{0,1:T(4,128)(2,1)} %param.24) | copy-start | bytes 18436
  55.4 26.3 %copy-start.6 = (s32[128]{0:T(128)S(1)}, s32[128]{0:T(128)}, u32[]{:S(2)}) copy-start(s32[128]{0:T(128)} %param.25) | copy-start | bytes 1540
  83.6 97.7 %reduce-scatter.4.cloned.1.call-start = ((), (), s32[]{:S(2)}) async-start(), calls=%async_computation.4 | async-start | bytes 1474560
Sparse Core Ops, SparseCore 0:
  10.9 66.9 all-gather.2
  83.7 49.1 all-gather.4
  136.9 24.5 reduce-scatter.3

commit v2 on v1

--- a/solution.py
+++ b/solution.py
@@ -109,9 +109,16 @@
     hidden_cols = student_hidden.shape[1]
     hidden_split = student_hidden.reshape(tok_rows, group, hidden_cols // group)
     hidden_split = jnp.transpose(hidden_split, (1, 0, 2))
-    hidden_mine = lax.all_to_all(hidden_split, "g", 0, 0, tiled=True)
-    hidden_mine = hidden_mine.reshape(group * tok_rows, hidden_cols // group)
-    grad_out_group = lax.all_gather(grad_out, "g", axis=0, tiled=True)
+    me = lax.axis_index("g")
+    pieces = [hidden_split[me]]
+    for k in range(1, group):
+        send = lax.dynamic_index_in_dim(hidden_split, (me - k) % group, 0, keepdims=False)
+        pieces.append(
+            lax.ppermute(send, "g", perm=[(i, (i - k) % group) for i in range(group)])
+        )
+    hidden_mine = jnp.concatenate(pieces, axis=0)
+    grad_out_group = lax.all_gather(grad_out, "g", axis=0, tiled=False)
+    grad_out_group = jnp.roll(grad_out_group, -me, axis=0).reshape(group * tok_rows, -1)
     grad_block = lax.dot_general(
         hidden_mine, grad_out_group, (((0,), (0,)), ((), ())), preferred_element_type=jnp.float32
     )
@@ -122,7 +129,7 @@
     packed = jnp.concatenate(
         [head_term.reshape(-1), jnp.stack([loss_part, jnp.sum(validity)])]
     )
-    packed = lax.psum(packed, TOKS)
+    packed = lax.psum(lax.psum(packed, "g"), ("c", "tensor"))
     head_total = packed[: head_term.size].reshape(-1, classes)
     return (grad_down, head_total, packed[head_term.size] / packed[head_term.size + 1])
 

time: 189 us -> 200 us (1.058)
  blocking collectives: 70.6 us -> 47.1 us
  waiting for transfers between devices: 66.7 us -> 89.4 us
  starting transfers between devices: 3.08 us -> 13.5 us
    all_to_all x1 -> x0, blocking collectives: 30.9 us -> none  [local(): hidden_mine = lax.all_to_all(hidden_split, 'g', 0, 0, tiled=True)]
    ppermute x0 -> x7, waiting for transfers between devices: none -> 17.9 us  [local(): lax.ppermute(send, 'g', perm=[(i, (i - k) % group) for i in range(group)])]
    ppermute x0 -> x7, starting transfers between devices: none -> 10.4 us  [local(): lax.ppermute(send, 'g', perm=[(i, (i - k) % group) for i in range(group)])]
    psum x1 -> x2, blocking collectives: 39.7 us -> 47.1 us  [local(): packed = lax.psum(lax.psum(packed, 'g'), ('c', 'tensor'))]
    all_gather x1, waiting for transfers between devices: 17.6 us -> 22.4 us  [local(): grad_out_group = lax.all_gather(grad_out, 'g', axis=0, tiled=False)]
  transfers between devices with their start and end apart: 4 -> 11, of which waited for: 3 -> 6; matrix products, arithmetic and copies ran while one was open for 12% -> 12% of each run, Pallas kernels for 0% -> 0%
where the time goes in v2:
time: 200 us
  waiting for transfers between devices  89.4 us (45%)
  blocking collectives  47.1 us (24%)
  matrix products  17.8 us (9%)
  between operations  16.8 us (8%)
  starting transfers between devices  13.5 us (7%)
  other arithmetic  9.23 us (5%)
  local copies, waits for them, and re-layouts  5.97 us (3%)
    psum x2, blocking collectives, local(): packed = lax.psum(lax.psum(packed, 'g'), ('c', 'tensor'))  47.1 us
    ppermute x1, waiting for transfers between devices, teacher_attention(): got = lax.ppermute(theirs, 'tensor', perm=[(0, 1), (1, 0)])  25.9 us
    all_gather x1, waiting for transfers between devices, local(): lax.all_gather(down_weight, TOKS, axis=0, tiled=True)  22.5 us
    all_gather x1, waiting for transfers between devices, local(): grad_out_group = lax.all_gather(grad_out, 'g', axis=0, tiled=False)  22.4 us
    ppermute x7, waiting for transfers between devices, local(): lax.ppermute(send, 'g', perm=[(i, (i - k) % group) for i in range(group)])  17.9 us
    ppermute x7, starting transfers between devices, local(): lax.ppermute(send, 'g', perm=[(i, (i - k) % group) for i in range(group)])  10.4 us
    dot_general x1, matrix products, teacher_attention(): jnp.dot(context, w_out, preferred_element_type=jnp.float32)  8.41 us
  transfers between devices with their start and end apart: 11, of which 6 were waited for; matrix products, arithmetic and copies ran while one was open for 12% of the time, Pallas kernels for 0%

profile of v2, /device:TPU:0, one launch (start us, length us, event | category | flops | bytes accessed | tf_op | source)
XLA Modules:
  0.0 199.8 jit_solution(2542479842686428383)
XLA Ops:
  8.4 8.4 %convolution_convert_fusion = bf16[256,4096]{1,0:T(8,128)(2,1)S(1)} fusion(bf16[256,2048]{1,0:T(8,128)(2,1)S(1)} %copy-done, bf16[2048,4096]{1,0:T(8,128)(2,1)} %param.15), kind=kOutput, calls=%fused_computation | convolution fusion | flops 4296015872 | bytes 19922944 | tf_op jit(solution)/shard_map/dot_general | solution.py:32
  16.9 1.1 broadcast_select_fusion
  18.0 3.0 %collective-permute-start.7 = (bf16[128,4096]{1,0:T(8,128)(2,1)}, bf16[128,4096]{1,0:T(8,128)(2,1)}, u32[]{:S(2)}, u32[]{:S(2)}) collective-permute-start(bf16[128,4096]{1,0:T(8,128)(2,1)} %broadcast_select_fusion), channel_id=1, source_target_pairs={{0,1},{1,0},{2,3},{3,2},{4,5},{5,4},{6,7},{7,6},{8,9},{9,8},{10,11... | collective-permute-start | bytes 3145736 | tf_op jit(solution)/shard_map/ppermute | solution.py:41
  21.7 25.9 %collective-permute-done.7 = bf16[128,4096]{1,0:T(8,128)(2,1)} collective-permute-done((bf16[128,4096]{1,0:T(8,128)(2,1)}, bf16[128,4096]{1,0:T(8,128)(2,1)}, u32[]{:S(2)}, u32[]{:S(2)}) %collective-permute-start.7) | collective-permute-done | bytes 1048608 | tf_op jit(solution)/shard_map/ppermute | solution.py:41
  47.6 2.2 %fusion.3 = (f32[128]{0:T(128)S(1)}, bf16[128,4096]{1,0:T(8,128)(2,1)S(1)}) fusion(bf16[128,4096]{1,0:T(8,128)(2,1)} %collective-permute-done.7, bf16[128,4096]{1,0:T(8,128)(2,1)} %param.16, bf16[256,4096]{1,0:T(8,128)(2,1)S(1)} %convolution_convert_fusion, pred[]{:T(512)S(6)} %eq.46), kind=kLoop, calls=%fused_computation.11 | loop fusion | flops 3669888 | bytes 5243393 | tf_op jit(solution)/shard_map/reduce_sum | solution.py:19
  49.8 1.9 multiply_reduce_fusion
  51.7 3.6 %fusion.12 = (f32[128]{0:T(128)S(1)}, f32[128,4]{0,1:T(4,128)S(1)}) fusion(bf16[4096,4]{0,1:T(4,128)(2,1)S(1)} %copy-done.9, bf16[128,4096]{1,0:T(8,128)(2,1)S(1)} %copy-done.1, bf16[128,4096]{1,0:T(8,128)(2,1)} %collective-permute-done.7, bf16[128,4096]{1,0:T(8,128)(2,1)S(1)} %get-tuple-element.21, f32[4096]{0:T(1024)S(1)} %convert_element_type.49, ...), kind=kOutput, calls=%fused_computation.65 | convolution fusion | flops 10486144 | bytes 3198472 | tf_op jit(solution)/shard_map/dot_general | solution.py:65
  55.4 22.5 %all-gather.4.cloned.1.call-done = bf16[3072,768]{1,0:T(8,128)(2,1)} async-done(((bf16[96,768]{1,0:T(8,128)(2,1)}), bf16[3072,768]{1,0:T(8,128)(2,1)}) %all-gather.4.cloned.1.call-update) | async-done | bytes 4718608 | tf_op jit(solution)/shard_map/all_gather | solution.py:68
  77.9 3.2 %fusion.11 = (f32[128]{0:T(128)S(1)}, f32[128,768]{1,0:T(8,128)S(1)}) fusion(bf16[128,3072]{1,0:T(8,128)(2,1)S(1)} %copy-done.2, bf16[3072,768]{1,0:T(8,128)(2,1)} %all-gather.4.cloned.1.call-done, bf16[128,768]{1,0:T(8,128)(2,1)S(1)} %copy-done.3), kind=kOutput, calls=%fused_computation.64 | convolution fusion | flops 604274560 | bytes 6095360 | tf_op jit(solution)/shard_map/dot_general | solution.py:27
  82.7 0.8 multiply_convert_fusion
  84.4 3.0 %collective-permute-start = (bf16[128,384]{1,0:T(8,128)(2,1)S(1)}, bf16[128,384]{1,0:T(8,128)(2,1)S(1)}, u32[]{:S(2)}, u32[]{:S(2)}) collective-permute-start(bf16[128,384]{1,0:T(8,128)(2,1)S(1)} %bitcast.35), channel_id=1, source_target_pairs={{0,28},{4,0},{8,4},{12,8},{16,12},{20,16},{24,20},{28,24},{1,29},{... | collective-permute-start | bytes 294920 | tf_op jit(solution)/shard_map/ppermute | solution.py:117
  87.6 1.5 collective-permute-start.1
  89.8 1.8 collective-permute-start.3
  91.7 0.9 collective-permute-start.4
  93.0 2.7 %collective-permute-start.5 = (bf16[128,384]{1,0:T(8,128)(2,1)S(1)}, bf16[128,384]{1,0:T(8,128)(2,1)S(1)}, u32[]{:S(2)}, u32[]{:S(2)}) collective-permute-start(bf16[128,384]{1,0:T(8,128)(2,1)S(1)} %bitcast.37), channel_id=1, source_target_pairs={{0,8},{4,12},{8,16},{12,20},{16,24},{20,28},{24,0},{28,4},{1,9},{5... | collective-permute-start | bytes 294920 | tf_op jit(solution)/shard_map/ppermute | solution.py:117
  95.9 1.3 collective-permute-done.2
  97.3 15.5 %collective-permute-done.3 = bf16[128,384]{1,0:T(8,128)(2,1)S(1)} collective-permute-done((bf16[128,384]{1,0:T(8,128)(2,1)S(1)}, bf16[128,384]{1,0:T(8,128)(2,1)S(1)}, u32[]{:S(2)}, u32[]{:S(2)}) %collective-permute-start.3) | collective-permute-done | bytes 98336 | tf_op jit(solution)/shard_map/ppermute | solution.py:117
  112.8 1.1 collective-permute-done.4
  113.9 22.4 %all-gather.6.cloned.1.call-done = bf16[1024,768]{1,0:T(8,128)(2,1)} async-done(((bf16[128,768]{1,0:T(8,128)(2,1)}), bf16[1024,768]{1,0:T(8,128)(2,1)}) %all-gather.6.cloned.1.call-update) | async-done | bytes 1572880 | tf_op jit(solution)/shard_map/all_gather | solution.py:120
  136.3 2.0 fusion.2
  138.3 1.8 fusion.15
  140.6 1.4 concatenate.12
  142.0 35.0 %psum.14 = f32[3074]{0:T(1024)S(1)} all-reduce(f32[3074]{0:T(1024)S(1)} %concatenate.12), channel_id=1, replica_groups=mesh['g'=8,'c'=2,'tensor'=2] {'g'}, use_global_device_ids=true, to_apply=%region_14.16 | all-reduce | flops 3074 | bytes 24592 | tf_op jit(solution)/shard_map/psum | solution.py:132
  176.9 12.1 %psum.15 = f32[3074]{0:T(1024)S(1)} all-reduce(f32[3074]{0:T(1024)S(1)} %psum.14), channel_id=1, replica_groups=mesh['g'=8,'c'=2,'tensor'=2] {'c','tensor'}, use_global_device_ids=true, to_apply=%region_15.17 | all-reduce | flops 3074 | bytes 24592 | tf_op jit(solution)/shard_map/psum | solution.py:132
  (80 shorter events, 7.9 us)
Async XLA Ops:
  7.2 1.2 copy-start
  7.2 70.7 %all-gather.4.cloned.1.call-start = ((), (), s32[]{:S(2)}) async-start(), calls=%async_computation.1 | async-start | bytes 4866048 | tf_op jit(solution)/shard_map/all_gather | solution.py:68
  7.9 128.4 %all-gather.6.cloned.1.call-start = ((), (), s32[]{:S(2)}) async-start(), calls=%async_computation.3 | async-start | bytes 1769472 | tf_op jit(solution)/shard_map/all_gather | solution.py:120
  16.8 4.1 %copy-start.5 = (bf16[4096]{0:T(1024)(128)(2,1)S(1)}, bf16[4096]{0:T(1024)(128)(2,1)}, u32[]{:S(2)}) copy-start(bf16[4096]{0:T(1024)(128)(2,1)} %param.17) | copy-start | bytes 24580
  16.8 4.1 %copy-start.7 = (bf16[768]{0:T(1024)(128)(2,1)S(1)}, bf16[768]{0:T(1024)(128)(2,1)}, u32[]{:S(2)}) copy-start(bf16[768]{0:T(1024)(128)(2,1)} %param.23) | copy-start | bytes 4612
  16.8 4.2 %copy-start.8 = (f32[2]{0:T(128)S(1)}, f32[2]{0:T(128)}, u32[]{:S(2)}) copy-start(f32[2]{0:T(128)} %param.18) | copy-start | bytes 28
  16.8 4.8 %copy-start.10 = (s32[8]{0:T(128)S(1)}, s32[8]{0:T(128)}, u32[]{:S(2)}) copy-start(s32[8]{0:T(128)} %param.26) | copy-start | bytes 100
  18.0 29.6 %collective-permute-start.7 = (bf16[128,4096]{1,0:T(8,128)(2,1)}, bf16[128,4096]{1,0:T(8,128)(2,1)}, u32[]{:S(2)}, u32[]{:S(2)}) collective-permute-start(bf16[128,4096]{1,0:T(8,128)(2,1)} %broadcast_select_fusion), channel_id=1, source_target_pairs={{0,1},{1,0},{2,3},{3,2},{4,5},{5,4},{6,7},{7,6},{8,9},{9,8},{10,11... | collective-permute-start | bytes 3145736 | tf_op jit(solution)/shard_map/ppermute | solution.py:41
  21.7 28.1 %copy-start.1 = (bf16[128,4096]{1,0:T(8,128)(2,1)S(1)}, bf16[128,4096]{1,0:T(8,128)(2,1)}, u32[]{:S(2)}) copy-start(bf16[128,4096]{1,0:T(8,128)(2,1)} %param.16) | copy-start | bytes 3145732
  49.8 1.9 copy-start.9
  51.7 26.2 %copy-start.2 = (bf16[128,3072]{1,0:T(8,128)(2,1)S(1)}, bf16[128,3072]{1,0:T(8,128)(2,1)}, u32[]{:S(2)}) copy-start(bf16[128,3072]{1,0:T(8,128)(2,1)} %param.20) | copy-start | bytes 2359300
  51.7 26.2 %copy-start.3 = (bf16[128,768]{1,0:T(8,128)(2,1)S(1)}, bf16[128,768]{1,0:T(8,128)(2,1)}, u32[]{:S(2)}) copy-start(bf16[128,768]{1,0:T(8,128)(2,1)} %param.21) | copy-start | bytes 589828
  55.4 26.1 %copy-start.4 = (bf16[768,4]{0,1:T(4,128)(2,1)S(1)}, bf16[768,4]{0,1:T(4,128)(2,1)}, u32[]{:S(2)}) copy-start(bf16[768,4]{0,1:T(4,128)(2,1)} %param.24) | copy-start | bytes 18436
  55.4 26.3 %copy-start.6 = (s32[128]{0:T(128)S(1)}, s32[128]{0:T(128)}, u32[]{:S(2)}) copy-start(s32[128]{0:T(128)} %param.25) | copy-start | bytes 1540
  83.6 108.5 %reduce-scatter.2.cloned.1.call-start = ((), (), s32[]{:S(2)}) async-start(), calls=%async_computation.2 | async-start | bytes 1474560 | tf_op jit(solution)/shard_map/reduce_scatter | solution.py:125
  84.4 8.6 %collective-permute-start = (bf16[128,384]{1,0:T(8,128)(2,1)S(1)}, bf16[128,384]{1,0:T(8,128)(2,1)S(1)}, u32[]{:S(2)}, u32[]{:S(2)}) collective-permute-start(bf16[128,384]{1,0:T(8,128)(2,1)S(1)} %bitcast.35), channel_id=1, source_target_pairs={{0,28},{4,0},{8,4},{12,8},{16,12},{20,16},{24,20},{28,24},{1,29},{... | collective-permute-start | bytes 294920 | tf_op jit(solution)/shard_map/ppermute | solution.py:117
  87.6 8.2 %collective-permute-start.1 = (bf16[128,384]{1,0:T(8,128)(2,1)S(1)}, bf16[128,384]{1,0:T(8,128)(2,1)S(1)}, u32[]{:S(2)}, u32[]{:S(2)}) collective-permute-start(bf16[128,384]{1,0:T(8,128)(2,1)S(1)} %bitcast.34), channel_id=1, source_target_pairs={{0,24},{4,28},{8,0},{12,4},{16,8},{20,12},{24,16},{28,20},{1,25},{... | collective-permute-start | bytes 294920 | tf_op jit(solution)/shard_map/ppermute | solution.py:117
  89.2 8.0 %collective-permute-start.2 = (bf16[128,384]{1,0:T(8,128)(2,1)S(1)}, bf16[128,384]{1,0:T(8,128)(2,1)S(1)}, u32[]{:S(2)}, u32[]{:S(2)}) collective-permute-start(bf16[128,384]{1,0:T(8,128)(2,1)S(1)} %bitcast.33), channel_id=1, source_target_pairs={{0,20},{4,24},{8,28},{12,0},{16,4},{20,8},{24,12},{28,16},{1,21},{... | collective-permute-start | bytes 294920 | tf_op jit(solution)/shard_map/ppermute | solution.py:117
  89.8 23.0 %collective-permute-start.3 = (bf16[128,384]{1,0:T(8,128)(2,1)S(1)}, bf16[128,384]{1,0:T(8,128)(2,1)S(1)}, u32[]{:S(2)}, u32[]{:S(2)}) collective-permute-start(bf16[128,384]{1,0:T(8,128)(2,1)S(1)} %bitcast.32), channel_id=1, source_target_pairs={{0,16},{4,20},{8,24},{12,28},{16,0},{20,4},{24,8},{28,12},{1,17},{... | collective-permute-start | bytes 294920 | tf_op jit(solution)/shard_map/ppermute | solution.py:117
  91.7 22.2 %collective-permute-start.4 = (bf16[128,384]{1,0:T(8,128)(2,1)S(1)}, bf16[128,384]{1,0:T(8,128)(2,1)S(1)}, u32[]{:S(2)}, u32[]{:S(2)}) collective-permute-start(bf16[128,384]{1,0:T(8,128)(2,1)S(1)} %bitcast.31), channel_id=1, source_target_pairs={{0,12},{4,16},{8,20},{12,24},{16,28},{20,0},{24,4},{28,8},{1,13},{... | collective-permute-start | bytes 294920 | tf_op jit(solution)/shard_map/ppermute | solution.py:117
  93.0 20.8 %collective-permute-start.5 = (bf16[128,384]{1,0:T(8,128)(2,1)S(1)}, bf16[128,384]{1,0:T(8,128)(2,1)S(1)}, u32[]{:S(2)}, u32[]{:S(2)}) collective-permute-start(bf16[128,384]{1,0:T(8,128)(2,1)S(1)} %bitcast.37), channel_id=1, source_target_pairs={{0,8},{4,12},{8,16},{12,20},{16,24},{20,28},{24,0},{28,4},{1,9},{5... | collective-permute-start | bytes 294920 | tf_op jit(solution)/shard_map/ppermute | solution.py:117
  95.8 18.1 %collective-permute-start.6 = (bf16[128,384]{1,0:T(8,128)(2,1)S(1)}, bf16[128,384]{1,0:T(8,128)(2,1)S(1)}, u32[]{:S(2)}, u32[]{:S(2)}) collective-permute-start(bf16[128,384]{1,0:T(8,128)(2,1)S(1)} %bitcast.36), channel_id=1, source_target_pairs={{0,4},{4,8},{8,12},{12,16},{16,20},{20,24},{24,28},{28,0},{1,5},{5... | collective-permute-start | bytes 294920 | tf_op jit(solution)/shard_map/ppermute | solution.py:117
Sparse Core Ops, SparseCore 0:
  10.9 66.9 all-gather.3
  83.7 52.5 all-gather.5
  140.2 24.5 reduce-scatter.1

commit v3 on v2

--- a/solution.py
+++ b/solution.py
@@ -40,6 +40,21 @@
     theirs = jnp.where(me == 0, halves[1], halves[0])
     got = lax.ppermute(theirs, "tensor", perm=[(0, 1), (1, 0)])
     return mine.astype(jnp.float32) + got.astype(jnp.float32)
+
+
+def butterfly_sum(value, axes):
+    for axis in axes:
+        size = lax.axis_size(axis)
+        if size & (size - 1):
+            value = lax.psum(value, axis)
+            continue
+        step = 1
+        while step < size:
+            value = value + lax.ppermute(
+                value, axis, perm=[(i, i ^ step) for i in range(size)]
+            )
+            step *= 2
+    return value
 
 
 def local(
@@ -129,7 +144,7 @@
     packed = jnp.concatenate(
         [head_term.reshape(-1), jnp.stack([loss_part, jnp.sum(validity)])]
     )
-    packed = lax.psum(lax.psum(packed, "g"), ("c", "tensor"))
+    packed = butterfly_sum(packed, ("tensor", "c", "g"))
     head_total = packed[: head_term.size].reshape(-1, classes)
     return (grad_down, head_total, packed[head_term.size] / packed[head_term.size + 1])
 

time: 200 us -> 173 us (0.86)
  blocking collectives: 47.1 us -> 0 us
  waiting for transfers between devices: 89.4 us -> 103 us
  starting transfers between devices: 13.5 us -> 19.4 us
    psum x2 -> x0, blocking collectives: 47.1 us -> none  [local(): packed = lax.psum(lax.psum(packed, 'g'), ('c', 'tensor'))]
    ppermute x0 -> x5, waiting for transfers between devices: none -> 11.1 us  [butterfly_sum(): lax.ppermute(value, axis, perm=[(i, i ^ step) for i in range(size)])]
    ppermute x0 -> x5, starting transfers between devices: none -> 5.89 us  [butterfly_sum(): lax.ppermute(value, axis, perm=[(i, i ^ step) for i in range(size)])]
    reduce_scatter x1, waiting for transfers between devices: 0.02 us -> 2.78 us  [local(): lax.psum_scatter(grad_block, ('c', 'tensor'), scatter_dimension=0, tiled=...]
  transfers between devices with their start and end apart: 11 -> 16, of which waited for: 6 -> 12; matrix products, arithmetic and copies ran while one was open for 12% -> 13% of each run, Pallas kernels for 0% -> 0%
where the time goes in v3:
time: 173 us
  waiting for transfers between devices  103 us (60%)
  starting transfers between devices  19.4 us (11%)
  matrix products  17.8 us (10%)
  between operations  16.8 us (10%)
  other arithmetic  9.25 us (5%)
  local copies, waits for them, and re-layouts  5.97 us (3%)
    ppermute x1, waiting for transfers between devices, teacher_attention(): got = lax.ppermute(theirs, 'tensor', perm=[(0, 1), (1, 0)])  25.9 us
    all_gather x1, waiting for transfers between devices, local(): lax.all_gather(down_weight, TOKS, axis=0, tiled=True)  22.5 us
    all_gather x1, waiting for transfers between devices, local(): grad_out_group = lax.all_gather(grad_out, 'g', axis=0, tiled=False)  22.4 us
    ppermute x7, waiting for transfers between devices, local(): lax.ppermute(send, 'g', perm=[(i, (i - k) % group) for i in range(group)])  17.9 us
    ppermute x5, waiting for transfers between devices, butterfly_sum(): lax.ppermute(value, axis, perm=[(i, i ^ step) for i in range(size)])  11.1 us
    ppermute x7, starting transfers between devices, local(): lax.ppermute(send, 'g', perm=[(i, (i - k) % group) for i in range(group)])  10.4 us
    dot_general x1, matrix products, teacher_attention(): jnp.dot(context, w_out, preferred_element_type=jnp.float32)  8.41 us
    ppermute x5, starting transfers between devices, butterfly_sum(): lax.ppermute(value, axis, perm=[(i, i ^ step) for i in range(size)])  5.89 us
  transfers between devices with their start and end apart: 16, of which 12 were waited for; matrix products, arithmetic and copies ran while one was open for 13% of the time, Pallas kernels for 0%

profile of v3, /device:TPU:0, one launch (start us, length us, event | category | flops | bytes accessed | tf_op | source)
XLA Modules:
  0.0 172.5 jit_solution(7965506259104192016)
XLA Ops:
  8.4 8.4 %convolution_convert_fusion = bf16[256,4096]{1,0:T(8,128)(2,1)S(1)} fusion(bf16[256,2048]{1,0:T(8,128)(2,1)S(1)} %copy-done, bf16[2048,4096]{1,0:T(8,128)(2,1)} %param.15), kind=kOutput, calls=%fused_computation | convolution fusion | flops 4296015872 | bytes 19922944 | tf_op jit(solution)/shard_map/dot_general | solution.py:32
  18.0 3.0 %collective-permute-start.7 = (bf16[128,4096]{1,0:T(8,128)(2,1)}, bf16[128,4096]{1,0:T(8,128)(2,1)}, u32[]{:S(2)}, u32[]{:S(2)}) collective-permute-start(bf16[128,4096]{1,0:T(8,128)(2,1)} %broadcast_select_fusion), channel_id=1, source_target_pairs={{0,1},{1,0},{2,3},{3,2},{4,5},{5,4},{6,7},{7,6},{8,9},{9,8},{10,11... | collective-permute-start | bytes 3145736 | tf_op jit(solution)/shard_map/ppermute | solution.py:41
  21.7 25.9 %collective-permute-done.7 = bf16[128,4096]{1,0:T(8,128)(2,1)} collective-permute-done((bf16[128,4096]{1,0:T(8,128)(2,1)}, bf16[128,4096]{1,0:T(8,128)(2,1)}, u32[]{:S(2)}, u32[]{:S(2)}) %collective-permute-start.7) | collective-permute-done | bytes 1048608 | tf_op jit(solution)/shard_map/ppermute | solution.py:41
  47.6 2.2 %fusion.3 = (f32[128]{0:T(128)S(1)}, bf16[128,4096]{1,0:T(8,128)(2,1)S(1)}) fusion(bf16[128,4096]{1,0:T(8,128)(2,1)} %collective-permute-done.7, bf16[128,4096]{1,0:T(8,128)(2,1)} %param.16, bf16[256,4096]{1,0:T(8,128)(2,1)S(1)} %convolution_convert_fusion, pred[]{:T(512)S(6)} %eq.46), kind=kLoop, calls=%fused_computation.11 | loop fusion | flops 3669888 | bytes 5243393 | tf_op jit(solution)/shard_map/reduce_sum | solution.py:19
  49.8 1.9 %multiply_reduce_fusion = f32[128]{0:T(128)S(1)} fusion(bf16[128,4096]{1,0:T(8,128)(2,1)} %collective-permute-done.7, bf16[128,4096]{1,0:T(8,128)(2,1)S(1)} %get-tuple-element.21, bf16[128,4096]{1,0:T(8,128)(2,1)S(1)} %copy-done.1, f32[128]{0:T(128)S(1)} %broadcast_multiply_fusion), kind=kLoop, calls=%fused_computation.7 | loop fusion | flops 4194176 | bytes 3146752 | tf_op jit(solution)/shard_map/reduce_sum | solution.py:20
  51.7 3.6 %fusion.12 = (f32[128]{0:T(128)S(1)}, f32[128,4]{0,1:T(4,128)S(1)}) fusion(bf16[4096,4]{0,1:T(4,128)(2,1)S(1)} %copy-done.9, bf16[128,4096]{1,0:T(8,128)(2,1)S(1)} %copy-done.1, bf16[128,4096]{1,0:T(8,128)(2,1)} %collective-permute-done.7, bf16[128,4096]{1,0:T(8,128)(2,1)S(1)} %get-tuple-element.21, f32[4096]{0:T(1024)S(1)} %convert_element_type.49, ...), kind=kOutput, calls=%fused_computation.65 | convolution fusion | flops 10486144 | bytes 3198472 | tf_op jit(solution)/shard_map/dot_general | solution.py:80
  55.4 22.5 %all-gather.4.cloned.1.call-done = bf16[3072,768]{1,0:T(8,128)(2,1)} async-done(((bf16[96,768]{1,0:T(8,128)(2,1)}), bf16[3072,768]{1,0:T(8,128)(2,1)}) %all-gather.4.cloned.1.call-update) | async-done | bytes 4718608 | tf_op jit(solution)/shard_map/all_gather | solution.py:83
  77.9 3.2 %fusion.11 = (f32[128]{0:T(128)S(1)}, f32[128,768]{1,0:T(8,128)S(1)}) fusion(bf16[128,3072]{1,0:T(8,128)(2,1)S(1)} %copy-done.2, bf16[3072,768]{1,0:T(8,128)(2,1)} %all-gather.4.cloned.1.call-done, bf16[128,768]{1,0:T(8,128)(2,1)S(1)} %copy-done.3), kind=kOutput, calls=%fused_computation.64 | convolution fusion | flops 604274560 | bytes 6095360 | tf_op jit(solution)/shard_map/dot_general | solution.py:27
  84.4 3.0 %collective-permute-start = (bf16[128,384]{1,0:T(8,128)(2,1)S(1)}, bf16[128,384]{1,0:T(8,128)(2,1)S(1)}, u32[]{:S(2)}, u32[]{:S(2)}) collective-permute-start(bf16[128,384]{1,0:T(8,128)(2,1)S(1)} %bitcast.35), channel_id=1, source_target_pairs={{0,28},{4,0},{8,4},{12,8},{16,12},{20,16},{24,20},{28,24},{1,29},{... | collective-permute-start | bytes 294920 | tf_op jit(solution)/shard_map/ppermute | solution.py:132
  87.6 1.5 collective-permute-start.1
  89.8 1.8 %collective-permute-start.3 = (bf16[128,384]{1,0:T(8,128)(2,1)S(1)}, bf16[128,384]{1,0:T(8,128)(2,1)S(1)}, u32[]{:S(2)}, u32[]{:S(2)}) collective-permute-start(bf16[128,384]{1,0:T(8,128)(2,1)S(1)} %bitcast.32), channel_id=1, source_target_pairs={{0,16},{4,20},{8,24},{12,28},{16,0},{20,4},{24,8},{28,12},{1,17},{... | collective-permute-start | bytes 294920 | tf_op jit(solution)/shard_map/ppermute | solution.py:132
  93.0 2.7 %collective-permute-start.5 = (bf16[128,384]{1,0:T(8,128)(2,1)S(1)}, bf16[128,384]{1,0:T(8,128)(2,1)S(1)}, u32[]{:S(2)}, u32[]{:S(2)}) collective-permute-start(bf16[128,384]{1,0:T(8,128)(2,1)S(1)} %bitcast.37), channel_id=1, source_target_pairs={{0,8},{4,12},{8,16},{12,20},{16,24},{20,28},{24,0},{28,4},{1,9},{5... | collective-permute-start | bytes 294920 | tf_op jit(solution)/shard_map/ppermute | solution.py:132
  97.3 15.5 %collective-permute-done.3 = bf16[128,384]{1,0:T(8,128)(2,1)S(1)} collective-permute-done((bf16[128,384]{1,0:T(8,128)(2,1)S(1)}, bf16[128,384]{1,0:T(8,128)(2,1)S(1)}, u32[]{:S(2)}, u32[]{:S(2)}) %collective-permute-start.3) | collective-permute-done | bytes 98336 | tf_op jit(solution)/shard_map/ppermute | solution.py:132
  113.9 22.4 %all-gather.6.cloned.1.call-done = bf16[1024,768]{1,0:T(8,128)(2,1)} async-done(((bf16[128,768]{1,0:T(8,128)(2,1)}), bf16[1024,768]{1,0:T(8,128)(2,1)}) %all-gather.6.cloned.1.call-update) | async-done | bytes 1572880 | tf_op jit(solution)/shard_map/all_gather | solution.py:135
  136.3 2.0 %fusion.2 = bf16[8,128,768]{2,1,0:T(8,128)(2,1)S(1)} fusion(s32[]{:T(128)S(6)} %select_n.125, bf16[8,128,768]{2,1,0:T(8,128)(2,1)} %bitcast.30), kind=kLoop, calls=%fused_computation.8 | loop fusion | flops 786432 | bytes 3145732 | tf_op jit(solution)/shard_map/jit(_roll_dynamic)/concatenate | solution.py:136
  138.3 1.8 %fusion.15 = f32[384,768]{1,0:T(8,128)} fusion(bf16[1024,384]{1,0:T(8,128)(2,1)S(1)} %constant_dynamic-update-slice_fusion, bf16[1024,768]{1,0:T(8,128)(2,1)S(1)} %bitcast.28), kind=kOutput, calls=%fused_computation.68 | convolution fusion | flops 603979776 | bytes 3538944 | tf_op jit(solution)/shard_map/dot_general | solution.py:137
  142.0 1.5 collective-permute-start.8
  143.4 2.3 %collective-permute-done.8 = f32[3074]{0:T(1024)S(1)} collective-permute-done((f32[3074]{0:T(1024)S(1)}, f32[3074]{0:T(1024)S(1)}, u32[]{:S(2)}, u32[]{:S(2)}) %collective-permute-start.8) | collective-permute-done | bytes 12328 | tf_op jit(solution)/shard_map/ppermute | solution.py:53
  147.4 3.2 %collective-permute-done.10 = f32[3074]{0:T(1024)S(1)} collective-permute-done((f32[3074]{0:T(1024)S(1)}, f32[3074]{0:T(1024)S(1)}, u32[]{:S(2)}, u32[]{:S(2)}) %collective-permute-start.10) | collective-permute-done | bytes 12328 | tf_op jit(solution)/shard_map/ppermute | solution.py:53
  150.6 1.8 %collective-permute-start.11 = (f32[3074]{0:T(1024)S(1)}, f32[3074]{0:T(1024)S(1)}, u32[]{:S(2)}, u32[]{:S(2)}) collective-permute-start(f32[3074]{0:T(1024)S(1)} %add.181), channel_id=1, source_target_pairs={{0,8},{4,12},{8,0},{12,4},{16,24},{20,28},{24,16},{28,20},{1,9},{5... | collective-permute-start | bytes 36896 | tf_op jit(solution)/shard_map/ppermute | solution.py:53
  152.5 1.9 %collective-permute-done.11 = f32[3074]{0:T(1024)S(1)} collective-permute-done((f32[3074]{0:T(1024)S(1)}, f32[3074]{0:T(1024)S(1)}, u32[]{:S(2)}, u32[]{:S(2)}) %collective-permute-start.11) | collective-permute-done | bytes 12328 | tf_op jit(solution)/shard_map/ppermute | solution.py:53
  154.4 2.1 %collective-permute-start.12 = (f32[3074]{0:T(1024)S(1)}, f32[3074]{0:T(1024)S(1)}, u32[]{:S(2)}, u32[]{:S(2)}) collective-permute-start(f32[3074]{0:T(1024)S(1)} %add.182), channel_id=1, source_target_pairs={{0,16},{4,20},{8,24},{12,28},{16,0},{20,4},{24,8},{28,12},{1,17},{... | collective-permute-start | bytes 36896 | tf_op jit(solution)/shard_map/ppermute | solution.py:53
  156.5 2.5 %collective-permute-done.12 = f32[3074]{0:T(1024)S(1)} collective-permute-done((f32[3074]{0:T(1024)S(1)}, f32[3074]{0:T(1024)S(1)}, u32[]{:S(2)}, u32[]{:S(2)}) %collective-permute-start.12) | collective-permute-done | bytes 12328 | tf_op jit(solution)/shard_map/ppermute | solution.py:53
  162.1 2.8 %reduce-scatter.2.cloned.1.call-done = f32[96,768]{1,0:T(8,128)} async-done(((f32[384,768]{1,0:T(8,128)}), f32[96,768]{1,0:T(8,128)}) %reduce-scatter.2.cloned.1.call-update) | async-done | bytes 294928 | tf_op jit(solution)/shard_map/reduce_scatter | solution.py:140
  (93 shorter events, 16.2 us)
Async XLA Ops:
  7.2 70.7 %all-gather.4.cloned.1.call-start = ((), (), s32[]{:S(2)}) async-start(), calls=%async_computation.1 | async-start | bytes 4866048 | tf_op jit(solution)/shard_map/all_gather | solution.py:83
  7.9 128.4 %all-gather.6.cloned.1.call-start = ((), (), s32[]{:S(2)}) async-start(), calls=%async_computation.3 | async-start | bytes 1769472 | tf_op jit(solution)/shard_map/all_gather | solution.py:135
  16.8 4.1 %copy-start.5 = (bf16[4096]{0:T(1024)(128)(2,1)S(1)}, bf16[4096]{0:T(1024)(128)(2,1)}, u32[]{:S(2)}) copy-start(bf16[4096]{0:T(1024)(128)(2,1)} %param.17) | copy-start | bytes 24580
  16.8 4.2 %copy-start.8 = (f32[2]{0:T(128)S(1)}, f32[2]{0:T(128)}, u32[]{:S(2)}) copy-start(f32[2]{0:T(128)} %param.18) | copy-start | bytes 28
  16.8 4.8 %copy-start.10 = (s32[8]{0:T(128)S(1)}, s32[8]{0:T(128)}, u32[]{:S(2)}) copy-start(s32[8]{0:T(128)} %param.26) | copy-start | bytes 100
  18.0 29.6 %collective-permute-start.7 = (bf16[128,4096]{1,0:T(8,128)(2,1)}, bf16[128,4096]{1,0:T(8,128)(2,1)}, u32[]{:S(2)}, u32[]{:S(2)}) collective-permute-start(bf16[128,4096]{1,0:T(8,128)(2,1)} %broadcast_select_fusion), channel_id=1, source_target_pairs={{0,1},{1,0},{2,3},{3,2},{4,5},{5,4},{6,7},{7,6},{8,9},{9,8},{10,11... | collective-permute-start | bytes 3145736 | tf_op jit(solution)/shard_map/ppermute | solution.py:41
  21.7 28.1 %copy-start.1 = (bf16[128,4096]{1,0:T(8,128)(2,1)S(1)}, bf16[128,4096]{1,0:T(8,128)(2,1)}, u32[]{:S(2)}) copy-start(bf16[128,4096]{1,0:T(8,128)(2,1)} %param.16) | copy-start | bytes 3145732
  51.7 26.2 %copy-start.2 = (bf16[128,3072]{1,0:T(8,128)(2,1)S(1)}, bf16[128,3072]{1,0:T(8,128)(2,1)}, u32[]{:S(2)}) copy-start(bf16[128,3072]{1,0:T(8,128)(2,1)} %param.20) | copy-start | bytes 2359300
  51.7 26.2 %copy-start.3 = (bf16[128,768]{1,0:T(8,128)(2,1)S(1)}, bf16[128,768]{1,0:T(8,128)(2,1)}, u32[]{:S(2)}) copy-start(bf16[128,768]{1,0:T(8,128)(2,1)} %param.21) | copy-start | bytes 589828
  55.4 26.1 %copy-start.4 = (bf16[768,4]{0,1:T(4,128)(2,1)S(1)}, bf16[768,4]{0,1:T(4,128)(2,1)}, u32[]{:S(2)}) copy-start(bf16[768,4]{0,1:T(4,128)(2,1)} %param.24) | copy-start | bytes 18436
  55.4 26.3 %copy-start.6 = (s32[128]{0:T(128)S(1)}, s32[128]{0:T(128)}, u32[]{:S(2)}) copy-start(s32[128]{0:T(128)} %param.25) | copy-start | bytes 1540
  83.6 81.2 %reduce-scatter.2.cloned.1.call-start = ((), (), s32[]{:S(2)}) async-start(), calls=%async_computation.2 | async-start | bytes 1474560 | tf_op jit(solution)/shard_map/reduce_scatter | solution.py:140
  84.4 8.6 %collective-permute-start = (bf16[128,384]{1,0:T(8,128)(2,1)S(1)}, bf16[128,384]{1,0:T(8,128)(2,1)S(1)}, u32[]{:S(2)}, u32[]{:S(2)}) collective-permute-start(bf16[128,384]{1,0:T(8,128)(2,1)S(1)} %bitcast.35), channel_id=1, source_target_pairs={{0,28},{4,0},{8,4},{12,8},{16,12},{20,16},{24,20},{28,24},{1,29},{... | collective-permute-start | bytes 294920 | tf_op jit(solution)/shard_map/ppermute | solution.py:132
  87.6 8.2 %collective-permute-start.1 = (bf16[128,384]{1,0:T(8,128)(2,1)S(1)}, bf16[128,384]{1,0:T(8,128)(2,1)S(1)}, u32[]{:S(2)}, u32[]{:S(2)}) collective-permute-start(bf16[128,384]{1,0:T(8,128)(2,1)S(1)} %bitcast.34), channel_id=1, source_target_pairs={{0,24},{4,28},{8,0},{12,4},{16,8},{20,12},{24,16},{28,20},{1,25},{... | collective-permute-start | bytes 294920 | tf_op jit(solution)/shard_map/ppermute | solution.py:132
  89.2 8.0 %collective-permute-start.2 = (bf16[128,384]{1,0:T(8,128)(2,1)S(1)}, bf16[128,384]{1,0:T(8,128)(2,1)S(1)}, u32[]{:S(2)}, u32[]{:S(2)}) collective-permute-start(bf16[128,384]{1,0:T(8,128)(2,1)S(1)} %bitcast.33), channel_id=1, source_target_pairs={{0,20},{4,24},{8,28},{12,0},{16,4},{20,8},{24,12},{28,16},{1,21},{... | collective-permute-start | bytes 294920 | tf_op jit(solution)/shard_map/ppermute | solution.py:132
  89.8 23.0 %collective-permute-start.3 = (bf16[128,384]{1,0:T(8,128)(2,1)S(1)}, bf16[128,384]{1,0:T(8,128)(2,1)S(1)}, u32[]{:S(2)}, u32[]{:S(2)}) collective-permute-start(bf16[128,384]{1,0:T(8,128)(2,1)S(1)} %bitcast.32), channel_id=1, source_target_pairs={{0,16},{4,20},{8,24},{12,28},{16,0},{20,4},{24,8},{28,12},{1,17},{... | collective-permute-start | bytes 294920 | tf_op jit(solution)/shard_map/ppermute | solution.py:132
  91.7 22.2 %collective-permute-start.4 = (bf16[128,384]{1,0:T(8,128)(2,1)S(1)}, bf16[128,384]{1,0:T(8,128)(2,1)S(1)}, u32[]{:S(2)}, u32[]{:S(2)}) collective-permute-start(bf16[128,384]{1,0:T(8,128)(2,1)S(1)} %bitcast.31), channel_id=1, source_target_pairs={{0,12},{4,16},{8,20},{12,24},{16,28},{20,0},{24,4},{28,8},{1,13},{... | collective-permute-start | bytes 294920 | tf_op jit(solution)/shard_map/ppermute | solution.py:132
  93.0 20.8 %collective-permute-start.5 = (bf16[128,384]{1,0:T(8,128)(2,1)S(1)}, bf16[128,384]{1,0:T(8,128)(2,1)S(1)}, u32[]{:S(2)}, u32[]{:S(2)}) collective-permute-start(bf16[128,384]{1,0:T(8,128)(2,1)S(1)} %bitcast.37), channel_id=1, source_target_pairs={{0,8},{4,12},{8,16},{12,20},{16,24},{20,28},{24,0},{28,4},{1,9},{5... | collective-permute-start | bytes 294920 | tf_op jit(solution)/shard_map/ppermute | solution.py:132
  95.8 18.1 %collective-permute-start.6 = (bf16[128,384]{1,0:T(8,128)(2,1)S(1)}, bf16[128,384]{1,0:T(8,128)(2,1)S(1)}, u32[]{:S(2)}, u32[]{:S(2)}) collective-permute-start(bf16[128,384]{1,0:T(8,128)(2,1)S(1)} %bitcast.36), channel_id=1, source_target_pairs={{0,4},{4,8},{8,12},{12,16},{16,20},{20,24},{24,28},{28,0},{1,5},{5... | collective-permute-start | bytes 294920 | tf_op jit(solution)/shard_map/ppermute | solution.py:132
  142.0 3.7 %collective-permute-start.8 = (f32[3074]{0:T(1024)S(1)}, f32[3074]{0:T(1024)S(1)}, u32[]{:S(2)}, u32[]{:S(2)}) collective-permute-start(f32[3074]{0:T(1024)S(1)} %concatenate.12), channel_id=1, source_target_pairs={{0,1},{1,0},{2,3},{3,2},{4,5},{5,4},{6,7},{7,6},{8,9},{9,8},{10,11... | collective-permute-start | bytes 36896 | tf_op jit(solution)/shard_map/ppermute | solution.py:53
  145.7 1.2 collective-permute-start.9
  146.9 3.7 %collective-permute-start.10 = (f32[3074]{0:T(1024)S(1)}, f32[3074]{0:T(1024)S(1)}, u32[]{:S(2)}, u32[]{:S(2)}) collective-permute-start(f32[3074]{0:T(1024)S(1)} %add.180), channel_id=1, source_target_pairs={{0,4},{4,0},{8,12},{12,8},{16,20},{20,16},{24,28},{28,24},{1,5},{5... | collective-permute-start | bytes 36896 | tf_op jit(solution)/shard_map/ppermute | solution.py:53
  150.6 3.7 %collective-permute-start.11 = (f32[3074]{0:T(1024)S(1)}, f32[3074]{0:T(1024)S(1)}, u32[]{:S(2)}, u32[]{:S(2)}) collective-permute-start(f32[3074]{0:T(1024)S(1)} %add.181), channel_id=1, source_target_pairs={{0,8},{4,12},{8,0},{12,4},{16,24},{20,28},{24,16},{28,20},{1,9},{5... | collective-permute-start | bytes 36896 | tf_op jit(solution)/shard_map/ppermute | solution.py:53
  154.4 4.6 %collective-permute-start.12 = (f32[3074]{0:T(1024)S(1)}, f32[3074]{0:T(1024)S(1)}, u32[]{:S(2)}, u32[]{:S(2)}) collective-permute-start(f32[3074]{0:T(1024)S(1)} %add.182), channel_id=1, source_target_pairs={{0,16},{4,20},{8,24},{12,28},{16,0},{20,4},{24,8},{28,12},{1,17},{... | collective-permute-start | bytes 36896 | tf_op jit(solution)/shard_map/ppermute | solution.py:53
  (3 other events, 7.3 us)
Sparse Core Ops, SparseCore 0:
  10.9 66.9 all-gather.3
  83.7 52.5 all-gather.5
  140.2 24.5 reduce-scatter.1

commit v4 on v3

--- a/solution.py
+++ b/solution.py
@@ -55,6 +55,32 @@
             )
             step *= 2
     return value
+
+
+def butterfly_gather(value, axes):
+    for axis in reversed(axes):
+        size = lax.axis_size(axis)
+        me = lax.axis_index(axis)
+        step = 1
+        while step < size:
+            got = lax.ppermute(value, axis, perm=[(i, i ^ step) for i in range(size)])
+            low = (me & step) == 0
+            value = jnp.where(
+                low, jnp.concatenate([value, got], 0), jnp.concatenate([got, value], 0)
+            )
+            step *= 2
+    return value
+
+
+def split_gather(value, axes):
+    half = value.shape[1] // 2
+    pow2 = all((lax.axis_size(a) & (lax.axis_size(a) - 1)) == 0 for a in axes)
+    if not pow2 or half % 128:
+        return (lax.all_gather(value, axes, axis=0, tiled=True),)
+    return (
+        lax.all_gather(value[:, :half], axes, axis=0, tiled=True),
+        butterfly_gather(value[:, half:], axes),
+    )
 
 
 def local(
@@ -80,7 +106,9 @@
     teacher_logits = jnp.dot(blended, teacher_head, preferred_element_type=jnp.float32)
     teacher_logp = jax.nn.log_softmax(teacher_logits, axis=-1)
     teacher_prob = jnp.exp(teacher_logp)
-    ffn_out = folder(student_hidden, lax.all_gather(down_weight, TOKS, axis=0, tiled=True))
+    ffn_out = jnp.concatenate(
+        [folder(student_hidden, part) for part in split_gather(down_weight, TOKS)], axis=1
+    )
     student_scale = student_gain.astype(jnp.float32)
     normed, scaled, inverse = norm_rows(
         student_input.astype(jnp.float32) + ffn_out, student_scale, student_eps
@@ -132,10 +160,18 @@
             lax.ppermute(send, "g", perm=[(i, (i - k) % group) for i in range(group)])
         )
     hidden_mine = jnp.concatenate(pieces, axis=0)
-    grad_out_group = lax.all_gather(grad_out, "g", axis=0, tiled=False)
-    grad_out_group = jnp.roll(grad_out_group, -me, axis=0).reshape(group * tok_rows, -1)
-    grad_block = lax.dot_general(
-        hidden_mine, grad_out_group, (((0,), (0,)), ((), ())), preferred_element_type=jnp.float32
+    grad_out_parts = split_gather(grad_out, ("g",))
+    grad_block = jnp.concatenate(
+        [
+            lax.dot_general(
+                hidden_mine,
+                jnp.roll(part, -me * tok_rows, axis=0),
+                (((0,), (0,)), ((), ())),
+                preferred_element_type=jnp.float32,
+            )
+            for part in grad_out_parts
+        ],
+        axis=1,
     )
     grad_down = lax.psum_scatter(
         grad_block, ("c", "tensor"), scatter_dimension=0, tiled=True

time: 173 us -> 231 us (1.34)
  blocking collectives: 0 us -> 39.5 us
  local copies, waits for them, and re-layouts: 5.97 us -> 29.9 us
  waiting for transfers between devices: 103 us -> 88.2 us
  starting transfers between devices: 19.4 us -> 27.3 us
    ppermute x0 -> x8, waiting for transfers between devices: none -> 70.7 us  [butterfly_gather(): got = lax.ppermute(value, axis, perm=[(i, i ^ step) for i in range(size)])]
    all_gather x2 -> x1, waiting for transfers between devices: 44.9 us -> 0.02 us  [split_gather(): lax.all_gather(value[:, :half], axes, axis=0, tiled=True)]
    all_gather x0 -> x1, blocking collectives: none -> 39.5 us  [split_gather(): lax.all_gather(value[:, :half], axes, axis=0, tiled=True)]
    ppermute x1, waiting for transfers between devices: 25.9 us -> 0.01 us  [teacher_attention(): got = lax.ppermute(theirs, 'tensor', perm=[(0, 1), (1, 0)])]
    ppermute x7, waiting for transfers between devices: 17.9 us -> 0.02 us  [local(): lax.ppermute(send, 'g', perm=[(i, (i - k) % group) for i in range(group)])]
    another operation x9, local copies, waits for them, and re-layouts: 1.05 us -> 11.8 us
    unnamed x31 -> x36, local copies, waits for them, and re-layouts: 1.74 us -> 12.3 us
    ppermute x0 -> x8, starting transfers between devices: none -> 9.98 us  [butterfly_gather(): got = lax.ppermute(value, axis, perm=[(i, i ^ step) for i in range(size)])]
  transfers between devices with their start and end apart: 16 -> 23, of which waited for: 12 -> 11; matrix products, arithmetic and copies ran while one was open for 13% -> 23% of each run, Pallas kernels for 0% -> 0%
where the time goes in v4:
time: 231 us; the launch traced here: 230 us
  waiting for transfers between devices  88.2 us (38%)
  blocking collectives  39.5 us (17%)
  local copies, waits for them, and re-layouts  29.9 us (13%)
  starting transfers between devices  27.3 us (12%)
  matrix products  18.7 us (8%)
  between operations  16.9 us (7%)
  other arithmetic  9.72 us (4%)
    ppermute x8, waiting for transfers between devices, butterfly_gather(): got = lax.ppermute(value, axis, perm=[(i, i ^ step) for i in range(size)])  70.7 us
    all_gather x1, blocking collectives, split_gather(): lax.all_gather(value[:, :half], axes, axis=0, tiled=True)  39.5 us
    ppermute x7, starting transfers between devices, local(): lax.ppermute(send, 'g', perm=[(i, (i - k) % group) for i in range(group)])  12.8 us
    ppermute x5, waiting for transfers between devices, butterfly_sum(): lax.ppermute(value, axis, perm=[(i, i ^ step) for i in range(size)])  12.6 us
    unnamed x36, local copies, waits for them, and re-layouts  12.3 us
    another operation x9, local copies, waits for them, and re-layouts  11.8 us
    ppermute x8, starting transfers between devices, butterfly_gather(): got = lax.ppermute(value, axis, perm=[(i, i ^ step) for i in range(size)])  9.98 us
    dot_general x1, matrix products, teacher_attention(): jnp.dot(context, w_out, preferred_element_type=jnp.float32)  8.41 us
  transfers between devices with their start and end apart: 23, of which 11 were waited for; matrix products, arithmetic and copies ran while one was open for 23% of the time, Pallas kernels for 0%

profile of v4, /device:TPU:0, one launch (start us, length us, event | category | flops | bytes accessed | tf_op | source)
XLA Modules:
  0.0 230.2 jit_solution(3472037084100465693)
XLA Ops:
  8.9 3.0 %collective-permute-start.7 = (bf16[96,384]{1,0:T(8,128)(2,1)}, bf16[96,384]{1,0:T(8,128)(2,1)}, u32[]{:S(2)}, u32[]{:S(2)}) collective-permute-start(bf16[96,384]{1,0:T(8,128)(2,1)} %get-tuple-element.40), channel_id=1, source_target_pairs={{0,1},{1,0},{2,3},{3,2},{4,5},{5,4},{6,7},{7,6},{8,9},{9,8},{10,11... | collective-permute-start | bytes 221192 | tf_op jit(solution)/shard_map/ppermute | solution.py:66
  11.9 8.4 %convolution_convert_fusion = bf16[256,4096]{1,0:T(8,128)(2,1)S(1)} fusion(bf16[256,2048]{1,0:T(8,128)(2,1)S(1)} %copy-done, bf16[2048,4096]{1,0:T(8,128)(2,1)} %param.17), kind=kOutput, calls=%fused_computation | convolution fusion | flops 4296015872 | bytes 19922944 | tf_op jit(solution)/shard_map/dot_general | solution.py:32
  21.5 2.3 %copy.48 = bf16[128,3072]{0,1:T(8,128)(2,1)} copy(bf16[128,3072]{1,0:T(8,128)(2,1)} %param.22) | data formatting | bytes 1572864 | tf_op args[6]
  23.8 2.0 constant_dynamic-slice_fusion
  27.4 5.0 %collective-permute-start = (bf16[128,384]{1,0:T(8,128)(2,1)}, bf16[128,384]{1,0:T(8,128)(2,1)}, u32[]{:S(2)}, u32[]{:S(2)}) collective-permute-start(bf16[128,384]{1,0:T(8,128)(2,1)} %bitcast.36), channel_id=1, source_target_pairs={{0,28},{4,0},{8,4},{12,8},{16,12},{20,16},{24,20},{28,24},{1,29},{... | collective-permute-start | bytes 294920 | tf_op jit(solution)/shard_map/ppermute | solution.py:160
  45.0 2.0 collective-permute-start.9
  47.7 2.6 %collective-permute-start.3 = (bf16[128,384]{1,0:T(8,128)(2,1)}, bf16[128,384]{1,0:T(8,128)(2,1)S(1)}, u32[]{:S(2)}, u32[]{:S(2)}) collective-permute-start(bf16[128,384]{1,0:T(8,128)(2,1)} %bitcast.37), channel_id=1, source_target_pairs={{0,16},{4,20},{8,24},{12,28},{16,0},{20,4},{24,8},{28,12},{1,17},{... | collective-permute-start | bytes 294920 | tf_op jit(solution)/shard_map/ppermute | solution.py:160
  51.8 2.9 %collective-permute-done.9 = bf16[384,384]{1,0:T(8,128)(2,1)S(1)} collective-permute-done((bf16[384,384]{1,0:T(8,128)(2,1)S(1)}, bf16[384,384]{1,0:T(8,128)(2,1)S(1)}, u32[]{:S(2)}, u32[]{:S(2)}) %collective-permute-start.9) | collective-permute-done | bytes 294944 | tf_op jit(solution)/shard_map/ppermute | solution.py:66
  54.6 2.8 %collective-permute-start.4 = (bf16[128,384]{1,0:T(8,128)(2,1)}, bf16[128,384]{1,0:T(8,128)(2,1)S(1)}, u32[]{:S(2)}, u32[]{:S(2)}) collective-permute-start(bf16[128,384]{1,0:T(8,128)(2,1)} %bitcast.33), channel_id=1, source_target_pairs={{0,12},{4,16},{8,20},{12,24},{16,28},{20,0},{24,4},{28,8},{1,13},{... | collective-permute-start | bytes 294920 | tf_op jit(solution)/shard_map/ppermute | solution.py:160
  65.0 1.9 fusion.10
  66.9 14.8 %collective-permute-done.10 = bf16[768,384]{1,0:T(8,128)(2,1)S(1)} collective-permute-done((bf16[768,384]{1,0:T(8,128)(2,1)S(1)}, bf16[768,384]{1,0:T(8,128)(2,1)S(1)}, u32[]{:S(2)}, u32[]{:S(2)}) %collective-permute-start.10) | collective-permute-done | bytes 589856 | tf_op jit(solution)/shard_map/ppermute | solution.py:66
  83.3 1.9 multiply_reduce_fusion
  85.2 3.6 %fusion.32 = (f32[128]{0:T(128)S(1)}, f32[128,4]{0,1:T(4,128)S(1)}) fusion(bf16[4096,4]{0,1:T(4,128)(2,1)S(1)} %copy-done.11, bf16[128,4096]{1,0:T(8,128)(2,1)S(1)} %copy-done.1, bf16[128,4096]{1,0:T(8,128)(2,1)} %collective-permute-done.12, bf16[128,4096]{1,0:T(8,128)(2,1)S(1)} %get-tuple-element.28, f32[4096]{0:T(1024)S(1)} %convert_element_type.49, ...), kind=kOutput, calls=%fused_computation.94 | convolution fusion | flops 10486144 | bytes 3198472 | tf_op jit(solution)/shard_map/dot_general | solution.py:106
  88.8 45.8 %collective-permute-done.11 = bf16[1536,384]{1,0:T(8,128)(2,1)S(1)} collective-permute-done((bf16[1536,384]{1,0:T(8,128)(2,1)S(1)}, bf16[1536,384]{1,0:T(8,128)(2,1)S(1)}, u32[]{:S(2)}, u32[]{:S(2)}) %collective-permute-start.11) | collective-permute-done | bytes 1179680 | tf_op jit(solution)/shard_map/ppermute | solution.py:66
  135.5 2.3 fusion.35
  139.7 2.0 collective-permute-start.13
  141.8 3.0 %collective-permute-done.13 = bf16[128,384]{1,0:T(8,128)(2,1)S(1)} collective-permute-done((bf16[128,384]{1,0:T(8,128)(2,1)S(1)}, bf16[128,384]{1,0:T(8,128)(2,1)S(1)}, u32[]{:S(2)}, u32[]{:S(2)}) %collective-permute-start.13) | collective-permute-done | bytes 98336 | tf_op jit(solution)/shard_map/ppermute | solution.py:66
  146.7 4.3 %collective-permute-done.14 = bf16[256,384]{1,0:T(8,128)(2,1)S(1)} collective-permute-done((bf16[256,384]{1,0:T(8,128)(2,1)S(1)}, bf16[256,384]{1,0:T(8,128)(2,1)S(1)}, u32[]{:S(2)}, u32[]{:S(2)}) %collective-permute-start.14) | collective-permute-done | bytes 196640 | tf_op jit(solution)/shard_map/ppermute | solution.py:66
  151.2 39.5 %all_gather.7 = bf16[1024,384]{1,0:T(8,128)(2,1)S(1)} all-gather(bf16[128,384]{1,0:T(8,128)(2,1)S(1)} %get-tuple-element.37), channel_id=1, replica_groups=mesh['g'=8,'c'=2,'tensor'=2] {'g'}, dimensions={0}, use_global_device_ids=true | all-gather | bytes 884736 | tf_op jit(solution)/shard_map/all_gather | solution.py:81
  198.8 2.1 collective-permute-done.16
  203.6 2.3 %collective-permute-done.18 = f32[3074]{0:T(1024)S(1)} collective-permute-done((f32[3074]{0:T(1024)S(1)}, f32[3074]{0:T(1024)S(1)}, u32[]{:S(2)}, u32[]{:S(2)}) %collective-permute-start.18) | collective-permute-done | bytes 12328 | tf_op jit(solution)/shard_map/ppermute | solution.py:53
  206.1 3.6 %collective-permute-done.19 = f32[3074]{0:T(1024)S(1)} collective-permute-done((f32[3074]{0:T(1024)S(1)}, f32[3074]{0:T(1024)S(1)}, u32[]{:S(2)}, u32[]{:S(2)}) %collective-permute-start.19) | collective-permute-done | bytes 12328 | tf_op jit(solution)/shard_map/ppermute | solution.py:53
  210.9 3.4 %collective-permute-done.20 = f32[3074]{0:T(1024)S(1)} collective-permute-done((f32[3074]{0:T(1024)S(1)}, f32[3074]{0:T(1024)S(1)}, u32[]{:S(2)}, u32[]{:S(2)}) %collective-permute-start.20) | collective-permute-done | bytes 12328 | tf_op jit(solution)/shard_map/ppermute | solution.py:53
  217.4 4.8 %reduce-scatter.4.cloned.1.call-done = f32[96,768]{1,0:T(8,128)} async-done(((f32[384,768]{1,0:T(8,128)}), f32[96,768]{1,0:T(8,128)}) %reduce-scatter.4.cloned.1.call-update) | async-done | bytes 294928
  (124 shorter events, 47.1 us)
Async XLA Ops:
  7.2 128.3 %all-gather.2.cloned.1.call-start = ((), (), s32[]{:S(2)}) async-start(), calls=%async_computation.1 | async-start | bytes 2433024 | tf_op jit(solution)/shard_map/all_gather | solution.py:81
  8.9 28.0 %collective-permute-start.7 = (bf16[96,384]{1,0:T(8,128)(2,1)}, bf16[96,384]{1,0:T(8,128)(2,1)}, u32[]{:S(2)}, u32[]{:S(2)}) collective-permute-start(bf16[96,384]{1,0:T(8,128)(2,1)} %get-tuple-element.40), channel_id=1, source_target_pairs={{0,1},{1,0},{2,3},{3,2},{4,5},{5,4},{6,7},{7,6},{8,9},{9,8},{10,11... | collective-permute-start | bytes 221192 | tf_op jit(solution)/shard_map/ppermute | solution.py:66
  11.9 210.3 %reduce-scatter.4.cloned.1.call-start = ((), (), s32[]{:S(2)}) async-start(), calls=%async_computation.2 | async-start | bytes 1474560
  21.5 43.5 %collective-permute-start.12 = (bf16[128,4096]{1,0:T(8,128)(2,1)}, bf16[128,4096]{1,0:T(8,128)(2,1)}, u32[]{:S(2)}, u32[]{:S(2)}) collective-permute-start(bf16[128,4096]{1,0:T(8,128)(2,1)} %broadcast_select_fusion), channel_id=1, source_target_pairs={{0,1},{1,0},{2,3},{3,2},{4,5},{5,4},{6,7},{7,6},{8,9},{9,8},{10,11... | collective-permute-start | bytes 3145736 | tf_op jit(solution)/shard_map/ppermute | solution.py:41
  27.4 20.2 %collective-permute-start = (bf16[128,384]{1,0:T(8,128)(2,1)}, bf16[128,384]{1,0:T(8,128)(2,1)}, u32[]{:S(2)}, u32[]{:S(2)}) collective-permute-start(bf16[128,384]{1,0:T(8,128)(2,1)} %bitcast.36), channel_id=1, source_target_pairs={{0,28},{4,0},{8,4},{12,8},{16,12},{20,16},{24,20},{28,24},{1,29},{... | collective-permute-start | bytes 294920 | tf_op jit(solution)/shard_map/ppermute | solution.py:160
  34.1 23.5 %collective-permute-start.1 = (bf16[128,384]{1,0:T(8,128)(2,1)}, bf16[128,384]{1,0:T(8,128)(2,1)}, u32[]{:S(2)}, u32[]{:S(2)}) collective-permute-start(bf16[128,384]{1,0:T(8,128)(2,1)} %bitcast.35), channel_id=1, source_target_pairs={{0,24},{4,28},{8,0},{12,4},{16,8},{20,12},{24,16},{28,20},{1,25},{... | collective-permute-start | bytes 294920 | tf_op jit(solution)/shard_map/ppermute | solution.py:160
  36.2 24.6 %collective-permute-start.2 = (bf16[128,384]{1,0:T(8,128)(2,1)}, bf16[128,384]{1,0:T(8,128)(2,1)}, u32[]{:S(2)}, u32[]{:S(2)}) collective-permute-start(bf16[128,384]{1,0:T(8,128)(2,1)} %bitcast.34), channel_id=1, source_target_pairs={{0,20},{4,24},{8,28},{12,0},{16,4},{20,8},{24,12},{28,16},{1,21},{... | collective-permute-start | bytes 294920 | tf_op jit(solution)/shard_map/ppermute | solution.py:160
  38.0 5.9 %collective-permute-start.8 = (bf16[192,384]{1,0:T(8,128)(2,1)S(1)}, bf16[192,384]{1,0:T(8,128)(2,1)}, u32[]{:S(2)}, u32[]{:S(2)}) collective-permute-start(bf16[192,384]{1,0:T(8,128)(2,1)S(1)} %maximum_select_fusion.10), channel_id=1, source_target_pairs={{0,2},{2,0},{1,3},{3,1},{4,6},{6,4},{5,7},{7,5},{8,10},{10,8},{9,1... | collective-permute-start | bytes 442376 | tf_op jit(solution)/shard_map/ppermute | solution.py:66
  45.0 9.6 %collective-permute-start.9 = (bf16[384,384]{1,0:T(8,128)(2,1)S(1)}, bf16[384,384]{1,0:T(8,128)(2,1)S(1)}, u32[]{:S(2)}, u32[]{:S(2)}) collective-permute-start(bf16[384,384]{1,0:T(8,128)(2,1)S(1)} %maximum_select_fusion.8), channel_id=1, source_target_pairs={{0,4},{4,0},{8,12},{12,8},{16,20},{20,16},{24,28},{28,24},{1,5},{5... | collective-permute-start | bytes 884744 | tf_op jit(solution)/shard_map/ppermute | solution.py:66
  47.7 15.1 %collective-permute-start.3 = (bf16[128,384]{1,0:T(8,128)(2,1)}, bf16[128,384]{1,0:T(8,128)(2,1)S(1)}, u32[]{:S(2)}, u32[]{:S(2)}) collective-permute-start(bf16[128,384]{1,0:T(8,128)(2,1)} %bitcast.37), channel_id=1, source_target_pairs={{0,16},{4,20},{8,24},{12,28},{16,0},{20,4},{24,8},{28,12},{1,17},{... | collective-permute-start | bytes 294920 | tf_op jit(solution)/shard_map/ppermute | solution.py:160
  54.6 87.1 %collective-permute-start.4 = (bf16[128,384]{1,0:T(8,128)(2,1)}, bf16[128,384]{1,0:T(8,128)(2,1)S(1)}, u32[]{:S(2)}, u32[]{:S(2)}) collective-permute-start(bf16[128,384]{1,0:T(8,128)(2,1)} %bitcast.33), channel_id=1, source_target_pairs={{0,12},{4,16},{8,20},{12,24},{16,28},{20,0},{24,4},{28,8},{1,13},{... | collective-permute-start | bytes 294920 | tf_op jit(solution)/shard_map/ppermute | solution.py:160
  57.6 24.1 %collective-permute-start.10 = (bf16[768,384]{1,0:T(8,128)(2,1)S(1)}, bf16[768,384]{1,0:T(8,128)(2,1)S(1)}, u32[]{:S(2)}, u32[]{:S(2)}) collective-permute-start(bf16[768,384]{1,0:T(8,128)(2,1)S(1)} %maximum_select_fusion.6), channel_id=1, source_target_pairs={{0,8},{4,12},{8,0},{12,4},{16,24},{20,28},{24,16},{28,20},{1,9},{5... | collective-permute-start | bytes 1769480 | tf_op jit(solution)/shard_map/ppermute | solution.py:66
  60.8 84.0 %collective-permute-start.5 = (bf16[128,384]{1,0:T(8,128)(2,1)S(1)}, bf16[128,384]{1,0:T(8,128)(2,1)}, u32[]{:S(2)}, u32[]{:S(2)}) collective-permute-start(bf16[128,384]{1,0:T(8,128)(2,1)S(1)} %bitcast.32), channel_id=1, source_target_pairs={{0,8},{4,12},{8,16},{12,20},{16,24},{20,28},{24,0},{28,4},{1,9},{5... | collective-permute-start | bytes 294920 | tf_op jit(solution)/shard_map/ppermute | solution.py:160
  62.8 83.0 %collective-permute-start.6 = (bf16[128,384]{1,0:T(8,128)(2,1)S(1)}, bf16[128,384]{1,0:T(8,128)(2,1)}, u32[]{:S(2)}, u32[]{:S(2)}) collective-permute-start(bf16[128,384]{1,0:T(8,128)(2,1)S(1)} %bitcast.31), channel_id=1, source_target_pairs={{0,4},{4,8},{8,12},{12,16},{16,20},{20,24},{24,28},{28,0},{1,5},{5... | collective-permute-start | bytes 294920 | tf_op jit(solution)/shard_map/ppermute | solution.py:160
  82.1 52.5 %collective-permute-start.11 = (bf16[1536,384]{1,0:T(8,128)(2,1)S(1)}, bf16[1536,384]{1,0:T(8,128)(2,1)S(1)}, u32[]{:S(2)}, u32[]{:S(2)}) collective-permute-start(bf16[1536,384]{1,0:T(8,128)(2,1)S(1)} %maximum_select_fusion.2), channel_id=1, source_target_pairs={{0,16},{4,20},{8,24},{12,28},{16,0},{20,4},{24,8},{28,12},{1,17},{... | collective-permute-start | bytes 3538952 | tf_op jit(solution)/shard_map/ppermute | solution.py:66
  85.1 49.4 %copy-start.2 = (bf16[128,3072]{1,0:T(8,128)(2,1)S(1)}, bf16[128,3072]{1,0:T(8,128)(2,1)}, u32[]{:S(2)}) copy-start(bf16[128,3072]{1,0:T(8,128)(2,1)} %param.22) | copy-start | bytes 2359300
  139.7 5.0 %collective-permute-start.13 = (bf16[128,384]{1,0:T(8,128)(2,1)S(1)}, bf16[128,384]{1,0:T(8,128)(2,1)S(1)}, u32[]{:S(2)}, u32[]{:S(2)}) collective-permute-start(bf16[128,384]{1,0:T(8,128)(2,1)S(1)} %get-tuple-element.38), channel_id=1, source_target_pairs={{0,4},{4,0},{8,12},{12,8},{16,20},{20,16},{24,28},{28,24},{1,5},{5... | collective-permute-start | bytes 294920 | tf_op jit(solution)/shard_map/ppermute | solution.py:66
  144.8 6.2 %collective-permute-start.14 = (bf16[256,384]{1,0:T(8,128)(2,1)S(1)}, bf16[256,384]{1,0:T(8,128)(2,1)S(1)}, u32[]{:S(2)}, u32[]{:S(2)}) collective-permute-start(bf16[256,384]{1,0:T(8,128)(2,1)S(1)} %maximum_select_fusion.9), channel_id=1, source_target_pairs={{0,8},{4,12},{8,0},{12,4},{16,24},{20,28},{24,16},{28,20},{1,9},{5... | collective-permute-start | bytes 589832 | tf_op jit(solution)/shard_map/ppermute | solution.py:66
  151.1 41.0 %collective-permute-start.15 = (bf16[512,384]{1,0:T(8,128)(2,1)S(1)}, bf16[512,384]{1,0:T(8,128)(2,1)S(1)}, u32[]{:S(2)}, u32[]{:S(2)}) collective-permute-start(bf16[512,384]{1,0:T(8,128)(2,1)S(1)} %maximum_select_fusion.7), channel_id=1, source_target_pairs={{0,16},{4,20},{8,24},{12,28},{16,0},{20,4},{24,8},{28,12},{1,17},{... | collective-permute-start | bytes 1179656 | tf_op jit(solution)/shard_map/ppermute | solution.py:66
  197.2 3.7 %collective-permute-start.16 = (f32[3074]{0:T(1024)S(1)}, f32[3074]{0:T(1024)S(1)}, u32[]{:S(2)}, u32[]{:S(2)}) collective-permute-start(f32[3074]{0:T(1024)S(1)} %concatenate.82), channel_id=1, source_target_pairs={{0,1},{1,0},{2,3},{3,2},{4,5},{5,4},{6,7},{7,6},{8,9},{9,8},{10,11... | collective-permute-start | bytes 36896 | tf_op jit(solution)/shard_map/ppermute | solution.py:53
  201.0 1.2 collective-permute-start.17
  202.2 3.7 %collective-permute-start.18 = (f32[3074]{0:T(1024)S(1)}, f32[3074]{0:T(1024)S(1)}, u32[]{:S(2)}, u32[]{:S(2)}) collective-permute-start(f32[3074]{0:T(1024)S(1)} %add.176), channel_id=1, source_target_pairs={{0,4},{4,0},{8,12},{12,8},{16,20},{20,16},{24,28},{28,24},{1,5},{5... | collective-permute-start | bytes 36896 | tf_op jit(solution)/shard_map/ppermute | solution.py:53
  205.9 3.7 %collective-permute-start.19 = (f32[3074]{0:T(1024)S(1)}, f32[3074]{0:T(1024)S(1)}, u32[]{:S(2)}, u32[]{:S(2)}) collective-permute-start(f32[3074]{0:T(1024)S(1)} %add.177), channel_id=1, source_target_pairs={{0,8},{4,12},{8,0},{12,4},{16,24},{20,28},{24,16},{28,20},{1,9},{5... | collective-permute-start | bytes 36896 | tf_op jit(solution)/shard_map/ppermute | solution.py:53
  209.7 4.6 %collective-permute-start.20 = (f32[3074]{0:T(1024)S(1)}, f32[3074]{0:T(1024)S(1)}, u32[]{:S(2)}, u32[]{:S(2)}) collective-permute-start(f32[3074]{0:T(1024)S(1)} %add.178), channel_id=1, source_target_pairs={{0,16},{4,20},{8,24},{12,28},{16,0},{20,4},{24,8},{28,12},{1,17},{... | collective-permute-start | bytes 36896 | tf_op jit(solution)/shard_map/ppermute | solution.py:53
  (12 other events, 141.0 us)
Sparse Core Ops, SparseCore 0:
  12.0 63.2 all-gather.1
  195.5 26.6 reduce-scatter.3

commit v5 on v3

--- a/solution.py
+++ b/solution.py
@@ -74,6 +74,19 @@
 ):
     tok_rows = teacher_input.shape[0]
     attention = teacher_attention(context, w_out, tok_rows)
+    group = lax.axis_size("g")
+    hidden_cols = student_hidden.shape[1]
+    hidden_split = student_hidden.reshape(tok_rows, group, hidden_cols // group)
+    hidden_split = jnp.transpose(hidden_split, (1, 0, 2))
+    me = lax.axis_index("g")
+    pieces = [hidden_split[me]]
+    for k in range(1, group):
+        send = lax.dynamic_index_in_dim(hidden_split, (me - k) % group, 0, keepdims=False)
+        pieces.append(
+            lax.ppermute(send, "g", perm=[(i, (i - k) % group) for i in range(group)])
+        )
+    hidden_mine = jnp.concatenate(pieces, axis=0)
+    hidden_mine, attention = lax.optimization_barrier((hidden_mine, attention))
     residual = teacher_input.astype(jnp.float32)
     layer_out = norm_rows(residual + attention, teacher_gain.astype(jnp.float32), teacher_eps)[0]
     blended = (layer_weights[0] * residual + layer_weights[1] * layer_out).astype(jnp.bfloat16)
@@ -120,20 +133,14 @@
         )
         * inverse
     ).astype(jnp.bfloat16)
-    group = lax.axis_size("g")
-    hidden_cols = student_hidden.shape[1]
-    hidden_split = student_hidden.reshape(tok_rows, group, hidden_cols // group)
-    hidden_split = jnp.transpose(hidden_split, (1, 0, 2))
-    me = lax.axis_index("g")
-    pieces = [hidden_split[me]]
-    for k in range(1, group):
-        send = lax.dynamic_index_in_dim(hidden_split, (me - k) % group, 0, keepdims=False)
-        pieces.append(
-            lax.ppermute(send, "g", perm=[(i, (i - k) % group) for i in range(group)])
-        )
-    hidden_mine = jnp.concatenate(pieces, axis=0)
-    grad_out_group = lax.all_gather(grad_out, "g", axis=0, tiled=False)
-    grad_out_group = jnp.roll(grad_out_group, -me, axis=0).reshape(group * tok_rows, -1)
+    grad_out_group = jnp.concatenate(
+        [grad_out]
+        + [
+            lax.ppermute(grad_out, "g", perm=[(i, (i - k) % group) for i in range(group)])
+            for k in range(1, group)
+        ],
+        axis=0,
+    )
     grad_block = lax.dot_general(
         hidden_mine, grad_out_group, (((0,), (0,)), ((), ())), preferred_element_type=jnp.float32
     )

time: 173 us -> 159 us (0.919)
  waiting for transfers between devices: 103 us -> 72.6 us
  local copies, waits for them, and re-layouts: 5.97 us -> 19.7 us
  starting transfers between devices: 19.4 us -> 26.4 us
  other arithmetic: 9.25 us -> 6.08 us
    ppermute x0 -> x7, waiting for transfers between devices: none -> 29.8 us  [local(): lax.ppermute(grad_out, 'g', perm=[(i, (i - k) % group) for i in range(gro...]
    all_gather x1 -> x0, waiting for transfers between devices: 22.4 us -> none  [local(): grad_out_group = lax.all_gather(grad_out, 'g', axis=0, tiled=False)]
    ppermute x1, waiting for transfers between devices: 25.9 us -> 3.61 us  [teacher_attention(): got = lax.ppermute(theirs, 'tensor', perm=[(0, 1), (1, 0)])]
    ppermute x7, waiting for transfers between devices: 17.9 us -> 5.39 us  [local(): lax.ppermute(send, 'g', perm=[(i, (i - k) % group) for i in range(group)])]
    unnamed x31 -> x37, local copies, waits for them, and re-layouts: 1.74 us -> 11.7 us
    ppermute x0 -> x7, starting transfers between devices: none -> 9.21 us  [local(): lax.ppermute(grad_out, 'g', perm=[(i, (i - k) % group) for i in range(gro...]
    all_gather x1, waiting for transfers between devices: 22.5 us -> 16.9 us  [local(): lax.all_gather(down_weight, TOKS, axis=0, tiled=True)]
    another operation x9, local copies, waits for them, and re-layouts: 1.05 us -> 4.19 us
  transfers between devices with their start and end apart: 16 -> 22, of which waited for: 12 -> 14; matrix products, arithmetic and copies ran while one was open for 13% -> 22% of each run, Pallas kernels for 0% -> 0%
where the time goes in v5:
time: 159 us; the launch traced here: 158 us
  waiting for transfers between devices  72.6 us (46%)
  starting transfers between devices  26.4 us (17%)
  local copies, waits for them, and re-layouts  19.7 us (12%)
  between operations  17 us (11%)
  matrix products  16.3 us (10%)
  other arithmetic  6.08 us (4%)
    ppermute x7, waiting for transfers between devices, local(): lax.ppermute(grad_out, 'g', perm=[(i, (i - k) % group) for i in range(gro...  29.8 us
    all_gather x1, waiting for transfers between devices, local(): lax.all_gather(down_weight, TOKS, axis=0, tiled=True)  16.9 us
    ppermute x5, waiting for transfers between devices, butterfly_sum(): lax.ppermute(value, axis, perm=[(i, i ^ step) for i in range(size)])  13.9 us
    ppermute x7, starting transfers between devices, local(): lax.ppermute(send, 'g', perm=[(i, (i - k) % group) for i in range(group)])  12.5 us
    unnamed x37, local copies, waits for them, and re-layouts  11.7 us
    ppermute x7, starting transfers between devices, local(): lax.ppermute(grad_out, 'g', perm=[(i, (i - k) % group) for i in range(gro...  9.21 us
    dot_general x1, matrix products, teacher_attention(): jnp.dot(context, w_out, preferred_element_type=jnp.float32)  8.45 us
    ppermute x7, waiting for transfers between devices, local(): lax.ppermute(send, 'g', perm=[(i, (i - k) % group) for i in range(group)])  5.39 us
  transfers between devices with their start and end apart: 22, of which 14 were waited for; matrix products, arithmetic and copies ran while one was open for 22% of the time, Pallas kernels for 0%

profile of v5, /device:TPU:0, one launch (start us, length us, event | category | flops | bytes accessed | tf_op | source)
XLA Modules:
  0.0 158.2 jit_solution(7998313243351268975)
XLA Ops:
  10.5 6.0 %collective-permute-start = (bf16[128,384]{1,0:T(8,128)(2,1)}, bf16[128,384]{1,0:T(8,128)(2,1)}, u32[]{:S(2)}, u32[]{:S(2)}) collective-permute-start(bf16[128,384]{1,0:T(8,128)(2,1)} %bitcast.2), channel_id=1, source_target_pairs={{0,28},{4,0},{8,4},{12,8},{16,12},{20,16},{24,20},{28,24},{1,29},{... | collective-permute-start | bytes 294920 | tf_op jit(solution)/shard_map/ppermute | solution.py:86
  19.1 3.0 %collective-permute-start.3 = (bf16[128,384]{1,0:T(8,128)(2,1)}, bf16[128,384]{1,0:T(8,128)(2,1)}, u32[]{:S(2)}, u32[]{:S(2)}) collective-permute-start(bf16[128,384]{1,0:T(8,128)(2,1)} %bitcast.5), channel_id=1, source_target_pairs={{0,16},{4,20},{8,24},{12,28},{16,0},{20,4},{24,8},{28,12},{1,17},{... | collective-permute-start | bytes 294920 | tf_op jit(solution)/shard_map/ppermute | solution.py:86
  22.2 8.5 %convolution_convert_fusion = bf16[256,4096]{1,0:T(8,128)(2,1)S(1)} fusion(bf16[256,2048]{1,0:T(8,128)(2,1)S(1)} %copy-done, bf16[2048,4096]{1,0:T(8,128)(2,1)} %param.15), kind=kOutput, calls=%fused_computation | convolution fusion | flops 4296015872 | bytes 19922944 | tf_op jit(solution)/shard_map/dot_general | solution.py:32
  39.5 1.9 %collective-permute-start.5 = (bf16[128,384]{1,0:T(8,128)(2,1)S(1)}, bf16[128,384]{1,0:T(8,128)(2,1)S(1)}, u32[]{:S(2)}, u32[]{:S(2)}) collective-permute-start(bf16[128,384]{1,0:T(8,128)(2,1)S(1)} %bitcast.28), channel_id=1, source_target_pairs={{0,8},{4,12},{8,16},{12,20},{16,24},{20,28},{24,0},{28,4},{1,9},{5... | collective-permute-start | bytes 294920 | tf_op jit(solution)/shard_map/ppermute | solution.py:86
  44.0 1.5 constant_dynamic-update-slice_fusion.4
  47.1 5.4 %collective-permute-done.4 = bf16[128,384]{1,0:T(8,128)(2,1)S(1)} collective-permute-done((bf16[128,384]{1,0:T(8,128)(2,1)S(1)}, bf16[128,384]{1,0:T(8,128)(2,1)S(1)}, u32[]{:S(2)}, u32[]{:S(2)}) %collective-permute-start.4) | collective-permute-done | bytes 98336 | tf_op jit(solution)/shard_map/ppermute | solution.py:86
  54.5 3.6 %collective-permute-done.7 = bf16[128,4096]{1,0:T(8,128)(2,1)} collective-permute-done((bf16[128,4096]{1,0:T(8,128)(2,1)}, bf16[128,4096]{1,0:T(8,128)(2,1)}, u32[]{:S(2)}, u32[]{:S(2)}) %collective-permute-start.7) | collective-permute-done | bytes 1048608 | tf_op jit(solution)/shard_map/ppermute | solution.py:41
  58.1 1.6 %convert_add_fusion.1 = f32[128,4096]{1,0:T(8,128)S(1)} fusion(bf16[128,4096]{1,0:T(8,128)(2,1)} %collective-permute-done.7, pred[]{:T(512)S(6)} %eq.40, bf16[256,4096]{1,0:T(8,128)(2,1)S(1)} %convolution_convert_fusion), kind=kLoop, calls=%fused_computation.6 | loop fusion | flops 2097152 | bytes 5242881 | tf_op jit(solution)/shard_map/add | solution.py:42
  60.8 2.1 %fusion.11 = (f32[128]{0:T(128)S(1)}, f32[128,4]{0,1:T(4,128)S(1)}) fusion(bf16[4096,4]{0,1:T(4,128)(2,1)S(1)} %copy-done.10, bf16[128,4096]{1,0:T(8,128)(2,1)S(1)} %copy-done.1, f32[128,4096]{1,0:T(8,128)S(1)} %convert_add_fusion.1, f32[4096]{0:T(1024)S(1)} %convert_element_type.49, f32[128]{0:T(128)S(1)} %add_rsqrt_fusion, ...), kind=kOutput, calls=%fused_computation.70 | convolution fusion | flops 8913280 | bytes 3198472 | tf_op jit(solution)/shard_map/dot_general | solution.py:93
  63.0 16.9 %all-gather.2.cloned.1.call-done = bf16[3072,768]{1,0:T(8,128)(2,1)} async-done(((bf16[96,768]{1,0:T(8,128)(2,1)}), bf16[3072,768]{1,0:T(8,128)(2,1)}) %all-gather.2.cloned.1.call-update) | async-done | bytes 4718608 | tf_op jit(solution)/shard_map/all_gather | solution.py:96
  79.9 3.2 %fusion.10 = (f32[128]{0:T(128)S(1)}, f32[128,768]{1,0:T(8,128)S(1)}) fusion(bf16[128,3072]{1,0:T(8,128)(2,1)S(1)} %copy-done.2, bf16[3072,768]{1,0:T(8,128)(2,1)} %all-gather.2.cloned.1.call-done, bf16[128,768]{1,0:T(8,128)(2,1)S(1)} %copy-done.4), kind=kOutput, calls=%fused_computation.69 | convolution fusion | flops 604274560 | bytes 6095360 | tf_op jit(solution)/shard_map/dot_general | solution.py:27
  84.9 3.0 %collective-permute-start.8 = (bf16[128,768]{1,0:T(8,128)(2,1)S(1)}, bf16[128,768]{1,0:T(8,128)(2,1)S(1)}, u32[]{:S(2)}, u32[]{:S(2)}) collective-permute-start(bf16[128,768]{1,0:T(8,128)(2,1)S(1)} %get-tuple-element.25), channel_id=1, source_target_pairs={{0,28},{4,0},{8,4},{12,8},{16,12},{20,16},{24,20},{28,24},{1,29},{... | collective-permute-start | bytes 589832 | tf_op jit(solution)/shard_map/ppermute | solution.py:139
  89.8 1.7 %collective-permute-start.11 = (bf16[128,768]{1,0:T(8,128)(2,1)S(1)}, bf16[128,768]{1,0:T(8,128)(2,1)S(1)}, u32[]{:S(2)}, u32[]{:S(2)}) collective-permute-start(bf16[128,768]{1,0:T(8,128)(2,1)S(1)} %get-tuple-element.25), channel_id=1, source_target_pairs={{0,16},{4,20},{8,24},{12,28},{16,0},{20,4},{24,8},{28,12},{1,17},{... | collective-permute-start | bytes 589832 | tf_op jit(solution)/shard_map/ppermute | solution.py:139
  93.3 1.8 %collective-permute-start.13 = (bf16[128,768]{1,0:T(8,128)(2,1)S(1)}, bf16[128,768]{1,0:T(8,128)(2,1)S(1)}, u32[]{:S(2)}, u32[]{:S(2)}) collective-permute-start(bf16[128,768]{1,0:T(8,128)(2,1)S(1)} %get-tuple-element.25), channel_id=1, source_target_pairs={{0,8},{4,12},{8,16},{12,20},{16,24},{20,28},{24,0},{28,4},{1,9},{5... | collective-permute-start | bytes 589832 | tf_op jit(solution)/shard_map/ppermute | solution.py:139
  95.1 2.5 %collective-permute-done.9 = bf16[128,768]{1,0:T(8,128)(2,1)S(1)} collective-permute-done((bf16[128,768]{1,0:T(8,128)(2,1)S(1)}, bf16[128,768]{1,0:T(8,128)(2,1)S(1)}, u32[]{:S(2)}, u32[]{:S(2)}) %collective-permute-start.9) | collective-permute-done | bytes 196640 | tf_op jit(solution)/shard_map/ppermute | solution.py:139
  97.5 4.2 %collective-permute-done.10 = bf16[128,768]{1,0:T(8,128)(2,1)S(1)} collective-permute-done((bf16[128,768]{1,0:T(8,128)(2,1)S(1)}, bf16[128,768]{1,0:T(8,128)(2,1)S(1)}, u32[]{:S(2)}, u32[]{:S(2)}) %collective-permute-start.10) | collective-permute-done | bytes 196640 | tf_op jit(solution)/shard_map/ppermute | solution.py:139
  101.8 21.9 %collective-permute-done.11 = bf16[128,768]{1,0:T(8,128)(2,1)S(1)} collective-permute-done((bf16[128,768]{1,0:T(8,128)(2,1)S(1)}, bf16[128,768]{1,0:T(8,128)(2,1)S(1)}, u32[]{:S(2)}, u32[]{:S(2)}) %collective-permute-start.11) | collective-permute-done | bytes 196640 | tf_op jit(solution)/shard_map/ppermute | solution.py:139
  124.1 1.8 %fusion.14 = f32[384,768]{1,0:T(8,128)} fusion(bf16[1024,384]{1,0:T(8,128)(2,1)S(1)} %copy-done.3, bf16[1024,768]{1,0:T(8,128)(2,1)S(1)} %constant_dynamic-update-slice_fusion.7), kind=kOutput, calls=%fused_computation.73 | convolution fusion | flops 603979776 | bytes 3538944 | tf_op jit(solution)/shard_map/dot_general | solution.py:144
  129.3 2.3 %collective-permute-done.15 = f32[3074]{0:T(1024)S(1)} collective-permute-done((f32[3074]{0:T(1024)S(1)}, f32[3074]{0:T(1024)S(1)}, u32[]{:S(2)}, u32[]{:S(2)}) %collective-permute-start.15) | collective-permute-done | bytes 12328 | tf_op jit(solution)/shard_map/ppermute | solution.py:53
  132.8 3.7 %collective-permute-done.17 = f32[3074]{0:T(1024)S(1)} collective-permute-done((f32[3074]{0:T(1024)S(1)}, f32[3074]{0:T(1024)S(1)}, u32[]{:S(2)}, u32[]{:S(2)}) %collective-permute-start.17) | collective-permute-done | bytes 12328 | tf_op jit(solution)/shard_map/ppermute | solution.py:53
  136.5 3.7 %collective-permute-done.18 = f32[3074]{0:T(1024)S(1)} collective-permute-done((f32[3074]{0:T(1024)S(1)}, f32[3074]{0:T(1024)S(1)}, u32[]{:S(2)}, u32[]{:S(2)}) %collective-permute-start.18) | collective-permute-done | bytes 12328 | tf_op jit(solution)/shard_map/ppermute | solution.py:53
  140.2 1.6 %collective-permute-start.19 = (f32[3074]{0:T(1024)S(1)}, f32[3074]{0:T(1024)S(1)}, u32[]{:S(2)}, u32[]{:S(2)}) collective-permute-start(f32[3074]{0:T(1024)S(1)} %add.170), channel_id=1, source_target_pairs={{0,16},{4,20},{8,24},{12,28},{16,0},{20,4},{24,8},{28,12},{1,17},{... | collective-permute-start | bytes 36896 | tf_op jit(solution)/shard_map/ppermute | solution.py:53
  141.9 3.0 %collective-permute-done.19 = f32[3074]{0:T(1024)S(1)} collective-permute-done((f32[3074]{0:T(1024)S(1)}, f32[3074]{0:T(1024)S(1)}, u32[]{:S(2)}, u32[]{:S(2)}) %collective-permute-start.19) | collective-permute-done | bytes 12328 | tf_op jit(solution)/shard_map/ppermute | solution.py:53
  147.9 2.2 %reduce-scatter.2.cloned.1.call-done = f32[96,768]{1,0:T(8,128)} async-done(((f32[384,768]{1,0:T(8,128)}), f32[96,768]{1,0:T(8,128)}) %reduce-scatter.2.cloned.1.call-update) | async-done | bytes 294928 | tf_op jit(solution)/shard_map/reduce_scatter | solution.py:147
  (111 shorter events, 33.9 us)
Async XLA Ops:
  7.2 72.7 %all-gather.2.cloned.1.call-start = ((), (), s32[]{:S(2)}) async-start(), calls=%async_computation.1 | async-start | bytes 4866048 | tf_op jit(solution)/shard_map/all_gather | solution.py:96
  7.9 142.3 %reduce-scatter.2.cloned.1.call-start = ((), (), s32[]{:S(2)}) async-start(), calls=%async_computation.2 | async-start | bytes 1474560 | tf_op jit(solution)/shard_map/reduce_scatter | solution.py:147
  10.5 27.4 %collective-permute-start = (bf16[128,384]{1,0:T(8,128)(2,1)}, bf16[128,384]{1,0:T(8,128)(2,1)}, u32[]{:S(2)}, u32[]{:S(2)}) collective-permute-start(bf16[128,384]{1,0:T(8,128)(2,1)} %bitcast.2), channel_id=1, source_target_pairs={{0,28},{4,0},{8,4},{12,8},{16,12},{20,16},{24,20},{28,24},{1,29},{... | collective-permute-start | bytes 294920 | tf_op jit(solution)/shard_map/ppermute | solution.py:86
  17.2 22.3 %collective-permute-start.1 = (bf16[128,384]{1,0:T(8,128)(2,1)}, bf16[128,384]{1,0:T(8,128)(2,1)}, u32[]{:S(2)}, u32[]{:S(2)}) collective-permute-start(bf16[128,384]{1,0:T(8,128)(2,1)} %bitcast.3), channel_id=1, source_target_pairs={{0,24},{4,28},{8,0},{12,4},{16,8},{20,12},{24,16},{28,20},{1,25},{... | collective-permute-start | bytes 294920 | tf_op jit(solution)/shard_map/ppermute | solution.py:86
  18.4 24.5 %collective-permute-start.2 = (bf16[128,384]{1,0:T(8,128)(2,1)}, bf16[128,384]{1,0:T(8,128)(2,1)}, u32[]{:S(2)}, u32[]{:S(2)}) collective-permute-start(bf16[128,384]{1,0:T(8,128)(2,1)} %bitcast.4), channel_id=1, source_target_pairs={{0,20},{4,24},{8,28},{12,0},{16,4},{20,8},{24,12},{28,16},{1,21},{... | collective-permute-start | bytes 294920 | tf_op jit(solution)/shard_map/ppermute | solution.py:86
  19.1 26.5 %collective-permute-start.3 = (bf16[128,384]{1,0:T(8,128)(2,1)}, bf16[128,384]{1,0:T(8,128)(2,1)}, u32[]{:S(2)}, u32[]{:S(2)}) collective-permute-start(bf16[128,384]{1,0:T(8,128)(2,1)} %bitcast.5), channel_id=1, source_target_pairs={{0,16},{4,20},{8,24},{12,28},{16,0},{20,4},{24,8},{28,12},{1,17},{... | collective-permute-start | bytes 294920 | tf_op jit(solution)/shard_map/ppermute | solution.py:86
  31.8 26.3 %collective-permute-start.7 = (bf16[128,4096]{1,0:T(8,128)(2,1)}, bf16[128,4096]{1,0:T(8,128)(2,1)}, u32[]{:S(2)}, u32[]{:S(2)}) collective-permute-start(bf16[128,4096]{1,0:T(8,128)(2,1)} %broadcast_select_fusion), channel_id=1, source_target_pairs={{0,1},{1,0},{2,3},{3,2},{4,5},{5,4},{6,7},{7,6},{8,9},{9,8},{10,11... | collective-permute-start | bytes 3145736 | tf_op jit(solution)/shard_map/ppermute | solution.py:41
  37.9 14.6 %collective-permute-start.4 = (bf16[128,384]{1,0:T(8,128)(2,1)S(1)}, bf16[128,384]{1,0:T(8,128)(2,1)S(1)}, u32[]{:S(2)}, u32[]{:S(2)}) collective-permute-start(bf16[128,384]{1,0:T(8,128)(2,1)S(1)} %bitcast.29), channel_id=1, source_target_pairs={{0,12},{4,16},{8,20},{12,24},{16,28},{20,0},{24,4},{28,8},{1,13},{... | collective-permute-start | bytes 294920 | tf_op jit(solution)/shard_map/ppermute | solution.py:86
  39.5 13.7 %collective-permute-start.5 = (bf16[128,384]{1,0:T(8,128)(2,1)S(1)}, bf16[128,384]{1,0:T(8,128)(2,1)S(1)}, u32[]{:S(2)}, u32[]{:S(2)}) collective-permute-start(bf16[128,384]{1,0:T(8,128)(2,1)S(1)} %bitcast.28), channel_id=1, source_target_pairs={{0,8},{4,12},{8,16},{12,20},{16,24},{20,28},{24,0},{28,4},{1,9},{5... | collective-permute-start | bytes 294920 | tf_op jit(solution)/shard_map/ppermute | solution.py:86
  42.9 10.9 %collective-permute-start.6 = (bf16[128,384]{1,0:T(8,128)(2,1)S(1)}, bf16[128,384]{1,0:T(8,128)(2,1)S(1)}, u32[]{:S(2)}, u32[]{:S(2)}) collective-permute-start(bf16[128,384]{1,0:T(8,128)(2,1)S(1)} %bitcast.27), channel_id=1, source_target_pairs={{0,4},{4,8},{8,12},{12,16},{16,20},{20,24},{24,28},{28,0},{1,5},{5... | collective-permute-start | bytes 294920 | tf_op jit(solution)/shard_map/ppermute | solution.py:86
  63.0 20.7 %copy-start.7 = (s32[128]{0:T(128)S(1)}, s32[128]{0:T(128)}, u32[]{:S(2)}) copy-start(s32[128]{0:T(128)} %param.25) | copy-start | bytes 1540
  84.7 39.4 %copy-start.3 = (bf16[1024,384]{1,0:T(8,128)(2,1)S(1)}, bf16[1024,384]{1,0:T(8,128)(2,1)}, u32[]{:S(2)}) copy-start(bf16[1024,384]{1,0:T(8,128)(2,1)} %constant_dynamic-update-slice_fusion) | copy-start | bytes 2359300
  84.9 8.3 %collective-permute-start.8 = (bf16[128,768]{1,0:T(8,128)(2,1)S(1)}, bf16[128,768]{1,0:T(8,128)(2,1)S(1)}, u32[]{:S(2)}, u32[]{:S(2)}) collective-permute-start(bf16[128,768]{1,0:T(8,128)(2,1)S(1)} %get-tuple-element.25), channel_id=1, source_target_pairs={{0,28},{4,0},{8,4},{12,8},{16,12},{20,16},{24,20},{28,24},{1,29},{... | collective-permute-start | bytes 589832 | tf_op jit(solution)/shard_map/ppermute | solution.py:139
  88.0 9.5 %collective-permute-start.9 = (bf16[128,768]{1,0:T(8,128)(2,1)S(1)}, bf16[128,768]{1,0:T(8,128)(2,1)S(1)}, u32[]{:S(2)}, u32[]{:S(2)}) collective-permute-start(bf16[128,768]{1,0:T(8,128)(2,1)S(1)} %get-tuple-element.25), channel_id=1, source_target_pairs={{0,24},{4,28},{8,0},{12,4},{16,8},{20,12},{24,16},{28,20},{1,25},{... | collective-permute-start | bytes 589832 | tf_op jit(solution)/shard_map/ppermute | solution.py:139
  89.4 12.4 %collective-permute-start.10 = (bf16[128,768]{1,0:T(8,128)(2,1)S(1)}, bf16[128,768]{1,0:T(8,128)(2,1)S(1)}, u32[]{:S(2)}, u32[]{:S(2)}) collective-permute-start(bf16[128,768]{1,0:T(8,128)(2,1)S(1)} %get-tuple-element.25), channel_id=1, source_target_pairs={{0,20},{4,24},{8,28},{12,0},{16,4},{20,8},{24,12},{28,16},{1,21},{... | collective-permute-start | bytes 589832 | tf_op jit(solution)/shard_map/ppermute | solution.py:139
  89.8 33.9 %collective-permute-start.11 = (bf16[128,768]{1,0:T(8,128)(2,1)S(1)}, bf16[128,768]{1,0:T(8,128)(2,1)S(1)}, u32[]{:S(2)}, u32[]{:S(2)}) collective-permute-start(bf16[128,768]{1,0:T(8,128)(2,1)S(1)} %get-tuple-element.25), channel_id=1, source_target_pairs={{0,16},{4,20},{8,24},{12,28},{16,0},{20,4},{24,8},{28,12},{1,17},{... | collective-permute-start | bytes 589832 | tf_op jit(solution)/shard_map/ppermute | solution.py:139
  91.5 32.6 %collective-permute-start.12 = (bf16[128,768]{1,0:T(8,128)(2,1)S(1)}, bf16[128,768]{1,0:T(8,128)(2,1)S(1)}, u32[]{:S(2)}, u32[]{:S(2)}) collective-permute-start(bf16[128,768]{1,0:T(8,128)(2,1)S(1)} %get-tuple-element.25), channel_id=1, source_target_pairs={{0,12},{4,16},{8,20},{12,24},{16,28},{20,0},{24,4},{28,8},{1,13},{... | collective-permute-start | bytes 589832 | tf_op jit(solution)/shard_map/ppermute | solution.py:139
  93.3 30.8 %collective-permute-start.13 = (bf16[128,768]{1,0:T(8,128)(2,1)S(1)}, bf16[128,768]{1,0:T(8,128)(2,1)S(1)}, u32[]{:S(2)}, u32[]{:S(2)}) collective-permute-start(bf16[128,768]{1,0:T(8,128)(2,1)S(1)} %get-tuple-element.25), channel_id=1, source_target_pairs={{0,8},{4,12},{8,16},{12,20},{16,24},{20,28},{24,0},{28,4},{1,9},{5... | collective-permute-start | bytes 589832 | tf_op jit(solution)/shard_map/ppermute | solution.py:139
  97.5 26.6 %collective-permute-start.14 = (bf16[128,768]{1,0:T(8,128)(2,1)S(1)}, bf16[128,768]{1,0:T(8,128)(2,1)S(1)}, u32[]{:S(2)}, u32[]{:S(2)}) collective-permute-start(bf16[128,768]{1,0:T(8,128)(2,1)S(1)} %get-tuple-element.25), channel_id=1, source_target_pairs={{0,4},{4,8},{8,12},{12,16},{16,20},{20,24},{24,28},{28,0},{1,5},{5... | collective-permute-start | bytes 589832 | tf_op jit(solution)/shard_map/ppermute | solution.py:139
  127.8 3.7 %collective-permute-start.15 = (f32[3074]{0:T(1024)S(1)}, f32[3074]{0:T(1024)S(1)}, u32[]{:S(2)}, u32[]{:S(2)}) collective-permute-start(f32[3074]{0:T(1024)S(1)} %concatenate.11), channel_id=1, source_target_pairs={{0,1},{1,0},{2,3},{3,2},{4,5},{5,4},{6,7},{7,6},{8,9},{9,8},{10,11... | collective-permute-start | bytes 36896 | tf_op jit(solution)/shard_map/ppermute | solution.py:53
  131.6 1.2 collective-permute-start.16
  132.8 3.7 %collective-permute-start.17 = (f32[3074]{0:T(1024)S(1)}, f32[3074]{0:T(1024)S(1)}, u32[]{:S(2)}, u32[]{:S(2)}) collective-permute-start(f32[3074]{0:T(1024)S(1)} %add.168), channel_id=1, source_target_pairs={{0,4},{4,0},{8,12},{12,8},{16,20},{20,16},{24,28},{28,24},{1,5},{5... | collective-permute-start | bytes 36896 | tf_op jit(solution)/shard_map/ppermute | solution.py:53
  136.5 3.7 %collective-permute-start.18 = (f32[3074]{0:T(1024)S(1)}, f32[3074]{0:T(1024)S(1)}, u32[]{:S(2)}, u32[]{:S(2)}) collective-permute-start(f32[3074]{0:T(1024)S(1)} %add.169), channel_id=1, source_target_pairs={{0,8},{4,12},{8,0},{12,4},{16,24},{20,28},{24,16},{28,20},{1,9},{5... | collective-permute-start | bytes 36896 | tf_op jit(solution)/shard_map/ppermute | solution.py:53
  140.2 4.6 %collective-permute-start.19 = (f32[3074]{0:T(1024)S(1)}, f32[3074]{0:T(1024)S(1)}, u32[]{:S(2)}, u32[]{:S(2)}) collective-permute-start(f32[3074]{0:T(1024)S(1)} %add.170), channel_id=1, source_target_pairs={{0,16},{4,20},{8,24},{12,28},{16,0},{20,4},{24,8},{28,12},{1,17},{... | collective-permute-start | bytes 36896 | tf_op jit(solution)/shard_map/ppermute | solution.py:53
  (9 other events, 98.2 us)
Sparse Core Ops, SparseCore 0:
  10.9 68.9 all-gather.1
  126.1 24.0 reduce-scatter.1

commit v6 on v5

--- a/solution.py
+++ b/solution.py
@@ -12,7 +12,8 @@
 teacher_eps = 1e-05
 student_eps = 1e-07
 
-TOKS = ("g", "c", "tensor")
+TOKS = ("q", "x", "c", "tensor")
+GROUP = ("x", "c", "tensor")
 
 
 def norm_rows(values, gain_vec, epsilon):
@@ -74,16 +75,18 @@
 ):
     tok_rows = teacher_input.shape[0]
     attention = teacher_attention(context, w_out, tok_rows)
-    group = lax.axis_size("g")
+    group = lax.axis_size(GROUP)
+    outer = lax.axis_size("q")
     hidden_cols = student_hidden.shape[1]
-    hidden_split = student_hidden.reshape(tok_rows, group, hidden_cols // group)
-    hidden_split = jnp.transpose(hidden_split, (1, 0, 2))
-    me = lax.axis_index("g")
+    block = hidden_cols // (group * outer)
+    hidden_split = student_hidden.reshape(tok_rows, outer, group, block)
+    hidden_split = jnp.transpose(hidden_split, (2, 0, 1, 3)).reshape(group, tok_rows, outer * block)
+    me = lax.axis_index(GROUP)
     pieces = [hidden_split[me]]
     for k in range(1, group):
         send = lax.dynamic_index_in_dim(hidden_split, (me - k) % group, 0, keepdims=False)
         pieces.append(
-            lax.ppermute(send, "g", perm=[(i, (i - k) % group) for i in range(group)])
+            lax.ppermute(send, GROUP, perm=[(i, (i - k) % group) for i in range(group)])
         )
     hidden_mine = jnp.concatenate(pieces, axis=0)
     hidden_mine, attention = lax.optimization_barrier((hidden_mine, attention))
@@ -136,7 +139,7 @@
     grad_out_group = jnp.concatenate(
         [grad_out]
         + [
-            lax.ppermute(grad_out, "g", perm=[(i, (i - k) % group) for i in range(group)])
+            lax.ppermute(grad_out, GROUP, perm=[(i, (i - k) % group) for i in range(group)])
             for k in range(1, group)
         ],
         axis=0,
@@ -145,13 +148,13 @@
         hidden_mine, grad_out_group, (((0,), (0,)), ((), ())), preferred_element_type=jnp.float32
     )
     grad_down = lax.psum_scatter(
-        grad_block, ("c", "tensor"), scatter_dimension=0, tiled=True
+        grad_block, "q", scatter_dimension=0, tiled=True
     )
     classes = head_term.shape[1]
     packed = jnp.concatenate(
         [head_term.reshape(-1), jnp.stack([loss_part, jnp.sum(validity)])]
     )
-    packed = butterfly_sum(packed, ("tensor", "c", "g"))
+    packed = butterfly_sum(packed, ("tensor", "c", "x", "q"))
     head_total = packed[: head_term.size].reshape(-1, classes)
     return (grad_down, head_total, packed[head_term.size] / packed[head_term.size + 1])
 
@@ -159,14 +162,14 @@
 def solution(mesh):
     dp = mesh.shape["dp"]
     tensor = mesh.shape["tensor"]
-    devices = np.asarray(mesh.devices).reshape(dp // 2, 2, tensor)
+    devices = np.asarray(mesh.devices).reshape(dp // 4, 2, 2, tensor)
     fine = Mesh(devices, TOKS)
     rows = P(TOKS, None)
     return jax.shard_map(
         local,
         mesh=fine,
         in_specs=(
-            P(("g", "c"), "tensor"),
+            P(("q", "x", "c"), "tensor"),
             P("tensor", None),
             rows,
             P(),

time: 159 us -> 144 us (0.906)
  local copies, waits for them, and re-layouts: 19.7 us -> 12.4 us
  waiting for transfers between devices: 72.6 us -> 67.7 us
  starting transfers between devices: 26.4 us -> 22.9 us
    ppermute x14, starting transfers between devices: 21.7 us -> 15.3 us  [the longest x7 7.9 us: local(): lax.ppermute(send, GROUP, perm=[(i, (i - k) % group) for i in range(group)])]
    another operation x9 -> x0, local copies, waits for them, and re-layouts: 4.19 us -> none
    ppermute x1, waiting for transfers between devices: 3.61 us -> 0.01 us  [teacher_attention(): got = lax.ppermute(theirs, 'tensor', perm=[(0, 1), (1, 0)])]
    unnamed x37 -> x45, local copies, waits for them, and re-layouts: 11.7 us -> 8.21 us
    ppermute x5, starting transfers between devices: 3.12 us -> 6.18 us  [butterfly_sum(): lax.ppermute(value, axis, perm=[(i, i ^ step) for i in range(size)])]
    reduce_scatter x1, waiting for transfers between devices: 2.24 us -> 4.73 us  [local(): lax.psum_scatter(grad_block, 'q', scatter_dimension=0, tiled=True)]
    ppermute x14, waiting for transfers between devices: 35.2 us -> 33.3 us  [the longest x7 19.2 us: local(): lax.ppermute(send, GROUP, perm=[(i, (i - k) % group) for i in range(group)])]
  transfers between devices with their start and end apart: 22 -> 22, of which waited for: 14 -> 15; matrix products, arithmetic and copies ran while one was open for 22% -> 19% of each run, Pallas kernels for 0% -> 0%
where the time goes in v6:
time: 144 us; the launch traced here: 143 us
  waiting for transfers between devices  67.7 us (47%)
  starting transfers between devices  22.9 us (16%)
  between operations  17.1 us (12%)
  matrix products  16.3 us (11%)
  local copies, waits for them, and re-layouts  12.4 us (9%)
  other arithmetic  6.83 us (5%)
    ppermute x7, waiting for transfers between devices, local(): lax.ppermute(send, GROUP, perm=[(i, (i - k) % group) for i in range(group)])  19.2 us
    all_gather x1, waiting for transfers between devices, local(): lax.all_gather(down_weight, TOKS, axis=0, tiled=True)  16.1 us
    ppermute x7, waiting for transfers between devices, local(): lax.ppermute(grad_out, GROUP, perm=[(i, (i - k) % group) for i in range(g...  14.1 us
    ppermute x5, waiting for transfers between devices, butterfly_sum(): lax.ppermute(value, axis, perm=[(i, i ^ step) for i in range(size)])  12.8 us
    dot_general x1, matrix products, teacher_attention(): jnp.dot(context, w_out, preferred_element_type=jnp.float32)  8.46 us
    unnamed x45, local copies, waits for them, and re-layouts  8.21 us
    ppermute x7, starting transfers between devices, local(): lax.ppermute(send, GROUP, perm=[(i, (i - k) % group) for i in range(group)])  7.9 us
    ppermute x7, starting transfers between devices, local(): lax.ppermute(grad_out, GROUP, perm=[(i, (i - k) % group) for i in range(g...  7.42 us
  transfers between devices with their start and end apart: 22, of which 15 were waited for; matrix products, arithmetic and copies ran while one was open for 19% of the time, Pallas kernels for 0%

profile of v6, /device:TPU:0, one launch (start us, length us, event | category | flops | bytes accessed | tf_op | source)
XLA Modules:
  0.0 143.2 jit_solution(1859343840226462808)
XLA Ops:
  8.1 1.5 %copy.20 = bf16[128,3072]{0,1:T(8,128)(2,1)S(1)} copy(bf16[128,3072]{1,0:T(8,128)(2,1)} %param.20) | data formatting | bytes 1572864 | tf_op args[6]
  10.6 3.3 %collective-permute-start = (bf16[128,384]{0,1:T(8,128)(2,1)}, bf16[128,384]{0,1:T(8,128)(2,1)}, u32[]{:S(2)}, u32[]{:S(2)}) collective-permute-start(bf16[128,384]{0,1:T(8,128)(2,1)} %get-tuple-element.29), channel_id=1, source_target_pairs={{0,7},{1,0},{2,1},{3,2},{4,3},{5,4},{6,5},{7,6},{8,15},{9,8},{10,9... | collective-permute-start | bytes 294920 | tf_op jit(solution)/shard_map/ppermute | solution.py:89
  16.2 8.5 %convolution_convert_fusion = bf16[256,4096]{1,0:T(8,128)(2,1)S(1)} fusion(bf16[256,2048]{1,0:T(8,128)(2,1)S(1)} %copy-done, bf16[2048,4096]{1,0:T(8,128)(2,1)} %param.15), kind=kOutput, calls=%fused_computation | convolution fusion | flops 4296015872 | bytes 19922944 | tf_op jit(solution)/shard_map/dot_general | solution.py:33
  36.7 18.2 %collective-permute-done.4 = bf16[128,384]{0,1:T(8,128)(2,1)S(1)} collective-permute-done((bf16[128,384]{0,1:T(8,128)(2,1)S(1)}, bf16[128,384]{0,1:T(8,128)(2,1)S(1)}, u32[]{:S(2)}, u32[]{:S(2)}) %collective-permute-start.4) | collective-permute-done | bytes 98336 | tf_op jit(solution)/shard_map/ppermute | solution.py:89
  56.8 1.7 %convert_add_fusion.1 = f32[128,4096]{1,0:T(8,128)S(1)} fusion(bf16[128,4096]{1,0:T(8,128)(2,1)} %collective-permute-done.7, pred[]{:T(512)S(6)} %eq.40, bf16[256,4096]{1,0:T(8,128)(2,1)S(1)} %convolution_convert_fusion), kind=kLoop, calls=%fused_computation.6 | loop fusion | flops 2097152 | bytes 5242881 | tf_op jit(solution)/shard_map/add | solution.py:43
  59.6 2.1 %fusion.11 = (f32[128]{0:T(128)S(1)}, f32[128,4]{0,1:T(4,128)S(1)}) fusion(bf16[4096,4]{0,1:T(4,128)(2,1)S(1)} %copy-done.14, bf16[128,4096]{1,0:T(8,128)(2,1)S(1)} %copy-done.1, f32[128,4096]{1,0:T(8,128)S(1)} %convert_add_fusion.1, f32[4096]{0:T(1024)S(1)} %copy-done.6, f32[128]{0:T(128)S(1)} %add_rsqrt_fusion, f32[128]{0:T(128)S(1)} %broadcast_multiply_fusion, ...), kind=kOutput, calls=%fused_computation.69 | convolution fusion | flops 8913280 | bytes 3198472 | tf_op jit(solution)/shard_map/dot_general | solution.py:96
  61.8 16.1 %all-gather.2.cloned.1.call-done = bf16[3072,768]{1,0:T(8,128)(2,1)} async-done(((bf16[96,768]{1,0:T(8,128)(2,1)}), bf16[3072,768]{1,0:T(8,128)(2,1)}) %all-gather.2.cloned.1.call-update) | async-done | bytes 4718608 | tf_op jit(solution)/shard_map/all_gather | solution.py:99
  78.0 3.2 %fusion.10 = (f32[128]{0:T(128)S(1)}, f32[128,768]{1,0:T(8,128)S(1)}) fusion(bf16[128,3072]{1,0:T(8,128)(2,1)S(1)} %copy-done.2, bf16[3072,768]{1,0:T(8,128)(2,1)} %all-gather.2.cloned.1.call-done, bf16[128,768]{1,0:T(8,128)(2,1)S(1)} %copy-done.4), kind=kOutput, calls=%fused_computation.68 | convolution fusion | flops 604274560 | bytes 6095360 | tf_op jit(solution)/shard_map/dot_general | solution.py:28
  83.0 1.4 collective-permute-start.8
  84.8 1.3 collective-permute-start.10
  86.2 1.4 collective-permute-start.11
  87.8 3.3 %collective-permute-done.8 = bf16[128,768]{1,0:T(8,128)(2,1)S(1)} collective-permute-done((bf16[128,768]{1,0:T(8,128)(2,1)S(1)}, bf16[128,768]{1,0:T(8,128)(2,1)S(1)}, u32[]{:S(2)}, u32[]{:S(2)}) %collective-permute-start.8) | collective-permute-done | bytes 196640 | tf_op jit(solution)/shard_map/ppermute | solution.py:142
  92.9 1.6 %collective-permute-start.14 = (bf16[128,768]{1,0:T(8,128)(2,1)S(1)}, bf16[128,768]{1,0:T(8,128)(2,1)S(1)}, u32[]{:S(2)}, u32[]{:S(2)}) collective-permute-start(bf16[128,768]{1,0:T(8,128)(2,1)S(1)} %get-tuple-element.22), channel_id=1, source_target_pairs={{0,1},{1,2},{2,3},{3,4},{4,5},{5,6},{6,7},{7,0},{8,9},{9,10},{10,1... | collective-permute-start | bytes 589832 | tf_op jit(solution)/shard_map/ppermute | solution.py:142
  94.6 2.6 %collective-permute-done.10 = bf16[128,768]{1,0:T(8,128)(2,1)S(1)} collective-permute-done((bf16[128,768]{1,0:T(8,128)(2,1)S(1)}, bf16[128,768]{1,0:T(8,128)(2,1)S(1)}, u32[]{:S(2)}, u32[]{:S(2)}) %collective-permute-start.10) | collective-permute-done | bytes 196640 | tf_op jit(solution)/shard_map/ppermute | solution.py:142
  97.2 6.9 %collective-permute-done.11 = bf16[128,768]{1,0:T(8,128)(2,1)S(1)} collective-permute-done((bf16[128,768]{1,0:T(8,128)(2,1)S(1)}, bf16[128,768]{1,0:T(8,128)(2,1)S(1)}, u32[]{:S(2)}, u32[]{:S(2)}) %collective-permute-start.11) | collective-permute-done | bytes 196640 | tf_op jit(solution)/shard_map/ppermute | solution.py:142
  104.7 1.8 %fusion.14 = f32[384,768]{1,0:T(8,128)} fusion(bf16[1024,384]{0,1:T(8,128)(2,1)S(1)} %copy-done.8, bf16[1024,768]{1,0:T(8,128)(2,1)S(1)} %constant_dynamic-update-slice_fusion.7), kind=kOutput, calls=%fused_computation.72 | convolution fusion | flops 603979776 | bytes 3538944 | tf_op jit(solution)/shard_map/dot_general | solution.py:147
  107.0 1.4 concatenate.11
  109.4 2.7 %collective-permute-done.15 = f32[3074]{0:T(1024)S(1)} collective-permute-done((f32[3074]{0:T(1024)S(1)}, f32[3074]{0:T(1024)S(1)}, u32[]{:S(2)}, u32[]{:S(2)}) %collective-permute-start.15) | collective-permute-done | bytes 12328 | tf_op jit(solution)/shard_map/ppermute | solution.py:54
  114.6 2.4 %collective-permute-done.17 = f32[3074]{0:T(1024)S(1)} collective-permute-done((f32[3074]{0:T(1024)S(1)}, f32[3074]{0:T(1024)S(1)}, u32[]{:S(2)}, u32[]{:S(2)}) %collective-permute-start.17) | collective-permute-done | bytes 12328 | tf_op jit(solution)/shard_map/ppermute | solution.py:54
  117.1 1.9 %collective-permute-start.18 = (f32[3074]{0:T(1024)S(1)}, f32[3074]{0:T(1024)S(1)}, u32[]{:S(2)}, u32[]{:S(2)}) collective-permute-start(f32[3074]{0:T(1024)S(1)} %add.175), channel_id=1, source_target_pairs={{0,8},{8,0},{16,24},{24,16},{1,9},{9,1},{17,25},{25,17},{2,10},{10... | collective-permute-start | bytes 36896 | tf_op jit(solution)/shard_map/ppermute | solution.py:54
  119.0 2.5 %collective-permute-done.18 = f32[3074]{0:T(1024)S(1)} collective-permute-done((f32[3074]{0:T(1024)S(1)}, f32[3074]{0:T(1024)S(1)}, u32[]{:S(2)}, u32[]{:S(2)}) %collective-permute-start.18) | collective-permute-done | bytes 12328 | tf_op jit(solution)/shard_map/ppermute | solution.py:54
  121.5 1.9 %collective-permute-start.19 = (f32[3074]{0:T(1024)S(1)}, f32[3074]{0:T(1024)S(1)}, u32[]{:S(2)}, u32[]{:S(2)}) collective-permute-start(f32[3074]{0:T(1024)S(1)} %add.176), channel_id=1, source_target_pairs={{0,16},{8,24},{16,0},{24,8},{1,17},{9,25},{17,1},{25,9},{2,18},{10... | collective-permute-start | bytes 36896 | tf_op jit(solution)/shard_map/ppermute | solution.py:54
  123.4 4.0 %collective-permute-done.19 = f32[3074]{0:T(1024)S(1)} collective-permute-done((f32[3074]{0:T(1024)S(1)}, f32[3074]{0:T(1024)S(1)}, u32[]{:S(2)}, u32[]{:S(2)}) %collective-permute-start.19) | collective-permute-done | bytes 12328 | tf_op jit(solution)/shard_map/ppermute | solution.py:54
  130.5 4.7 %reduce-scatter.2.cloned.1.call-done = f32[96,768]{1,0:T(8,128)} async-done(((f32[384,768]{1,0:T(8,128)}), f32[96,768]{1,0:T(8,128)}) %reduce-scatter.2.cloned.1.call-update) | async-done | bytes 294928 | tf_op jit(solution)/shard_map/reduce_scatter | solution.py:150
  (112 shorter events, 29.5 us)
Async XLA Ops:
  7.2 70.8 %all-gather.2.cloned.1.call-start = ((), (), s32[]{:S(2)}) async-start(), calls=%async_computation.1 | async-start | bytes 4866048 | tf_op jit(solution)/shard_map/all_gather | solution.py:99
  7.9 127.3 %reduce-scatter.2.cloned.1.call-start = ((), (), s32[]{:S(2)}) async-start(), calls=%async_computation.2 | async-start | bytes 1474560 | tf_op jit(solution)/shard_map/reduce_scatter | solution.py:150
  10.6 20.0 %collective-permute-start = (bf16[128,384]{0,1:T(8,128)(2,1)}, bf16[128,384]{0,1:T(8,128)(2,1)}, u32[]{:S(2)}, u32[]{:S(2)}) collective-permute-start(bf16[128,384]{0,1:T(8,128)(2,1)} %get-tuple-element.29), channel_id=1, source_target_pairs={{0,7},{1,0},{2,1},{3,2},{4,3},{5,4},{6,5},{7,6},{8,15},{9,8},{10,9... | collective-permute-start | bytes 294920 | tf_op jit(solution)/shard_map/ppermute | solution.py:89
  14.0 17.6 %collective-permute-start.1 = (bf16[128,384]{0,1:T(8,128)(2,1)}, bf16[128,384]{0,1:T(8,128)(2,1)}, u32[]{:S(2)}, u32[]{:S(2)}) collective-permute-start(bf16[128,384]{0,1:T(8,128)(2,1)} %get-tuple-element.28), channel_id=1, source_target_pairs={{0,6},{1,7},{2,0},{3,1},{4,2},{5,3},{6,4},{7,5},{8,14},{9,15},{10,... | collective-permute-start | bytes 294920 | tf_op jit(solution)/shard_map/ppermute | solution.py:89
  14.8 18.8 %collective-permute-start.2 = (bf16[128,384]{0,1:T(8,128)(2,1)}, bf16[128,384]{0,1:T(8,128)(2,1)}, u32[]{:S(2)}, u32[]{:S(2)}) collective-permute-start(bf16[128,384]{0,1:T(8,128)(2,1)} %get-tuple-element.27), channel_id=1, source_target_pairs={{0,5},{1,6},{2,7},{3,0},{4,1},{5,2},{6,3},{7,4},{8,13},{9,14},{10,... | collective-permute-start | bytes 294920 | tf_op jit(solution)/shard_map/ppermute | solution.py:89
  15.0 20.7 %collective-permute-start.3 = (bf16[128,384]{0,1:T(8,128)(2,1)S(1)}, bf16[128,384]{0,1:T(8,128)(2,1)}, u32[]{:S(2)}, u32[]{:S(2)}) collective-permute-start(bf16[128,384]{0,1:T(8,128)(2,1)S(1)} %get-tuple-element.26), channel_id=1, source_target_pairs={{0,4},{1,5},{2,6},{3,7},{4,0},{5,1},{6,2},{7,3},{8,12},{9,13},{10,... | collective-permute-start | bytes 294920 | tf_op jit(solution)/shard_map/ppermute | solution.py:89
  25.9 31.0 %collective-permute-start.7 = (bf16[128,4096]{1,0:T(8,128)(2,1)}, bf16[128,4096]{1,0:T(8,128)(2,1)}, u32[]{:S(2)}, u32[]{:S(2)}) collective-permute-start(bf16[128,4096]{1,0:T(8,128)(2,1)} %broadcast_select_fusion), channel_id=1, source_target_pairs={{0,1},{1,0},{2,3},{3,2},{4,5},{5,4},{6,7},{7,6},{8,9},{9,8},{10,11... | collective-permute-start | bytes 3145736 | tf_op jit(solution)/shard_map/ppermute | solution.py:42
  30.6 24.2 %collective-permute-start.4 = (bf16[128,384]{0,1:T(8,128)(2,1)S(1)}, bf16[128,384]{0,1:T(8,128)(2,1)S(1)}, u32[]{:S(2)}, u32[]{:S(2)}) collective-permute-start(bf16[128,384]{0,1:T(8,128)(2,1)S(1)} %get-tuple-element.25), channel_id=1, source_target_pairs={{0,3},{1,4},{2,5},{3,6},{4,7},{5,0},{6,1},{7,2},{8,11},{9,12},{10,... | collective-permute-start | bytes 294920 | tf_op jit(solution)/shard_map/ppermute | solution.py:89
  31.6 23.3 %collective-permute-start.5 = (bf16[128,384]{0,1:T(8,128)(2,1)S(1)}, bf16[128,384]{0,1:T(8,128)(2,1)S(1)}, u32[]{:S(2)}, u32[]{:S(2)}) collective-permute-start(bf16[128,384]{0,1:T(8,128)(2,1)S(1)} %get-tuple-element.24), channel_id=1, source_target_pairs={{0,2},{1,3},{2,4},{3,5},{4,6},{5,7},{6,0},{7,1},{8,10},{9,11},{10,... | collective-permute-start | bytes 294920 | tf_op jit(solution)/shard_map/ppermute | solution.py:89
  33.6 22.3 %collective-permute-start.6 = (bf16[128,384]{0,1:T(8,128)(2,1)S(1)}, bf16[128,384]{0,1:T(8,128)(2,1)S(1)}, u32[]{:S(2)}, u32[]{:S(2)}) collective-permute-start(bf16[128,384]{0,1:T(8,128)(2,1)S(1)} %get-tuple-element.23), channel_id=1, source_target_pairs={{0,1},{1,2},{2,3},{3,4},{4,5},{5,6},{6,7},{7,0},{8,9},{9,10},{10,1... | collective-permute-start | bytes 294920 | tf_op jit(solution)/shard_map/ppermute | solution.py:89
  61.8 20.0 %copy-start.13 = (s32[128]{0:T(128)S(1)}, s32[128]{0:T(128)}, u32[]{:S(2)}) copy-start(s32[128]{0:T(128)} %select_reduce_fusion) | copy-start | bytes 1540
  82.8 21.9 %copy-start.8 = (bf16[1024,384]{0,1:T(8,128)(2,1)S(1)}, bf16[1024,384]{0,1:T(8,128)(2,1)}, u32[]{:S(2)}) copy-start(bf16[1024,384]{0,1:T(8,128)(2,1)} %copy-done.7) | copy-start | bytes 2359300
  83.0 8.0 %collective-permute-start.8 = (bf16[128,768]{1,0:T(8,128)(2,1)S(1)}, bf16[128,768]{1,0:T(8,128)(2,1)S(1)}, u32[]{:S(2)}, u32[]{:S(2)}) collective-permute-start(bf16[128,768]{1,0:T(8,128)(2,1)S(1)} %get-tuple-element.22), channel_id=1, source_target_pairs={{0,7},{1,0},{2,1},{3,2},{4,3},{5,4},{6,5},{7,6},{8,15},{9,8},{10,9... | collective-permute-start | bytes 589832 | tf_op jit(solution)/shard_map/ppermute | solution.py:142
  84.4 8.5 %collective-permute-start.9 = (bf16[128,768]{1,0:T(8,128)(2,1)S(1)}, bf16[128,768]{1,0:T(8,128)(2,1)S(1)}, u32[]{:S(2)}, u32[]{:S(2)}) collective-permute-start(bf16[128,768]{1,0:T(8,128)(2,1)S(1)} %get-tuple-element.22), channel_id=1, source_target_pairs={{0,6},{1,7},{2,0},{3,1},{4,2},{5,3},{6,4},{7,5},{8,14},{9,15},{10,... | collective-permute-start | bytes 589832 | tf_op jit(solution)/shard_map/ppermute | solution.py:142
  84.8 12.3 %collective-permute-start.10 = (bf16[128,768]{1,0:T(8,128)(2,1)S(1)}, bf16[128,768]{1,0:T(8,128)(2,1)S(1)}, u32[]{:S(2)}, u32[]{:S(2)}) collective-permute-start(bf16[128,768]{1,0:T(8,128)(2,1)S(1)} %get-tuple-element.22), channel_id=1, source_target_pairs={{0,5},{1,6},{2,7},{3,0},{4,1},{5,2},{6,3},{7,4},{8,13},{9,14},{10,... | collective-permute-start | bytes 589832 | tf_op jit(solution)/shard_map/ppermute | solution.py:142
  86.2 18.0 %collective-permute-start.11 = (bf16[128,768]{1,0:T(8,128)(2,1)S(1)}, bf16[128,768]{1,0:T(8,128)(2,1)S(1)}, u32[]{:S(2)}, u32[]{:S(2)}) collective-permute-start(bf16[128,768]{1,0:T(8,128)(2,1)S(1)} %get-tuple-element.22), channel_id=1, source_target_pairs={{0,4},{1,5},{2,6},{3,7},{4,0},{5,1},{6,2},{7,3},{8,12},{9,13},{10,... | collective-permute-start | bytes 589832 | tf_op jit(solution)/shard_map/ppermute | solution.py:142
  87.6 16.6 %collective-permute-start.12 = (bf16[128,768]{1,0:T(8,128)(2,1)S(1)}, bf16[128,768]{1,0:T(8,128)(2,1)S(1)}, u32[]{:S(2)}, u32[]{:S(2)}) collective-permute-start(bf16[128,768]{1,0:T(8,128)(2,1)S(1)} %get-tuple-element.22), channel_id=1, source_target_pairs={{0,3},{1,4},{2,5},{3,6},{4,7},{5,0},{6,1},{7,2},{8,11},{9,12},{10,... | collective-permute-start | bytes 589832 | tf_op jit(solution)/shard_map/ppermute | solution.py:142
  91.1 13.3 %collective-permute-start.13 = (bf16[128,768]{1,0:T(8,128)(2,1)S(1)}, bf16[128,768]{1,0:T(8,128)(2,1)S(1)}, u32[]{:S(2)}, u32[]{:S(2)}) collective-permute-start(bf16[128,768]{1,0:T(8,128)(2,1)S(1)} %get-tuple-element.22), channel_id=1, source_target_pairs={{0,2},{1,3},{2,4},{3,5},{4,6},{5,7},{6,0},{7,1},{8,10},{9,11},{10,... | collective-permute-start | bytes 589832 | tf_op jit(solution)/shard_map/ppermute | solution.py:142
  92.9 11.8 %collective-permute-start.14 = (bf16[128,768]{1,0:T(8,128)(2,1)S(1)}, bf16[128,768]{1,0:T(8,128)(2,1)S(1)}, u32[]{:S(2)}, u32[]{:S(2)}) collective-permute-start(bf16[128,768]{1,0:T(8,128)(2,1)S(1)} %get-tuple-element.22), channel_id=1, source_target_pairs={{0,1},{1,2},{2,3},{3,4},{4,5},{5,6},{6,7},{7,0},{8,9},{9,10},{10,1... | collective-permute-start | bytes 589832 | tf_op jit(solution)/shard_map/ppermute | solution.py:142
  108.4 3.7 %collective-permute-start.15 = (f32[3074]{0:T(1024)S(1)}, f32[3074]{0:T(1024)S(1)}, u32[]{:S(2)}, u32[]{:S(2)}) collective-permute-start(f32[3074]{0:T(1024)S(1)} %concatenate.11), channel_id=1, source_target_pairs={{0,1},{1,0},{2,3},{3,2},{4,5},{5,4},{6,7},{7,6},{8,9},{9,8},{10,11... | collective-permute-start | bytes 36896 | tf_op jit(solution)/shard_map/ppermute | solution.py:54
  112.1 1.2 collective-permute-start.16
  113.3 3.7 %collective-permute-start.17 = (f32[3074]{0:T(1024)S(1)}, f32[3074]{0:T(1024)S(1)}, u32[]{:S(2)}, u32[]{:S(2)}) collective-permute-start(f32[3074]{0:T(1024)S(1)} %add.174), channel_id=1, source_target_pairs={{0,4},{4,0},{1,5},{5,1},{2,6},{6,2},{3,7},{7,3},{8,12},{12,8},{9,1... | collective-permute-start | bytes 36896 | tf_op jit(solution)/shard_map/ppermute | solution.py:54
  117.1 4.4 %collective-permute-start.18 = (f32[3074]{0:T(1024)S(1)}, f32[3074]{0:T(1024)S(1)}, u32[]{:S(2)}, u32[]{:S(2)}) collective-permute-start(f32[3074]{0:T(1024)S(1)} %add.175), channel_id=1, source_target_pairs={{0,8},{8,0},{16,24},{24,16},{1,9},{9,1},{17,25},{25,17},{2,10},{10... | collective-permute-start | bytes 36896 | tf_op jit(solution)/shard_map/ppermute | solution.py:54
  121.5 5.9 %collective-permute-start.19 = (f32[3074]{0:T(1024)S(1)}, f32[3074]{0:T(1024)S(1)}, u32[]{:S(2)}, u32[]{:S(2)}) collective-permute-start(f32[3074]{0:T(1024)S(1)} %add.176), channel_id=1, source_target_pairs={{0,16},{8,24},{16,0},{24,8},{1,17},{9,25},{17,1},{25,9},{2,18},{10... | collective-permute-start | bytes 36896 | tf_op jit(solution)/shard_map/ppermute | solution.py:54
  (13 other events, 109.6 us)
Sparse Core Ops, SparseCore 0:
  10.9 67.0 all-gather.1
  106.7 28.5 reduce-scatter.1

commit v7 on v6

--- a/solution.py
+++ b/solution.py
@@ -96,7 +96,17 @@
     teacher_logits = jnp.dot(blended, teacher_head, preferred_element_type=jnp.float32)
     teacher_logp = jax.nn.log_softmax(teacher_logits, axis=-1)
     teacher_prob = jnp.exp(teacher_logp)
-    ffn_out = folder(student_hidden, lax.all_gather(down_weight, TOKS, axis=0, tiled=True))
+    per_core = lax.all_gather(down_weight, ("q", "x", "tensor"), axis=0, tiled=True)
+    other_core = lax.ppermute(per_core, "c", perm=[(0, 1), (1, 0)])
+    core = lax.axis_index("c")
+    by_core = student_hidden.reshape(
+        tok_rows, -1, 2, lax.axis_size("tensor") * down_weight.shape[0]
+    )
+    hidden_mine_core = lax.dynamic_index_in_dim(by_core, core, 2, keepdims=False)
+    hidden_other_core = lax.dynamic_index_in_dim(by_core, 1 - core, 2, keepdims=False)
+    ffn_out = folder(hidden_mine_core.reshape(tok_rows, -1), per_core) + folder(
+        hidden_other_core.reshape(tok_rows, -1), other_core
+    )
     student_scale = student_gain.astype(jnp.float32)
     normed, scaled, inverse = norm_rows(
         student_input.astype(jnp.float32) + ffn_out, student_scale, student_eps

time: 144 us -> 146 us (1.014)
  local copies, waits for them, and re-layouts: 12.4 us -> 19.1 us
  matrix products: 16.3 us -> 14.3 us
    ppermute x7, waiting for transfers between devices: 19.2 us -> 14.6 us  [local(): lax.ppermute(send, GROUP, perm=[(i, (i - k) % group) for i in range(group)])]
    unnamed x45 -> x47, local copies, waits for them, and re-layouts: 8.21 us -> 12.3 us
    all_gather x1, waiting for transfers between devices: 16.1 us -> 20 us  [local(): lax.all_gather(down_weight, ('q', 'x', 'tensor'), axis=0, tiled=True)]
    dot_general x1 -> x2, matrix products: 3.21 us -> 1.12 us  [folder(): return jnp.dot(ordered, row_piece, preferred_element_type=jnp.float32)]
    dynamic_slice x0 -> x1, local copies, waits for them, and re-layouts: none -> 1.93 us  [local(): lax.dynamic_index_in_dim(by_core, 1 - core, 2, keepdims=False)]
  transfers between devices with their start and end apart: 22 -> 23, of which waited for: 15 -> 13; matrix products, arithmetic and copies ran while one was open for 19% -> 23% of each run, Pallas kernels for 0% -> 0%
where the time goes in v7:
time: 146 us
  waiting for transfers between devices  67.5 us (46%)
  starting transfers between devices  22.5 us (15%)
  local copies, waits for them, and re-layouts  19.1 us (13%)
  between operations  17 us (12%)
  matrix products  14.3 us (10%)
  other arithmetic  5.56 us (4%)
    all_gather x1, waiting for transfers between devices, local(): lax.all_gather(down_weight, ('q', 'x', 'tensor'), axis=0, tiled=True)  20 us
    ppermute x7, waiting for transfers between devices, local(): lax.ppermute(grad_out, GROUP, perm=[(i, (i - k) % group) for i in range(g...  14.6 us
    ppermute x7, waiting for transfers between devices, local(): lax.ppermute(send, GROUP, perm=[(i, (i - k) % group) for i in range(group)])  14.6 us
    ppermute x5, waiting for transfers between devices, butterfly_sum(): lax.ppermute(value, axis, perm=[(i, i ^ step) for i in range(size)])  12.4 us
    unnamed x47, local copies, waits for them, and re-layouts  12.3 us
    dot_general x1, matrix products, teacher_attention(): jnp.dot(context, w_out, preferred_element_type=jnp.float32)  8.48 us
    ppermute x7, starting transfers between devices, local(): lax.ppermute(send, GROUP, perm=[(i, (i - k) % group) for i in range(group)])  7.75 us
    ppermute x7, starting transfers between devices, local(): lax.ppermute(grad_out, GROUP, perm=[(i, (i - k) % group) for i in range(g...  7.13 us
  transfers between devices with their start and end apart: 23, of which 13 were waited for; matrix products, arithmetic and copies ran while one was open for 23% of the time, Pallas kernels for 0%

profile of v7, /device:TPU:0, one launch (start us, length us, event | category | flops | bytes accessed | tf_op | source)
XLA Modules:
  0.0 146.0 jit_solution(4373763416672627441)
XLA Ops:
  10.8 3.3 %collective-permute-start = (bf16[128,384]{0,1:T(8,128)(2,1)}, bf16[128,384]{0,1:T(8,128)(2,1)}, u32[]{:S(2)}, u32[]{:S(2)}) collective-permute-start(bf16[128,384]{0,1:T(8,128)(2,1)} %get-tuple-element.31), channel_id=1, source_target_pairs={{0,7},{1,0},{2,1},{3,2},{4,3},{5,4},{6,5},{7,6},{8,15},{9,8},{10,9... | collective-permute-start | bytes 294920 | tf_op jit(solution)/shard_map/ppermute | solution.py:89
  16.4 8.5 %convolution_convert_fusion = bf16[256,4096]{1,0:T(8,128)(2,1)S(1)} fusion(bf16[256,2048]{1,0:T(8,128)(2,1)S(1)} %copy-done, bf16[2048,4096]{1,0:T(8,128)(2,1)} %param.15), kind=kOutput, calls=%fused_computation | convolution fusion | flops 4296015872 | bytes 19922944 | tf_op jit(solution)/shard_map/dot_general | solution.py:33
  27.3 1.5 %bitcast_dynamic-update-slice_fusion = bf16[1024,384]{0,1:T(8,128)(2,1)} fusion(bf16[8,128,384]{1,2,0:T(8,128)(2,1)} %bitcast.44, s32[]{:T(128)S(6)} %select_n.98), kind=kLoop, calls=%fused_computation.18 | loop fusion | bytes 196612
  29.6 1.9 %constant_dynamic-slice_fusion = (bf16[128,8,1,192]{0,3,2,1:T(8,128)(2,1)}, bf16[128,8,1,192]{0,3,2,1:T(8,128)(2,1)S(1)}) fusion(bf16[128,8,2,192]{0,3,2,1:T(8,128)(2,1)} %bitcast.42, s32[]{:T(128)S(6)} %select_n.120, s32[]{:T(128)S(6)} %select_n.119), kind=kLoop, calls=%fused_computation.43 | loop fusion | bytes 1572872 | tf_op jit(solution)/shard_map/jit(dynamic_index_in_dim)/dynamic_slice | solution.py:106
  32.1 1.6 %constant_dynamic-update-slice_fusion.6 = bf16[1024,384]{0,1:T(8,128)(2,1)} fusion(bf16[1024,384]{0,1:T(8,128)(2,1)} %bitcast_dynamic-update-slice_fusion, bf16[128,384]{0,1:T(8,128)(2,1)} %collective-permute-done), kind=kLoop, calls=%fused_computation.32 | loop fusion | bytes 196608
  34.7 1.5 %constant_dynamic-update-slice_fusion.5 = bf16[1024,384]{0,1:T(8,128)(2,1)} fusion(bf16[1024,384]{0,1:T(8,128)(2,1)} %constant_dynamic-update-slice_fusion.6, bf16[128,384]{0,1:T(8,128)(2,1)} %collective-permute-done.1), kind=kLoop, calls=%fused_computation.31 | loop fusion | bytes 196608
  37.4 1.6 %constant_dynamic-update-slice_fusion.4 = bf16[1024,384]{0,1:T(8,128)(2,1)} fusion(bf16[1024,384]{0,1:T(8,128)(2,1)} %constant_dynamic-update-slice_fusion.5, bf16[128,384]{0,1:T(8,128)(2,1)} %collective-permute-done.2), kind=kLoop, calls=%fused_computation.30 | loop fusion | bytes 196608
  39.0 1.6 %constant_dynamic-update-slice_fusion.3 = bf16[1024,384]{0,1:T(8,128)(2,1)} fusion(bf16[1024,384]{0,1:T(8,128)(2,1)} %constant_dynamic-update-slice_fusion.4, bf16[128,384]{0,1:T(8,128)(2,1)} %collective-permute-done.3), kind=kLoop, calls=%fused_computation.29 | loop fusion | bytes 196608
  40.5 14.6 %collective-permute-done.4 = bf16[128,384]{0,1:T(8,128)(2,1)S(1)} collective-permute-done((bf16[128,384]{0,1:T(8,128)(2,1)}, bf16[128,384]{0,1:T(8,128)(2,1)S(1)}, u32[]{:S(2)}, u32[]{:S(2)}) %collective-permute-start.4) | collective-permute-done | bytes 98336 | tf_op jit(solution)/shard_map/ppermute | solution.py:89
  57.1 20.0 %all-gather.2.cloned.1.call-done = bf16[1536,768]{1,0:T(8,128)(2,1)} async-done(((bf16[96,768]{1,0:T(8,128)(2,1)}), bf16[1536,768]{1,0:T(8,128)(2,1)}) %all-gather.2.cloned.1.call-update) | async-done | bytes 2359312 | tf_op jit(solution)/shard_map/all_gather | solution.py:99
  77.1 1.7 %convert_add_fusion.1 = f32[128,4096]{1,0:T(8,128)S(1)} fusion(bf16[128,4096]{1,0:T(8,128)(2,1)} %collective-permute-done.7, pred[]{:T(512)S(6)} %eq.40, bf16[256,4096]{1,0:T(8,128)(2,1)S(1)} %convolution_convert_fusion), kind=kLoop, calls=%fused_computation.6 | loop fusion | flops 2097152 | bytes 5242881 | tf_op jit(solution)/shard_map/add | solution.py:43
  79.9 2.2 %fusion.12 = (f32[128]{0:T(128)S(1)}, f32[128,4]{0,1:T(4,128)S(1)}) fusion(bf16[4096,4]{0,1:T(4,128)(2,1)S(1)} %copy-done.14, bf16[128,4096]{1,0:T(8,128)(2,1)S(1)} %copy-done.2, f32[128,4096]{1,0:T(8,128)S(1)} %convert_add_fusion.1, f32[4096]{0:T(1024)S(1)} %copy-done.8, f32[128]{0:T(128)S(1)} %add_rsqrt_fusion, f32[128]{0:T(128)S(1)} %broadcast_multiply_fusion, ...), kind=kOutput, calls=%fused_computation.72 | convolution fusion | flops 8913280 | bytes 3198472 | tf_op jit(solution)/shard_map/dot_general | solution.py:96
  85.6 1.5 %collective-permute-start.9 = (bf16[128,768]{1,0:T(8,128)(2,1)S(1)}, bf16[128,768]{1,0:T(8,128)(2,1)S(1)}, u32[]{:S(2)}, u32[]{:S(2)}) collective-permute-start(bf16[128,768]{1,0:T(8,128)(2,1)S(1)} %get-tuple-element.22), channel_id=1, source_target_pairs={{0,7},{1,0},{2,1},{3,2},{4,3},{5,4},{6,5},{7,6},{8,15},{9,8},{10,9... | collective-permute-start | bytes 589832 | tf_op jit(solution)/shard_map/ppermute | solution.py:152
  90.3 3.0 %collective-permute-done.9 = bf16[128,768]{1,0:T(8,128)(2,1)S(1)} collective-permute-done((bf16[128,768]{1,0:T(8,128)(2,1)S(1)}, bf16[128,768]{1,0:T(8,128)(2,1)S(1)}, u32[]{:S(2)}, u32[]{:S(2)}) %collective-permute-start.9) | collective-permute-done | bytes 196640 | tf_op jit(solution)/shard_map/ppermute | solution.py:152
  97.0 3.0 %collective-permute-done.11 = bf16[128,768]{1,0:T(8,128)(2,1)S(1)} collective-permute-done((bf16[128,768]{1,0:T(8,128)(2,1)S(1)}, bf16[128,768]{1,0:T(8,128)(2,1)S(1)}, u32[]{:S(2)}, u32[]{:S(2)}) %collective-permute-start.11) | collective-permute-done | bytes 196640 | tf_op jit(solution)/shard_map/ppermute | solution.py:152
  100.0 7.0 %collective-permute-done.12 = bf16[128,768]{1,0:T(8,128)(2,1)S(1)} collective-permute-done((bf16[128,768]{1,0:T(8,128)(2,1)S(1)}, bf16[128,768]{1,0:T(8,128)(2,1)S(1)}, u32[]{:S(2)}, u32[]{:S(2)}) %collective-permute-start.12) | collective-permute-done | bytes 196640 | tf_op jit(solution)/shard_map/ppermute | solution.py:152
  107.5 1.8 %fusion.16 = f32[384,768]{1,0:T(8,128)} fusion(bf16[1024,384]{0,1:T(8,128)(2,1)S(1)} %copy-done.9, bf16[1024,768]{1,0:T(8,128)(2,1)S(1)} %constant_dynamic-update-slice_fusion.7), kind=kOutput, calls=%fused_computation.76 | convolution fusion | flops 603979776 | bytes 3538944 | tf_op jit(solution)/shard_map/dot_general | solution.py:157
  112.1 2.8 %collective-permute-done.16 = f32[3074]{0:T(1024)S(1)} collective-permute-done((f32[3074]{0:T(1024)S(1)}, f32[3074]{0:T(1024)S(1)}, u32[]{:S(2)}, u32[]{:S(2)}) %collective-permute-start.16) | collective-permute-done | bytes 12328 | tf_op jit(solution)/shard_map/ppermute | solution.py:54
  117.4 2.4 %collective-permute-done.18 = f32[3074]{0:T(1024)S(1)} collective-permute-done((f32[3074]{0:T(1024)S(1)}, f32[3074]{0:T(1024)S(1)}, u32[]{:S(2)}, u32[]{:S(2)}) %collective-permute-start.18) | collective-permute-done | bytes 12328 | tf_op jit(solution)/shard_map/ppermute | solution.py:54
  119.8 1.9 %collective-permute-start.19 = (f32[3074]{0:T(1024)S(1)}, f32[3074]{0:T(1024)S(1)}, u32[]{:S(2)}, u32[]{:S(2)}) collective-permute-start(f32[3074]{0:T(1024)S(1)} %add.189), channel_id=1, source_target_pairs={{0,8},{8,0},{16,24},{24,16},{1,9},{9,1},{17,25},{25,17},{2,10},{10... | collective-permute-start | bytes 36896 | tf_op jit(solution)/shard_map/ppermute | solution.py:54
  121.7 2.5 %collective-permute-done.19 = f32[3074]{0:T(1024)S(1)} collective-permute-done((f32[3074]{0:T(1024)S(1)}, f32[3074]{0:T(1024)S(1)}, u32[]{:S(2)}, u32[]{:S(2)}) %collective-permute-start.19) | collective-permute-done | bytes 12328 | tf_op jit(solution)/shard_map/ppermute | solution.py:54
  124.2 2.0 %collective-permute-start.20 = (f32[3074]{0:T(1024)S(1)}, f32[3074]{0:T(1024)S(1)}, u32[]{:S(2)}, u32[]{:S(2)}) collective-permute-start(f32[3074]{0:T(1024)S(1)} %add.190), channel_id=1, source_target_pairs={{0,16},{8,24},{16,0},{24,8},{1,17},{9,25},{17,1},{25,9},{2,18},{10... | collective-permute-start | bytes 36896 | tf_op jit(solution)/shard_map/ppermute | solution.py:54
  126.2 3.5 %collective-permute-done.20 = f32[3074]{0:T(1024)S(1)} collective-permute-done((f32[3074]{0:T(1024)S(1)}, f32[3074]{0:T(1024)S(1)}, u32[]{:S(2)}, u32[]{:S(2)}) %collective-permute-start.20) | collective-permute-done | bytes 12328 | tf_op jit(solution)/shard_map/ppermute | solution.py:54
  132.8 5.2 %reduce-scatter.2.cloned.1.call-done = f32[96,768]{1,0:T(8,128)} async-done(((f32[384,768]{1,0:T(8,128)}), f32[96,768]{1,0:T(8,128)}) %reduce-scatter.2.cloned.1.call-update) | async-done | bytes 294928 | tf_op jit(solution)/shard_map/reduce_scatter | solution.py:160
  (118 shorter events, 32.3 us)
Async XLA Ops:
  7.2 69.9 %all-gather.2.cloned.1.call-start = ((), (), s32[]{:S(2)}) async-start(), calls=%async_computation.1 | async-start | bytes 2506752 | tf_op jit(solution)/shard_map/all_gather | solution.py:99
  7.9 130.1 %reduce-scatter.2.cloned.1.call-start = ((), (), s32[]{:S(2)}) async-start(), calls=%async_computation.2 | async-start | bytes 1474560 | tf_op jit(solution)/shard_map/reduce_scatter | solution.py:160
  10.8 21.3 %collective-permute-start = (bf16[128,384]{0,1:T(8,128)(2,1)}, bf16[128,384]{0,1:T(8,128)(2,1)}, u32[]{:S(2)}, u32[]{:S(2)}) collective-permute-start(bf16[128,384]{0,1:T(8,128)(2,1)} %get-tuple-element.31), channel_id=1, source_target_pairs={{0,7},{1,0},{2,1},{3,2},{4,3},{5,4},{6,5},{7,6},{8,15},{9,8},{10,9... | collective-permute-start | bytes 294920 | tf_op jit(solution)/shard_map/ppermute | solution.py:89
  14.1 19.6 %collective-permute-start.1 = (bf16[128,384]{0,1:T(8,128)(2,1)}, bf16[128,384]{0,1:T(8,128)(2,1)}, u32[]{:S(2)}, u32[]{:S(2)}) collective-permute-start(bf16[128,384]{0,1:T(8,128)(2,1)} %get-tuple-element.30), channel_id=1, source_target_pairs={{0,6},{1,7},{2,0},{3,1},{4,2},{5,3},{6,4},{7,5},{8,14},{9,15},{10,... | collective-permute-start | bytes 294920 | tf_op jit(solution)/shard_map/ppermute | solution.py:89
  15.0 21.3 %collective-permute-start.2 = (bf16[128,384]{0,1:T(8,128)(2,1)}, bf16[128,384]{0,1:T(8,128)(2,1)}, u32[]{:S(2)}, u32[]{:S(2)}) collective-permute-start(bf16[128,384]{0,1:T(8,128)(2,1)} %get-tuple-element.29), channel_id=1, source_target_pairs={{0,5},{1,6},{2,7},{3,0},{4,1},{5,2},{6,3},{7,4},{8,13},{9,14},{10,... | collective-permute-start | bytes 294920 | tf_op jit(solution)/shard_map/ppermute | solution.py:89
  15.2 23.8 %collective-permute-start.3 = (bf16[128,384]{0,1:T(8,128)(2,1)}, bf16[128,384]{0,1:T(8,128)(2,1)}, u32[]{:S(2)}, u32[]{:S(2)}) collective-permute-start(bf16[128,384]{0,1:T(8,128)(2,1)} %get-tuple-element.28), channel_id=1, source_target_pairs={{0,4},{1,5},{2,6},{3,7},{4,0},{5,1},{6,2},{7,3},{8,12},{9,13},{10,... | collective-permute-start | bytes 294920 | tf_op jit(solution)/shard_map/ppermute | solution.py:89
  26.0 51.1 %collective-permute-start.7 = (bf16[128,4096]{1,0:T(8,128)(2,1)}, bf16[128,4096]{1,0:T(8,128)(2,1)}, u32[]{:S(2)}, u32[]{:S(2)}) collective-permute-start(bf16[128,4096]{1,0:T(8,128)(2,1)} %broadcast_select_fusion), channel_id=1, source_target_pairs={{0,1},{1,0},{2,3},{3,2},{4,5},{5,4},{6,7},{7,6},{8,9},{9,8},{10,11... | collective-permute-start | bytes 3145736 | tf_op jit(solution)/shard_map/ppermute | solution.py:42
  32.1 23.0 %collective-permute-start.4 = (bf16[128,384]{0,1:T(8,128)(2,1)}, bf16[128,384]{0,1:T(8,128)(2,1)S(1)}, u32[]{:S(2)}, u32[]{:S(2)}) collective-permute-start(bf16[128,384]{0,1:T(8,128)(2,1)} %get-tuple-element.27), channel_id=1, source_target_pairs={{0,3},{1,4},{2,5},{3,6},{4,7},{5,0},{6,1},{7,2},{8,11},{9,12},{10,... | collective-permute-start | bytes 294920 | tf_op jit(solution)/shard_map/ppermute | solution.py:89
  33.7 22.1 %collective-permute-start.5 = (bf16[128,384]{0,1:T(8,128)(2,1)}, bf16[128,384]{0,1:T(8,128)(2,1)S(1)}, u32[]{:S(2)}, u32[]{:S(2)}) collective-permute-start(bf16[128,384]{0,1:T(8,128)(2,1)} %get-tuple-element.26), channel_id=1, source_target_pairs={{0,2},{1,3},{2,4},{3,5},{4,6},{5,7},{6,0},{7,1},{8,10},{9,11},{10,... | collective-permute-start | bytes 294920 | tf_op jit(solution)/shard_map/ppermute | solution.py:89
  36.3 20.1 %collective-permute-start.6 = (bf16[128,384]{0,1:T(8,128)(2,1)}, bf16[128,384]{0,1:T(8,128)(2,1)S(1)}, u32[]{:S(2)}, u32[]{:S(2)}) collective-permute-start(bf16[128,384]{0,1:T(8,128)(2,1)} %get-tuple-element.25), channel_id=1, source_target_pairs={{0,1},{1,2},{2,3},{3,4},{4,5},{5,6},{6,7},{7,0},{8,9},{9,10},{10,1... | collective-permute-start | bytes 294920 | tf_op jit(solution)/shard_map/ppermute | solution.py:89
  77.1 5.6 %collective-permute-start.8 = (bf16[1536,768]{1,0:T(8,128)(2,1)}, bf16[1536,768]{1,0:T(8,128)(2,1)S(1)}, u32[]{:S(2)}, u32[]{:S(2)}) collective-permute-start(bf16[1536,768]{1,0:T(8,128)(2,1)} %all-gather.2.cloned.1.call-done), channel_id=1, source_target_pairs={{0,2},{2,0},{1,3},{3,1},{4,6},{6,4},{5,7},{7,5},{8,10},{10,8},{9,1... | collective-permute-start | bytes 7077896 | tf_op jit(solution)/shard_map/ppermute | solution.py:100
  85.4 22.1 %copy-start.9 = (bf16[1024,384]{0,1:T(8,128)(2,1)S(1)}, bf16[1024,384]{0,1:T(8,128)(2,1)}, u32[]{:S(2)}) copy-start(bf16[1024,384]{0,1:T(8,128)(2,1)} %constant_dynamic-update-slice_fusion) | copy-start | bytes 2359300
  85.6 7.8 %collective-permute-start.9 = (bf16[128,768]{1,0:T(8,128)(2,1)S(1)}, bf16[128,768]{1,0:T(8,128)(2,1)S(1)}, u32[]{:S(2)}, u32[]{:S(2)}) collective-permute-start(bf16[128,768]{1,0:T(8,128)(2,1)S(1)} %get-tuple-element.22), channel_id=1, source_target_pairs={{0,7},{1,0},{2,1},{3,2},{4,3},{5,4},{6,5},{7,6},{8,15},{9,8},{10,9... | collective-permute-start | bytes 589832 | tf_op jit(solution)/shard_map/ppermute | solution.py:152
  87.1 8.6 %collective-permute-start.10 = (bf16[128,768]{1,0:T(8,128)(2,1)S(1)}, bf16[128,768]{1,0:T(8,128)(2,1)S(1)}, u32[]{:S(2)}, u32[]{:S(2)}) collective-permute-start(bf16[128,768]{1,0:T(8,128)(2,1)S(1)} %get-tuple-element.22), channel_id=1, source_target_pairs={{0,6},{1,7},{2,0},{3,1},{4,2},{5,3},{6,4},{7,5},{8,14},{9,15},{10,... | collective-permute-start | bytes 589832 | tf_op jit(solution)/shard_map/ppermute | solution.py:152
  87.4 12.6 %collective-permute-start.11 = (bf16[128,768]{1,0:T(8,128)(2,1)S(1)}, bf16[128,768]{1,0:T(8,128)(2,1)S(1)}, u32[]{:S(2)}, u32[]{:S(2)}) collective-permute-start(bf16[128,768]{1,0:T(8,128)(2,1)S(1)} %get-tuple-element.22), channel_id=1, source_target_pairs={{0,5},{1,6},{2,7},{3,0},{4,1},{5,2},{6,3},{7,4},{8,13},{9,14},{10,... | collective-permute-start | bytes 589832 | tf_op jit(solution)/shard_map/ppermute | solution.py:152
  88.9 18.1 %collective-permute-start.12 = (bf16[128,768]{1,0:T(8,128)(2,1)S(1)}, bf16[128,768]{1,0:T(8,128)(2,1)S(1)}, u32[]{:S(2)}, u32[]{:S(2)}) collective-permute-start(bf16[128,768]{1,0:T(8,128)(2,1)S(1)} %get-tuple-element.22), channel_id=1, source_target_pairs={{0,4},{1,5},{2,6},{3,7},{4,0},{5,1},{6,2},{7,3},{8,12},{9,13},{10,... | collective-permute-start | bytes 589832 | tf_op jit(solution)/shard_map/ppermute | solution.py:152
  90.3 16.7 %collective-permute-start.13 = (bf16[128,768]{1,0:T(8,128)(2,1)S(1)}, bf16[128,768]{1,0:T(8,128)(2,1)S(1)}, u32[]{:S(2)}, u32[]{:S(2)}) collective-permute-start(bf16[128,768]{1,0:T(8,128)(2,1)S(1)} %get-tuple-element.22), channel_id=1, source_target_pairs={{0,3},{1,4},{2,5},{3,6},{4,7},{5,0},{6,1},{7,2},{8,11},{9,12},{10,... | collective-permute-start | bytes 589832 | tf_op jit(solution)/shard_map/ppermute | solution.py:152
  93.4 13.7 %collective-permute-start.14 = (bf16[128,768]{1,0:T(8,128)(2,1)S(1)}, bf16[128,768]{1,0:T(8,128)(2,1)S(1)}, u32[]{:S(2)}, u32[]{:S(2)}) collective-permute-start(bf16[128,768]{1,0:T(8,128)(2,1)S(1)} %get-tuple-element.22), channel_id=1, source_target_pairs={{0,2},{1,3},{2,4},{3,5},{4,6},{5,7},{6,0},{7,1},{8,10},{9,11},{10,... | collective-permute-start | bytes 589832 | tf_op jit(solution)/shard_map/ppermute | solution.py:152
  95.7 11.7 %collective-permute-start.15 = (bf16[128,768]{1,0:T(8,128)(2,1)S(1)}, bf16[128,768]{1,0:T(8,128)(2,1)S(1)}, u32[]{:S(2)}, u32[]{:S(2)}) collective-permute-start(bf16[128,768]{1,0:T(8,128)(2,1)S(1)} %get-tuple-element.22), channel_id=1, source_target_pairs={{0,1},{1,2},{2,3},{3,4},{4,5},{5,6},{6,7},{7,0},{8,9},{9,10},{10,1... | collective-permute-start | bytes 589832 | tf_op jit(solution)/shard_map/ppermute | solution.py:152
  111.1 3.7 %collective-permute-start.16 = (f32[3074]{0:T(1024)S(1)}, f32[3074]{0:T(1024)S(1)}, u32[]{:S(2)}, u32[]{:S(2)}) collective-permute-start(f32[3074]{0:T(1024)S(1)} %concatenate.11), channel_id=1, source_target_pairs={{0,1},{1,0},{2,3},{3,2},{4,5},{5,4},{6,7},{7,6},{8,9},{9,8},{10,11... | collective-permute-start | bytes 36896 | tf_op jit(solution)/shard_map/ppermute | solution.py:54
  114.9 1.2 collective-permute-start.17
  116.1 3.7 %collective-permute-start.18 = (f32[3074]{0:T(1024)S(1)}, f32[3074]{0:T(1024)S(1)}, u32[]{:S(2)}, u32[]{:S(2)}) collective-permute-start(f32[3074]{0:T(1024)S(1)} %add.188), channel_id=1, source_target_pairs={{0,4},{4,0},{1,5},{5,1},{2,6},{6,2},{3,7},{7,3},{8,12},{12,8},{9,1... | collective-permute-start | bytes 36896 | tf_op jit(solution)/shard_map/ppermute | solution.py:54
  119.8 4.4 %collective-permute-start.19 = (f32[3074]{0:T(1024)S(1)}, f32[3074]{0:T(1024)S(1)}, u32[]{:S(2)}, u32[]{:S(2)}) collective-permute-start(f32[3074]{0:T(1024)S(1)} %add.189), channel_id=1, source_target_pairs={{0,8},{8,0},{16,24},{24,16},{1,9},{9,1},{17,25},{25,17},{2,10},{10... | collective-permute-start | bytes 36896 | tf_op jit(solution)/shard_map/ppermute | solution.py:54
  124.2 5.5 %collective-permute-start.20 = (f32[3074]{0:T(1024)S(1)}, f32[3074]{0:T(1024)S(1)}, u32[]{:S(2)}, u32[]{:S(2)}) collective-permute-start(f32[3074]{0:T(1024)S(1)} %add.190), channel_id=1, source_target_pairs={{0,16},{8,24},{16,0},{24,8},{1,17},{9,25},{17,1},{25,9},{2,18},{10... | collective-permute-start | bytes 36896 | tf_op jit(solution)/shard_map/ppermute | solution.py:54
  (15 other events, 51.2 us)
Sparse Core Ops, SparseCore 0:
  10.8 66.2 all-gather.1
  109.4 28.5 reduce-scatter.1

commit v8 on v6

--- a/solution.py
+++ b/solution.py
@@ -58,6 +58,23 @@
     return value
 
 
+def group_gather(value):
+    chips = ("x", "tensor")
+    n = lax.axis_size(chips)
+    j = lax.axis_index(chips)
+    parts = [value] + [
+        lax.ppermute(value, chips, perm=[(i, (i - k) % n) for i in range(n)])
+        for k in range(1, n)
+    ]
+    plane = jnp.roll(jnp.stack(parts), j, axis=0)
+    other = lax.ppermute(plane, "c", perm=[(0, 1), (1, 0)])
+    low = lax.axis_index("c") == 0
+    both = jnp.where(low, jnp.stack([plane, other]), jnp.stack([other, plane]))
+    both = both.reshape(2, lax.axis_size("x"), lax.axis_size("tensor"), *value.shape)
+    both = jnp.transpose(both, (1, 0, 2, 3, 4))
+    return both.reshape(-1, value.shape[1])
+
+
 def local(
     context,
     w_out,
@@ -88,7 +105,7 @@
         pieces.append(
             lax.ppermute(send, GROUP, perm=[(i, (i - k) % group) for i in range(group)])
         )
-    hidden_mine = jnp.concatenate(pieces, axis=0)
+    hidden_mine = jnp.roll(jnp.stack(pieces), me, axis=0).reshape(group * tok_rows, -1)
     hidden_mine, attention = lax.optimization_barrier((hidden_mine, attention))
     residual = teacher_input.astype(jnp.float32)
     layer_out = norm_rows(residual + attention, teacher_gain.astype(jnp.float32), teacher_eps)[0]
@@ -136,14 +153,7 @@
         )
         * inverse
     ).astype(jnp.bfloat16)
-    grad_out_group = jnp.concatenate(
-        [grad_out]
-        + [
-            lax.ppermute(grad_out, GROUP, perm=[(i, (i - k) % group) for i in range(group)])
-            for k in range(1, group)
-        ],
-        axis=0,
-    )
+    grad_out_group = group_gather(grad_out)
     grad_block = lax.dot_general(
         hidden_mine, grad_out_group, (((0,), (0,)), ((), ())), preferred_element_type=jnp.float32
     )

time: 144 us -> 143 us (level)
  local copies, waits for them, and re-layouts: 12.4 us -> 20 us
  starting transfers between devices: 22.9 us -> 18.9 us
  waiting for transfers between devices: 67.7 us -> 64.1 us
    ppermute x1, waiting for transfers between devices: 0.01 us -> 20 us  [teacher_attention(): got = lax.ppermute(theirs, 'tensor', perm=[(0, 1), (1, 0)])]
    ppermute x7, waiting for transfers between devices: 19.2 us -> 1.94 us  [local(): lax.ppermute(send, GROUP, perm=[(i, (i - k) % group) for i in range(group)])]
    dynamic_slice x0 -> x3, local copies, waits for them, and re-layouts: none -> 4.5 us  [the longest x2 3.31 us: local(): jnp.roll(jnp.stack(pieces), me, axis=0).reshape(group * tok_rows, -1)]
    ppermute x7 -> x4, starting transfers between devices: 7.42 us -> 3.52 us  [the longest x3 3.45 us: group_gather(): lax.ppermute(value, chips, perm=[(i, (i - k) % n) for i in range(n)])]
    ppermute x7 -> x4, waiting for transfers between devices: 14.1 us -> 10.4 us  [the longest x3 8.1 us: group_gather(): lax.ppermute(value, chips, perm=[(i, (i - k) % n) for i in range(n)])]
    all_gather x1, waiting for transfers between devices: 16.1 us -> 13.4 us  [local(): lax.all_gather(down_weight, TOKS, axis=0, tiled=True)]
    unnamed x45 -> x56, local copies, waits for them, and re-layouts: 8.21 us -> 10.5 us
  transfers between devices with their start and end apart: 22 -> 19, of which waited for: 15 -> 12; matrix products, arithmetic and copies ran while one was open for 19% -> 20% of each run, Pallas kernels for 0% -> 0%
where the time goes in v8:
time: 143 us
  waiting for transfers between devices  64.1 us (45%)
  local copies, waits for them, and re-layouts  20 us (14%)
  starting transfers between devices  18.9 us (13%)
  between operations  17.1 us (12%)
  matrix products  16.4 us (11%)
  other arithmetic  6.43 us (4%)
    ppermute x1, waiting for transfers between devices, teacher_attention(): got = lax.ppermute(theirs, 'tensor', perm=[(0, 1), (1, 0)])  20 us
    all_gather x1, waiting for transfers between devices, local(): lax.all_gather(down_weight, TOKS, axis=0, tiled=True)  13.4 us
    ppermute x5, waiting for transfers between devices, butterfly_sum(): lax.ppermute(value, axis, perm=[(i, i ^ step) for i in range(size)])  12.5 us
    unnamed x56, local copies, waits for them, and re-layouts  10.5 us
    dot_general x1, matrix products, teacher_attention(): jnp.dot(context, w_out, preferred_element_type=jnp.float32)  8.56 us
    ppermute x3, waiting for transfers between devices, group_gather(): lax.ppermute(value, chips, perm=[(i, (i - k) % n) for i in range(n)])  8.1 us
    ppermute x7, starting transfers between devices, local(): lax.ppermute(send, GROUP, perm=[(i, (i - k) % group) for i in range(group)])  8.06 us
    ppermute x5, starting transfers between devices, butterfly_sum(): lax.ppermute(value, axis, perm=[(i, i ^ step) for i in range(size)])  5.76 us
  transfers between devices with their start and end apart: 19, of which 12 were waited for; matrix products, arithmetic and copies ran while one was open for 20% of the time, Pallas kernels for 0%

profile of v8, /device:TPU:0, one launch (start us, length us, event | category | flops | bytes accessed | tf_op | source)
XLA Modules:
  0.0 142.9 jit_solution(15872478160450297012)
XLA Ops:
  8.1 1.5 %copy.29 = bf16[128,3072]{0,1:T(8,128)(2,1)S(1)} copy(bf16[128,3072]{1,0:T(8,128)(2,1)} %param.20) | data formatting | bytes 1572864 | tf_op args[6]
  10.8 3.3 %collective-permute-start = (bf16[128,384]{0,1:T(8,128)(2,1)}, bf16[128,384]{0,1:T(8,128)(2,1)S(1)}, u32[]{:S(2)}, u32[]{:S(2)}) collective-permute-start(bf16[128,384]{0,1:T(8,128)(2,1)} %get-tuple-element.33), channel_id=1, source_target_pairs={{0,7},{1,0},{2,1},{3,2},{4,3},{5,4},{6,5},{7,6},{8,15},{9,8},{10,9... | collective-permute-start | bytes 294920 | tf_op jit(solution)/shard_map/ppermute | solution.py:106
  17.7 8.6 %convolution_convert_fusion = bf16[256,4096]{1,0:T(8,128)(2,1)S(1)} fusion(bf16[256,2048]{1,0:T(8,128)(2,1)S(1)} %copy-done, bf16[2048,4096]{1,0:T(8,128)(2,1)} %param.15), kind=kOutput, calls=%fused_computation | convolution fusion | flops 4296015872 | bytes 19922944 | tf_op jit(solution)/shard_map/dot_general | solution.py:33
  29.9 1.5 %collective-permute-start.7 = (bf16[128,4096]{1,0:T(8,128)(2,1)}, bf16[128,4096]{1,0:T(8,128)(2,1)}, u32[]{:S(2)}, u32[]{:S(2)}) collective-permute-start(bf16[128,4096]{1,0:T(8,128)(2,1)} %broadcast_select_fusion), channel_id=1, source_target_pairs={{0,1},{1,0},{2,3},{3,2},{4,5},{5,4},{6,7},{7,6},{8,9},{9,8},{10,11... | collective-permute-start | bytes 3145736 | tf_op jit(solution)/shard_map/ppermute | solution.py:42
  32.4 1.9 %collective-permute-done.6 = bf16[128,384]{0,1:T(8,128)(2,1)S(1)} collective-permute-done((bf16[128,384]{0,1:T(8,128)(2,1)S(1)}, bf16[128,384]{0,1:T(8,128)(2,1)S(1)}, u32[]{:S(2)}, u32[]{:S(2)}) %collective-permute-start.6) | collective-permute-done | bytes 98336 | tf_op jit(solution)/shard_map/ppermute | solution.py:106
  37.3 2.3 %copy.31 = bf16[8,128,384]{2,1,0:T(8,128)(2,1)} copy(bf16[8,128,384]{1,2,0:T(8,128)(2,1)} %constant_dynamic-slice_fusion.1) | data formatting | bytes 1572864 | tf_op jit(solution)/shard_map/jit(_roll_dynamic)/dynamic_slice | solution.py:108
  39.6 20.0 %collective-permute-done.7 = bf16[128,4096]{1,0:T(8,128)(2,1)} collective-permute-done((bf16[128,4096]{1,0:T(8,128)(2,1)}, bf16[128,4096]{1,0:T(8,128)(2,1)}, u32[]{:S(2)}, u32[]{:S(2)}) %collective-permute-start.7) | collective-permute-done | bytes 1048608 | tf_op jit(solution)/shard_map/ppermute | solution.py:42
  59.6 1.6 %convert_add_fusion.1 = f32[128,4096]{1,0:T(8,128)S(1)} fusion(bf16[128,4096]{1,0:T(8,128)(2,1)} %collective-permute-done.7, pred[]{:T(512)S(6)} %eq.48, bf16[256,4096]{1,0:T(8,128)(2,1)S(1)} %convolution_convert_fusion), kind=kLoop, calls=%fused_computation.6 | loop fusion | flops 2097152 | bytes 5242881 | tf_op jit(solution)/shard_map/add | solution.py:43
  62.4 2.1 %fusion.11 = (f32[128]{0:T(128)S(1)}, f32[128,4]{0,1:T(4,128)S(1)}) fusion(bf16[4096,4]{0,1:T(4,128)(2,1)S(1)} %copy-done.15, bf16[128,4096]{1,0:T(8,128)(2,1)S(1)} %copy-done.1, f32[128,4096]{1,0:T(8,128)S(1)} %convert_add_fusion.1, f32[4096]{0:T(1024)S(1)} %copy-done.10, f32[128]{0:T(128)S(1)} %add_rsqrt_fusion, f32[128]{0:T(128)S(1)} %broadcast_multiply_fusion, ...), kind=kOutput, calls=%fused_computation.80 | convolution fusion | flops 8913280 | bytes 3198472 | tf_op jit(solution)/shard_map/dot_general | solution.py:113
  64.6 13.4 %all-gather.2.cloned.1.call-done = bf16[3072,768]{1,0:T(8,128)(2,1)} async-done(((bf16[96,768]{1,0:T(8,128)(2,1)}), bf16[3072,768]{1,0:T(8,128)(2,1)}) %all-gather.2.cloned.1.call-update) | async-done | bytes 4718608 | tf_op jit(solution)/shard_map/all_gather | solution.py:116
  78.0 3.2 %fusion.10 = (f32[128]{0:T(128)S(1)}, f32[128,768]{1,0:T(8,128)S(1)}) fusion(bf16[128,3072]{1,0:T(8,128)(2,1)S(1)} %copy-done.3, bf16[3072,768]{1,0:T(8,128)(2,1)} %all-gather.2.cloned.1.call-done, bf16[128,768]{1,0:T(8,128)(2,1)S(1)} %copy-done.6), kind=kOutput, calls=%fused_computation.79 | convolution fusion | flops 604274560 | bytes 6095360 | tf_op jit(solution)/shard_map/dot_general | solution.py:28
  83.7 1.5 %collective-permute-start.8 = (bf16[128,768]{1,0:T(8,128)(2,1)S(1)}, bf16[128,768]{1,0:T(8,128)(2,1)S(1)}, u32[]{:S(2)}, u32[]{:S(2)}) collective-permute-start(bf16[128,768]{1,0:T(8,128)(2,1)S(1)} %get-tuple-element.25), channel_id=1, source_target_pairs={{0,5},{1,0},{4,1},{5,4},{2,7},{3,2},{6,3},{7,6},{8,13},{9,8},{12,9... | collective-permute-start | bytes 589832 | tf_op jit(solution)/shard_map/ppermute | solution.py:66
  85.1 1.5 %collective-permute-start.9 = (bf16[128,768]{1,0:T(8,128)(2,1)S(1)}, bf16[128,768]{1,0:T(8,128)(2,1)S(1)}, u32[]{:S(2)}, u32[]{:S(2)}) collective-permute-start(bf16[128,768]{1,0:T(8,128)(2,1)S(1)} %get-tuple-element.25), channel_id=1, source_target_pairs={{0,4},{1,5},{4,0},{5,1},{2,6},{3,7},{6,2},{7,3},{8,12},{9,13},{12,... | collective-permute-start | bytes 589832 | tf_op jit(solution)/shard_map/ppermute | solution.py:66
  87.1 3.6 %collective-permute-done.8 = bf16[128,768]{1,0:T(8,128)(2,1)S(1)} collective-permute-done((bf16[128,768]{1,0:T(8,128)(2,1)S(1)}, bf16[128,768]{1,0:T(8,128)(2,1)S(1)}, u32[]{:S(2)}, u32[]{:S(2)}) %collective-permute-start.8) | collective-permute-done | bytes 196640 | tf_op jit(solution)/shard_map/ppermute | solution.py:66
  91.5 4.5 %collective-permute-done.9 = bf16[128,768]{1,0:T(8,128)(2,1)S(1)} collective-permute-done((bf16[128,768]{1,0:T(8,128)(2,1)S(1)}, bf16[128,768]{1,0:T(8,128)(2,1)S(1)}, u32[]{:S(2)}, u32[]{:S(2)}) %collective-permute-start.9) | collective-permute-done | bytes 196640 | tf_op jit(solution)/shard_map/ppermute | solution.py:66
  101.3 2.3 %collective-permute-done.11 = bf16[4,128,768]{2,1,0:T(8,128)(2,1)S(1)} collective-permute-done((bf16[4,128,768]{2,1,0:T(8,128)(2,1)S(1)}, bf16[4,128,768]{2,1,0:T(8,128)(2,1)S(1)}, u32[]{:S(2)}, u32[]{:S(2)}) %collective-permute-start.11) | collective-permute-done | bytes 786464 | tf_op jit(solution)/shard_map/ppermute | solution.py:70
  104.7 1.8 %fusion.14 = f32[384,768]{1,0:T(8,128)} fusion(bf16[1024,384]{1,0:T(8,128)(2,1)S(1)} %bitcast.79, bf16[1024,768]{1,0:T(8,128)(2,1)S(1)} %bitcast.76), kind=kOutput, calls=%fused_computation.83 | convolution fusion | flops 603979776 | bytes 3538944 | tf_op jit(solution)/shard_map/dot_general | solution.py:157
  109.2 3.0 %collective-permute-done.12 = f32[3074]{0:T(1024)S(1)} collective-permute-done((f32[3074]{0:T(1024)S(1)}, f32[3074]{0:T(1024)S(1)}, u32[]{:S(2)}, u32[]{:S(2)}) %collective-permute-start.12) | collective-permute-done | bytes 12328 | tf_op jit(solution)/shard_map/ppermute | solution.py:54
  114.3 2.8 %collective-permute-done.14 = f32[3074]{0:T(1024)S(1)} collective-permute-done((f32[3074]{0:T(1024)S(1)}, f32[3074]{0:T(1024)S(1)}, u32[]{:S(2)}, u32[]{:S(2)}) %collective-permute-start.14) | collective-permute-done | bytes 12328 | tf_op jit(solution)/shard_map/ppermute | solution.py:54
  117.1 1.9 %collective-permute-start.15 = (f32[3074]{0:T(1024)S(1)}, f32[3074]{0:T(1024)S(1)}, u32[]{:S(2)}, u32[]{:S(2)}) collective-permute-start(f32[3074]{0:T(1024)S(1)} %add.202), channel_id=1, source_target_pairs={{0,8},{8,0},{16,24},{24,16},{1,9},{9,1},{17,25},{25,17},{2,10},{10... | collective-permute-start | bytes 36896 | tf_op jit(solution)/shard_map/ppermute | solution.py:54
  119.0 2.3 %collective-permute-done.15 = f32[3074]{0:T(1024)S(1)} collective-permute-done((f32[3074]{0:T(1024)S(1)}, f32[3074]{0:T(1024)S(1)}, u32[]{:S(2)}, u32[]{:S(2)}) %collective-permute-start.15) | collective-permute-done | bytes 12328 | tf_op jit(solution)/shard_map/ppermute | solution.py:54
  121.3 2.2 %collective-permute-start.16 = (f32[3074]{0:T(1024)S(1)}, f32[3074]{0:T(1024)S(1)}, u32[]{:S(2)}, u32[]{:S(2)}) collective-permute-start(f32[3074]{0:T(1024)S(1)} %add.203), channel_id=1, source_target_pairs={{0,16},{8,24},{16,0},{24,8},{1,17},{9,25},{17,1},{25,9},{2,18},{10... | collective-permute-start | bytes 36896 | tf_op jit(solution)/shard_map/ppermute | solution.py:54
  123.5 3.2 %collective-permute-done.16 = f32[3074]{0:T(1024)S(1)} collective-permute-done((f32[3074]{0:T(1024)S(1)}, f32[3074]{0:T(1024)S(1)}, u32[]{:S(2)}, u32[]{:S(2)}) %collective-permute-start.16) | collective-permute-done | bytes 12328 | tf_op jit(solution)/shard_map/ppermute | solution.py:54
  129.7 5.2 %reduce-scatter.2.cloned.1.call-done = f32[96,768]{1,0:T(8,128)} async-done(((f32[384,768]{1,0:T(8,128)}), f32[96,768]{1,0:T(8,128)}) %reduce-scatter.2.cloned.1.call-update) | async-done | bytes 294928 | tf_op jit(solution)/shard_map/reduce_scatter | solution.py:160
  (121 shorter events, 30.7 us)
Async XLA Ops:
  7.2 70.8 %all-gather.2.cloned.1.call-start = ((), (), s32[]{:S(2)}) async-start(), calls=%async_computation.1 | async-start | bytes 4866048 | tf_op jit(solution)/shard_map/all_gather | solution.py:116
  7.9 127.0 %reduce-scatter.2.cloned.1.call-start = ((), (), s32[]{:S(2)}) async-start(), calls=%async_computation.2 | async-start | bytes 1474560 | tf_op jit(solution)/shard_map/reduce_scatter | solution.py:160
  10.8 17.2 %collective-permute-start = (bf16[128,384]{0,1:T(8,128)(2,1)}, bf16[128,384]{0,1:T(8,128)(2,1)S(1)}, u32[]{:S(2)}, u32[]{:S(2)}) collective-permute-start(bf16[128,384]{0,1:T(8,128)(2,1)} %get-tuple-element.33), channel_id=1, source_target_pairs={{0,7},{1,0},{2,1},{3,2},{4,3},{5,4},{6,5},{7,6},{8,15},{9,8},{10,9... | collective-permute-start | bytes 294920 | tf_op jit(solution)/shard_map/ppermute | solution.py:106
  14.1 15.0 %collective-permute-start.1 = (bf16[128,384]{0,1:T(8,128)(2,1)}, bf16[128,384]{0,1:T(8,128)(2,1)S(1)}, u32[]{:S(2)}, u32[]{:S(2)}) collective-permute-start(bf16[128,384]{0,1:T(8,128)(2,1)} %get-tuple-element.32), channel_id=1, source_target_pairs={{0,6},{1,7},{2,0},{3,1},{4,2},{5,3},{6,4},{7,5},{8,14},{9,15},{10,... | collective-permute-start | bytes 294920 | tf_op jit(solution)/shard_map/ppermute | solution.py:106
  14.9 15.0 %collective-permute-start.2 = (bf16[128,384]{0,1:T(8,128)(2,1)}, bf16[128,384]{0,1:T(8,128)(2,1)S(1)}, u32[]{:S(2)}, u32[]{:S(2)}) collective-permute-start(bf16[128,384]{0,1:T(8,128)(2,1)} %get-tuple-element.31), channel_id=1, source_target_pairs={{0,5},{1,6},{2,7},{3,0},{4,1},{5,2},{6,3},{7,4},{8,13},{9,14},{10,... | collective-permute-start | bytes 294920 | tf_op jit(solution)/shard_map/ppermute | solution.py:106
  15.2 16.3 %collective-permute-start.3 = (bf16[128,384]{0,1:T(8,128)(2,1)}, bf16[128,384]{0,1:T(8,128)(2,1)S(1)}, u32[]{:S(2)}, u32[]{:S(2)}) collective-permute-start(bf16[128,384]{0,1:T(8,128)(2,1)} %get-tuple-element.30), channel_id=1, source_target_pairs={{0,4},{1,5},{2,6},{3,7},{4,0},{5,1},{6,2},{7,3},{8,12},{9,13},{10,... | collective-permute-start | bytes 294920 | tf_op jit(solution)/shard_map/ppermute | solution.py:106
  16.4 15.1 %collective-permute-start.4 = (bf16[128,384]{0,1:T(8,128)(2,1)}, bf16[128,384]{0,1:T(8,128)(2,1)}, u32[]{:S(2)}, u32[]{:S(2)}) collective-permute-start(bf16[128,384]{0,1:T(8,128)(2,1)} %get-tuple-element.29), channel_id=1, source_target_pairs={{0,3},{1,4},{2,5},{3,6},{4,7},{5,0},{6,1},{7,2},{8,11},{9,12},{10,... | collective-permute-start | bytes 294920 | tf_op jit(solution)/shard_map/ppermute | solution.py:106
  28.0 4.4 %collective-permute-start.5 = (bf16[128,384]{0,1:T(8,128)(2,1)S(1)}, bf16[128,384]{0,1:T(8,128)(2,1)S(1)}, u32[]{:S(2)}, u32[]{:S(2)}) collective-permute-start(bf16[128,384]{0,1:T(8,128)(2,1)S(1)} %copy-done.8), channel_id=1, source_target_pairs={{0,2},{1,3},{2,4},{3,5},{4,6},{5,7},{6,0},{7,1},{8,10},{9,11},{10,... | collective-permute-start | bytes 294920 | tf_op jit(solution)/shard_map/ppermute | solution.py:106
  29.1 5.2 %collective-permute-start.6 = (bf16[128,384]{0,1:T(8,128)(2,1)S(1)}, bf16[128,384]{0,1:T(8,128)(2,1)S(1)}, u32[]{:S(2)}, u32[]{:S(2)}) collective-permute-start(bf16[128,384]{0,1:T(8,128)(2,1)S(1)} %copy-done.7), channel_id=1, source_target_pairs={{0,1},{1,2},{2,3},{3,4},{4,5},{5,6},{6,7},{7,0},{8,9},{9,10},{10,1... | collective-permute-start | bytes 294920 | tf_op jit(solution)/shard_map/ppermute | solution.py:106
  29.9 29.7 %collective-permute-start.7 = (bf16[128,4096]{1,0:T(8,128)(2,1)}, bf16[128,4096]{1,0:T(8,128)(2,1)}, u32[]{:S(2)}, u32[]{:S(2)}) collective-permute-start(bf16[128,4096]{1,0:T(8,128)(2,1)} %broadcast_select_fusion), channel_id=1, source_target_pairs={{0,1},{1,0},{2,3},{3,2},{4,5},{5,4},{6,7},{7,6},{8,9},{9,8},{10,11... | collective-permute-start | bytes 3145736 | tf_op jit(solution)/shard_map/ppermute | solution.py:42
  39.6 21.6 %copy-start.1 = (bf16[128,4096]{1,0:T(8,128)(2,1)S(1)}, bf16[128,4096]{1,0:T(8,128)(2,1)}, u32[]{:S(2)}) copy-start(bf16[128,4096]{1,0:T(8,128)(2,1)} %param.16) | copy-start | bytes 3145732
  62.4 15.6 %copy-start.3 = (bf16[128,3072]{1,0:T(8,128)(2,1)S(1)}, bf16[128,3072]{1,0:T(8,128)(2,1)}, u32[]{:S(2)}) copy-start(bf16[128,3072]{1,0:T(8,128)(2,1)} %param.20) | copy-start | bytes 2359300
  62.4 15.6 %copy-start.6 = (bf16[128,768]{1,0:T(8,128)(2,1)S(1)}, bf16[128,768]{1,0:T(8,128)(2,1)}, u32[]{:S(2)}) copy-start(bf16[128,768]{1,0:T(8,128)(2,1)} %param.21) | copy-start | bytes 589828
  64.5 17.0 %copy-start.9 = (bf16[768,4]{0,1:T(4,128)(2,1)S(1)}, bf16[768,4]{0,1:T(4,128)(2,1)}, u32[]{:S(2)}) copy-start(bf16[768,4]{0,1:T(4,128)(2,1)} %param.24) | copy-start | bytes 18436
  64.5 17.2 %copy-start.12 = (s32[128]{0:T(128)S(1)}, s32[128]{0:T(128)}, u32[]{:S(2)}) copy-start(s32[128]{0:T(128)} %param.25) | copy-start | bytes 1540
  83.7 7.1 %collective-permute-start.8 = (bf16[128,768]{1,0:T(8,128)(2,1)S(1)}, bf16[128,768]{1,0:T(8,128)(2,1)S(1)}, u32[]{:S(2)}, u32[]{:S(2)}) collective-permute-start(bf16[128,768]{1,0:T(8,128)(2,1)S(1)} %get-tuple-element.25), channel_id=1, source_target_pairs={{0,5},{1,0},{4,1},{5,4},{2,7},{3,2},{6,3},{7,6},{8,13},{9,8},{12,9... | collective-permute-start | bytes 589832 | tf_op jit(solution)/shard_map/ppermute | solution.py:66
  85.1 10.8 %collective-permute-start.9 = (bf16[128,768]{1,0:T(8,128)(2,1)S(1)}, bf16[128,768]{1,0:T(8,128)(2,1)S(1)}, u32[]{:S(2)}, u32[]{:S(2)}) collective-permute-start(bf16[128,768]{1,0:T(8,128)(2,1)S(1)} %get-tuple-element.25), channel_id=1, source_target_pairs={{0,4},{1,5},{4,0},{5,1},{2,6},{3,7},{6,2},{7,3},{8,12},{9,13},{12,... | collective-permute-start | bytes 589832 | tf_op jit(solution)/shard_map/ppermute | solution.py:66
  86.6 10.0 %collective-permute-start.10 = (bf16[128,768]{1,0:T(8,128)(2,1)S(1)}, bf16[128,768]{1,0:T(8,128)(2,1)S(1)}, u32[]{:S(2)}, u32[]{:S(2)}) collective-permute-start(bf16[128,768]{1,0:T(8,128)(2,1)S(1)} %get-tuple-element.25), channel_id=1, source_target_pairs={{0,1},{1,4},{4,5},{5,0},{2,3},{3,6},{6,7},{7,2},{8,9},{9,12},{12,1... | collective-permute-start | bytes 589832 | tf_op jit(solution)/shard_map/ppermute | solution.py:66
  101.3 2.4 %collective-permute-start.11 = (bf16[4,128,768]{2,1,0:T(8,128)(2,1)S(1)}, bf16[4,128,768]{2,1,0:T(8,128)(2,1)S(1)}, u32[]{:S(2)}, u32[]{:S(2)}) collective-permute-start(bf16[4,128,768]{2,1,0:T(8,128)(2,1)S(1)} %constant_dynamic-slice_fusion), channel_id=1, source_target_pairs={{0,2},{2,0},{1,3},{3,1},{4,6},{6,4},{5,7},{7,5},{8,10},{10,8},{9,1... | collective-permute-start | bytes 2359304 | tf_op jit(solution)/shard_map/ppermute | solution.py:70
  108.4 3.7 %collective-permute-start.12 = (f32[3074]{0:T(1024)S(1)}, f32[3074]{0:T(1024)S(1)}, u32[]{:S(2)}, u32[]{:S(2)}) collective-permute-start(f32[3074]{0:T(1024)S(1)} %concatenate.17), channel_id=1, source_target_pairs={{0,1},{1,0},{2,3},{3,2},{4,5},{5,4},{6,7},{7,6},{8,9},{9,8},{10,11... | collective-permute-start | bytes 36896 | tf_op jit(solution)/shard_map/ppermute | solution.py:54
  112.2 1.2 collective-permute-start.13
  113.4 3.7 %collective-permute-start.14 = (f32[3074]{0:T(1024)S(1)}, f32[3074]{0:T(1024)S(1)}, u32[]{:S(2)}, u32[]{:S(2)}) collective-permute-start(f32[3074]{0:T(1024)S(1)} %add.201), channel_id=1, source_target_pairs={{0,4},{4,0},{1,5},{5,1},{2,6},{6,2},{3,7},{7,3},{8,12},{12,8},{9,1... | collective-permute-start | bytes 36896 | tf_op jit(solution)/shard_map/ppermute | solution.py:54
  117.1 4.2 %collective-permute-start.15 = (f32[3074]{0:T(1024)S(1)}, f32[3074]{0:T(1024)S(1)}, u32[]{:S(2)}, u32[]{:S(2)}) collective-permute-start(f32[3074]{0:T(1024)S(1)} %add.202), channel_id=1, source_target_pairs={{0,8},{8,0},{16,24},{24,16},{1,9},{9,1},{17,25},{25,17},{2,10},{10... | collective-permute-start | bytes 36896 | tf_op jit(solution)/shard_map/ppermute | solution.py:54
  121.3 5.4 %collective-permute-start.16 = (f32[3074]{0:T(1024)S(1)}, f32[3074]{0:T(1024)S(1)}, u32[]{:S(2)}, u32[]{:S(2)}) collective-permute-start(f32[3074]{0:T(1024)S(1)} %add.203), channel_id=1, source_target_pairs={{0,16},{8,24},{16,0},{24,8},{1,17},{9,25},{17,1},{25,9},{2,18},{10... | collective-permute-start | bytes 36896 | tf_op jit(solution)/shard_map/ppermute | solution.py:54
  (12 other events, 52.7 us)
Sparse Core Ops, SparseCore 0:
  10.9 67.0 all-gather.1
  106.7 28.1 reduce-scatter.1

commit v9 on v8

--- a/solution.py
+++ b/solution.py
@@ -73,6 +73,33 @@
     both = both.reshape(2, lax.axis_size("x"), lax.axis_size("tensor"), *value.shape)
     both = jnp.transpose(both, (1, 0, 2, 3, 4))
     return both.reshape(-1, value.shape[1])
+
+
+def ring_gather(value, axes):
+    n = lax.axis_size(axes)
+    j = lax.axis_index(axes)
+    parts = [value] + [
+        lax.ppermute(value, axes, perm=[(i, (i - k) % n) for i in range(n)])
+        for k in range(1, n)
+    ]
+    return jnp.roll(jnp.stack(parts), j, axis=0)
+
+
+def down_weight_ffn(student_hidden, down_weight):
+    along_z = ring_gather(down_weight, "q")
+    plane = ring_gather(along_z, ("x", "tensor"))
+    other = lax.ppermute(plane, "c", perm=[(0, 1), (1, 0)])
+    core = lax.axis_index("c")
+    sizes = (lax.axis_size("q"), lax.axis_size("x"), 2, lax.axis_size("tensor"))
+    tok_rows = student_hidden.shape[0]
+    order = student_hidden.reshape(tok_rows, *sizes, down_weight.shape[0])
+    order = jnp.transpose(order, (0, 3, 2, 4, 1, 5)).reshape(tok_rows, 2, -1)
+    mine_cols = lax.dynamic_index_in_dim(order, core, 1, keepdims=False)
+    other_cols = lax.dynamic_index_in_dim(order, 1 - core, 1, keepdims=False)
+    width = down_weight.shape[1]
+    return folder(mine_cols, plane.reshape(-1, width)) + folder(
+        other_cols, other.reshape(-1, width)
+    )
 
 
 def local(
@@ -113,7 +140,7 @@
     teacher_logits = jnp.dot(blended, teacher_head, preferred_element_type=jnp.float32)
     teacher_logp = jax.nn.log_softmax(teacher_logits, axis=-1)
     teacher_prob = jnp.exp(teacher_logp)
-    ffn_out = folder(student_hidden, lax.all_gather(down_weight, TOKS, axis=0, tiled=True))
+    ffn_out = down_weight_ffn(student_hidden, down_weight)
     student_scale = student_gain.astype(jnp.float32)
     normed, scaled, inverse = norm_rows(
         student_input.astype(jnp.float32) + ffn_out, student_scale, student_eps

time: 143 us -> 175 us (1.22)
  local copies, waits for them, and re-layouts: 20 us -> 36.1 us
  waiting for transfers between devices: 64.1 us -> 78.7 us
  starting transfers between devices: 18.9 us -> 21.7 us
  matrix products: 16.4 us -> 14.2 us
    ppermute x0 -> x7, waiting for transfers between devices: none -> 34 us  [the longest x6 34 us: ring_gather(): lax.ppermute(value, axes, perm=[(i, (i - k) % n) for i in range(n)])]
    ppermute x1, waiting for transfers between devices: 20 us -> 0.01 us  [teacher_attention(): got = lax.ppermute(theirs, 'tensor', perm=[(0, 1), (1, 0)])]
    all_gather x1 -> x0, waiting for transfers between devices: 13.4 us -> none  [local(): lax.all_gather(down_weight, TOKS, axis=0, tiled=True)]
    unnamed x56 -> x80, local copies, waits for them, and re-layouts: 10.5 us -> 23 us
    ppermute x7, waiting for transfers between devices: 1.94 us -> 13.4 us  [local(): lax.ppermute(send, GROUP, perm=[(i, (i - k) % group) for i in range(group)])]
    ppermute x0 -> x7, starting transfers between devices: none -> 8.35 us  [the longest x6 8.28 us: ring_gather(): lax.ppermute(value, axes, perm=[(i, (i - k) % n) for i in range(n)])]
    ppermute x7, starting transfers between devices: 8.06 us -> 4.44 us  [local(): lax.ppermute(send, GROUP, perm=[(i, (i - k) % group) for i in range(group)])]
    concatenate x0 -> x2, local copies, waits for them, and re-layouts: none -> 2.83 us  [ring_gather(): return jnp.roll(jnp.stack(parts), j, axis=0)]
  transfers between devices with their start and end apart: 19 -> 25, of which waited for: 12 -> 15; matrix products, arithmetic and copies ran while one was open for 20% -> 28% of each run, Pallas kernels for 0% -> 0%
where the time goes in v9:
time: 175 us; the launch traced here: 174 us
  waiting for transfers between devices  78.7 us (45%)
  local copies, waits for them, and re-layouts  36.1 us (21%)
  starting transfers between devices  21.7 us (12%)
  between operations  17.1 us (10%)
  matrix products  14.2 us (8%)
  other arithmetic  5.82 us (3%)
    ppermute x6, waiting for transfers between devices, ring_gather(): lax.ppermute(value, axes, perm=[(i, (i - k) % n) for i in range(n)])  34 us
    unnamed x80, local copies, waits for them, and re-layouts  23 us
    ppermute x5, waiting for transfers between devices, butterfly_sum(): lax.ppermute(value, axis, perm=[(i, i ^ step) for i in range(size)])  14.7 us
    ppermute x7, waiting for transfers between devices, local(): lax.ppermute(send, GROUP, perm=[(i, (i - k) % group) for i in range(group)])  13.4 us
    ppermute x3, waiting for transfers between devices, group_gather(): lax.ppermute(value, chips, perm=[(i, (i - k) % n) for i in range(n)])  8.97 us
    dot_general x1, matrix products, teacher_attention(): jnp.dot(context, w_out, preferred_element_type=jnp.float32)  8.41 us
    ppermute x6, starting transfers between devices, ring_gather(): lax.ppermute(value, axes, perm=[(i, (i - k) % n) for i in range(n)])  8.28 us
    reduce_scatter x1, waiting for transfers between devices, local(): lax.psum_scatter(grad_block, 'q', scatter_dimension=0, tiled=True)  5.26 us
  transfers between devices with their start and end apart: 25, of which 15 were waited for; matrix products, arithmetic and copies ran while one was open for 28% of the time, Pallas kernels for 0%

profile of v9, /device:TPU:0, one launch (start us, length us, event | category | flops | bytes accessed | tf_op | source)
XLA Modules:
  0.0 173.7 jit_solution(10708444346297779843)
XLA Ops:
  7.2 5.1 %collective-permute-start.8 = (bf16[96,768]{1,0:T(8,128)(2,1)}, bf16[96,768]{1,0:T(8,128)(2,1)S(1)}, u32[]{:S(2)}, u32[]{:S(2)}) collective-permute-start(bf16[96,768]{1,0:T(8,128)(2,1)} %param.22), channel_id=1, source_target_pairs={{0,24},{8,0},{16,8},{24,16},{1,25},{9,1},{17,9},{25,17},{2,26},{10... | collective-permute-start | bytes 442376 | tf_op jit(solution)/shard_map/ppermute | solution.py:82
  20.9 8.4 %convolution_convert_fusion = bf16[256,4096]{1,0:T(8,128)(2,1)S(1)} fusion(bf16[256,2048]{1,0:T(8,128)(2,1)S(1)} %copy-done, bf16[2048,4096]{1,0:T(8,128)(2,1)} %param.15), kind=kOutput, calls=%fused_computation | convolution fusion | flops 4296015872 | bytes 19922944 | tf_op jit(solution)/shard_map/dot_general | solution.py:33
  33.0 3.3 %collective-permute-done.2 = bf16[128,384]{0,1:T(8,128)(2,1)S(1)} collective-permute-done((bf16[128,384]{0,1:T(8,128)(2,1)S(1)}, bf16[128,384]{0,1:T(8,128)(2,1)S(1)}, u32[]{:S(2)}, u32[]{:S(2)}) %collective-permute-start.2) | collective-permute-done | bytes 98336 | tf_op jit(solution)/shard_map/ppermute | solution.py:133
  38.1 4.5 %collective-permute-done.4 = bf16[128,384]{0,1:T(8,128)(2,1)S(1)} collective-permute-done((bf16[128,384]{0,1:T(8,128)(2,1)S(1)}, bf16[128,384]{0,1:T(8,128)(2,1)S(1)}, u32[]{:S(2)}, u32[]{:S(2)}) %collective-permute-start.4) | collective-permute-done | bytes 98336 | tf_op jit(solution)/shard_map/ppermute | solution.py:133
  43.1 4.6 %collective-permute-done.6 = bf16[128,384]{0,1:T(8,128)(2,1)S(1)} collective-permute-done((bf16[128,384]{0,1:T(8,128)(2,1)S(1)}, bf16[128,384]{0,1:T(8,128)(2,1)S(1)}, u32[]{:S(2)}, u32[]{:S(2)}) %collective-permute-start.6) | collective-permute-done | bytes 98336 | tf_op jit(solution)/shard_map/ppermute | solution.py:133
  57.8 2.3 %copy.39 = bf16[8,128,384]{2,1,0:T(8,128)(2,1)} copy(bf16[8,128,384]{1,2,0:T(8,128)(2,1)} %constant_dynamic-slice_fusion.3) | data formatting | bytes 1572864 | tf_op jit(solution)/shard_map/jit(_roll_dynamic)/dynamic_slice | solution.py:135
  60.1 34.0 %collective-permute-done.11 = bf16[4,96,768]{2,1,0:T(8,128)(2,1)} collective-permute-done((bf16[4,96,768]{2,1,0:T(8,128)(2,1)}, bf16[4,96,768]{2,1,0:T(8,128)(2,1)}, u32[]{:S(2)}, u32[]{:S(2)}) %collective-permute-start.11) | collective-permute-done | bytes 589856 | tf_op jit(solution)/shard_map/ppermute | solution.py:82
  94.1 1.9 %bitcast_dynamic-update-slice_fusion.4 = bf16[8,4,96,768]{3,2,1,0:T(8,128)(2,1)} fusion(bf16[8,4,96,768]{3,2,1,0:T(8,128)(2,1)} %get-tuple-element.26, bf16[4,96,768]{2,1,0:T(8,128)(2,1)} %collective-permute-done.11), kind=kLoop, calls=%fused_computation.18 | loop fusion | bytes 1179648
  96.0 1.9 %bitcast_dynamic-update-slice_fusion.2 = bf16[8,4,96,768]{3,2,1,0:T(8,128)(2,1)} fusion(bf16[8,4,96,768]{3,2,1,0:T(8,128)(2,1)} %bitcast_dynamic-update-slice_fusion.4, bf16[4,96,768]{2,1,0:T(8,128)(2,1)} %collective-permute-done.12), kind=kLoop, calls=%fused_computation.16 | loop fusion | bytes 1179648
  98.0 1.9 %bitcast_dynamic-update-slice_fusion = bf16[8,4,96,768]{3,2,1,0:T(8,128)(2,1)} fusion(bf16[8,4,96,768]{3,2,1,0:T(8,128)(2,1)} %bitcast_dynamic-update-slice_fusion.2, bf16[4,96,768]{2,1,0:T(8,128)(2,1)} %collective-permute-done.13), kind=kLoop, calls=%fused_computation.14 | loop fusion | bytes 1179648
  99.9 1.9 %bitcast_dynamic-update-slice_fusion.7 = bf16[8,4,96,768]{3,2,1,0:T(8,128)(2,1)} fusion(bf16[8,4,96,768]{3,2,1,0:T(8,128)(2,1)} %bitcast_dynamic-update-slice_fusion, bf16[4,96,768]{2,1,0:T(8,128)(2,1)} %get-tuple-element.27), kind=kLoop, calls=%fused_computation.21 | loop fusion | bytes 1179648
  101.8 1.9 %bitcast_dynamic-update-slice_fusion.5 = bf16[8,4,96,768]{3,2,1,0:T(8,128)(2,1)} fusion(bf16[8,4,96,768]{3,2,1,0:T(8,128)(2,1)} %bitcast_dynamic-update-slice_fusion.7, bf16[4,96,768]{2,1,0:T(8,128)(2,1)} %collective-permute-done.11), kind=kLoop, calls=%fused_computation.19 | loop fusion | bytes 1179648
  103.7 1.9 %bitcast_dynamic-update-slice_fusion.3 = bf16[8,4,96,768]{3,2,1,0:T(8,128)(2,1)} fusion(bf16[8,4,96,768]{3,2,1,0:T(8,128)(2,1)} %bitcast_dynamic-update-slice_fusion.5, bf16[4,96,768]{2,1,0:T(8,128)(2,1)} %collective-permute-done.12), kind=kLoop, calls=%fused_computation.17 | loop fusion | bytes 1179648
  112.3 2.1 %fusion.19 = (f32[128]{0:T(128)S(1)}, f32[128,4]{0,1:T(4,128)S(1)}) fusion(bf16[4096,4]{0,1:T(4,128)(2,1)S(1)} %copy-done.20, bf16[128,4096]{1,0:T(8,128)(2,1)S(1)} %copy-done.1, f32[128,4096]{1,0:T(8,128)S(1)} %convert_add_fusion.1, f32[4096]{0:T(1024)S(1)} %copy-done.15, f32[128]{0:T(128)S(1)} %add_rsqrt_fusion, f32[128]{0:T(128)S(1)} %broadcast_multiply_fusion, ...), kind=kOutput, calls=%fused_computation.106 | convolution fusion | flops 8913280 | bytes 3198472 | tf_op jit(solution)/shard_map/dot_general | solution.py:140
  119.6 1.9 %collective-permute-start.17 = (bf16[128,768]{1,0:T(8,128)(2,1)S(1)}, bf16[128,768]{1,0:T(8,128)(2,1)S(1)}, u32[]{:S(2)}, u32[]{:S(2)}) collective-permute-start(bf16[128,768]{1,0:T(8,128)(2,1)S(1)} %get-tuple-element.25), channel_id=1, source_target_pairs={{0,1},{1,4},{4,5},{5,0},{2,3},{3,6},{6,7},{7,2},{8,9},{9,12},{12,1... | collective-permute-start | bytes 589832 | tf_op jit(solution)/shard_map/ppermute | solution.py:66
  121.5 3.6 %collective-permute-done.15 = bf16[128,768]{1,0:T(8,128)(2,1)S(1)} collective-permute-done((bf16[128,768]{1,0:T(8,128)(2,1)S(1)}, bf16[128,768]{1,0:T(8,128)(2,1)S(1)}, u32[]{:S(2)}, u32[]{:S(2)}) %collective-permute-start.15) | collective-permute-done | bytes 196640 | tf_op jit(solution)/shard_map/ppermute | solution.py:66
  125.1 4.1 %collective-permute-done.16 = bf16[128,768]{1,0:T(8,128)(2,1)S(1)} collective-permute-done((bf16[128,768]{1,0:T(8,128)(2,1)S(1)}, bf16[128,768]{1,0:T(8,128)(2,1)S(1)}, u32[]{:S(2)}, u32[]{:S(2)}) %collective-permute-start.16) | collective-permute-done | bytes 196640 | tf_op jit(solution)/shard_map/ppermute | solution.py:66
  130.8 2.3 %collective-permute-done.18 = bf16[4,128,768]{2,1,0:T(8,128)(2,1)S(1)} collective-permute-done((bf16[4,128,768]{2,1,0:T(8,128)(2,1)S(1)}, bf16[4,128,768]{2,1,0:T(8,128)(2,1)S(1)}, u32[]{:S(2)}, u32[]{:S(2)}) %collective-permute-start.18) | collective-permute-done | bytes 786464 | tf_op jit(solution)/shard_map/ppermute | solution.py:70
  138.0 3.6 %collective-permute-done.19 = f32[3074]{0:T(1024)S(1)} collective-permute-done((f32[3074]{0:T(1024)S(1)}, f32[3074]{0:T(1024)S(1)}, u32[]{:S(2)}, u32[]{:S(2)}) %collective-permute-start.19) | collective-permute-done | bytes 12328 | tf_op jit(solution)/shard_map/ppermute | solution.py:54
  144.4 2.1 %collective-permute-done.21 = f32[3074]{0:T(1024)S(1)} collective-permute-done((f32[3074]{0:T(1024)S(1)}, f32[3074]{0:T(1024)S(1)}, u32[]{:S(2)}, u32[]{:S(2)}) %collective-permute-start.21) | collective-permute-done | bytes 12328 | tf_op jit(solution)/shard_map/ppermute | solution.py:54
  146.6 2.5 %collective-permute-start.22 = (f32[3074]{0:T(1024)S(1)}, f32[3074]{0:T(1024)S(1)}, u32[]{:S(2)}, u32[]{:S(2)}) collective-permute-start(f32[3074]{0:T(1024)S(1)} %add.232), channel_id=1, source_target_pairs={{0,8},{8,0},{16,24},{24,16},{1,9},{9,1},{17,25},{25,17},{2,10},{10... | collective-permute-start | bytes 36896 | tf_op jit(solution)/shard_map/ppermute | solution.py:54
  149.0 2.9 %collective-permute-done.22 = f32[3074]{0:T(1024)S(1)} collective-permute-done((f32[3074]{0:T(1024)S(1)}, f32[3074]{0:T(1024)S(1)}, u32[]{:S(2)}, u32[]{:S(2)}) %collective-permute-start.22) | collective-permute-done | bytes 12328 | tf_op jit(solution)/shard_map/ppermute | solution.py:54
  152.5 4.9 %collective-permute-done.23 = f32[3074]{0:T(1024)S(1)} collective-permute-done((f32[3074]{0:T(1024)S(1)}, f32[3074]{0:T(1024)S(1)}, u32[]{:S(2)}, u32[]{:S(2)}) %collective-permute-start.23) | collective-permute-done | bytes 12328 | tf_op jit(solution)/shard_map/ppermute | solution.py:54
  160.4 5.3 %reduce-scatter.2.cloned.1.call-done = f32[96,768]{1,0:T(8,128)} async-done(((f32[384,768]{1,0:T(8,128)}), f32[96,768]{1,0:T(8,128)}) %reduce-scatter.2.cloned.1.call-update) | async-done | bytes 294928 | tf_op jit(solution)/shard_map/reduce_scatter | solution.py:187
  (161 shorter events, 47.4 us)
Async XLA Ops:
  7.2 158.5 %reduce-scatter.2.cloned.1.call-start = ((), (), s32[]{:S(2)}) async-start(), calls=%async_computation.1 | async-start | bytes 1474560 | tf_op jit(solution)/shard_map/reduce_scatter | solution.py:187
  7.2 42.4 %collective-permute-start.8 = (bf16[96,768]{1,0:T(8,128)(2,1)}, bf16[96,768]{1,0:T(8,128)(2,1)S(1)}, u32[]{:S(2)}, u32[]{:S(2)}) collective-permute-start(bf16[96,768]{1,0:T(8,128)(2,1)} %param.22), channel_id=1, source_target_pairs={{0,24},{8,0},{16,8},{24,16},{1,25},{9,1},{17,9},{25,17},{2,26},{10... | collective-permute-start | bytes 442376 | tf_op jit(solution)/shard_map/ppermute | solution.py:82
  12.3 37.4 %collective-permute-start.9 = (bf16[96,768]{1,0:T(8,128)(2,1)}, bf16[96,768]{1,0:T(8,128)(2,1)}, u32[]{:S(2)}, u32[]{:S(2)}) collective-permute-start(bf16[96,768]{1,0:T(8,128)(2,1)} %param.22), channel_id=1, source_target_pairs={{0,16},{8,24},{16,0},{24,8},{1,17},{9,25},{17,1},{25,9},{2,18},{10... | collective-permute-start | bytes 442376 | tf_op jit(solution)/shard_map/ppermute | solution.py:82
  12.3 38.3 %collective-permute-start.10 = (bf16[96,768]{1,0:T(8,128)(2,1)}, bf16[96,768]{1,0:T(8,128)(2,1)}, u32[]{:S(2)}, u32[]{:S(2)}) collective-permute-start(bf16[96,768]{1,0:T(8,128)(2,1)} %param.22), channel_id=1, source_target_pairs={{0,8},{8,16},{16,24},{24,0},{1,9},{9,17},{17,25},{25,1},{2,10},{10... | collective-permute-start | bytes 442376 | tf_op jit(solution)/shard_map/ppermute | solution.py:82
  15.9 15.3 %collective-permute-start = (bf16[128,384]{0,1:T(8,128)(2,1)}, bf16[128,384]{0,1:T(8,128)(2,1)S(1)}, u32[]{:S(2)}, u32[]{:S(2)}) collective-permute-start(bf16[128,384]{0,1:T(8,128)(2,1)} %get-tuple-element.35), channel_id=1, source_target_pairs={{0,7},{1,0},{2,1},{3,2},{4,3},{5,4},{6,5},{7,6},{8,15},{9,8},{10,9... | collective-permute-start | bytes 294920 | tf_op jit(solution)/shard_map/ppermute | solution.py:133
  16.9 14.5 %collective-permute-start.1 = (bf16[128,384]{0,1:T(8,128)(2,1)}, bf16[128,384]{0,1:T(8,128)(2,1)}, u32[]{:S(2)}, u32[]{:S(2)}) collective-permute-start(bf16[128,384]{0,1:T(8,128)(2,1)} %get-tuple-element.34), channel_id=1, source_target_pairs={{0,6},{1,7},{2,0},{3,1},{4,2},{5,3},{6,4},{7,5},{8,14},{9,15},{10,... | collective-permute-start | bytes 294920 | tf_op jit(solution)/shard_map/ppermute | solution.py:133
  31.2 5.1 %collective-permute-start.2 = (bf16[128,384]{0,1:T(8,128)(2,1)S(1)}, bf16[128,384]{0,1:T(8,128)(2,1)S(1)}, u32[]{:S(2)}, u32[]{:S(2)}) collective-permute-start(bf16[128,384]{0,1:T(8,128)(2,1)S(1)} %copy-done.13), channel_id=1, source_target_pairs={{0,5},{1,6},{2,7},{3,0},{4,1},{5,2},{6,3},{7,4},{8,13},{9,14},{10,... | collective-permute-start | bytes 294920 | tf_op jit(solution)/shard_map/ppermute | solution.py:133
  31.5 5.8 %collective-permute-start.3 = (bf16[128,384]{0,1:T(8,128)(2,1)S(1)}, bf16[128,384]{0,1:T(8,128)(2,1)S(1)}, u32[]{:S(2)}, u32[]{:S(2)}) collective-permute-start(bf16[128,384]{0,1:T(8,128)(2,1)S(1)} %copy-done.12), channel_id=1, source_target_pairs={{0,4},{1,5},{2,6},{3,7},{4,0},{5,1},{6,2},{7,3},{8,12},{9,13},{10,... | collective-permute-start | bytes 294920 | tf_op jit(solution)/shard_map/ppermute | solution.py:133
  36.3 6.4 %collective-permute-start.4 = (bf16[128,384]{0,1:T(8,128)(2,1)S(1)}, bf16[128,384]{0,1:T(8,128)(2,1)S(1)}, u32[]{:S(2)}, u32[]{:S(2)}) collective-permute-start(bf16[128,384]{0,1:T(8,128)(2,1)S(1)} %copy-done.11), channel_id=1, source_target_pairs={{0,3},{1,4},{2,5},{3,6},{4,7},{5,0},{6,1},{7,2},{8,11},{9,12},{10,... | collective-permute-start | bytes 294920 | tf_op jit(solution)/shard_map/ppermute | solution.py:133
  37.2 5.5 %collective-permute-start.5 = (bf16[128,384]{0,1:T(8,128)(2,1)S(1)}, bf16[128,384]{0,1:T(8,128)(2,1)S(1)}, u32[]{:S(2)}, u32[]{:S(2)}) collective-permute-start(bf16[128,384]{0,1:T(8,128)(2,1)S(1)} %copy-done.10), channel_id=1, source_target_pairs={{0,2},{1,3},{2,4},{3,5},{4,6},{5,7},{6,0},{7,1},{8,10},{9,11},{10,... | collective-permute-start | bytes 294920 | tf_op jit(solution)/shard_map/ppermute | solution.py:133
  42.7 5.0 %collective-permute-start.6 = (bf16[128,384]{0,1:T(8,128)(2,1)S(1)}, bf16[128,384]{0,1:T(8,128)(2,1)S(1)}, u32[]{:S(2)}, u32[]{:S(2)}) collective-permute-start(bf16[128,384]{0,1:T(8,128)(2,1)S(1)} %copy-done.9), channel_id=1, source_target_pairs={{0,1},{1,2},{2,3},{3,4},{4,5},{5,6},{6,7},{7,0},{8,9},{9,10},{10,1... | collective-permute-start | bytes 294920 | tf_op jit(solution)/shard_map/ppermute | solution.py:133
  42.7 66.8 %collective-permute-start.7 = (bf16[128,4096]{1,0:T(8,128)(2,1)}, bf16[128,4096]{1,0:T(8,128)(2,1)}, u32[]{:S(2)}, u32[]{:S(2)}) collective-permute-start(bf16[128,4096]{1,0:T(8,128)(2,1)} %broadcast_select_fusion), channel_id=1, source_target_pairs={{0,1},{1,0},{2,3},{3,2},{4,5},{5,4},{6,7},{7,6},{8,9},{9,8},{10,11... | collective-permute-start | bytes 3145736 | tf_op jit(solution)/shard_map/ppermute | solution.py:42
  54.6 39.5 %collective-permute-start.11 = (bf16[4,96,768]{2,1,0:T(8,128)(2,1)}, bf16[4,96,768]{2,1,0:T(8,128)(2,1)}, u32[]{:S(2)}, u32[]{:S(2)}) collective-permute-start(bf16[4,96,768]{2,1,0:T(8,128)(2,1)} %get-tuple-element.27), channel_id=1, source_target_pairs={{0,5},{1,0},{4,1},{5,4},{2,7},{3,2},{6,3},{7,6},{8,13},{9,8},{12,9... | collective-permute-start | bytes 1769480 | tf_op jit(solution)/shard_map/ppermute | solution.py:82
  54.6 41.4 %collective-permute-start.12 = (bf16[4,96,768]{2,1,0:T(8,128)(2,1)}, bf16[4,96,768]{2,1,0:T(8,128)(2,1)}, u32[]{:S(2)}, u32[]{:S(2)}) collective-permute-start(bf16[4,96,768]{2,1,0:T(8,128)(2,1)} %get-tuple-element.27), channel_id=1, source_target_pairs={{0,4},{1,5},{4,0},{5,1},{2,6},{3,7},{6,2},{7,3},{8,12},{9,13},{12,... | collective-permute-start | bytes 1769480 | tf_op jit(solution)/shard_map/ppermute | solution.py:82
  56.1 41.9 %collective-permute-start.13 = (bf16[4,96,768]{2,1,0:T(8,128)(2,1)}, bf16[4,96,768]{2,1,0:T(8,128)(2,1)}, u32[]{:S(2)}, u32[]{:S(2)}) collective-permute-start(bf16[4,96,768]{2,1,0:T(8,128)(2,1)} %get-tuple-element.27), channel_id=1, source_target_pairs={{0,1},{1,4},{4,5},{5,0},{2,3},{3,6},{6,7},{7,2},{8,9},{9,12},{12,1... | collective-permute-start | bytes 1769480 | tf_op jit(solution)/shard_map/ppermute | solution.py:82
  109.4 5.0 %collective-permute-start.14 = (bf16[4,4,96,768]{3,2,1,0:T(8,128)(2,1)S(1)}, bf16[4,4,96,768]{3,2,1,0:T(8,128)(2,1)S(1)}, u32[]{:S(2)}, u32[]{:S(2)}) collective-permute-start(bf16[4,4,96,768]{3,2,1,0:T(8,128)(2,1)S(1)} %constant_dynamic-slice_fusion.1), channel_id=1, source_target_pairs={{0,2},{2,0},{1,3},{3,1},{4,6},{6,4},{5,7},{7,5},{8,10},{10,8},{9,1... | collective-permute-start | bytes 7077896 | tf_op jit(solution)/shard_map/ppermute | solution.py:91
  117.8 7.3 %collective-permute-start.15 = (bf16[128,768]{1,0:T(8,128)(2,1)S(1)}, bf16[128,768]{1,0:T(8,128)(2,1)S(1)}, u32[]{:S(2)}, u32[]{:S(2)}) collective-permute-start(bf16[128,768]{1,0:T(8,128)(2,1)S(1)} %get-tuple-element.25), channel_id=1, source_target_pairs={{0,5},{1,0},{4,1},{5,4},{2,7},{3,2},{6,3},{7,6},{8,13},{9,8},{12,9... | collective-permute-start | bytes 589832 | tf_op jit(solution)/shard_map/ppermute | solution.py:66
  118.5 10.8 %collective-permute-start.16 = (bf16[128,768]{1,0:T(8,128)(2,1)S(1)}, bf16[128,768]{1,0:T(8,128)(2,1)S(1)}, u32[]{:S(2)}, u32[]{:S(2)}) collective-permute-start(bf16[128,768]{1,0:T(8,128)(2,1)S(1)} %get-tuple-element.25), channel_id=1, source_target_pairs={{0,4},{1,5},{4,0},{5,1},{2,6},{3,7},{6,2},{7,3},{8,12},{9,13},{12,... | collective-permute-start | bytes 589832 | tf_op jit(solution)/shard_map/ppermute | solution.py:66
  119.6 11.0 %collective-permute-start.17 = (bf16[128,768]{1,0:T(8,128)(2,1)S(1)}, bf16[128,768]{1,0:T(8,128)(2,1)S(1)}, u32[]{:S(2)}, u32[]{:S(2)}) collective-permute-start(bf16[128,768]{1,0:T(8,128)(2,1)S(1)} %get-tuple-element.25), channel_id=1, source_target_pairs={{0,1},{1,4},{4,5},{5,0},{2,3},{3,6},{6,7},{7,2},{8,9},{9,12},{12,1... | collective-permute-start | bytes 589832 | tf_op jit(solution)/shard_map/ppermute | solution.py:66
  130.7 2.4 %collective-permute-start.18 = (bf16[4,128,768]{2,1,0:T(8,128)(2,1)S(1)}, bf16[4,128,768]{2,1,0:T(8,128)(2,1)S(1)}, u32[]{:S(2)}, u32[]{:S(2)}) collective-permute-start(bf16[4,128,768]{2,1,0:T(8,128)(2,1)S(1)} %constant_dynamic-slice_fusion), channel_id=1, source_target_pairs={{0,2},{2,0},{1,3},{3,1},{4,6},{6,4},{5,7},{7,5},{8,10},{10,8},{9,1... | collective-permute-start | bytes 2359304 | tf_op jit(solution)/shard_map/ppermute | solution.py:70
  137.9 3.7 %collective-permute-start.19 = (f32[3074]{0:T(1024)S(1)}, f32[3074]{0:T(1024)S(1)}, u32[]{:S(2)}, u32[]{:S(2)}) collective-permute-start(f32[3074]{0:T(1024)S(1)} %concatenate.29), channel_id=1, source_target_pairs={{0,1},{1,0},{2,3},{3,2},{4,5},{5,4},{6,7},{7,6},{8,9},{9,8},{10,11... | collective-permute-start | bytes 36896 | tf_op jit(solution)/shard_map/ppermute | solution.py:54
  142.8 3.7 %collective-permute-start.21 = (f32[3074]{0:T(1024)S(1)}, f32[3074]{0:T(1024)S(1)}, u32[]{:S(2)}, u32[]{:S(2)}) collective-permute-start(f32[3074]{0:T(1024)S(1)} %add.231), channel_id=1, source_target_pairs={{0,4},{4,0},{1,5},{5,1},{2,6},{6,2},{3,7},{7,3},{8,12},{12,8},{9,1... | collective-permute-start | bytes 36896 | tf_op jit(solution)/shard_map/ppermute | solution.py:54
  146.6 5.4 %collective-permute-start.22 = (f32[3074]{0:T(1024)S(1)}, f32[3074]{0:T(1024)S(1)}, u32[]{:S(2)}, u32[]{:S(2)}) collective-permute-start(f32[3074]{0:T(1024)S(1)} %add.232), channel_id=1, source_target_pairs={{0,8},{8,0},{16,24},{24,16},{1,9},{9,1},{17,25},{25,17},{2,10},{10... | collective-permute-start | bytes 36896 | tf_op jit(solution)/shard_map/ppermute | solution.py:54
  151.9 5.5 %collective-permute-start.23 = (f32[3074]{0:T(1024)S(1)}, f32[3074]{0:T(1024)S(1)}, u32[]{:S(2)}, u32[]{:S(2)}) collective-permute-start(f32[3074]{0:T(1024)S(1)} %add.233), channel_id=1, source_target_pairs={{0,16},{8,24},{16,0},{24,8},{1,17},{9,25},{17,1},{25,9},{2,18},{10... | collective-permute-start | bytes 36896 | tf_op jit(solution)/shard_map/ppermute | solution.py:54
  (23 other events, 99.9 us)
Sparse Core Ops, SparseCore 0:
  136.2 29.4 reduce-scatter.1

commit v10 on v8

--- a/solution.py
+++ b/solution.py
@@ -157,9 +157,14 @@
     grad_block = lax.dot_general(
         hidden_mine, grad_out_group, (((0,), (0,)), ((), ())), preferred_element_type=jnp.float32
     )
-    grad_down = lax.psum_scatter(
-        grad_block, "q", scatter_dimension=0, tiled=True
-    )
+    outer_me = lax.axis_index("q")
+    row_blocks = grad_block.reshape(outer, -1, grad_block.shape[1])
+    grad_down = lax.dynamic_index_in_dim(row_blocks, outer_me, 0, keepdims=False)
+    for k in range(1, outer):
+        send = lax.dynamic_index_in_dim(row_blocks, (outer_me - k) % outer, 0, keepdims=False)
+        grad_down = grad_down + lax.ppermute(
+            send, "q", perm=[(i, (i - k) % outer) for i in range(outer)]
+        )
     classes = head_term.shape[1]
     packed = jnp.concatenate(
         [head_term.reshape(-1), jnp.stack([loss_part, jnp.sum(validity)])]

time: 143 us -> 155 us (1.084)
  local copies, waits for them, and re-layouts: 20 us -> 44.9 us
  waiting for transfers between devices: 64.1 us -> 47.5 us
  other arithmetic: 6.43 us -> 9.72 us
    ppermute x1, waiting for transfers between devices: 20 us -> 6.8 us  [teacher_attention(): got = lax.ppermute(theirs, 'tensor', perm=[(0, 1), (1, 0)])]
    unnamed x56 -> x58, local copies, waits for them, and re-layouts: 10.5 us -> 20.5 us
    ppermute x5, waiting for transfers between devices: 12.5 us -> 21.2 us  [butterfly_sum(): lax.ppermute(value, axis, perm=[(i, i ^ step) for i in range(size)])]
    another operation x0 -> x7, local copies, waits for them, and re-layouts: none -> 6.31 us  [local(): jnp.stack(pieces)]
    dynamic_slice x0 -> x8, local copies, waits for them, and re-layouts: none -> 5.55 us  [local(): lax.dynamic_index_in_dim(hidden_split, (me - k) % group, 0, keepdims=False)]
    reduce_scatter x1 -> x0, waiting for transfers between devices: 5.24 us -> none  [local(): lax.psum_scatter(grad_block, 'q', scatter_dimension=0, tiled=True)]
    ppermute x0 -> x3, starting transfers between devices: none -> 4.32 us  [local(): lax.ppermute(send, 'q', perm=[(i, (i - k) % outer) for i in range(outer)])]
    all_gather x1, waiting for transfers between devices: 13.4 us -> 9.4 us  [local(): lax.all_gather(down_weight, TOKS, axis=0, tiled=True)]
  transfers between devices with their start and end apart: 19 -> 21, of which waited for: 12 -> 11; matrix products, arithmetic and copies ran while one was open for 20% -> 34% of each run, Pallas kernels for 0% -> 0%
where the time goes in v10:
time: 155 us
  waiting for transfers between devices  47.5 us (31%)
  local copies, waits for them, and re-layouts  44.9 us (29%)
  starting transfers between devices  19.9 us (13%)
  between operations  17.2 us (11%)
  matrix products  15.3 us (10%)
  other arithmetic  9.72 us (6%)
    ppermute x5, waiting for transfers between devices, butterfly_sum(): lax.ppermute(value, axis, perm=[(i, i ^ step) for i in range(size)])  21.2 us
    unnamed x58, local copies, waits for them, and re-layouts  20.5 us
    all_gather x1, waiting for transfers between devices, local(): lax.all_gather(down_weight, TOKS, axis=0, tiled=True)  9.4 us
    dot_general x1, matrix products, teacher_attention(): jnp.dot(context, w_out, preferred_element_type=jnp.float32)  8.46 us
    ppermute x3, waiting for transfers between devices, group_gather(): lax.ppermute(value, chips, perm=[(i, (i - k) % n) for i in range(n)])  8.28 us
    ppermute x7, starting transfers between devices, local(): lax.ppermute(send, GROUP, perm=[(i, (i - k) % group) for i in range(group)])  8.08 us
    ppermute x1, waiting for transfers between devices, teacher_attention(): got = lax.ppermute(theirs, 'tensor', perm=[(0, 1), (1, 0)])  6.8 us
    another operation x7, local copies, waits for them, and re-layouts, local(): jnp.stack(pieces)  6.31 us
  transfers between devices with their start and end apart: 21, of which 11 were waited for; matrix products, arithmetic and copies ran while one was open for 34% of the time, Pallas kernels for 0%

profile of v10, /device:TPU:0, one launch (start us, length us, event | category | flops | bytes accessed | tf_op | source)
XLA Modules:
  0.0 154.5 jit_solution(2903678731725020134)
XLA Ops:
  11.4 3.3 %collective-permute-start = (bf16[128,384]{1,0:T(8,128)(2,1)}, bf16[128,384]{1,0:T(8,128)(2,1)S(1)}, u32[]{:S(2)}, u32[]{:S(2)}) collective-permute-start(bf16[128,384]{1,0:T(8,128)(2,1)} %bitcast.3), channel_id=1, source_target_pairs={{0,7},{1,0},{2,1},{3,2},{4,3},{5,4},{6,5},{7,6},{8,15},{9,8},{10,9... | collective-permute-start | bytes 294920 | tf_op jit(solution)/shard_map/ppermute | solution.py:106
  22.1 8.5 %convolution_convert_fusion = bf16[256,4096]{1,0:T(8,128)(2,1)S(1)} fusion(bf16[256,2048]{1,0:T(8,128)(2,1)S(1)} %copy-done, bf16[2048,4096]{1,0:T(8,128)(2,1)} %param.15), kind=kOutput, calls=%fused_computation | convolution fusion | flops 4296015872 | bytes 19922944 | tf_op jit(solution)/shard_map/dot_general | solution.py:33
  37.2 1.6 %copy.112 = bf16[1,128,384]{1,2,0:T(8,128)(2,1)} copy(bf16[1,128,384]{2,1,0:T(8,128)(2,1)} %bitcast.12) | data formatting | bytes 196608 | tf_op jit(solution)/shard_map/stack | solution.py:108
  38.8 1.6 %copy.113 = bf16[1,128,384]{1,2,0:T(8,128)(2,1)} copy(bf16[1,128,384]{2,1,0:T(8,128)(2,1)} %bitcast.14) | data formatting | bytes 196608 | tf_op jit(solution)/shard_map/stack | solution.py:108
  40.5 1.6 %copy.114 = bf16[1,128,384]{1,2,0:T(8,128)(2,1)} copy(bf16[1,128,384]{2,1,0:T(8,128)(2,1)} %bitcast.16) | data formatting | bytes 196608 | tf_op jit(solution)/shard_map/stack | solution.py:108
  46.3 1.5 constant_dynamic-update-slice_fusion.8
  47.8 1.6 %constant_dynamic-update-slice_fusion.7 = bf16[16,128,384]{1,2,0:T(8,128)(2,1)} fusion(bf16[16,128,384]{1,2,0:T(8,128)(2,1)} %constant_dynamic-update-slice_fusion.8, bf16[1,128,384]{1,2,0:T(8,128)(2,1)} %copy.114), kind=kLoop, calls=%fused_computation.42 | loop fusion | bytes 196608
  49.3 1.6 %dynamic-slice_dynamic-update-slice_fusion.1 = bf16[16,128,384]{1,2,0:T(8,128)(2,1)} fusion(bf16[16,128,384]{1,2,0:T(8,128)(2,1)} %constant_dynamic-update-slice_fusion.7, bf16[8,128,384]{1,2,0:T(8,128)(2,1)} %bitcast.69, s32[]{:T(128)S(6)} %select_n.147), kind=kLoop, calls=%fused_computation.34 | loop fusion | bytes 196612
  55.5 2.1 %constant_dynamic-slice_fusion.1 = bf16[8,128,384]{1,2,0:T(8,128)(2,1)} fusion(bf16[16,128,384]{1,2,0:T(8,128)(2,1)} %constant_dynamic-update-slice_fusion, s32[]{:T(128)S(6)} %select_n.163), kind=kLoop, calls=%fused_computation.52 | loop fusion | bytes 1572868 | tf_op jit(solution)/shard_map/jit(_roll_dynamic)/dynamic_slice | solution.py:108
  57.6 2.6 %copy.122 = bf16[8,128,384]{2,1,0:T(8,128)(2,1)} copy(bf16[8,128,384]{1,2,0:T(8,128)(2,1)} %constant_dynamic-slice_fusion.1) | data formatting | bytes 1572864 | tf_op jit(solution)/shard_map/jit(_roll_dynamic)/dynamic_slice | solution.py:108
  60.2 6.8 %collective-permute-done.7 = bf16[128,4096]{1,0:T(8,128)(2,1)} collective-permute-done((bf16[128,4096]{1,0:T(8,128)(2,1)}, bf16[128,4096]{1,0:T(8,128)(2,1)}, u32[]{:S(2)}, u32[]{:S(2)}) %collective-permute-start.7) | collective-permute-done | bytes 1048608 | tf_op jit(solution)/shard_map/ppermute | solution.py:42
  67.0 1.6 %convert_add_fusion.1 = f32[128,4096]{1,0:T(8,128)S(1)} fusion(bf16[128,4096]{1,0:T(8,128)(2,1)} %collective-permute-done.7, pred[]{:T(512)S(6)} %eq.51, bf16[256,4096]{1,0:T(8,128)(2,1)S(1)} %convolution_convert_fusion), kind=kLoop, calls=%fused_computation.6 | loop fusion | flops 2097152 | bytes 5242881 | tf_op jit(solution)/shard_map/add | solution.py:43
  69.7 2.1 %fusion.14 = (f32[128]{0:T(128)S(1)}, f32[128,4]{0,1:T(4,128)S(1)}) fusion(bf16[4096,4]{0,1:T(4,128)(2,1)S(1)} %copy-done.16, bf16[128,4096]{1,0:T(8,128)(2,1)S(1)} %copy-done.1, f32[128,4096]{1,0:T(8,128)S(1)} %convert_add_fusion.1, f32[4096]{0:T(1024)S(1)} %copy-done.11, f32[128]{0:T(128)S(1)} %add_rsqrt_fusion, f32[128]{0:T(128)S(1)} %broadcast_multiply_fusion, ...), kind=kOutput, calls=%fused_computation.87 | convolution fusion | flops 8913280 | bytes 3198472 | tf_op jit(solution)/shard_map/dot_general | solution.py:113
  71.9 9.4 %all-gather.2.cloned.1.call-done = bf16[3072,768]{1,0:T(8,128)(2,1)} async-done(((bf16[96,768]{1,0:T(8,128)(2,1)}), bf16[3072,768]{1,0:T(8,128)(2,1)}) %all-gather.2.cloned.1.call-update) | async-done | bytes 4718608 | tf_op jit(solution)/shard_map/all_gather | solution.py:116
  81.3 3.2 %fusion.13 = (f32[128]{0:T(128)S(1)}, f32[128,768]{1,0:T(8,128)S(1)}) fusion(bf16[128,3072]{1,0:T(8,128)(2,1)S(1)} %copy-done.3, bf16[3072,768]{1,0:T(8,128)(2,1)} %all-gather.2.cloned.1.call-done, bf16[128,768]{1,0:T(8,128)(2,1)S(1)} %copy-done.9), kind=kOutput, calls=%fused_computation.86 | convolution fusion | flops 604274560 | bytes 6095360 | tf_op jit(solution)/shard_map/dot_general | solution.py:28
  89.8 4.3 %collective-permute-done.8 = bf16[128,768]{1,0:T(8,128)(2,1)S(1)} collective-permute-done((bf16[128,768]{1,0:T(8,128)(2,1)S(1)}, bf16[128,768]{1,0:T(8,128)(2,1)S(1)}, u32[]{:S(2)}, u32[]{:S(2)}) %collective-permute-start.8) | collective-permute-done | bytes 196640 | tf_op jit(solution)/shard_map/ppermute | solution.py:66
  94.8 3.6 %collective-permute-done.9 = bf16[128,768]{1,0:T(8,128)(2,1)S(1)} collective-permute-done((bf16[128,768]{1,0:T(8,128)(2,1)S(1)}, bf16[128,768]{1,0:T(8,128)(2,1)S(1)}, u32[]{:S(2)}, u32[]{:S(2)}) %collective-permute-start.9) | collective-permute-done | bytes 196640 | tf_op jit(solution)/shard_map/ppermute | solution.py:66
  106.6 1.6 %fusion.2 = bf16[2,2,2,128,768]{4,3,2,0,1:T(8,128)(2,1)S(1)} fusion(bf16[1,2,2,128,768]{4,3,2,1,0:T(8,128)(2,1)} %bitcast.27, bf16[1,2,2,128,768]{4,3,2,1,0:T(8,128)(2,1)S(1)} %bitcast.72, pred[]{:T(512)S(6)} %eq.52), kind=kLoop, calls=%fused_computation.8 | loop fusion | flops 2359296 | bytes 3145729 | tf_op jit(solution)/shard_map/transpose | solution.py:74
  111.0 2.2 %collective-permute-start.12 = (f32[96,768]{1,0:T(8,128)}, f32[96,768]{1,0:T(8,128)}, u32[]{:S(2)}, u32[]{:S(2)}) collective-permute-start(f32[96,768]{1,0:T(8,128)} %get-tuple-element.29), channel_id=1, source_target_pairs={{0,24},{8,0},{16,8},{24,16},{1,25},{9,1},{17,9},{25,17},{2,26},{10... | collective-permute-start | bytes 884744 | tf_op jit(solution)/shard_map/ppermute | solution.py:165
  117.4 3.4 %collective-permute-done.15 = f32[3074]{0:T(1024)S(1)} collective-permute-done((f32[3074]{0:T(1024)S(1)}, f32[3074]{0:T(1024)S(1)}, u32[]{:S(2)}, u32[]{:S(2)}) %collective-permute-start.15) | collective-permute-done | bytes 12328 | tf_op jit(solution)/shard_map/ppermute | solution.py:54
  122.9 2.9 %collective-permute-done.17 = f32[3074]{0:T(1024)S(1)} collective-permute-done((f32[3074]{0:T(1024)S(1)}, f32[3074]{0:T(1024)S(1)}, u32[]{:S(2)}, u32[]{:S(2)}) %collective-permute-start.17) | collective-permute-done | bytes 12328 | tf_op jit(solution)/shard_map/ppermute | solution.py:54
  127.2 7.8 %collective-permute-done.18 = f32[3074]{0:T(1024)S(1)} collective-permute-done((f32[3074]{0:T(1024)S(1)}, f32[3074]{0:T(1024)S(1)}, u32[]{:S(2)}, u32[]{:S(2)}) %collective-permute-start.18) | collective-permute-done | bytes 12328 | tf_op jit(solution)/shard_map/ppermute | solution.py:54
  135.6 5.8 %collective-permute-done.19 = f32[3074]{0:T(1024)S(1)} collective-permute-done((f32[3074]{0:T(1024)S(1)}, f32[3074]{0:T(1024)S(1)}, u32[]{:S(2)}, u32[]{:S(2)}) %collective-permute-start.19) | collective-permute-done | bytes 12328 | tf_op jit(solution)/shard_map/ppermute | solution.py:54
  144.6 1.9 %fusion.7 = f32[96,768]{1,0:T(8,128)} fusion(f32[96,768]{1,0:T(8,128)} %collective-permute-done.14, f32[96,768]{1,0:T(8,128)} %collective-permute-done.13, f32[96,768]{1,0:T(8,128)} %collective-permute-done.12, f32[4,96,768]{2,1,0:T(8,128)S(1)} %fusion.17, s32[]{:T(128)S(6)} %select_n.174), kind=kLoop, calls=%fused_computation.21 | loop fusion | flops 221184 | bytes 1474564 | tf_op jit(solution)/shard_map/add | solution.py:165
  (144 shorter events, 54.5 us)
Async XLA Ops:
  7.2 15.0 %copy-start = (bf16[256,2048]{1,0:T(8,128)(2,1)S(1)}, bf16[256,2048]{1,0:T(8,128)(2,1)}, u32[]{:S(2)}) copy-start(bf16[256,2048]{1,0:T(8,128)(2,1)} %param.14) | copy-start | bytes 3145732
  7.2 74.1 %all-gather.2.cloned.1.call-start = ((), (), s32[]{:S(2)}) async-start(), calls=%async_computation | async-start | bytes 4866048 | tf_op jit(solution)/shard_map/all_gather | solution.py:116
  11.4 20.4 %collective-permute-start = (bf16[128,384]{1,0:T(8,128)(2,1)}, bf16[128,384]{1,0:T(8,128)(2,1)S(1)}, u32[]{:S(2)}, u32[]{:S(2)}) collective-permute-start(bf16[128,384]{1,0:T(8,128)(2,1)} %bitcast.3), channel_id=1, source_target_pairs={{0,7},{1,0},{2,1},{3,2},{4,3},{5,4},{6,5},{7,6},{8,15},{9,8},{10,9... | collective-permute-start | bytes 294920 | tf_op jit(solution)/shard_map/ppermute | solution.py:106
  14.8 18.1 %collective-permute-start.1 = (bf16[128,384]{1,0:T(8,128)(2,1)S(1)}, bf16[128,384]{1,0:T(8,128)(2,1)S(1)}, u32[]{:S(2)}, u32[]{:S(2)}) collective-permute-start(bf16[128,384]{1,0:T(8,128)(2,1)S(1)} %bitcast.78), channel_id=1, source_target_pairs={{0,6},{1,7},{2,0},{3,1},{4,2},{5,3},{6,4},{7,5},{8,14},{9,15},{10,... | collective-permute-start | bytes 294920 | tf_op jit(solution)/shard_map/ppermute | solution.py:106
  16.5 18.0 %collective-permute-start.2 = (bf16[128,384]{1,0:T(8,128)(2,1)}, bf16[128,384]{1,0:T(8,128)(2,1)S(1)}, u32[]{:S(2)}, u32[]{:S(2)}) collective-permute-start(bf16[128,384]{1,0:T(8,128)(2,1)} %bitcast.7), channel_id=1, source_target_pairs={{0,5},{1,6},{2,7},{3,0},{4,1},{5,2},{6,3},{7,4},{8,13},{9,14},{10,... | collective-permute-start | bytes 294920 | tf_op jit(solution)/shard_map/ppermute | solution.py:106
  17.5 18.7 %collective-permute-start.3 = (bf16[128,384]{1,0:T(8,128)(2,1)}, bf16[128,384]{1,0:T(8,128)(2,1)}, u32[]{:S(2)}, u32[]{:S(2)}) collective-permute-start(bf16[128,384]{1,0:T(8,128)(2,1)} %bitcast.9), channel_id=1, source_target_pairs={{0,4},{1,5},{2,6},{3,7},{4,0},{5,1},{6,2},{7,3},{8,12},{9,13},{10,... | collective-permute-start | bytes 294920 | tf_op jit(solution)/shard_map/ppermute | solution.py:106
  19.4 17.8 %collective-permute-start.4 = (bf16[128,384]{1,0:T(8,128)(2,1)}, bf16[128,384]{1,0:T(8,128)(2,1)}, u32[]{:S(2)}, u32[]{:S(2)}) collective-permute-start(bf16[128,384]{1,0:T(8,128)(2,1)} %bitcast.11), channel_id=1, source_target_pairs={{0,3},{1,4},{2,5},{3,6},{4,7},{5,0},{6,1},{7,2},{8,11},{9,12},{10,... | collective-permute-start | bytes 294920 | tf_op jit(solution)/shard_map/ppermute | solution.py:106
  31.8 7.0 %collective-permute-start.5 = (bf16[128,384]{1,0:T(8,128)(2,1)}, bf16[128,384]{1,0:T(8,128)(2,1)}, u32[]{:S(2)}, u32[]{:S(2)}) collective-permute-start(bf16[128,384]{1,0:T(8,128)(2,1)} %bitcast.13), channel_id=1, source_target_pairs={{0,2},{1,3},{2,4},{3,5},{4,6},{5,7},{6,0},{7,1},{8,10},{9,11},{10,... | collective-permute-start | bytes 294920 | tf_op jit(solution)/shard_map/ppermute | solution.py:106
  32.9 7.6 %collective-permute-start.6 = (bf16[128,384]{1,0:T(8,128)(2,1)}, bf16[128,384]{1,0:T(8,128)(2,1)}, u32[]{:S(2)}, u32[]{:S(2)}) collective-permute-start(bf16[128,384]{1,0:T(8,128)(2,1)} %bitcast.15), channel_id=1, source_target_pairs={{0,1},{1,2},{2,3},{3,4},{4,5},{5,6},{6,7},{7,0},{8,9},{9,10},{10,1... | collective-permute-start | bytes 294920 | tf_op jit(solution)/shard_map/ppermute | solution.py:106
  34.5 32.5 %collective-permute-start.7 = (bf16[128,4096]{1,0:T(8,128)(2,1)}, bf16[128,4096]{1,0:T(8,128)(2,1)}, u32[]{:S(2)}, u32[]{:S(2)}) collective-permute-start(bf16[128,4096]{1,0:T(8,128)(2,1)} %broadcast_select_fusion), channel_id=1, source_target_pairs={{0,1},{1,0},{2,3},{3,2},{4,5},{5,4},{6,7},{7,6},{8,9},{9,8},{10,11... | collective-permute-start | bytes 3145736 | tf_op jit(solution)/shard_map/ppermute | solution.py:42
  71.9 13.0 %copy-start.10 = (bf16[768,4]{0,1:T(4,128)(2,1)S(1)}, bf16[768,4]{0,1:T(4,128)(2,1)}, u32[]{:S(2)}) copy-start(bf16[768,4]{0,1:T(4,128)(2,1)} %param.24) | copy-start | bytes 18436
  71.9 13.2 %copy-start.13 = (s32[128]{0:T(128)S(1)}, s32[128]{0:T(128)}, u32[]{:S(2)}) copy-start(s32[128]{0:T(128)} %param.25) | copy-start | bytes 1540
  87.0 7.1 %collective-permute-start.8 = (bf16[128,768]{1,0:T(8,128)(2,1)S(1)}, bf16[128,768]{1,0:T(8,128)(2,1)S(1)}, u32[]{:S(2)}, u32[]{:S(2)}) collective-permute-start(bf16[128,768]{1,0:T(8,128)(2,1)S(1)} %get-tuple-element.28), channel_id=1, source_target_pairs={{0,5},{1,0},{4,1},{5,4},{2,7},{3,2},{6,3},{7,6},{8,13},{9,8},{12,9... | collective-permute-start | bytes 589832 | tf_op jit(solution)/shard_map/ppermute | solution.py:66
  88.1 10.2 %collective-permute-start.9 = (bf16[128,768]{1,0:T(8,128)(2,1)S(1)}, bf16[128,768]{1,0:T(8,128)(2,1)S(1)}, u32[]{:S(2)}, u32[]{:S(2)}) collective-permute-start(bf16[128,768]{1,0:T(8,128)(2,1)S(1)} %get-tuple-element.28), channel_id=1, source_target_pairs={{0,4},{1,5},{4,0},{5,1},{2,6},{3,7},{6,2},{7,3},{8,12},{9,13},{12,... | collective-permute-start | bytes 589832 | tf_op jit(solution)/shard_map/ppermute | solution.py:66
  89.1 10.4 %collective-permute-start.10 = (bf16[128,768]{1,0:T(8,128)(2,1)S(1)}, bf16[128,768]{1,0:T(8,128)(2,1)S(1)}, u32[]{:S(2)}, u32[]{:S(2)}) collective-permute-start(bf16[128,768]{1,0:T(8,128)(2,1)S(1)} %get-tuple-element.28), channel_id=1, source_target_pairs={{0,1},{1,4},{4,5},{5,0},{2,3},{3,6},{6,7},{7,2},{8,9},{9,12},{12,1... | collective-permute-start | bytes 589832 | tf_op jit(solution)/shard_map/ppermute | solution.py:66
  104.1 2.5 %collective-permute-start.11 = (bf16[4,128,768]{2,1,0:T(8,128)(2,1)S(1)}, bf16[4,128,768]{2,1,0:T(8,128)(2,1)}, u32[]{:S(2)}, u32[]{:S(2)}) collective-permute-start(bf16[4,128,768]{2,1,0:T(8,128)(2,1)S(1)} %constant_dynamic-slice_fusion), channel_id=1, source_target_pairs={{0,2},{2,0},{1,3},{3,1},{4,6},{6,4},{5,7},{7,5},{8,10},{10,8},{9,1... | collective-permute-start | bytes 2359304 | tf_op jit(solution)/shard_map/ppermute | solution.py:70
  111.0 33.6 %collective-permute-start.12 = (f32[96,768]{1,0:T(8,128)}, f32[96,768]{1,0:T(8,128)}, u32[]{:S(2)}, u32[]{:S(2)}) collective-permute-start(f32[96,768]{1,0:T(8,128)} %get-tuple-element.29), channel_id=1, source_target_pairs={{0,24},{8,0},{16,8},{24,16},{1,25},{9,1},{17,9},{25,17},{2,26},{10... | collective-permute-start | bytes 884744 | tf_op jit(solution)/shard_map/ppermute | solution.py:165
  113.2 31.4 %collective-permute-start.13 = (f32[96,768]{1,0:T(8,128)S(1)}, f32[96,768]{1,0:T(8,128)}, u32[]{:S(2)}, u32[]{:S(2)}) collective-permute-start(f32[96,768]{1,0:T(8,128)S(1)} %get-tuple-element.31), channel_id=1, source_target_pairs={{0,16},{8,24},{16,0},{24,8},{1,17},{9,25},{17,1},{25,9},{2,18},{10... | collective-permute-start | bytes 884744 | tf_op jit(solution)/shard_map/ppermute | solution.py:165
  114.5 30.1 %collective-permute-start.14 = (f32[96,768]{1,0:T(8,128)S(1)}, f32[96,768]{1,0:T(8,128)}, u32[]{:S(2)}, u32[]{:S(2)}) collective-permute-start(f32[96,768]{1,0:T(8,128)S(1)} %get-tuple-element.30), channel_id=1, source_target_pairs={{0,8},{8,16},{16,24},{24,0},{1,9},{9,17},{17,25},{25,1},{2,10},{10... | collective-permute-start | bytes 884744 | tf_op jit(solution)/shard_map/ppermute | solution.py:165
  117.1 3.7 %collective-permute-start.15 = (f32[3074]{0:T(1024)S(1)}, f32[3074]{0:T(1024)S(1)}, u32[]{:S(2)}, u32[]{:S(2)}) collective-permute-start(f32[3074]{0:T(1024)S(1)} %concatenate.17), channel_id=1, source_target_pairs={{0,1},{1,0},{2,3},{3,2},{4,5},{5,4},{6,7},{7,6},{8,9},{9,8},{10,11... | collective-permute-start | bytes 36896 | tf_op jit(solution)/shard_map/ppermute | solution.py:54
  120.9 1.2 collective-permute-start.16
  122.1 3.7 %collective-permute-start.17 = (f32[3074]{0:T(1024)S(1)}, f32[3074]{0:T(1024)S(1)}, u32[]{:S(2)}, u32[]{:S(2)}) collective-permute-start(f32[3074]{0:T(1024)S(1)} %add.243), channel_id=1, source_target_pairs={{0,4},{4,0},{1,5},{5,1},{2,6},{6,2},{3,7},{7,3},{8,12},{12,8},{9,1... | collective-permute-start | bytes 36896 | tf_op jit(solution)/shard_map/ppermute | solution.py:54
  125.8 9.2 %collective-permute-start.18 = (f32[3074]{0:T(1024)S(1)}, f32[3074]{0:T(1024)S(1)}, u32[]{:S(2)}, u32[]{:S(2)}) collective-permute-start(f32[3074]{0:T(1024)S(1)} %add.244), channel_id=1, source_target_pairs={{0,8},{8,0},{16,24},{24,16},{1,9},{9,1},{17,25},{25,17},{2,10},{10... | collective-permute-start | bytes 36896 | tf_op jit(solution)/shard_map/ppermute | solution.py:54
  135.0 6.4 %collective-permute-start.19 = (f32[3074]{0:T(1024)S(1)}, f32[3074]{0:T(1024)S(1)}, u32[]{:S(2)}, u32[]{:S(2)}) collective-permute-start(f32[3074]{0:T(1024)S(1)} %add.245), channel_id=1, source_target_pairs={{0,16},{8,24},{16,0},{24,8},{1,17},{9,25},{17,1},{25,9},{2,18},{10... | collective-permute-start | bytes 36896 | tf_op jit(solution)/shard_map/ppermute | solution.py:54
  (15 other events, 115.5 us)
Sparse Core Ops, SparseCore 0:
  10.9 70.3 all-gather.1

commit v11 on v8

--- a/solution.py
+++ b/solution.py
@@ -153,12 +153,23 @@
         )
         * inverse
     ).astype(jnp.bfloat16)
-    grad_out_group = group_gather(grad_out)
-    grad_block = lax.dot_general(
-        hidden_mine, grad_out_group, (((0,), (0,)), ((), ())), preferred_element_type=jnp.float32
-    )
-    grad_down = lax.psum_scatter(
-        grad_block, "q", scatter_dimension=0, tiled=True
+    half = grad_out.shape[1] // 2
+    grad_down = jnp.concatenate(
+        [
+            lax.psum_scatter(
+                lax.dot_general(
+                    hidden_mine,
+                    group_gather(cols),
+                    (((0,), (0,)), ((), ())),
+                    preferred_element_type=jnp.float32,
+                ),
+                "q",
+                scatter_dimension=0,
+                tiled=True,
+            )
+            for cols in (grad_out[:, :half], grad_out[:, half:])
+        ],
+        axis=1,
     )
     classes = head_term.shape[1]
     packed = jnp.concatenate(

time: 143 us -> 149 us (1.042)
  local copies, waits for them, and re-layouts: 20 us -> 13.2 us
  waiting for transfers between devices: 64.1 us -> 70 us
  starting transfers between devices: 18.9 us -> 22.4 us
  other arithmetic: 6.43 us -> 8.41 us
    unnamed x56 -> x50, local copies, waits for them, and re-layouts: 10.5 us -> 5.52 us
    reduce_scatter x1 -> x2, waiting for transfers between devices: 5.24 us -> 9.3 us  [local(): lax.psum_scatter(lax.dot_general(hidden_mine, group_gather(cols), (((0,),...]
    ppermute x3 -> x6, starting transfers between devices: 3.45 us -> 6.8 us  [group_gather(): lax.ppermute(value, chips, perm=[(i, (i - k) % n) for i in range(n)])]
    concatenate x0 -> x3, other arithmetic: none -> 2.68 us  [the longest x1 1.71 us: local(): jnp.concatenate([lax.psum_scatter(lax.dot_general(hidden_mine, group_gath...]
    ppermute x3 -> x6, waiting for transfers between devices: 8.1 us -> 9.93 us  [group_gather(): lax.ppermute(value, chips, perm=[(i, (i - k) % n) for i in range(n)])]
    ppermute x1 -> x2, waiting for transfers between devices: 2.27 us -> 3.41 us  [group_gather(): other = lax.ppermute(plane, 'c', perm=[(0, 1), (1, 0)])]
  transfers between devices with their start and end apart: 19 -> 24, of which waited for: 12 -> 17; matrix products, arithmetic and copies ran while one was open for 20% -> 20% of each run, Pallas kernels for 0% -> 0%
where the time goes in v11:
time: 149 us; the launch traced here: 148 us
  waiting for transfers between devices  70 us (47%)
  starting transfers between devices  22.4 us (15%)
  matrix products  17.5 us (12%)
  between operations  16.9 us (11%)
  local copies, waits for them, and re-layouts  13.2 us (9%)
  other arithmetic  8.41 us (6%)
    ppermute x1, waiting for transfers between devices, teacher_attention(): got = lax.ppermute(theirs, 'tensor', perm=[(0, 1), (1, 0)])  20 us
    all_gather x1, waiting for transfers between devices, local(): lax.all_gather(down_weight, TOKS, axis=0, tiled=True)  13.4 us
    ppermute x5, waiting for transfers between devices, butterfly_sum(): lax.ppermute(value, axis, perm=[(i, i ^ step) for i in range(size)])  11.3 us
    ppermute x6, waiting for transfers between devices, group_gather(): lax.ppermute(value, chips, perm=[(i, (i - k) % n) for i in range(n)])  9.93 us
    reduce_scatter x2, waiting for transfers between devices, local(): lax.psum_scatter(lax.dot_general(hidden_mine, group_gather(cols), (((0,),...  9.3 us
    dot_general x1, matrix products, teacher_attention(): jnp.dot(context, w_out, preferred_element_type=jnp.float32)  8.56 us
    ppermute x7, starting transfers between devices, local(): lax.ppermute(send, GROUP, perm=[(i, (i - k) % group) for i in range(group)])  8.08 us
    ppermute x6, starting transfers between devices, group_gather(): lax.ppermute(value, chips, perm=[(i, (i - k) % n) for i in range(n)])  6.8 us
  transfers between devices with their start and end apart: 24, of which 17 were waited for; matrix products, arithmetic and copies ran while one was open for 20% of the time, Pallas kernels for 0%

profile of v11, /device:TPU:0, one launch (start us, length us, event | category | flops | bytes accessed | tf_op | source)
XLA Modules:
  0.0 148.3 jit_solution(11400384607365210425)
XLA Ops:
  10.8 3.3 %collective-permute-start = (bf16[128,384]{0,1:T(8,128)(2,1)}, bf16[128,384]{0,1:T(8,128)(2,1)S(1)}, u32[]{:S(2)}, u32[]{:S(2)}) collective-permute-start(bf16[128,384]{0,1:T(8,128)(2,1)} %get-tuple-element.32), channel_id=1, source_target_pairs={{0,7},{1,0},{2,1},{3,2},{4,3},{5,4},{6,5},{7,6},{8,15},{9,8},{10,9... | collective-permute-start | bytes 294920 | tf_op jit(solution)/shard_map/ppermute | solution.py:106
  17.7 8.6 %convolution_convert_fusion = bf16[256,4096]{1,0:T(8,128)(2,1)S(1)} fusion(bf16[256,2048]{1,0:T(8,128)(2,1)S(1)} %copy-done, bf16[2048,4096]{1,0:T(8,128)(2,1)} %param.17), kind=kOutput, calls=%fused_computation | convolution fusion | flops 4296015872 | bytes 19922944 | tf_op jit(solution)/shard_map/dot_general | solution.py:33
  32.4 1.9 %collective-permute-done.6 = bf16[128,384]{0,1:T(8,128)(2,1)S(1)} collective-permute-done((bf16[128,384]{0,1:T(8,128)(2,1)S(1)}, bf16[128,384]{0,1:T(8,128)(2,1)S(1)}, u32[]{:S(2)}, u32[]{:S(2)}) %collective-permute-start.6) | collective-permute-done | bytes 98336 | tf_op jit(solution)/shard_map/ppermute | solution.py:106
  37.4 2.3 %copy.35 = bf16[8,128,384]{2,1,0:T(8,128)(2,1)} copy(bf16[8,128,384]{1,2,0:T(8,128)(2,1)} %constant_dynamic-slice_fusion) | data formatting | bytes 1572864 | tf_op jit(solution)/shard_map/jit(_roll_dynamic)/dynamic_slice | solution.py:108
  39.7 20.0 %collective-permute-done.7 = bf16[128,4096]{1,0:T(8,128)(2,1)} collective-permute-done((bf16[128,4096]{1,0:T(8,128)(2,1)}, bf16[128,4096]{1,0:T(8,128)(2,1)}, u32[]{:S(2)}, u32[]{:S(2)}) %collective-permute-start.7) | collective-permute-done | bytes 1048608 | tf_op jit(solution)/shard_map/ppermute | solution.py:42
  59.6 1.6 %convert_add_fusion.1 = f32[128,4096]{1,0:T(8,128)S(1)} fusion(bf16[128,4096]{1,0:T(8,128)(2,1)} %collective-permute-done.7, pred[]{:T(512)S(6)} %eq.48, bf16[256,4096]{1,0:T(8,128)(2,1)S(1)} %convolution_convert_fusion), kind=kLoop, calls=%fused_computation.6 | loop fusion | flops 2097152 | bytes 5242881 | tf_op jit(solution)/shard_map/add | solution.py:43
  62.4 2.1 %fusion.26 = (f32[128]{0:T(128)S(1)}, f32[128,4]{0,1:T(4,128)S(1)}) fusion(bf16[4096,4]{0,1:T(4,128)(2,1)S(1)} %copy-done.15, bf16[128,4096]{1,0:T(8,128)(2,1)S(1)} %copy-done.1, f32[128,4096]{1,0:T(8,128)S(1)} %convert_add_fusion.1, f32[4096]{0:T(1024)S(1)} %copy-done.10, f32[128]{0:T(128)S(1)} %add_rsqrt_fusion, f32[128]{0:T(128)S(1)} %broadcast_multiply_fusion, ...), kind=kOutput, calls=%fused_computation.106 | convolution fusion | flops 8913280 | bytes 3198472 | tf_op jit(solution)/shard_map/dot_general | solution.py:113
  64.5 13.4 %all-gather.2.cloned.1.call-done = bf16[3072,768]{1,0:T(8,128)(2,1)} async-done(((bf16[96,768]{1,0:T(8,128)(2,1)}), bf16[3072,768]{1,0:T(8,128)(2,1)}) %all-gather.2.cloned.1.call-update) | async-done | bytes 4718608 | tf_op jit(solution)/shard_map/all_gather | solution.py:116
  78.0 3.2 %fusion.25 = (f32[128]{0:T(128)S(1)}, f32[128,768]{1,0:T(8,128)S(1)}) fusion(bf16[128,3072]{1,0:T(8,128)(2,1)S(1)} %copy-done.3, bf16[3072,768]{1,0:T(8,128)(2,1)} %all-gather.2.cloned.1.call-done, bf16[128,768]{1,0:T(8,128)(2,1)S(1)} %copy-done.6), kind=kOutput, calls=%fused_computation.105 | convolution fusion | flops 604274560 | bytes 6095360 | tf_op jit(solution)/shard_map/dot_general | solution.py:28
  83.1 1.5 %collective-permute-start.8 = (bf16[128,384]{1,0:T(8,128)(2,1)S(1)}, bf16[128,384]{1,0:T(8,128)(2,1)S(1)}, u32[]{:S(2)}, u32[]{:S(2)}) collective-permute-start(bf16[128,384]{1,0:T(8,128)(2,1)S(1)} %get-tuple-element.33), channel_id=1, source_target_pairs={{0,5},{1,0},{4,1},{5,4},{2,7},{3,2},{6,3},{7,6},{8,13},{9,8},{12,9... | collective-permute-start | bytes 294920 | tf_op jit(solution)/shard_map/ppermute | solution.py:66
  86.6 1.5 %collective-permute-done.8 = bf16[128,384]{1,0:T(8,128)(2,1)S(1)} collective-permute-done((bf16[128,384]{1,0:T(8,128)(2,1)S(1)}, bf16[128,384]{1,0:T(8,128)(2,1)S(1)}, u32[]{:S(2)}, u32[]{:S(2)}) %collective-permute-start.8) | collective-permute-done | bytes 98336 | tf_op jit(solution)/shard_map/ppermute | solution.py:66
  88.1 3.0 %collective-permute-done.9 = bf16[128,384]{1,0:T(8,128)(2,1)S(1)} collective-permute-done((bf16[128,384]{1,0:T(8,128)(2,1)S(1)}, bf16[128,384]{1,0:T(8,128)(2,1)S(1)}, u32[]{:S(2)}, u32[]{:S(2)}) %collective-permute-start.9) | collective-permute-done | bytes 98336 | tf_op jit(solution)/shard_map/ppermute | solution.py:66
  92.1 1.7 %collective-permute-done.11 = bf16[4,128,384]{2,1,0:T(8,128)(2,1)S(1)} collective-permute-done((bf16[4,128,384]{2,1,0:T(8,128)(2,1)S(1)}, bf16[4,128,384]{2,1,0:T(8,128)(2,1)S(1)}, u32[]{:S(2)}, u32[]{:S(2)}) %collective-permute-start.11) | collective-permute-done | bytes 393248 | tf_op jit(solution)/shard_map/ppermute | solution.py:70
  98.8 1.6 %collective-permute-done.12 = bf16[128,384]{1,0:T(8,128)(2,1)S(1)} collective-permute-done((bf16[128,384]{1,0:T(8,128)(2,1)S(1)}, bf16[128,384]{1,0:T(8,128)(2,1)S(1)}, u32[]{:S(2)}, u32[]{:S(2)}) %collective-permute-start.12) | collective-permute-done | bytes 98336 | tf_op jit(solution)/shard_map/ppermute | solution.py:66
  100.3 2.5 %collective-permute-done.13 = bf16[128,384]{1,0:T(8,128)(2,1)S(1)} collective-permute-done((bf16[128,384]{1,0:T(8,128)(2,1)S(1)}, bf16[128,384]{1,0:T(8,128)(2,1)S(1)}, u32[]{:S(2)}, u32[]{:S(2)}) %collective-permute-start.13) | collective-permute-done | bytes 98336 | tf_op jit(solution)/shard_map/ppermute | solution.py:66
  104.3 1.7 %collective-permute-done.15 = bf16[4,128,384]{2,1,0:T(8,128)(2,1)S(1)} collective-permute-done((bf16[4,128,384]{2,1,0:T(8,128)(2,1)S(1)}, bf16[4,128,384]{2,1,0:T(8,128)(2,1)S(1)}, u32[]{:S(2)}, u32[]{:S(2)}) %collective-permute-start.15) | collective-permute-done | bytes 393248 | tf_op jit(solution)/shard_map/ppermute | solution.py:70
  110.0 3.1 %collective-permute-done.16 = f32[3074]{0:T(1024)S(1)} collective-permute-done((f32[3074]{0:T(1024)S(1)}, f32[3074]{0:T(1024)S(1)}, u32[]{:S(2)}, u32[]{:S(2)}) %collective-permute-start.16) | collective-permute-done | bytes 12328 | tf_op jit(solution)/shard_map/ppermute | solution.py:54
  115.5 2.6 %collective-permute-done.18 = f32[3074]{0:T(1024)S(1)} collective-permute-done((f32[3074]{0:T(1024)S(1)}, f32[3074]{0:T(1024)S(1)}, u32[]{:S(2)}, u32[]{:S(2)}) %collective-permute-start.18) | collective-permute-done | bytes 12328 | tf_op jit(solution)/shard_map/ppermute | solution.py:54
  118.1 1.9 %collective-permute-start.19 = (f32[3074]{0:T(1024)S(1)}, f32[3074]{0:T(1024)S(1)}, u32[]{:S(2)}, u32[]{:S(2)}) collective-permute-start(f32[3074]{0:T(1024)S(1)} %add.201), channel_id=1, source_target_pairs={{0,8},{8,0},{16,24},{24,16},{1,9},{9,1},{17,25},{25,17},{2,10},{10... | collective-permute-start | bytes 36896 | tf_op jit(solution)/shard_map/ppermute | solution.py:54
  120.0 1.8 %collective-permute-done.19 = f32[3074]{0:T(1024)S(1)} collective-permute-done((f32[3074]{0:T(1024)S(1)}, f32[3074]{0:T(1024)S(1)}, u32[]{:S(2)}, u32[]{:S(2)}) %collective-permute-start.19) | collective-permute-done | bytes 12328 | tf_op jit(solution)/shard_map/ppermute | solution.py:54
  121.8 2.1 %collective-permute-start.20 = (f32[3074]{0:T(1024)S(1)}, f32[3074]{0:T(1024)S(1)}, u32[]{:S(2)}, u32[]{:S(2)}) collective-permute-start(f32[3074]{0:T(1024)S(1)} %add.202), channel_id=1, source_target_pairs={{0,16},{8,24},{16,0},{24,8},{1,17},{9,25},{17,1},{25,9},{2,18},{10... | collective-permute-start | bytes 36896 | tf_op jit(solution)/shard_map/ppermute | solution.py:54
  123.9 2.6 %collective-permute-done.20 = f32[3074]{0:T(1024)S(1)} collective-permute-done((f32[3074]{0:T(1024)S(1)}, f32[3074]{0:T(1024)S(1)}, u32[]{:S(2)}, u32[]{:S(2)}) %collective-permute-start.20) | collective-permute-done | bytes 12328 | tf_op jit(solution)/shard_map/ppermute | solution.py:54
  129.6 9.3 %reduce-scatter.5.cloned.1.call-done = f32[96,384]{1,0:T(8,128)} async-done(((f32[384,384]{1,0:T(8,128)}), f32[96,384]{1,0:T(8,128)}) %reduce-scatter.5.cloned.1.call-update) | async-done | bytes 147472 | tf_op jit(solution)/shard_map/reduce_scatter | solution.py:159
  138.9 1.7 %pad_maximum_fusion = f32[96,768]{1,0:T(8,128)} fusion(f32[96,384]{1,0:T(8,128)} %reduce-scatter.5.cloned.1.call-done, f32[96,384]{1,0:T(8,128)} %reduce-scatter.3.cloned.1.call-done), kind=kLoop, calls=%fused_computation.49 | loop fusion | flops 73728 | bytes 589824 | tf_op jit(solution)/shard_map/concatenate | solution.py:157
  (130 shorter events, 36.3 us)
Async XLA Ops:
  7.2 70.8 %all-gather.2.cloned.1.call-start = ((), (), s32[]{:S(2)}) async-start(), calls=%async_computation.2 | async-start | bytes 4866048 | tf_op jit(solution)/shard_map/all_gather | solution.py:116
  7.9 121.7 %reduce-scatter.3.cloned.1.call-start = ((), (), s32[]{:S(2)}) async-start(), calls=%async_computation.3 | async-start | bytes 737280 | tf_op jit(solution)/shard_map/reduce_scatter | solution.py:159
  10.8 17.2 %collective-permute-start = (bf16[128,384]{0,1:T(8,128)(2,1)}, bf16[128,384]{0,1:T(8,128)(2,1)S(1)}, u32[]{:S(2)}, u32[]{:S(2)}) collective-permute-start(bf16[128,384]{0,1:T(8,128)(2,1)} %get-tuple-element.32), channel_id=1, source_target_pairs={{0,7},{1,0},{2,1},{3,2},{4,3},{5,4},{6,5},{7,6},{8,15},{9,8},{10,9... | collective-permute-start | bytes 294920 | tf_op jit(solution)/shard_map/ppermute | solution.py:106
  14.1 15.0 %collective-permute-start.1 = (bf16[128,384]{0,1:T(8,128)(2,1)}, bf16[128,384]{0,1:T(8,128)(2,1)S(1)}, u32[]{:S(2)}, u32[]{:S(2)}) collective-permute-start(bf16[128,384]{0,1:T(8,128)(2,1)} %get-tuple-element.31), channel_id=1, source_target_pairs={{0,6},{1,7},{2,0},{3,1},{4,2},{5,3},{6,4},{7,5},{8,14},{9,15},{10,... | collective-permute-start | bytes 294920 | tf_op jit(solution)/shard_map/ppermute | solution.py:106
  14.9 15.0 %collective-permute-start.2 = (bf16[128,384]{0,1:T(8,128)(2,1)}, bf16[128,384]{0,1:T(8,128)(2,1)S(1)}, u32[]{:S(2)}, u32[]{:S(2)}) collective-permute-start(bf16[128,384]{0,1:T(8,128)(2,1)} %get-tuple-element.30), channel_id=1, source_target_pairs={{0,5},{1,6},{2,7},{3,0},{4,1},{5,2},{6,3},{7,4},{8,13},{9,14},{10,... | collective-permute-start | bytes 294920 | tf_op jit(solution)/shard_map/ppermute | solution.py:106
  15.2 16.2 %collective-permute-start.3 = (bf16[128,384]{0,1:T(8,128)(2,1)}, bf16[128,384]{0,1:T(8,128)(2,1)S(1)}, u32[]{:S(2)}, u32[]{:S(2)}) collective-permute-start(bf16[128,384]{0,1:T(8,128)(2,1)} %get-tuple-element.29), channel_id=1, source_target_pairs={{0,4},{1,5},{2,6},{3,7},{4,0},{5,1},{6,2},{7,3},{8,12},{9,13},{10,... | collective-permute-start | bytes 294920 | tf_op jit(solution)/shard_map/ppermute | solution.py:106
  16.4 15.1 %collective-permute-start.4 = (bf16[128,384]{0,1:T(8,128)(2,1)}, bf16[128,384]{0,1:T(8,128)(2,1)}, u32[]{:S(2)}, u32[]{:S(2)}) collective-permute-start(bf16[128,384]{0,1:T(8,128)(2,1)} %get-tuple-element.28), channel_id=1, source_target_pairs={{0,3},{1,4},{2,5},{3,6},{4,7},{5,0},{6,1},{7,2},{8,11},{9,12},{10,... | collective-permute-start | bytes 294920 | tf_op jit(solution)/shard_map/ppermute | solution.py:106
  28.0 4.4 %collective-permute-start.5 = (bf16[128,384]{0,1:T(8,128)(2,1)S(1)}, bf16[128,384]{0,1:T(8,128)(2,1)S(1)}, u32[]{:S(2)}, u32[]{:S(2)}) collective-permute-start(bf16[128,384]{0,1:T(8,128)(2,1)S(1)} %copy-done.8), channel_id=1, source_target_pairs={{0,2},{1,3},{2,4},{3,5},{4,6},{5,7},{6,0},{7,1},{8,10},{9,11},{10,... | collective-permute-start | bytes 294920 | tf_op jit(solution)/shard_map/ppermute | solution.py:106
  29.1 5.2 %collective-permute-start.6 = (bf16[128,384]{0,1:T(8,128)(2,1)S(1)}, bf16[128,384]{0,1:T(8,128)(2,1)S(1)}, u32[]{:S(2)}, u32[]{:S(2)}) collective-permute-start(bf16[128,384]{0,1:T(8,128)(2,1)S(1)} %copy-done.7), channel_id=1, source_target_pairs={{0,1},{1,2},{2,3},{3,4},{4,5},{5,6},{6,7},{7,0},{8,9},{9,10},{10,1... | collective-permute-start | bytes 294920 | tf_op jit(solution)/shard_map/ppermute | solution.py:106
  30.0 29.7 %collective-permute-start.7 = (bf16[128,4096]{1,0:T(8,128)(2,1)}, bf16[128,4096]{1,0:T(8,128)(2,1)}, u32[]{:S(2)}, u32[]{:S(2)}) collective-permute-start(bf16[128,4096]{1,0:T(8,128)(2,1)} %broadcast_select_fusion), channel_id=1, source_target_pairs={{0,1},{1,0},{2,3},{3,2},{4,5},{5,4},{6,7},{7,6},{8,9},{9,8},{10,11... | collective-permute-start | bytes 3145736 | tf_op jit(solution)/shard_map/ppermute | solution.py:42
  83.1 5.0 %collective-permute-start.8 = (bf16[128,384]{1,0:T(8,128)(2,1)S(1)}, bf16[128,384]{1,0:T(8,128)(2,1)S(1)}, u32[]{:S(2)}, u32[]{:S(2)}) collective-permute-start(bf16[128,384]{1,0:T(8,128)(2,1)S(1)} %get-tuple-element.33), channel_id=1, source_target_pairs={{0,5},{1,0},{4,1},{5,4},{2,7},{3,2},{6,3},{7,6},{8,13},{9,8},{12,9... | collective-permute-start | bytes 294920 | tf_op jit(solution)/shard_map/ppermute | solution.py:66
  84.6 6.5 %collective-permute-start.9 = (bf16[128,384]{1,0:T(8,128)(2,1)S(1)}, bf16[128,384]{1,0:T(8,128)(2,1)S(1)}, u32[]{:S(2)}, u32[]{:S(2)}) collective-permute-start(bf16[128,384]{1,0:T(8,128)(2,1)S(1)} %get-tuple-element.33), channel_id=1, source_target_pairs={{0,4},{1,5},{4,0},{5,1},{2,6},{3,7},{6,2},{7,3},{8,12},{9,13},{12,... | collective-permute-start | bytes 294920 | tf_op jit(solution)/shard_map/ppermute | solution.py:66
  86.0 5.5 %collective-permute-start.10 = (bf16[128,384]{1,0:T(8,128)(2,1)S(1)}, bf16[128,384]{1,0:T(8,128)(2,1)S(1)}, u32[]{:S(2)}, u32[]{:S(2)}) collective-permute-start(bf16[128,384]{1,0:T(8,128)(2,1)S(1)} %get-tuple-element.33), channel_id=1, source_target_pairs={{0,1},{1,4},{4,5},{5,0},{2,3},{3,6},{6,7},{7,2},{8,9},{9,12},{12,1... | collective-permute-start | bytes 294920 | tf_op jit(solution)/shard_map/ppermute | solution.py:66
  92.0 1.8 %collective-permute-start.11 = (bf16[4,128,384]{2,1,0:T(8,128)(2,1)S(1)}, bf16[4,128,384]{2,1,0:T(8,128)(2,1)S(1)}, u32[]{:S(2)}, u32[]{:S(2)}) collective-permute-start(bf16[4,128,384]{2,1,0:T(8,128)(2,1)S(1)} %fusion.15), channel_id=1, source_target_pairs={{0,2},{2,0},{1,3},{3,1},{4,6},{6,4},{5,7},{7,5},{8,10},{10,8},{9,1... | collective-permute-start | bytes 1179656 | tf_op jit(solution)/shard_map/ppermute | solution.py:70
  95.4 43.5 %reduce-scatter.5.cloned.1.call-start = ((), (), s32[]{:S(2)}) async-start(), calls=%async_computation.4 | async-start | bytes 737280 | tf_op jit(solution)/shard_map/reduce_scatter | solution.py:159
  95.5 4.9 %collective-permute-start.12 = (bf16[128,384]{1,0:T(8,128)(2,1)S(1)}, bf16[128,384]{1,0:T(8,128)(2,1)S(1)}, u32[]{:S(2)}, u32[]{:S(2)}) collective-permute-start(bf16[128,384]{1,0:T(8,128)(2,1)S(1)} %get-tuple-element.36), channel_id=1, source_target_pairs={{0,5},{1,0},{4,1},{5,4},{2,7},{3,2},{6,3},{7,6},{8,13},{9,8},{12,9... | collective-permute-start | bytes 294920 | tf_op jit(solution)/shard_map/ppermute | solution.py:66
  96.5 6.4 %collective-permute-start.13 = (bf16[128,384]{1,0:T(8,128)(2,1)S(1)}, bf16[128,384]{1,0:T(8,128)(2,1)S(1)}, u32[]{:S(2)}, u32[]{:S(2)}) collective-permute-start(bf16[128,384]{1,0:T(8,128)(2,1)S(1)} %get-tuple-element.36), channel_id=1, source_target_pairs={{0,4},{1,5},{4,0},{5,1},{2,6},{3,7},{6,2},{7,3},{8,12},{9,13},{12,... | collective-permute-start | bytes 294920 | tf_op jit(solution)/shard_map/ppermute | solution.py:66
  98.0 5.7 %collective-permute-start.14 = (bf16[128,384]{1,0:T(8,128)(2,1)S(1)}, bf16[128,384]{1,0:T(8,128)(2,1)S(1)}, u32[]{:S(2)}, u32[]{:S(2)}) collective-permute-start(bf16[128,384]{1,0:T(8,128)(2,1)S(1)} %get-tuple-element.36), channel_id=1, source_target_pairs={{0,1},{1,4},{4,5},{5,0},{2,3},{3,6},{6,7},{7,2},{8,9},{9,12},{12,1... | collective-permute-start | bytes 294920 | tf_op jit(solution)/shard_map/ppermute | solution.py:66
  104.2 1.8 %collective-permute-start.15 = (bf16[4,128,384]{2,1,0:T(8,128)(2,1)S(1)}, bf16[4,128,384]{2,1,0:T(8,128)(2,1)S(1)}, u32[]{:S(2)}, u32[]{:S(2)}) collective-permute-start(bf16[4,128,384]{2,1,0:T(8,128)(2,1)S(1)} %fusion.8), channel_id=1, source_target_pairs={{0,2},{2,0},{1,3},{3,1},{4,6},{6,4},{5,7},{7,5},{8,10},{10,8},{9,1... | collective-permute-start | bytes 1179656 | tf_op jit(solution)/shard_map/ppermute | solution.py:70
  109.4 3.7 %collective-permute-start.16 = (f32[3074]{0:T(1024)S(1)}, f32[3074]{0:T(1024)S(1)}, u32[]{:S(2)}, u32[]{:S(2)}) collective-permute-start(f32[3074]{0:T(1024)S(1)} %concatenate.20), channel_id=1, source_target_pairs={{0,1},{1,0},{2,3},{3,2},{4,5},{5,4},{6,7},{7,6},{8,9},{9,8},{10,11... | collective-permute-start | bytes 36896 | tf_op jit(solution)/shard_map/ppermute | solution.py:54
  113.1 1.2 collective-permute-start.17
  114.3 3.7 %collective-permute-start.18 = (f32[3074]{0:T(1024)S(1)}, f32[3074]{0:T(1024)S(1)}, u32[]{:S(2)}, u32[]{:S(2)}) collective-permute-start(f32[3074]{0:T(1024)S(1)} %add.200), channel_id=1, source_target_pairs={{0,4},{4,0},{1,5},{5,1},{2,6},{6,2},{3,7},{7,3},{8,12},{12,8},{9,1... | collective-permute-start | bytes 36896 | tf_op jit(solution)/shard_map/ppermute | solution.py:54
  118.1 3.7 %collective-permute-start.19 = (f32[3074]{0:T(1024)S(1)}, f32[3074]{0:T(1024)S(1)}, u32[]{:S(2)}, u32[]{:S(2)}) collective-permute-start(f32[3074]{0:T(1024)S(1)} %add.201), channel_id=1, source_target_pairs={{0,8},{8,0},{16,24},{24,16},{1,9},{9,1},{17,25},{25,17},{2,10},{10... | collective-permute-start | bytes 36896 | tf_op jit(solution)/shard_map/ppermute | solution.py:54
  121.8 4.7 %collective-permute-start.20 = (f32[3074]{0:T(1024)S(1)}, f32[3074]{0:T(1024)S(1)}, u32[]{:S(2)}, u32[]{:S(2)}) collective-permute-start(f32[3074]{0:T(1024)S(1)} %add.202), channel_id=1, source_target_pairs={{0,16},{8,24},{16,0},{24,8},{1,17},{9,25},{17,1},{25,9},{2,18},{10... | collective-permute-start | bytes 36896 | tf_op jit(solution)/shard_map/ppermute | solution.py:54
  (17 other events, 149.5 us)
Sparse Core Ops, SparseCore 0:
  10.9 66.9 all-gather.1
  95.5 20.4 reduce-scatter.2
  118.4 20.4 reduce-scatter.4

commit v12 on v8

--- a/solution.py
+++ b/solution.py
@@ -73,6 +73,26 @@
     both = both.reshape(2, lax.axis_size("x"), lax.axis_size("tensor"), *value.shape)
     both = jnp.transpose(both, (1, 0, 2, 3, 4))
     return both.reshape(-1, value.shape[1])
+
+
+def ring_gather(value, axes):
+    n = lax.axis_size(axes)
+    j = lax.axis_index(axes)
+    parts = [value] + [
+        lax.ppermute(value, axes, perm=[(i, (i - k) % n) for i in range(n)])
+        for k in range(1, n)
+    ]
+    return jnp.roll(jnp.stack(parts), j, axis=0)
+
+
+def ring_scatter_sum(blocks, axes):
+    n = lax.axis_size(axes)
+    j = lax.axis_index(axes)
+    total = lax.dynamic_index_in_dim(blocks, j, 0, keepdims=False)
+    for k in range(1, n):
+        send = lax.dynamic_index_in_dim(blocks, (j - k) % n, 0, keepdims=False)
+        total = total + lax.ppermute(send, axes, perm=[(i, (i - k) % n) for i in range(n)])
+    return total
 
 
 def local(
@@ -107,13 +127,15 @@
         )
     hidden_mine = jnp.roll(jnp.stack(pieces), me, axis=0).reshape(group * tok_rows, -1)
     hidden_mine, attention = lax.optimization_barrier((hidden_mine, attention))
+    strided_rows = ring_gather(down_weight, "q").reshape(-1, down_weight.shape[1])
+    ffn_terms = folder(hidden_mine, strided_rows).reshape(group, tok_rows, -1)
+    ffn_out = ring_scatter_sum(ffn_terms, GROUP)
     residual = teacher_input.astype(jnp.float32)
     layer_out = norm_rows(residual + attention, teacher_gain.astype(jnp.float32), teacher_eps)[0]
     blended = (layer_weights[0] * residual + layer_weights[1] * layer_out).astype(jnp.bfloat16)
     teacher_logits = jnp.dot(blended, teacher_head, preferred_element_type=jnp.float32)
     teacher_logp = jax.nn.log_softmax(teacher_logits, axis=-1)
     teacher_prob = jnp.exp(teacher_logp)
-    ffn_out = folder(student_hidden, lax.all_gather(down_weight, TOKS, axis=0, tiled=True))
     student_scale = student_gain.astype(jnp.float32)
     normed, scaled, inverse = norm_rows(
         student_input.astype(jnp.float32) + ffn_out, student_scale, student_eps

time: 143 us -> 211 us (1.48)
  starting transfers between devices: 18.9 us -> 45.7 us
  local copies, waits for them, and re-layouts: 20 us -> 43.2 us
  waiting for transfers between devices: 64.1 us -> 80.9 us
  other arithmetic: 6.43 us -> 9.36 us
  matrix products: 16.4 us -> 14 us
    ppermute x7, waiting for transfers between devices: 1.94 us -> 33.4 us  [local(): lax.ppermute(send, GROUP, perm=[(i, (i - k) % group) for i in range(group)])]
    ppermute x0 -> x10, starting transfers between devices: none -> 28 us  [the longest x7 21.9 us: ring_scatter_sum(): lax.ppermute(send, axes, perm=[(i, (i - k) % n) for i in range(n)])]
    ppermute x1, waiting for transfers between devices: 20 us -> 0.01 us  [teacher_attention(): got = lax.ppermute(theirs, 'tensor', perm=[(0, 1), (1, 0)])]
    ppermute x0 -> x10, waiting for transfers between devices: none -> 16.4 us  [the longest x7 16.4 us: ring_scatter_sum(): lax.ppermute(send, axes, perm=[(i, (i - k) % n) for i in range(n)])]
    unnamed x56 -> x51, local copies, waits for them, and re-layouts: 10.5 us -> 26.2 us
    all_gather x1 -> x0, waiting for transfers between devices: 13.4 us -> none  [local(): lax.all_gather(down_weight, TOKS, axis=0, tiled=True)]
    ppermute x7, starting transfers between devices: 8.06 us -> 5.32 us  [local(): lax.ppermute(send, GROUP, perm=[(i, (i - k) % group) for i in range(group)])]
    dot_general x1, matrix products: 3.21 us -> 0.98 us  [folder(): return jnp.dot(ordered, row_piece, preferred_element_type=jnp.float32)]
  transfers between devices with their start and end apart: 19 -> 28, of which waited for: 12 -> 18; matrix products, arithmetic and copies ran while one was open for 20% -> 25% of each run, Pallas kernels for 0% -> 0%
where the time goes in v12:
time: 211 us; the launch traced here: 210 us
  waiting for transfers between devices  80.9 us (38%)
  starting transfers between devices  45.7 us (22%)
  local copies, waits for them, and re-layouts  43.2 us (20%)
  between operations  16.7 us (8%)
  matrix products  14 us (7%)
  other arithmetic  9.36 us (4%)
    ppermute x7, waiting for transfers between devices, local(): lax.ppermute(send, GROUP, perm=[(i, (i - k) % group) for i in range(group)])  33.4 us
    unnamed x51, local copies, waits for them, and re-layouts  26.2 us
    ppermute x7, starting transfers between devices, ring_scatter_sum(): lax.ppermute(send, axes, perm=[(i, (i - k) % n) for i in range(n)])  21.9 us
    ppermute x7, waiting for transfers between devices, ring_scatter_sum(): lax.ppermute(send, axes, perm=[(i, (i - k) % n) for i in range(n)])  16.4 us
    ppermute x5, waiting for transfers between devices, butterfly_sum(): lax.ppermute(value, axis, perm=[(i, i ^ step) for i in range(size)])  13.3 us
    ppermute x3, waiting for transfers between devices, group_gather(): lax.ppermute(value, chips, perm=[(i, (i - k) % n) for i in range(n)])  9.1 us
    dot_general x1, matrix products, teacher_attention(): jnp.dot(context, w_out, preferred_element_type=jnp.float32)  8.4 us
    ppermute x5, starting transfers between devices, butterfly_sum(): lax.ppermute(value, axis, perm=[(i, i ^ step) for i in range(size)])  7.09 us
  transfers between devices with their start and end apart: 28, of which 18 were waited for; matrix products, arithmetic and copies ran while one was open for 25% of the time, Pallas kernels for 0%

profile of v12, /device:TPU:0, one launch (start us, length us, event | category | flops | bytes accessed | tf_op | source)
XLA Modules:
  0.0 209.9 jit_solution(1195521876454658818)
XLA Ops:
  7.2 5.1 %collective-permute-start.8 = (bf16[96,768]{1,0:T(8,128)(2,1)}, bf16[96,768]{1,0:T(8,128)(2,1)}, u32[]{:S(2)}, u32[]{:S(2)}) collective-permute-start(bf16[96,768]{1,0:T(8,128)(2,1)} %param.22), channel_id=1, source_target_pairs={{0,24},{8,0},{16,8},{24,16},{1,25},{9,1},{17,9},{25,17},{2,26},{10... | collective-permute-start | bytes 442376 | tf_op jit(solution)/shard_map/ppermute | solution.py:82
  13.3 8.4 %convolution_convert_fusion = bf16[256,4096]{1,0:T(8,128)(2,1)S(1)} fusion(bf16[256,2048]{1,0:T(8,128)(2,1)S(1)} %copy-done, bf16[2048,4096]{1,0:T(8,128)(2,1)} %param.15), kind=kOutput, calls=%fused_computation | convolution fusion | flops 4296015872 | bytes 19922944 | tf_op jit(solution)/shard_map/dot_general | solution.py:33
  24.4 2.3 %copy.29 = bf16[128,3072]{0,1:T(8,128)(2,1)} copy(bf16[128,3072]{1,0:T(8,128)(2,1)} %param.20) | data formatting | bytes 1572864 | tf_op args[6]
  26.7 2.1 %copy.30 = bf16[8,128,4,96]{1,3,2,0:T(8,128)(2,1)} copy(bf16[8,128,4,96]{1,3,0,2:T(8,128)(2,1)} %bitcast.127) | data formatting | bytes 1572864 | tf_op jit(solution)/shard_map/transpose | solution.py:120
  34.8 14.4 %collective-permute-done = bf16[128,384]{0,1:T(8,128)(2,1)S(1)} collective-permute-done((bf16[128,384]{0,1:T(8,128)(2,1)}, bf16[128,384]{0,1:T(8,128)(2,1)S(1)}, u32[]{:S(2)}, u32[]{:S(2)}) %collective-permute-start) | collective-permute-done | bytes 98336 | tf_op jit(solution)/shard_map/ppermute | solution.py:126
  53.9 2.5 %collective-permute-done.2 = bf16[128,384]{0,1:T(8,128)(2,1)S(1)} collective-permute-done((bf16[128,384]{0,1:T(8,128)(2,1)}, bf16[128,384]{0,1:T(8,128)(2,1)S(1)}, u32[]{:S(2)}, u32[]{:S(2)}) %collective-permute-start.2) | collective-permute-done | bytes 98336 | tf_op jit(solution)/shard_map/ppermute | solution.py:126
  58.1 3.1 %collective-permute-done.3 = bf16[128,384]{0,1:T(8,128)(2,1)S(1)} collective-permute-done((bf16[128,384]{0,1:T(8,128)(2,1)}, bf16[128,384]{0,1:T(8,128)(2,1)S(1)}, u32[]{:S(2)}, u32[]{:S(2)}) %collective-permute-start.3) | collective-permute-done | bytes 98336 | tf_op jit(solution)/shard_map/ppermute | solution.py:126
  63.6 4.4 %collective-permute-done.4 = bf16[128,384]{0,1:T(8,128)(2,1)S(1)} collective-permute-done((bf16[128,384]{0,1:T(8,128)(2,1)}, bf16[128,384]{0,1:T(8,128)(2,1)S(1)}, u32[]{:S(2)}, u32[]{:S(2)}) %collective-permute-start.4) | collective-permute-done | bytes 98336 | tf_op jit(solution)/shard_map/ppermute | solution.py:126
  68.6 3.6 %collective-permute-done.5 = bf16[128,384]{0,1:T(8,128)(2,1)S(1)} collective-permute-done((bf16[128,384]{0,1:T(8,128)(2,1)}, bf16[128,384]{0,1:T(8,128)(2,1)S(1)}, u32[]{:S(2)}, u32[]{:S(2)}) %collective-permute-start.5) | collective-permute-done | bytes 98336 | tf_op jit(solution)/shard_map/ppermute | solution.py:126
  73.8 3.6 %collective-permute-done.6 = bf16[128,384]{0,1:T(8,128)(2,1)S(1)} collective-permute-done((bf16[128,384]{0,1:T(8,128)(2,1)}, bf16[128,384]{0,1:T(8,128)(2,1)S(1)}, u32[]{:S(2)}, u32[]{:S(2)}) %collective-permute-start.6) | collective-permute-done | bytes 98336 | tf_op jit(solution)/shard_map/ppermute | solution.py:126
  84.0 2.1 constant_dynamic-slice_fusion.2
  86.1 2.3 %copy.31 = bf16[8,128,384]{2,1,0:T(8,128)(2,1)} copy(bf16[8,128,384]{1,2,0:T(8,128)(2,1)} %constant_dynamic-slice_fusion.2) | data formatting | bytes 1572864 | tf_op jit(solution)/shard_map/jit(_roll_dynamic)/dynamic_slice | solution.py:128
  106.6 13.3 %collective-permute-done.11 = f32[128,768]{1,0:T(8,128)S(1)} collective-permute-done((f32[128,768]{1,0:T(8,128)S(1)}, f32[128,768]{1,0:T(8,128)S(1)}, u32[]{:S(2)}, u32[]{:S(2)}) %collective-permute-start.11) | collective-permute-done | bytes 393248 | tf_op jit(solution)/shard_map/ppermute | solution.py:94
  120.1 17.4 %collective-permute-start.12 = (f32[128,768]{1,0:T(8,128)S(1)}, f32[128,768]{1,0:T(8,128)S(1)}, u32[]{:S(2)}, u32[]{:S(2)}) collective-permute-start(f32[128,768]{1,0:T(8,128)S(1)} %get-tuple-element.34), channel_id=1, source_target_pairs={{0,6},{1,7},{2,0},{3,1},{4,2},{5,3},{6,4},{7,5},{8,14},{9,15},{10,... | collective-permute-start | bytes 1179656 | tf_op jit(solution)/shard_map/ppermute | solution.py:94
  139.8 3.1 %collective-permute-done.12 = f32[128,768]{1,0:T(8,128)S(1)} collective-permute-done((f32[128,768]{1,0:T(8,128)S(1)}, f32[128,768]{1,0:T(8,128)S(1)}, u32[]{:S(2)}, u32[]{:S(2)}) %collective-permute-start.12) | collective-permute-done | bytes 393248 | tf_op jit(solution)/shard_map/ppermute | solution.py:94
  145.7 2.1 collective-permute-start.18
  149.3 8.4 %collective-permute-done.18 = bf16[128,768]{1,0:T(8,128)(2,1)S(1)} collective-permute-done((bf16[128,768]{1,0:T(8,128)(2,1)S(1)}, bf16[128,768]{1,0:T(8,128)(2,1)S(1)}, u32[]{:S(2)}, u32[]{:S(2)}) %collective-permute-start.18) | collective-permute-done | bytes 196640 | tf_op jit(solution)/shard_map/ppermute | solution.py:66
  164.5 2.4 %collective-permute-done.21 = bf16[4,128,768]{2,1,0:T(8,128)(2,1)} collective-permute-done((bf16[4,128,768]{2,1,0:T(8,128)(2,1)S(1)}, bf16[4,128,768]{2,1,0:T(8,128)(2,1)}, u32[]{:S(2)}, u32[]{:S(2)}) %collective-permute-start.21) | collective-permute-done | bytes 786464 | tf_op jit(solution)/shard_map/ppermute | solution.py:70
  173.9 2.1 %collective-permute-done.22 = f32[3074]{0:T(1024)S(1)} collective-permute-done((f32[3074]{0:T(1024)S(1)}, f32[3074]{0:T(1024)S(1)}, u32[]{:S(2)}, u32[]{:S(2)}) %collective-permute-start.22) | collective-permute-done | bytes 12328 | tf_op jit(solution)/shard_map/ppermute | solution.py:54
  178.4 2.6 %collective-permute-done.24 = f32[3074]{0:T(1024)S(1)} collective-permute-done((f32[3074]{0:T(1024)S(1)}, f32[3074]{0:T(1024)S(1)}, u32[]{:S(2)}, u32[]{:S(2)}) %collective-permute-start.24) | collective-permute-done | bytes 12328 | tf_op jit(solution)/shard_map/ppermute | solution.py:54
  180.9 3.4 %collective-permute-start.25 = (f32[3074]{0:T(1024)S(1)}, f32[3074]{0:T(1024)S(1)}, u32[]{:S(2)}, u32[]{:S(2)}) collective-permute-start(f32[3074]{0:T(1024)S(1)} %add.259), channel_id=1, source_target_pairs={{0,8},{8,0},{16,24},{24,16},{1,9},{9,1},{17,25},{25,17},{2,10},{10... | collective-permute-start | bytes 36896 | tf_op jit(solution)/shard_map/ppermute | solution.py:54
  184.3 2.5 %collective-permute-done.25 = f32[3074]{0:T(1024)S(1)} collective-permute-done((f32[3074]{0:T(1024)S(1)}, f32[3074]{0:T(1024)S(1)}, u32[]{:S(2)}, u32[]{:S(2)}) %collective-permute-start.25) | collective-permute-done | bytes 12328 | tf_op jit(solution)/shard_map/ppermute | solution.py:54
  187.7 5.0 %collective-permute-done.26 = f32[3074]{0:T(1024)S(1)} collective-permute-done((f32[3074]{0:T(1024)S(1)}, f32[3074]{0:T(1024)S(1)}, u32[]{:S(2)}, u32[]{:S(2)}) %collective-permute-start.26) | collective-permute-done | bytes 12328 | tf_op jit(solution)/shard_map/ppermute | solution.py:54
  195.7 6.2 %reduce-scatter.2.cloned.1.call-done = f32[96,768]{1,0:T(8,128)} async-done(((f32[384,768]{1,0:T(8,128)}), f32[96,768]{1,0:T(8,128)}) %reduce-scatter.2.cloned.1.call-update) | async-done | bytes 294928 | tf_op jit(solution)/shard_map/reduce_scatter | solution.py:182
  (137 shorter events, 70.8 us)
Async XLA Ops:
  7.2 194.7 %reduce-scatter.2.cloned.1.call-start = ((), (), s32[]{:S(2)}) async-start(), calls=%async_computation.1 | async-start | bytes 1474560 | tf_op jit(solution)/shard_map/reduce_scatter | solution.py:182
  7.2 81.2 %collective-permute-start.8 = (bf16[96,768]{1,0:T(8,128)(2,1)}, bf16[96,768]{1,0:T(8,128)(2,1)}, u32[]{:S(2)}, u32[]{:S(2)}) collective-permute-start(bf16[96,768]{1,0:T(8,128)(2,1)} %param.22), channel_id=1, source_target_pairs={{0,24},{8,0},{16,8},{24,16},{1,25},{9,1},{17,9},{25,17},{2,26},{10... | collective-permute-start | bytes 442376 | tf_op jit(solution)/shard_map/ppermute | solution.py:82
  12.3 79.3 %collective-permute-start.10 = (bf16[96,768]{1,0:T(8,128)(2,1)}, bf16[96,768]{1,0:T(8,128)(2,1)S(1)}, u32[]{:S(2)}, u32[]{:S(2)}) collective-permute-start(bf16[96,768]{1,0:T(8,128)(2,1)} %param.22), channel_id=1, source_target_pairs={{0,8},{8,16},{16,24},{24,0},{1,9},{9,17},{17,25},{25,1},{2,10},{10... | collective-permute-start | bytes 442376 | tf_op jit(solution)/shard_map/ppermute | solution.py:82
  12.3 77.7 %collective-permute-start.9 = (bf16[96,768]{1,0:T(8,128)(2,1)}, bf16[96,768]{1,0:T(8,128)(2,1)}, u32[]{:S(2)}, u32[]{:S(2)}) collective-permute-start(bf16[96,768]{1,0:T(8,128)(2,1)} %param.22), channel_id=1, source_target_pairs={{0,16},{8,24},{16,0},{24,8},{1,17},{9,25},{17,1},{25,9},{2,18},{10... | collective-permute-start | bytes 442376 | tf_op jit(solution)/shard_map/ppermute | solution.py:82
  22.8 75.0 %collective-permute-start.7 = (bf16[128,4096]{1,0:T(8,128)(2,1)}, bf16[128,4096]{1,0:T(8,128)(2,1)}, u32[]{:S(2)}, u32[]{:S(2)}) collective-permute-start(bf16[128,4096]{1,0:T(8,128)(2,1)} %broadcast_select_fusion), channel_id=1, source_target_pairs={{0,1},{1,0},{2,3},{3,2},{4,5},{5,4},{6,7},{7,6},{8,9},{9,8},{10,11... | collective-permute-start | bytes 3145736 | tf_op jit(solution)/shard_map/ppermute | solution.py:42
  30.9 18.3 %collective-permute-start = (bf16[128,384]{0,1:T(8,128)(2,1)}, bf16[128,384]{0,1:T(8,128)(2,1)S(1)}, u32[]{:S(2)}, u32[]{:S(2)}) collective-permute-start(bf16[128,384]{0,1:T(8,128)(2,1)} %get-tuple-element.42), channel_id=1, source_target_pairs={{0,7},{1,0},{2,1},{3,2},{4,3},{5,4},{6,5},{7,6},{8,15},{9,8},{10,9... | collective-permute-start | bytes 294920 | tf_op jit(solution)/shard_map/ppermute | solution.py:126
  51.8 4.6 %collective-permute-start.2 = (bf16[128,384]{0,1:T(8,128)(2,1)}, bf16[128,384]{0,1:T(8,128)(2,1)S(1)}, u32[]{:S(2)}, u32[]{:S(2)}) collective-permute-start(bf16[128,384]{0,1:T(8,128)(2,1)} %get-tuple-element.40), channel_id=1, source_target_pairs={{0,5},{1,6},{2,7},{3,0},{4,1},{5,2},{6,3},{7,4},{8,13},{9,14},{10,... | collective-permute-start | bytes 294920 | tf_op jit(solution)/shard_map/ppermute | solution.py:126
  56.4 4.8 %collective-permute-start.3 = (bf16[128,384]{0,1:T(8,128)(2,1)}, bf16[128,384]{0,1:T(8,128)(2,1)S(1)}, u32[]{:S(2)}, u32[]{:S(2)}) collective-permute-start(bf16[128,384]{0,1:T(8,128)(2,1)} %get-tuple-element.39), channel_id=1, source_target_pairs={{0,4},{1,5},{2,6},{3,7},{4,0},{5,1},{6,2},{7,3},{8,12},{9,13},{10,... | collective-permute-start | bytes 294920 | tf_op jit(solution)/shard_map/ppermute | solution.py:126
  61.2 6.8 %collective-permute-start.4 = (bf16[128,384]{0,1:T(8,128)(2,1)}, bf16[128,384]{0,1:T(8,128)(2,1)S(1)}, u32[]{:S(2)}, u32[]{:S(2)}) collective-permute-start(bf16[128,384]{0,1:T(8,128)(2,1)} %get-tuple-element.38), channel_id=1, source_target_pairs={{0,3},{1,4},{2,5},{3,6},{4,7},{5,0},{6,1},{7,2},{8,11},{9,12},{10,... | collective-permute-start | bytes 294920 | tf_op jit(solution)/shard_map/ppermute | solution.py:126
  68.0 4.3 %collective-permute-start.5 = (bf16[128,384]{0,1:T(8,128)(2,1)}, bf16[128,384]{0,1:T(8,128)(2,1)S(1)}, u32[]{:S(2)}, u32[]{:S(2)}) collective-permute-start(bf16[128,384]{0,1:T(8,128)(2,1)} %get-tuple-element.37), channel_id=1, source_target_pairs={{0,2},{1,3},{2,4},{3,5},{4,6},{5,7},{6,0},{7,1},{8,10},{9,11},{10,... | collective-permute-start | bytes 294920 | tf_op jit(solution)/shard_map/ppermute | solution.py:126
  72.2 5.2 %collective-permute-start.6 = (bf16[128,384]{0,1:T(8,128)(2,1)}, bf16[128,384]{0,1:T(8,128)(2,1)S(1)}, u32[]{:S(2)}, u32[]{:S(2)}) collective-permute-start(bf16[128,384]{0,1:T(8,128)(2,1)} %get-tuple-element.35), channel_id=1, source_target_pairs={{0,1},{1,2},{2,3},{3,4},{4,5},{5,6},{6,7},{7,0},{8,9},{9,10},{10,1... | collective-permute-start | bytes 294920 | tf_op jit(solution)/shard_map/ppermute | solution.py:126
  102.0 17.9 %collective-permute-start.11 = (f32[128,768]{1,0:T(8,128)S(1)}, f32[128,768]{1,0:T(8,128)S(1)}, u32[]{:S(2)}, u32[]{:S(2)}) collective-permute-start(f32[128,768]{1,0:T(8,128)S(1)} %get-tuple-element.28), channel_id=1, source_target_pairs={{0,7},{1,0},{2,1},{3,2},{4,3},{5,4},{6,5},{7,6},{8,15},{9,8},{10,9... | collective-permute-start | bytes 1179656 | tf_op jit(solution)/shard_map/ppermute | solution.py:94
  102.0 18.1 %collective-permute-start.17 = (f32[128,768]{1,0:T(8,128)S(1)}, f32[128,768]{1,0:T(8,128)S(1)}, u32[]{:S(2)}, u32[]{:S(2)}) collective-permute-start(f32[128,768]{1,0:T(8,128)S(1)} %get-tuple-element.29), channel_id=1, source_target_pairs={{0,1},{1,2},{2,3},{3,4},{4,5},{5,6},{6,7},{7,0},{8,9},{9,10},{10,1... | collective-permute-start | bytes 1179656 | tf_op jit(solution)/shard_map/ppermute | solution.py:94
  104.1 35.7 %collective-permute-start.16 = (f32[128,768]{1,0:T(8,128)S(1)}, f32[128,768]{1,0:T(8,128)S(1)}, u32[]{:S(2)}, u32[]{:S(2)}) collective-permute-start(f32[128,768]{1,0:T(8,128)S(1)} %get-tuple-element.30), channel_id=1, source_target_pairs={{0,2},{1,3},{2,4},{3,5},{4,6},{5,7},{6,0},{7,1},{8,10},{9,11},{10,... | collective-permute-start | bytes 1179656 | tf_op jit(solution)/shard_map/ppermute | solution.py:94
  104.1 35.7 %collective-permute-start.15 = (f32[128,768]{1,0:T(8,128)S(1)}, f32[128,768]{1,0:T(8,128)S(1)}, u32[]{:S(2)}, u32[]{:S(2)}) collective-permute-start(f32[128,768]{1,0:T(8,128)S(1)} %get-tuple-element.31), channel_id=1, source_target_pairs={{0,3},{1,4},{2,5},{3,6},{4,7},{5,0},{6,1},{7,2},{8,11},{9,12},{10,... | collective-permute-start | bytes 1179656 | tf_op jit(solution)/shard_map/ppermute | solution.py:94
  105.4 34.4 %collective-permute-start.14 = (f32[128,768]{1,0:T(8,128)S(1)}, f32[128,768]{1,0:T(8,128)S(1)}, u32[]{:S(2)}, u32[]{:S(2)}) collective-permute-start(f32[128,768]{1,0:T(8,128)S(1)} %get-tuple-element.32), channel_id=1, source_target_pairs={{0,4},{1,5},{2,6},{3,7},{4,0},{5,1},{6,2},{7,3},{8,12},{9,13},{10,... | collective-permute-start | bytes 1179656 | tf_op jit(solution)/shard_map/ppermute | solution.py:94
  119.9 19.9 %collective-permute-start.13 = (f32[128,768]{1,0:T(8,128)S(1)}, f32[128,768]{1,0:T(8,128)S(1)}, u32[]{:S(2)}, u32[]{:S(2)}) collective-permute-start(f32[128,768]{1,0:T(8,128)S(1)} %get-tuple-element.33), channel_id=1, source_target_pairs={{0,5},{1,6},{2,7},{3,0},{4,1},{5,2},{6,3},{7,4},{8,13},{9,14},{10,... | collective-permute-start | bytes 1179656 | tf_op jit(solution)/shard_map/ppermute | solution.py:94
  120.1 22.7 %collective-permute-start.12 = (f32[128,768]{1,0:T(8,128)S(1)}, f32[128,768]{1,0:T(8,128)S(1)}, u32[]{:S(2)}, u32[]{:S(2)}) collective-permute-start(f32[128,768]{1,0:T(8,128)S(1)} %get-tuple-element.34), channel_id=1, source_target_pairs={{0,6},{1,7},{2,0},{3,1},{4,2},{5,3},{6,4},{7,5},{8,14},{9,15},{10,... | collective-permute-start | bytes 1179656 | tf_op jit(solution)/shard_map/ppermute | solution.py:94
  145.7 12.1 %collective-permute-start.18 = (bf16[128,768]{1,0:T(8,128)(2,1)S(1)}, bf16[128,768]{1,0:T(8,128)(2,1)S(1)}, u32[]{:S(2)}, u32[]{:S(2)}) collective-permute-start(bf16[128,768]{1,0:T(8,128)(2,1)S(1)} %get-tuple-element.25), channel_id=1, source_target_pairs={{0,5},{1,0},{4,1},{5,4},{2,7},{3,2},{6,3},{7,6},{8,13},{9,8},{12,9... | collective-permute-start | bytes 589832 | tf_op jit(solution)/shard_map/ppermute | solution.py:66
  147.8 12.0 %collective-permute-start.20 = (bf16[128,768]{1,0:T(8,128)(2,1)S(1)}, bf16[128,768]{1,0:T(8,128)(2,1)S(1)}, u32[]{:S(2)}, u32[]{:S(2)}) collective-permute-start(bf16[128,768]{1,0:T(8,128)(2,1)S(1)} %get-tuple-element.25), channel_id=1, source_target_pairs={{0,1},{1,4},{4,5},{5,0},{2,3},{3,6},{6,7},{7,2},{8,9},{9,12},{12,1... | collective-permute-start | bytes 589832 | tf_op jit(solution)/shard_map/ppermute | solution.py:66
  147.9 11.2 %collective-permute-start.19 = (bf16[128,768]{1,0:T(8,128)(2,1)S(1)}, bf16[128,768]{1,0:T(8,128)(2,1)S(1)}, u32[]{:S(2)}, u32[]{:S(2)}) collective-permute-start(bf16[128,768]{1,0:T(8,128)(2,1)S(1)} %get-tuple-element.25), channel_id=1, source_target_pairs={{0,4},{1,5},{4,0},{5,1},{2,6},{3,7},{6,2},{7,3},{8,12},{9,13},{12,... | collective-permute-start | bytes 589832 | tf_op jit(solution)/shard_map/ppermute | solution.py:66
  177.2 3.7 %collective-permute-start.24 = (f32[3074]{0:T(1024)S(1)}, f32[3074]{0:T(1024)S(1)}, u32[]{:S(2)}, u32[]{:S(2)}) collective-permute-start(f32[3074]{0:T(1024)S(1)} %add.258), channel_id=1, source_target_pairs={{0,4},{4,0},{1,5},{5,1},{2,6},{6,2},{3,7},{7,3},{8,12},{12,8},{9,1... | collective-permute-start | bytes 36896 | tf_op jit(solution)/shard_map/ppermute | solution.py:54
  180.9 5.9 %collective-permute-start.25 = (f32[3074]{0:T(1024)S(1)}, f32[3074]{0:T(1024)S(1)}, u32[]{:S(2)}, u32[]{:S(2)}) collective-permute-start(f32[3074]{0:T(1024)S(1)} %add.259), channel_id=1, source_target_pairs={{0,8},{8,0},{16,24},{24,16},{1,9},{9,1},{17,25},{25,17},{2,10},{10... | collective-permute-start | bytes 36896 | tf_op jit(solution)/shard_map/ppermute | solution.py:54
  186.8 5.9 %collective-permute-start.26 = (f32[3074]{0:T(1024)S(1)}, f32[3074]{0:T(1024)S(1)}, u32[]{:S(2)}, u32[]{:S(2)}) collective-permute-start(f32[3074]{0:T(1024)S(1)} %add.260), channel_id=1, source_target_pairs={{0,16},{8,24},{16,0},{24,8},{1,17},{9,25},{17,1},{25,9},{2,18},{10... | collective-permute-start | bytes 36896 | tf_op jit(solution)/shard_map/ppermute | solution.py:54
  (15 other events, 111.7 us)
Sparse Core Ops, SparseCore 0:
  170.5 31.3 reduce-scatter.1

commit v13 on v8

--- a/solution.py
+++ b/solution.py
@@ -113,7 +113,11 @@
     teacher_logits = jnp.dot(blended, teacher_head, preferred_element_type=jnp.float32)
     teacher_logp = jax.nn.log_softmax(teacher_logits, axis=-1)
     teacher_prob = jnp.exp(teacher_logp)
-    ffn_out = folder(student_hidden, lax.all_gather(down_weight, TOKS, axis=0, tiled=True))
+    gathered = lax.all_gather(down_weight, TOKS[::-1], axis=0, tiled=True)
+    sizes = tuple(lax.axis_size(a) for a in TOKS)
+    by_block = student_hidden.reshape(tok_rows, *sizes, down_weight.shape[0])
+    by_block = jnp.transpose(by_block, (0, 4, 3, 2, 1, 5)).reshape(tok_rows, -1)
+    ffn_out = folder(by_block, gathered)
     student_scale = student_gain.astype(jnp.float32)
     normed, scaled, inverse = norm_rows(
         student_input.astype(jnp.float32) + ffn_out, student_scale, student_eps

time: 143 us -> 143 us (level)
  transfers between devices with their start and end apart: 19 -> 19, of which waited for: 12 -> 12; matrix products, arithmetic and copies ran while one was open for 20% -> 21% of each run, Pallas kernels for 0% -> 0%
where the time goes in v13:
time: 143 us
  waiting for transfers between devices  63.2 us (44%)
  local copies, waits for them, and re-layouts  20.9 us (15%)
  starting transfers between devices  18.7 us (13%)
  between operations  17 us (12%)
  matrix products  16.5 us (12%)
  other arithmetic  6.41 us (4%)
    ppermute x1, waiting for transfers between devices, teacher_attention(): got = lax.ppermute(theirs, 'tensor', perm=[(0, 1), (1, 0)])  20 us
    ppermute x5, waiting for transfers between devices, butterfly_sum(): lax.ppermute(value, axis, perm=[(i, i ^ step) for i in range(size)])  12.7 us
    all_gather x1, waiting for transfers between devices, local(): gathered = lax.all_gather(down_weight, TOKS[::-1], axis=0, tiled=True)  12.7 us
    unnamed x56, local copies, waits for them, and re-layouts  10.5 us
    dot_general x1, matrix products, teacher_attention(): jnp.dot(context, w_out, preferred_element_type=jnp.float32)  8.57 us
    ppermute x3, waiting for transfers between devices, group_gather(): lax.ppermute(value, chips, perm=[(i, (i - k) % n) for i in range(n)])  8.09 us
    ppermute x7, starting transfers between devices, local(): lax.ppermute(send, GROUP, perm=[(i, (i - k) % group) for i in range(group)])  8.07 us
    ppermute x5, starting transfers between devices, butterfly_sum(): lax.ppermute(value, axis, perm=[(i, i ^ step) for i in range(size)])  5.98 us
  transfers between devices with their start and end apart: 19, of which 12 were waited for; matrix products, arithmetic and copies ran while one was open for 21% of the time, Pallas kernels for 0%

profile of v13, /device:TPU:0, one launch (start us, length us, event | category | flops | bytes accessed | tf_op | source)
XLA Modules:
  0.0 142.8 jit_solution(12187260768942602155)
XLA Ops:
  8.1 1.5 %copy.33 = bf16[128,3072]{0,1:T(8,128)(2,1)S(1)} copy(bf16[128,3072]{1,0:T(8,128)(2,1)} %param.20) | data formatting | bytes 1572864 | tf_op args[6]
  10.7 3.3 %collective-permute-start = (bf16[128,384]{0,1:T(8,128)(2,1)}, bf16[128,384]{0,1:T(8,128)(2,1)S(1)}, u32[]{:S(2)}, u32[]{:S(2)}) collective-permute-start(bf16[128,384]{0,1:T(8,128)(2,1)} %get-tuple-element.33), channel_id=1, source_target_pairs={{0,7},{1,0},{2,1},{3,2},{4,3},{5,4},{6,5},{7,6},{8,15},{9,8},{10,9... | collective-permute-start | bytes 294920 | tf_op jit(solution)/shard_map/ppermute | solution.py:106
  18.5 8.6 %convolution_convert_fusion = bf16[256,4096]{1,0:T(8,128)(2,1)S(1)} fusion(bf16[256,2048]{1,0:T(8,128)(2,1)S(1)} %copy-done, bf16[2048,4096]{1,0:T(8,128)(2,1)} %param.15), kind=kOutput, calls=%fused_computation | convolution fusion | flops 4296015872 | bytes 19922944 | tf_op jit(solution)/shard_map/dot_general | solution.py:33
  30.8 1.5 %collective-permute-start.7 = (bf16[128,4096]{1,0:T(8,128)(2,1)}, bf16[128,4096]{1,0:T(8,128)(2,1)}, u32[]{:S(2)}, u32[]{:S(2)}) collective-permute-start(bf16[128,4096]{1,0:T(8,128)(2,1)} %broadcast_select_fusion), channel_id=1, source_target_pairs={{0,1},{1,0},{2,3},{3,2},{4,5},{5,4},{6,7},{7,6},{8,9},{9,8},{10,11... | collective-permute-start | bytes 3145736 | tf_op jit(solution)/shard_map/ppermute | solution.py:42
  33.3 1.9 %collective-permute-done.6 = bf16[128,384]{0,1:T(8,128)(2,1)S(1)} collective-permute-done((bf16[128,384]{0,1:T(8,128)(2,1)S(1)}, bf16[128,384]{0,1:T(8,128)(2,1)S(1)}, u32[]{:S(2)}, u32[]{:S(2)}) %collective-permute-start.6) | collective-permute-done | bytes 98336 | tf_op jit(solution)/shard_map/ppermute | solution.py:106
  38.2 2.4 %copy.35 = bf16[8,128,384]{2,1,0:T(8,128)(2,1)} copy(bf16[8,128,384]{1,2,0:T(8,128)(2,1)} %constant_dynamic-slice_fusion.1) | data formatting | bytes 1572864 | tf_op jit(solution)/shard_map/jit(_roll_dynamic)/dynamic_slice | solution.py:108
  40.6 20.0 %collective-permute-done.7 = bf16[128,4096]{1,0:T(8,128)(2,1)} collective-permute-done((bf16[128,4096]{1,0:T(8,128)(2,1)}, bf16[128,4096]{1,0:T(8,128)(2,1)}, u32[]{:S(2)}, u32[]{:S(2)}) %collective-permute-start.7) | collective-permute-done | bytes 1048608 | tf_op jit(solution)/shard_map/ppermute | solution.py:42
  60.6 1.6 %convert_add_fusion.1 = f32[128,4096]{1,0:T(8,128)S(1)} fusion(bf16[128,4096]{1,0:T(8,128)(2,1)} %collective-permute-done.7, pred[]{:T(512)S(6)} %eq.48, bf16[256,4096]{1,0:T(8,128)(2,1)S(1)} %convolution_convert_fusion), kind=kLoop, calls=%fused_computation.6 | loop fusion | flops 2097152 | bytes 5242881 | tf_op jit(solution)/shard_map/add | solution.py:43
  63.3 2.1 %fusion.11 = (f32[128]{0:T(128)S(1)}, f32[128,4]{0,1:T(4,128)S(1)}) fusion(bf16[4096,4]{0,1:T(4,128)(2,1)S(1)} %copy-done.15, bf16[128,4096]{1,0:T(8,128)(2,1)S(1)} %copy-done.1, f32[128,4096]{1,0:T(8,128)S(1)} %convert_add_fusion.1, f32[4096]{0:T(1024)S(1)} %copy-done.10, f32[128]{0:T(128)S(1)} %add_rsqrt_fusion, f32[128]{0:T(128)S(1)} %broadcast_multiply_fusion, ...), kind=kOutput, calls=%fused_computation.80 | convolution fusion | flops 8913280 | bytes 3198472 | tf_op jit(solution)/shard_map/dot_general | solution.py:113
  65.5 12.7 %all-gather.2.cloned.1.call-done = bf16[3072,768]{1,0:T(8,128)(2,1)} async-done(((bf16[96,768]{1,0:T(8,128)(2,1)}), bf16[3072,768]{1,0:T(8,128)(2,1)}) %all-gather.2.cloned.1.call-update) | async-done | bytes 4718608 | tf_op jit(solution)/shard_map/all_gather | solution.py:116
  78.2 3.3 %fusion.10 = (f32[128]{0:T(128)S(1)}, f32[128,768]{1,0:T(8,128)S(1)}) fusion(bf16[128,3072]{0,1:T(8,128)(2,1)S(1)} %bitcast.86, bf16[3072,768]{1,0:T(8,128)(2,1)} %all-gather.2.cloned.1.call-done, bf16[128,768]{1,0:T(8,128)(2,1)S(1)} %copy-done.6), kind=kOutput, calls=%fused_computation.79 | convolution fusion | flops 604274560 | bytes 6095360 | tf_op jit(solution)/shard_map/dot_general | solution.py:28
  85.0 1.5 %collective-permute-start.9 = (bf16[128,768]{1,0:T(8,128)(2,1)S(1)}, bf16[128,768]{1,0:T(8,128)(2,1)S(1)}, u32[]{:S(2)}, u32[]{:S(2)}) collective-permute-start(bf16[128,768]{1,0:T(8,128)(2,1)S(1)} %get-tuple-element.25), channel_id=1, source_target_pairs={{0,4},{1,5},{4,0},{5,1},{2,6},{3,7},{6,2},{7,3},{8,12},{9,13},{12,... | collective-permute-start | bytes 589832 | tf_op jit(solution)/shard_map/ppermute | solution.py:66
  87.0 4.0 %collective-permute-done.8 = bf16[128,768]{1,0:T(8,128)(2,1)S(1)} collective-permute-done((bf16[128,768]{1,0:T(8,128)(2,1)S(1)}, bf16[128,768]{1,0:T(8,128)(2,1)S(1)}, u32[]{:S(2)}, u32[]{:S(2)}) %collective-permute-start.8) | collective-permute-done | bytes 196640 | tf_op jit(solution)/shard_map/ppermute | solution.py:66
  91.7 4.1 %collective-permute-done.9 = bf16[128,768]{1,0:T(8,128)(2,1)S(1)} collective-permute-done((bf16[128,768]{1,0:T(8,128)(2,1)S(1)}, bf16[128,768]{1,0:T(8,128)(2,1)S(1)}, u32[]{:S(2)}, u32[]{:S(2)}) %collective-permute-start.9) | collective-permute-done | bytes 196640 | tf_op jit(solution)/shard_map/ppermute | solution.py:66
  101.2 2.3 %collective-permute-done.11 = bf16[4,128,768]{2,1,0:T(8,128)(2,1)S(1)} collective-permute-done((bf16[4,128,768]{2,1,0:T(8,128)(2,1)S(1)}, bf16[4,128,768]{2,1,0:T(8,128)(2,1)S(1)}, u32[]{:S(2)}, u32[]{:S(2)}) %collective-permute-start.11) | collective-permute-done | bytes 786464 | tf_op jit(solution)/shard_map/ppermute | solution.py:70
  104.6 1.8 %fusion.14 = f32[384,768]{1,0:T(8,128)} fusion(bf16[1024,384]{1,0:T(8,128)(2,1)S(1)} %bitcast.85, bf16[1024,768]{1,0:T(8,128)(2,1)S(1)} %bitcast.82), kind=kOutput, calls=%fused_computation.83 | convolution fusion | flops 603979776 | bytes 3538944 | tf_op jit(solution)/shard_map/dot_general | solution.py:161
  106.9 1.4 concatenate.17
  109.0 3.0 %collective-permute-done.12 = f32[3074]{0:T(1024)S(1)} collective-permute-done((f32[3074]{0:T(1024)S(1)}, f32[3074]{0:T(1024)S(1)}, u32[]{:S(2)}, u32[]{:S(2)}) %collective-permute-start.12) | collective-permute-done | bytes 12328 | tf_op jit(solution)/shard_map/ppermute | solution.py:54
  114.2 2.8 %collective-permute-done.14 = f32[3074]{0:T(1024)S(1)} collective-permute-done((f32[3074]{0:T(1024)S(1)}, f32[3074]{0:T(1024)S(1)}, u32[]{:S(2)}, u32[]{:S(2)}) %collective-permute-start.14) | collective-permute-done | bytes 12328 | tf_op jit(solution)/shard_map/ppermute | solution.py:54
  116.9 2.0 %collective-permute-start.15 = (f32[3074]{0:T(1024)S(1)}, f32[3074]{0:T(1024)S(1)}, u32[]{:S(2)}, u32[]{:S(2)}) collective-permute-start(f32[3074]{0:T(1024)S(1)} %add.202), channel_id=1, source_target_pairs={{0,8},{8,0},{16,24},{24,16},{1,9},{9,1},{17,25},{25,17},{2,10},{10... | collective-permute-start | bytes 36896 | tf_op jit(solution)/shard_map/ppermute | solution.py:54
  119.0 2.2 %collective-permute-done.15 = f32[3074]{0:T(1024)S(1)} collective-permute-done((f32[3074]{0:T(1024)S(1)}, f32[3074]{0:T(1024)S(1)}, u32[]{:S(2)}, u32[]{:S(2)}) %collective-permute-start.15) | collective-permute-done | bytes 12328 | tf_op jit(solution)/shard_map/ppermute | solution.py:54
  121.2 2.3 %collective-permute-start.16 = (f32[3074]{0:T(1024)S(1)}, f32[3074]{0:T(1024)S(1)}, u32[]{:S(2)}, u32[]{:S(2)}) collective-permute-start(f32[3074]{0:T(1024)S(1)} %add.203), channel_id=1, source_target_pairs={{0,16},{8,24},{16,0},{24,8},{1,17},{9,25},{17,1},{25,9},{2,18},{10... | collective-permute-start | bytes 36896 | tf_op jit(solution)/shard_map/ppermute | solution.py:54
  123.5 3.5 %collective-permute-done.16 = f32[3074]{0:T(1024)S(1)} collective-permute-done((f32[3074]{0:T(1024)S(1)}, f32[3074]{0:T(1024)S(1)}, u32[]{:S(2)}, u32[]{:S(2)}) %collective-permute-start.16) | collective-permute-done | bytes 12328 | tf_op jit(solution)/shard_map/ppermute | solution.py:54
  130.0 4.8 %reduce-scatter.2.cloned.1.call-done = f32[96,768]{1,0:T(8,128)} async-done(((f32[384,768]{1,0:T(8,128)}), f32[96,768]{1,0:T(8,128)}) %reduce-scatter.2.cloned.1.call-update) | async-done | bytes 294928 | tf_op jit(solution)/shard_map/reduce_scatter | solution.py:164
  (122 shorter events, 31.2 us)
Async XLA Ops:
  7.2 11.4 %copy-start = (bf16[256,2048]{1,0:T(8,128)(2,1)S(1)}, bf16[256,2048]{1,0:T(8,128)(2,1)}, u32[]{:S(2)}) copy-start(bf16[256,2048]{1,0:T(8,128)(2,1)} %param.14) | copy-start | bytes 3145732
  7.2 71.0 %all-gather.2.cloned.1.call-start = ((), (), s32[]{:S(2)}) async-start(), calls=%async_computation.1 | async-start | bytes 4866048 | tf_op jit(solution)/shard_map/all_gather | solution.py:116
  7.9 126.9 %reduce-scatter.2.cloned.1.call-start = ((), (), s32[]{:S(2)}) async-start(), calls=%async_computation.2 | async-start | bytes 1474560 | tf_op jit(solution)/shard_map/reduce_scatter | solution.py:164
  9.7 8.7 %copy-start.2 = (bf16[8,128,4,96]{1,3,2,0:T(8,128)(2,1)}, bf16[8,128,4,96]{1,3,2,0:T(8,128)(2,1)S(1)}, u32[]{:S(2)}) copy-start(bf16[8,128,4,96]{1,3,2,0:T(8,128)(2,1)S(1)} %copy.34) | copy-start | bytes 2359300
  10.7 18.2 %collective-permute-start = (bf16[128,384]{0,1:T(8,128)(2,1)}, bf16[128,384]{0,1:T(8,128)(2,1)S(1)}, u32[]{:S(2)}, u32[]{:S(2)}) collective-permute-start(bf16[128,384]{0,1:T(8,128)(2,1)} %get-tuple-element.33), channel_id=1, source_target_pairs={{0,7},{1,0},{2,1},{3,2},{4,3},{5,4},{6,5},{7,6},{8,15},{9,8},{10,9... | collective-permute-start | bytes 294920 | tf_op jit(solution)/shard_map/ppermute | solution.py:106
  14.0 15.9 %collective-permute-start.1 = (bf16[128,384]{0,1:T(8,128)(2,1)}, bf16[128,384]{0,1:T(8,128)(2,1)S(1)}, u32[]{:S(2)}, u32[]{:S(2)}) collective-permute-start(bf16[128,384]{0,1:T(8,128)(2,1)} %get-tuple-element.32), channel_id=1, source_target_pairs={{0,6},{1,7},{2,0},{3,1},{4,2},{5,3},{6,4},{7,5},{8,14},{9,15},{10,... | collective-permute-start | bytes 294920 | tf_op jit(solution)/shard_map/ppermute | solution.py:106
  14.9 16.0 %collective-permute-start.2 = (bf16[128,384]{0,1:T(8,128)(2,1)}, bf16[128,384]{0,1:T(8,128)(2,1)S(1)}, u32[]{:S(2)}, u32[]{:S(2)}) collective-permute-start(bf16[128,384]{0,1:T(8,128)(2,1)} %get-tuple-element.31), channel_id=1, source_target_pairs={{0,5},{1,6},{2,7},{3,0},{4,1},{5,2},{6,3},{7,4},{8,13},{9,14},{10,... | collective-permute-start | bytes 294920 | tf_op jit(solution)/shard_map/ppermute | solution.py:106
  15.1 17.2 %collective-permute-start.3 = (bf16[128,384]{0,1:T(8,128)(2,1)}, bf16[128,384]{0,1:T(8,128)(2,1)S(1)}, u32[]{:S(2)}, u32[]{:S(2)}) collective-permute-start(bf16[128,384]{0,1:T(8,128)(2,1)} %get-tuple-element.30), channel_id=1, source_target_pairs={{0,4},{1,5},{2,6},{3,7},{4,0},{5,1},{6,2},{7,3},{8,12},{9,13},{10,... | collective-permute-start | bytes 294920 | tf_op jit(solution)/shard_map/ppermute | solution.py:106
  16.3 16.1 %collective-permute-start.4 = (bf16[128,384]{0,1:T(8,128)(2,1)}, bf16[128,384]{0,1:T(8,128)(2,1)}, u32[]{:S(2)}, u32[]{:S(2)}) collective-permute-start(bf16[128,384]{0,1:T(8,128)(2,1)} %get-tuple-element.29), channel_id=1, source_target_pairs={{0,3},{1,4},{2,5},{3,6},{4,7},{5,0},{6,1},{7,2},{8,11},{9,12},{10,... | collective-permute-start | bytes 294920 | tf_op jit(solution)/shard_map/ppermute | solution.py:106
  28.9 4.4 %collective-permute-start.5 = (bf16[128,384]{0,1:T(8,128)(2,1)S(1)}, bf16[128,384]{0,1:T(8,128)(2,1)S(1)}, u32[]{:S(2)}, u32[]{:S(2)}) collective-permute-start(bf16[128,384]{0,1:T(8,128)(2,1)S(1)} %copy-done.8), channel_id=1, source_target_pairs={{0,2},{1,3},{2,4},{3,5},{4,6},{5,7},{6,0},{7,1},{8,10},{9,11},{10,... | collective-permute-start | bytes 294920 | tf_op jit(solution)/shard_map/ppermute | solution.py:106
  29.9 5.3 %collective-permute-start.6 = (bf16[128,384]{0,1:T(8,128)(2,1)S(1)}, bf16[128,384]{0,1:T(8,128)(2,1)S(1)}, u32[]{:S(2)}, u32[]{:S(2)}) collective-permute-start(bf16[128,384]{0,1:T(8,128)(2,1)S(1)} %copy-done.7), channel_id=1, source_target_pairs={{0,1},{1,2},{2,3},{3,4},{4,5},{5,6},{6,7},{7,0},{8,9},{9,10},{10,1... | collective-permute-start | bytes 294920 | tf_op jit(solution)/shard_map/ppermute | solution.py:106
  30.8 29.8 %collective-permute-start.7 = (bf16[128,4096]{1,0:T(8,128)(2,1)}, bf16[128,4096]{1,0:T(8,128)(2,1)}, u32[]{:S(2)}, u32[]{:S(2)}) collective-permute-start(bf16[128,4096]{1,0:T(8,128)(2,1)} %broadcast_select_fusion), channel_id=1, source_target_pairs={{0,1},{1,0},{2,3},{3,2},{4,5},{5,4},{6,7},{7,6},{8,9},{9,8},{10,11... | collective-permute-start | bytes 3145736 | tf_op jit(solution)/shard_map/ppermute | solution.py:42
  40.6 21.6 %copy-start.1 = (bf16[128,4096]{1,0:T(8,128)(2,1)S(1)}, bf16[128,4096]{1,0:T(8,128)(2,1)}, u32[]{:S(2)}) copy-start(bf16[128,4096]{1,0:T(8,128)(2,1)} %param.16) | copy-start | bytes 3145732
  63.3 14.8 %copy-start.4 = (bf16[128,2,2,2,4,96]{0,5,4,3,2,1:T(8,128)(2,1)S(1)}, bf16[128,2,2,2,4,96]{0,5,4,3,2,1:T(8,128)(2,1)}, u32[]{:S(2)}) copy-start(bf16[128,2,2,2,4,96]{0,5,4,3,2,1:T(8,128)(2,1)} %copy.37) | copy-start | bytes 2359300
  63.3 14.8 %copy-start.6 = (bf16[128,768]{1,0:T(8,128)(2,1)S(1)}, bf16[128,768]{1,0:T(8,128)(2,1)}, u32[]{:S(2)}) copy-start(bf16[128,768]{1,0:T(8,128)(2,1)} %param.21) | copy-start | bytes 589828
  83.9 7.1 %collective-permute-start.8 = (bf16[128,768]{1,0:T(8,128)(2,1)S(1)}, bf16[128,768]{1,0:T(8,128)(2,1)S(1)}, u32[]{:S(2)}, u32[]{:S(2)}) collective-permute-start(bf16[128,768]{1,0:T(8,128)(2,1)S(1)} %get-tuple-element.25), channel_id=1, source_target_pairs={{0,5},{1,0},{4,1},{5,4},{2,7},{3,2},{6,3},{7,6},{8,13},{9,8},{12,9... | collective-permute-start | bytes 589832 | tf_op jit(solution)/shard_map/ppermute | solution.py:66
  85.0 10.8 %collective-permute-start.9 = (bf16[128,768]{1,0:T(8,128)(2,1)S(1)}, bf16[128,768]{1,0:T(8,128)(2,1)S(1)}, u32[]{:S(2)}, u32[]{:S(2)}) collective-permute-start(bf16[128,768]{1,0:T(8,128)(2,1)S(1)} %get-tuple-element.25), channel_id=1, source_target_pairs={{0,4},{1,5},{4,0},{5,1},{2,6},{3,7},{6,2},{7,3},{8,12},{9,13},{12,... | collective-permute-start | bytes 589832 | tf_op jit(solution)/shard_map/ppermute | solution.py:66
  86.5 10.0 %collective-permute-start.10 = (bf16[128,768]{1,0:T(8,128)(2,1)S(1)}, bf16[128,768]{1,0:T(8,128)(2,1)S(1)}, u32[]{:S(2)}, u32[]{:S(2)}) collective-permute-start(bf16[128,768]{1,0:T(8,128)(2,1)S(1)} %get-tuple-element.25), channel_id=1, source_target_pairs={{0,1},{1,4},{4,5},{5,0},{2,3},{3,6},{6,7},{7,2},{8,9},{9,12},{12,1... | collective-permute-start | bytes 589832 | tf_op jit(solution)/shard_map/ppermute | solution.py:66
  101.1 2.4 %collective-permute-start.11 = (bf16[4,128,768]{2,1,0:T(8,128)(2,1)S(1)}, bf16[4,128,768]{2,1,0:T(8,128)(2,1)S(1)}, u32[]{:S(2)}, u32[]{:S(2)}) collective-permute-start(bf16[4,128,768]{2,1,0:T(8,128)(2,1)S(1)} %constant_dynamic-slice_fusion), channel_id=1, source_target_pairs={{0,2},{2,0},{1,3},{3,1},{4,6},{6,4},{5,7},{7,5},{8,10},{10,8},{9,1... | collective-permute-start | bytes 2359304 | tf_op jit(solution)/shard_map/ppermute | solution.py:70
  108.3 3.7 %collective-permute-start.12 = (f32[3074]{0:T(1024)S(1)}, f32[3074]{0:T(1024)S(1)}, u32[]{:S(2)}, u32[]{:S(2)}) collective-permute-start(f32[3074]{0:T(1024)S(1)} %concatenate.17), channel_id=1, source_target_pairs={{0,1},{1,0},{2,3},{3,2},{4,5},{5,4},{6,7},{7,6},{8,9},{9,8},{10,11... | collective-permute-start | bytes 36896 | tf_op jit(solution)/shard_map/ppermute | solution.py:54
  112.0 1.2 collective-permute-start.13
  113.2 3.7 %collective-permute-start.14 = (f32[3074]{0:T(1024)S(1)}, f32[3074]{0:T(1024)S(1)}, u32[]{:S(2)}, u32[]{:S(2)}) collective-permute-start(f32[3074]{0:T(1024)S(1)} %add.201), channel_id=1, source_target_pairs={{0,4},{4,0},{1,5},{5,1},{2,6},{6,2},{3,7},{7,3},{8,12},{12,8},{9,1... | collective-permute-start | bytes 36896 | tf_op jit(solution)/shard_map/ppermute | solution.py:54
  116.9 4.2 %collective-permute-start.15 = (f32[3074]{0:T(1024)S(1)}, f32[3074]{0:T(1024)S(1)}, u32[]{:S(2)}, u32[]{:S(2)}) collective-permute-start(f32[3074]{0:T(1024)S(1)} %add.202), channel_id=1, source_target_pairs={{0,8},{8,0},{16,24},{24,16},{1,9},{9,1},{17,25},{25,17},{2,10},{10... | collective-permute-start | bytes 36896 | tf_op jit(solution)/shard_map/ppermute | solution.py:54
  121.2 5.8 %collective-permute-start.16 = (f32[3074]{0:T(1024)S(1)}, f32[3074]{0:T(1024)S(1)}, u32[]{:S(2)}, u32[]{:S(2)}) collective-permute-start(f32[3074]{0:T(1024)S(1)} %add.203), channel_id=1, source_target_pairs={{0,16},{8,24},{16,0},{24,8},{1,17},{9,25},{17,1},{25,9},{2,18},{10... | collective-permute-start | bytes 36896 | tf_op jit(solution)/shard_map/ppermute | solution.py:54
  (12 other events, 43.2 us)
Sparse Core Ops, SparseCore 0:
  10.8 67.2 all-gather.1
  106.6 28.1 reduce-scatter.1

commit v14 on v8

--- a/solution.py
+++ b/solution.py
@@ -61,18 +61,23 @@
 def group_gather(value):
     chips = ("x", "tensor")
     n = lax.axis_size(chips)
-    j = lax.axis_index(chips)
     parts = [value] + [
         lax.ppermute(value, chips, perm=[(i, (i - k) % n) for i in range(n)])
         for k in range(1, n)
     ]
-    plane = jnp.roll(jnp.stack(parts), j, axis=0)
+    plane = jnp.concatenate(parts, axis=0)
     other = lax.ppermute(plane, "c", perm=[(0, 1), (1, 0)])
-    low = lax.axis_index("c") == 0
-    both = jnp.where(low, jnp.stack([plane, other]), jnp.stack([other, plane]))
-    both = both.reshape(2, lax.axis_size("x"), lax.axis_size("tensor"), *value.shape)
-    both = jnp.transpose(both, (1, 0, 2, 3, 4))
-    return both.reshape(-1, value.shape[1])
+    return jnp.concatenate([plane, other], axis=0)
+
+
+def group_order():
+    chips = ("x", "tensor")
+    n = lax.axis_size(chips)
+    tensor = lax.axis_size("tensor")
+    core = lax.axis_index("c")
+    chip = (lax.axis_index(chips) + jnp.arange(n, dtype=jnp.int32)) % n
+    x, t = chip // tensor, chip % tensor
+    return jnp.concatenate([(x * 2 + core) * tensor + t, (x * 2 + 1 - core) * tensor + t])
 
 
 def local(
@@ -105,7 +110,8 @@
         pieces.append(
             lax.ppermute(send, GROUP, perm=[(i, (i - k) % group) for i in range(group)])
         )
-    hidden_mine = jnp.roll(jnp.stack(pieces), me, axis=0).reshape(group * tok_rows, -1)
+    hidden_mine = jnp.take(jnp.roll(jnp.stack(pieces), me, axis=0), group_order(), axis=0)
+    hidden_mine = hidden_mine.reshape(group * tok_rows, -1)
     hidden_mine, attention = lax.optimization_barrier((hidden_mine, attention))
     residual = teacher_input.astype(jnp.float32)
     layer_out = norm_rows(residual + attention, teacher_gain.astype(jnp.float32), teacher_eps)[0]

time: 143 us -> 141 us (0.986)
  local copies, waits for them, and re-layouts: 20 us -> 16.1 us
  other arithmetic: 6.43 us -> 7.95 us
    gather x0 -> x2, local copies, waits for them, and re-layouts: none -> 5.01 us  [local(): jnp.take(jnp.roll(jnp.stack(pieces), me, axis=0), group_order(), axis=0)]
    unnamed x56 -> x53, local copies, waits for them, and re-layouts: 10.5 us -> 5.67 us
    ppermute x1, waiting for transfers between devices: 20 us -> 15.1 us  [teacher_attention(): got = lax.ppermute(theirs, 'tensor', perm=[(0, 1), (1, 0)])]
    all_gather x1, waiting for transfers between devices: 13.4 us -> 17.7 us  [local(): lax.all_gather(down_weight, TOKS, axis=0, tiled=True)]
    dynamic_slice x3 -> x1, local copies, waits for them, and re-layouts: 4.5 us -> 1 us  [local(): jnp.roll(jnp.stack(pieces), me, axis=0)]
    ppermute x5, waiting for transfers between devices: 12.5 us -> 15.7 us  [butterfly_sum(): lax.ppermute(value, axis, perm=[(i, i ^ step) for i in range(size)])]
    select_n x1 -> x2, other arithmetic: 0.26 us -> 2.3 us  [local(): jnp.take(jnp.roll(jnp.stack(pieces), me, axis=0), group_order(), axis=0)]
    ppermute x5, starting transfers between devices: 5.76 us -> 3.74 us  [butterfly_sum(): lax.ppermute(value, axis, perm=[(i, i ^ step) for i in range(size)])]
  transfers between devices with their start and end apart: 19 -> 19, of which waited for: 12 -> 13; matrix products, arithmetic and copies ran while one was open for 20% -> 22% of each run, Pallas kernels for 0% -> 0%
where the time goes in v14:
time: 141 us
  waiting for transfers between devices  65.3 us (46%)
  starting transfers between devices  18 us (13%)
  between operations  17.2 us (12%)
  matrix products  16.3 us (12%)
  local copies, waits for them, and re-layouts  16.1 us (11%)
  other arithmetic  7.95 us (6%)
    all_gather x1, waiting for transfers between devices, local(): lax.all_gather(down_weight, TOKS, axis=0, tiled=True)  17.7 us
    ppermute x5, waiting for transfers between devices, butterfly_sum(): lax.ppermute(value, axis, perm=[(i, i ^ step) for i in range(size)])  15.7 us
    ppermute x1, waiting for transfers between devices, teacher_attention(): got = lax.ppermute(theirs, 'tensor', perm=[(0, 1), (1, 0)])  15.1 us
    ppermute x3, waiting for transfers between devices, group_gather(): lax.ppermute(value, chips, perm=[(i, (i - k) % n) for i in range(n)])  9.02 us
    ppermute x7, starting transfers between devices, local(): lax.ppermute(send, GROUP, perm=[(i, (i - k) % group) for i in range(group)])  8.64 us
    dot_general x1, matrix products, teacher_attention(): jnp.dot(context, w_out, preferred_element_type=jnp.float32)  8.41 us
    unnamed x53, local copies, waits for them, and re-layouts  5.67 us
    gather x2, local copies, waits for them, and re-layouts, local(): jnp.take(jnp.roll(jnp.stack(pieces), me, axis=0), group_order(), axis=0)  5.01 us
  transfers between devices with their start and end apart: 19, of which 13 were waited for; matrix products, arithmetic and copies ran while one was open for 22% of the time, Pallas kernels for 0%

profile of v14, /device:TPU:0, one launch (start us, length us, event | category | flops | bytes accessed | tf_op | source)
XLA Modules:
  0.0 140.8 jit_solution(3195573045108366561)
XLA Ops:
  7.4 1.6 %copy.25 = bf16[128,3072]{0,1:T(8,128)(2,1)S(1)} copy(bf16[128,3072]{1,0:T(8,128)(2,1)} %param.20) | data formatting | bytes 1572864 | tf_op args[6]
  10.2 3.3 %collective-permute-start = (bf16[128,384]{0,1:T(8,128)(2,1)}, bf16[128,384]{0,1:T(8,128)(2,1)S(1)}, u32[]{:S(2)}, u32[]{:S(2)}) collective-permute-start(bf16[128,384]{0,1:T(8,128)(2,1)} %get-tuple-element.33), channel_id=1, source_target_pairs={{0,7},{1,0},{2,1},{3,2},{4,3},{5,4},{6,5},{7,6},{8,15},{9,8},{10,9... | collective-permute-start | bytes 294920 | tf_op jit(solution)/shard_map/ppermute | solution.py:111
  18.1 8.4 %convolution_convert_fusion = bf16[256,4096]{1,0:T(8,128)(2,1)S(1)} fusion(bf16[256,2048]{1,0:T(8,128)(2,1)S(1)} %copy-done, bf16[2048,4096]{1,0:T(8,128)(2,1)} %param.15), kind=kOutput, calls=%fused_computation.1 | convolution fusion | flops 4296015872 | bytes 19922944 | tf_op jit(solution)/shard_map/dot_general | solution.py:33
  32.2 1.9 %collective-permute-done.6 = bf16[128,384]{0,1:T(8,128)(2,1)S(1)} collective-permute-done((bf16[128,384]{0,1:T(8,128)(2,1)S(1)}, bf16[128,384]{0,1:T(8,128)(2,1)S(1)}, u32[]{:S(2)}, u32[]{:S(2)}) %collective-permute-start.6) | collective-permute-done | bytes 98336 | tf_op jit(solution)/shard_map/ppermute | solution.py:111
  37.0 2.7 %gather_fusion = bf16[8,128,384]{1,2,0:T(8,128)(2,1)} fusion(bf16[8,128,384]{1,2,0:T(8,128)(2,1)} %constant_dynamic-slice_fusion, s32[1024]{0:T(1024)S(1)} %pad_clamp_fusion), kind=kCustom, calls=%fused_computation | custom fusion | bytes 1572896 | tf_op jit(solution)/shard_map/jit(_take)/gather | solution.py:113
  39.7 2.3 %copy.27 = bf16[8,128,384]{2,1,0:T(8,128)(2,1)} copy(bf16[8,128,384]{1,2,0:T(8,128)(2,1)} %gather_fusion) | data formatting | bytes 1572864 | tf_op jit(solution)/shard_map/jit(_take)/gather | solution.py:113
  42.1 2.2 %bitcast_select_fusion = bf16[1024,384]{1,0:T(8,128)(2,1)} fusion(bf16[8,128,384]{2,1,0:T(8,128)(2,1)} %copy.27, pred[1024]{0:T(1024)(128)(4,1)S(1)} %broadcast_bitcast_fusion), kind=kLoop, calls=%fused_computation.14 | loop fusion | flops 393216 | bytes 1573888 | tf_op jit(solution)/shard_map/jit(_take)/select_n | solution.py:113
  44.3 15.1 %collective-permute-done.7 = bf16[128,4096]{1,0:T(8,128)(2,1)} collective-permute-done((bf16[128,4096]{1,0:T(8,128)(2,1)}, bf16[128,4096]{1,0:T(8,128)(2,1)}, u32[]{:S(2)}, u32[]{:S(2)}) %collective-permute-start.7) | collective-permute-done | bytes 1048608 | tf_op jit(solution)/shard_map/ppermute | solution.py:42
  59.4 1.6 %convert_add_fusion.1 = f32[128,4096]{1,0:T(8,128)S(1)} fusion(bf16[128,4096]{1,0:T(8,128)(2,1)} %collective-permute-done.7, pred[]{:T(512)S(6)} %eq.46, bf16[256,4096]{1,0:T(8,128)(2,1)S(1)} %convolution_convert_fusion), kind=kLoop, calls=%fused_computation.7 | loop fusion | flops 2097152 | bytes 5242881 | tf_op jit(solution)/shard_map/add | solution.py:43
  62.2 2.1 %fusion.14 = (f32[128]{0:T(128)S(1)}, f32[128,4]{0,1:T(4,128)S(1)}) fusion(bf16[4096,4]{0,1:T(4,128)(2,1)S(1)} %copy-done.15, bf16[128,4096]{1,0:T(8,128)(2,1)S(1)} %copy-done.1, f32[128,4096]{1,0:T(8,128)S(1)} %convert_add_fusion.1, f32[4096]{0:T(1024)S(1)} %copy-done.10, f32[128]{0:T(128)S(1)} %add_rsqrt_fusion, f32[128]{0:T(128)S(1)} %broadcast_multiply_fusion, ...), kind=kOutput, calls=%fused_computation.96 | convolution fusion | flops 8913280 | bytes 3198472 | tf_op jit(solution)/shard_map/dot_general | solution.py:119
  64.4 17.7 %all-gather.2.cloned.1.call-done = bf16[3072,768]{1,0:T(8,128)(2,1)} async-done(((bf16[96,768]{1,0:T(8,128)(2,1)}), bf16[3072,768]{1,0:T(8,128)(2,1)}) %all-gather.2.cloned.1.call-update) | async-done | bytes 4718608 | tf_op jit(solution)/shard_map/all_gather | solution.py:122
  82.0 3.2 %fusion.13 = (f32[128]{0:T(128)S(1)}, f32[128,768]{1,0:T(8,128)S(1)}) fusion(bf16[128,3072]{1,0:T(8,128)(2,1)S(1)} %copy-done.3, bf16[3072,768]{1,0:T(8,128)(2,1)} %all-gather.2.cloned.1.call-done, bf16[128,768]{1,0:T(8,128)(2,1)S(1)} %copy-done.6), kind=kOutput, calls=%fused_computation.95 | convolution fusion | flops 604274560 | bytes 6095360 | tf_op jit(solution)/shard_map/dot_general | solution.py:28
  87.1 1.6 %collective-permute-start.10 = (bf16[128,768]{1,0:T(8,128)(2,1)S(1)}, bf16[128,768]{1,0:T(8,128)(2,1)S(1)}, u32[]{:S(2)}, u32[]{:S(2)}) collective-permute-start(bf16[128,768]{1,0:T(8,128)(2,1)S(1)} %get-tuple-element.25), channel_id=1, source_target_pairs={{0,1},{1,4},{4,5},{5,0},{2,3},{3,6},{6,7},{7,2},{8,9},{9,12},{12,1... | collective-permute-start | bytes 589832 | tf_op jit(solution)/shard_map/ppermute | solution.py:65
  90.1 1.5 %collective-permute-start.9 = (bf16[128,768]{1,0:T(8,128)(2,1)S(1)}, bf16[128,768]{1,0:T(8,128)(2,1)S(1)}, u32[]{:S(2)}, u32[]{:S(2)}) collective-permute-start(bf16[128,768]{1,0:T(8,128)(2,1)S(1)} %get-tuple-element.25), channel_id=1, source_target_pairs={{0,4},{1,5},{4,0},{5,1},{2,6},{3,7},{6,2},{7,3},{8,12},{9,13},{12,... | collective-permute-start | bytes 589832 | tf_op jit(solution)/shard_map/ppermute | solution.py:65
  91.5 5.9 %collective-permute-done.10 = bf16[128,768]{1,0:T(8,128)(2,1)S(1)} collective-permute-done((bf16[128,768]{1,0:T(8,128)(2,1)S(1)}, bf16[128,768]{1,0:T(8,128)(2,1)S(1)}, u32[]{:S(2)}, u32[]{:S(2)}) %collective-permute-start.10) | collective-permute-done | bytes 196640 | tf_op jit(solution)/shard_map/ppermute | solution.py:65
  97.5 1.9 %collective-permute-done.8 = bf16[128,768]{1,0:T(8,128)(2,1)S(1)} collective-permute-done((bf16[128,768]{1,0:T(8,128)(2,1)S(1)}, bf16[128,768]{1,0:T(8,128)(2,1)S(1)}, u32[]{:S(2)}, u32[]{:S(2)}) %collective-permute-start.8) | collective-permute-done | bytes 196640 | tf_op jit(solution)/shard_map/ppermute | solution.py:65
  100.8 2.2 %collective-permute-done.11 = bf16[512,768]{1,0:T(8,128)(2,1)S(1)} collective-permute-done((bf16[512,768]{1,0:T(8,128)(2,1)S(1)}, bf16[512,768]{1,0:T(8,128)(2,1)S(1)}, u32[]{:S(2)}, u32[]{:S(2)}) %collective-permute-start.11) | collective-permute-done | bytes 786464 | tf_op jit(solution)/shard_map/ppermute | solution.py:69
  103.0 1.8 %fusion.17 = f32[384,768]{1,0:T(8,128)} fusion(bf16[1024,384]{1,0:T(8,128)(2,1)S(1)} %copy-done.4, bf16[1024,768]{1,0:T(8,128)(2,1)S(1)} %constant_dynamic-update-slice_fusion), kind=kOutput, calls=%fused_computation.99 | convolution fusion | flops 603979776 | bytes 3538944 | tf_op jit(solution)/shard_map/dot_general | solution.py:163
  106.7 3.7 %collective-permute-done.12 = f32[3074]{0:T(1024)S(1)} collective-permute-done((f32[3074]{0:T(1024)S(1)}, f32[3074]{0:T(1024)S(1)}, u32[]{:S(2)}, u32[]{:S(2)}) %collective-permute-start.12) | collective-permute-done | bytes 12328 | tf_op jit(solution)/shard_map/ppermute | solution.py:54
  112.2 3.2 %collective-permute-done.14 = f32[3074]{0:T(1024)S(1)} collective-permute-done((f32[3074]{0:T(1024)S(1)}, f32[3074]{0:T(1024)S(1)}, u32[]{:S(2)}, u32[]{:S(2)}) %collective-permute-start.14) | collective-permute-done | bytes 12328 | tf_op jit(solution)/shard_map/ppermute | solution.py:54
  115.4 1.8 %collective-permute-start.15 = (f32[3074]{0:T(1024)S(1)}, f32[3074]{0:T(1024)S(1)}, u32[]{:S(2)}, u32[]{:S(2)}) collective-permute-start(f32[3074]{0:T(1024)S(1)} %add.393), channel_id=1, source_target_pairs={{0,8},{8,0},{16,24},{24,16},{1,9},{9,1},{17,25},{25,17},{2,10},{10... | collective-permute-start | bytes 36896 | tf_op jit(solution)/shard_map/ppermute | solution.py:54
  117.3 3.2 %collective-permute-done.15 = f32[3074]{0:T(1024)S(1)} collective-permute-done((f32[3074]{0:T(1024)S(1)}, f32[3074]{0:T(1024)S(1)}, u32[]{:S(2)}, u32[]{:S(2)}) %collective-permute-start.15) | collective-permute-done | bytes 12328 | tf_op jit(solution)/shard_map/ppermute | solution.py:54
  121.8 4.4 %collective-permute-done.16 = f32[3074]{0:T(1024)S(1)} collective-permute-done((f32[3074]{0:T(1024)S(1)}, f32[3074]{0:T(1024)S(1)}, u32[]{:S(2)}, u32[]{:S(2)}) %collective-permute-start.16) | collective-permute-done | bytes 12328 | tf_op jit(solution)/shard_map/ppermute | solution.py:54
  129.2 3.7 %reduce-scatter.2.cloned.1.call-done = f32[96,768]{1,0:T(8,128)} async-done(((f32[384,768]{1,0:T(8,128)}), f32[96,768]{1,0:T(8,128)}) %reduce-scatter.2.cloned.1.call-update) | async-done | bytes 294928 | tf_op jit(solution)/shard_map/reduce_scatter | solution.py:166
  (125 shorter events, 26.6 us)
Async XLA Ops:
  7.2 74.9 %all-gather.2.cloned.1.call-start = ((), (), s32[]{:S(2)}) async-start(), calls=%async_computation.1 | async-start | bytes 4866048 | tf_op jit(solution)/shard_map/all_gather | solution.py:122
  10.2 17.4 %collective-permute-start = (bf16[128,384]{0,1:T(8,128)(2,1)}, bf16[128,384]{0,1:T(8,128)(2,1)S(1)}, u32[]{:S(2)}, u32[]{:S(2)}) collective-permute-start(bf16[128,384]{0,1:T(8,128)(2,1)} %get-tuple-element.33), channel_id=1, source_target_pairs={{0,7},{1,0},{2,1},{3,2},{4,3},{5,4},{6,5},{7,6},{8,15},{9,8},{10,9... | collective-permute-start | bytes 294920 | tf_op jit(solution)/shard_map/ppermute | solution.py:111
  13.6 15.2 %collective-permute-start.1 = (bf16[128,384]{0,1:T(8,128)(2,1)}, bf16[128,384]{0,1:T(8,128)(2,1)S(1)}, u32[]{:S(2)}, u32[]{:S(2)}) collective-permute-start(bf16[128,384]{0,1:T(8,128)(2,1)} %get-tuple-element.32), channel_id=1, source_target_pairs={{0,6},{1,7},{2,0},{3,1},{4,2},{5,3},{6,4},{7,5},{8,14},{9,15},{10,... | collective-permute-start | bytes 294920 | tf_op jit(solution)/shard_map/ppermute | solution.py:111
  14.4 15.8 %collective-permute-start.2 = (bf16[128,384]{0,1:T(8,128)(2,1)}, bf16[128,384]{0,1:T(8,128)(2,1)S(1)}, u32[]{:S(2)}, u32[]{:S(2)}) collective-permute-start(bf16[128,384]{0,1:T(8,128)(2,1)} %get-tuple-element.31), channel_id=1, source_target_pairs={{0,5},{1,6},{2,7},{3,0},{4,1},{5,2},{6,3},{7,4},{8,13},{9,14},{10,... | collective-permute-start | bytes 294920 | tf_op jit(solution)/shard_map/ppermute | solution.py:111
  14.6 16.6 %collective-permute-start.3 = (bf16[128,384]{0,1:T(8,128)(2,1)}, bf16[128,384]{0,1:T(8,128)(2,1)S(1)}, u32[]{:S(2)}, u32[]{:S(2)}) collective-permute-start(bf16[128,384]{0,1:T(8,128)(2,1)} %get-tuple-element.30), channel_id=1, source_target_pairs={{0,4},{1,5},{2,6},{3,7},{4,0},{5,1},{6,2},{7,3},{8,12},{9,13},{10,... | collective-permute-start | bytes 294920 | tf_op jit(solution)/shard_map/ppermute | solution.py:111
  15.8 15.4 %collective-permute-start.4 = (bf16[128,384]{0,1:T(8,128)(2,1)}, bf16[128,384]{0,1:T(8,128)(2,1)}, u32[]{:S(2)}, u32[]{:S(2)}) collective-permute-start(bf16[128,384]{0,1:T(8,128)(2,1)} %get-tuple-element.29), channel_id=1, source_target_pairs={{0,3},{1,4},{2,5},{3,6},{4,7},{5,0},{6,1},{7,2},{8,11},{9,12},{10,... | collective-permute-start | bytes 294920 | tf_op jit(solution)/shard_map/ppermute | solution.py:111
  16.4 116.4 %reduce-scatter.2.cloned.1.call-start = ((), (), s32[]{:S(2)}) async-start(), calls=%async_computation.2 | async-start | bytes 1474560 | tf_op jit(solution)/shard_map/reduce_scatter | solution.py:166
  27.7 4.5 %collective-permute-start.5 = (bf16[128,384]{0,1:T(8,128)(2,1)S(1)}, bf16[128,384]{0,1:T(8,128)(2,1)S(1)}, u32[]{:S(2)}, u32[]{:S(2)}) collective-permute-start(bf16[128,384]{0,1:T(8,128)(2,1)S(1)} %copy-done.8), channel_id=1, source_target_pairs={{0,2},{1,3},{2,4},{3,5},{4,6},{5,7},{6,0},{7,1},{8,10},{9,11},{10,... | collective-permute-start | bytes 294920 | tf_op jit(solution)/shard_map/ppermute | solution.py:111
  28.8 5.3 %collective-permute-start.6 = (bf16[128,384]{0,1:T(8,128)(2,1)S(1)}, bf16[128,384]{0,1:T(8,128)(2,1)S(1)}, u32[]{:S(2)}, u32[]{:S(2)}) collective-permute-start(bf16[128,384]{0,1:T(8,128)(2,1)S(1)} %copy-done.7), channel_id=1, source_target_pairs={{0,1},{1,2},{2,3},{3,4},{4,5},{5,6},{6,7},{7,0},{8,9},{9,10},{10,1... | collective-permute-start | bytes 294920 | tf_op jit(solution)/shard_map/ppermute | solution.py:111
  30.2 29.2 %collective-permute-start.7 = (bf16[128,4096]{1,0:T(8,128)(2,1)}, bf16[128,4096]{1,0:T(8,128)(2,1)}, u32[]{:S(2)}, u32[]{:S(2)}) collective-permute-start(bf16[128,4096]{1,0:T(8,128)(2,1)} %broadcast_select_fusion), channel_id=1, source_target_pairs={{0,1},{1,0},{2,3},{3,2},{4,5},{5,4},{6,7},{7,6},{8,9},{9,8},{10,11... | collective-permute-start | bytes 3145736 | tf_op jit(solution)/shard_map/ppermute | solution.py:42
  44.3 16.8 %copy-start.1 = (bf16[128,4096]{1,0:T(8,128)(2,1)S(1)}, bf16[128,4096]{1,0:T(8,128)(2,1)}, u32[]{:S(2)}) copy-start(bf16[128,4096]{1,0:T(8,128)(2,1)} %param.16) | copy-start | bytes 3145732
  62.2 19.9 %copy-start.3 = (bf16[128,3072]{1,0:T(8,128)(2,1)S(1)}, bf16[128,3072]{1,0:T(8,128)(2,1)}, u32[]{:S(2)}) copy-start(bf16[128,3072]{1,0:T(8,128)(2,1)} %param.20) | copy-start | bytes 2359300
  62.2 19.9 %copy-start.6 = (bf16[128,768]{1,0:T(8,128)(2,1)S(1)}, bf16[128,768]{1,0:T(8,128)(2,1)}, u32[]{:S(2)}) copy-start(bf16[128,768]{1,0:T(8,128)(2,1)} %param.21) | copy-start | bytes 589828
  64.3 21.3 %copy-start.9 = (bf16[768,4]{0,1:T(4,128)(2,1)S(1)}, bf16[768,4]{0,1:T(4,128)(2,1)}, u32[]{:S(2)}) copy-start(bf16[768,4]{0,1:T(4,128)(2,1)} %param.24) | copy-start | bytes 18436
  64.4 21.5 %copy-start.12 = (s32[128]{0:T(128)S(1)}, s32[128]{0:T(128)}, u32[]{:S(2)}) copy-start(s32[128]{0:T(128)} %param.25) | copy-start | bytes 1540
  87.1 10.4 %collective-permute-start.10 = (bf16[128,768]{1,0:T(8,128)(2,1)S(1)}, bf16[128,768]{1,0:T(8,128)(2,1)S(1)}, u32[]{:S(2)}, u32[]{:S(2)}) collective-permute-start(bf16[128,768]{1,0:T(8,128)(2,1)S(1)} %get-tuple-element.25), channel_id=1, source_target_pairs={{0,1},{1,4},{4,5},{5,0},{2,3},{3,6},{6,7},{7,2},{8,9},{9,12},{12,1... | collective-permute-start | bytes 589832 | tf_op jit(solution)/shard_map/ppermute | solution.py:65
  88.7 10.7 %collective-permute-start.8 = (bf16[128,768]{1,0:T(8,128)(2,1)S(1)}, bf16[128,768]{1,0:T(8,128)(2,1)S(1)}, u32[]{:S(2)}, u32[]{:S(2)}) collective-permute-start(bf16[128,768]{1,0:T(8,128)(2,1)S(1)} %get-tuple-element.25), channel_id=1, source_target_pairs={{0,5},{1,0},{4,1},{5,4},{2,7},{3,2},{6,3},{7,6},{8,13},{9,8},{12,9... | collective-permute-start | bytes 589832 | tf_op jit(solution)/shard_map/ppermute | solution.py:65
  90.1 10.5 %collective-permute-start.9 = (bf16[128,768]{1,0:T(8,128)(2,1)S(1)}, bf16[128,768]{1,0:T(8,128)(2,1)S(1)}, u32[]{:S(2)}, u32[]{:S(2)}) collective-permute-start(bf16[128,768]{1,0:T(8,128)(2,1)S(1)} %get-tuple-element.25), channel_id=1, source_target_pairs={{0,4},{1,5},{4,0},{5,1},{2,6},{3,7},{6,2},{7,3},{8,12},{9,13},{12,... | collective-permute-start | bytes 589832 | tf_op jit(solution)/shard_map/ppermute | solution.py:65
  100.6 2.4 %collective-permute-start.11 = (bf16[512,768]{1,0:T(8,128)(2,1)S(1)}, bf16[512,768]{1,0:T(8,128)(2,1)S(1)}, u32[]{:S(2)}, u32[]{:S(2)}) collective-permute-start(bf16[512,768]{1,0:T(8,128)(2,1)S(1)} %pad_maximum_fusion), channel_id=1, source_target_pairs={{0,2},{2,0},{1,3},{3,1},{4,6},{6,4},{5,7},{7,5},{8,10},{10,8},{9,1... | collective-permute-start | bytes 2359304 | tf_op jit(solution)/shard_map/ppermute | solution.py:69
  106.7 3.7 %collective-permute-start.12 = (f32[3074]{0:T(1024)S(1)}, f32[3074]{0:T(1024)S(1)}, u32[]{:S(2)}, u32[]{:S(2)}) collective-permute-start(f32[3074]{0:T(1024)S(1)} %concatenate.52), channel_id=1, source_target_pairs={{0,1},{1,0},{2,3},{3,2},{4,5},{5,4},{6,7},{7,6},{8,9},{9,8},{10,11... | collective-permute-start | bytes 36896 | tf_op jit(solution)/shard_map/ppermute | solution.py:54
  110.5 1.2 collective-permute-start.13
  111.7 3.7 %collective-permute-start.14 = (f32[3074]{0:T(1024)S(1)}, f32[3074]{0:T(1024)S(1)}, u32[]{:S(2)}, u32[]{:S(2)}) collective-permute-start(f32[3074]{0:T(1024)S(1)} %add.392), channel_id=1, source_target_pairs={{0,4},{4,0},{1,5},{5,1},{2,6},{6,2},{3,7},{7,3},{8,12},{12,8},{9,1... | collective-permute-start | bytes 36896 | tf_op jit(solution)/shard_map/ppermute | solution.py:54
  115.4 5.0 %collective-permute-start.15 = (f32[3074]{0:T(1024)S(1)}, f32[3074]{0:T(1024)S(1)}, u32[]{:S(2)}, u32[]{:S(2)}) collective-permute-start(f32[3074]{0:T(1024)S(1)} %add.393), channel_id=1, source_target_pairs={{0,8},{8,0},{16,24},{24,16},{1,9},{9,1},{17,25},{25,17},{2,10},{10... | collective-permute-start | bytes 36896 | tf_op jit(solution)/shard_map/ppermute | solution.py:54
  120.4 5.8 %collective-permute-start.16 = (f32[3074]{0:T(1024)S(1)}, f32[3074]{0:T(1024)S(1)}, u32[]{:S(2)}, u32[]{:S(2)}) collective-permute-start(f32[3074]{0:T(1024)S(1)} %add.394), channel_id=1, source_target_pairs={{0,16},{8,24},{16,0},{24,8},{1,17},{9,25},{17,1},{25,9},{2,18},{10... | collective-permute-start | bytes 36896 | tf_op jit(solution)/shard_map/ppermute | solution.py:54
  (12 other events, 62.3 us)
Sparse Core Ops, SparseCore 0:
  16.5 65.4 all-gather.1
  105.0 27.7 reduce-scatter.1

commit v15 on v14

--- a/solution.py
+++ b/solution.py
@@ -28,19 +28,20 @@
     return jnp.dot(ordered, row_piece, preferred_element_type=jnp.float32)
 
 
-def teacher_attention(context, w_out, tok_rows):
+def teacher_attention(context, w_out, tok_rows, ride):
     tensor_size = lax.axis_size("tensor")
     partial = jnp.dot(context, w_out, preferred_element_type=jnp.float32).astype(jnp.bfloat16)
+    partial, ride = lax.optimization_barrier((partial, ride))
     if tensor_size != 2:
         return lax.psum_scatter(
             partial, "tensor", scatter_dimension=0, tiled=True
-        ).astype(jnp.float32)
+        ).astype(jnp.float32), ride
     me = lax.axis_index("tensor")
     halves = partial.reshape(2, tok_rows, partial.shape[1])
     mine = jnp.where(me == 0, halves[0], halves[1])
     theirs = jnp.where(me == 0, halves[1], halves[0])
     got = lax.ppermute(theirs, "tensor", perm=[(0, 1), (1, 0)])
-    return mine.astype(jnp.float32) + got.astype(jnp.float32)
+    return mine.astype(jnp.float32) + got.astype(jnp.float32), ride
 
 
 def butterfly_sum(value, axes):
@@ -96,13 +97,13 @@
     lengths,
 ):
     tok_rows = teacher_input.shape[0]
-    attention = teacher_attention(context, w_out, tok_rows)
     group = lax.axis_size(GROUP)
     outer = lax.axis_size("q")
     hidden_cols = student_hidden.shape[1]
     block = hidden_cols // (group * outer)
     hidden_split = student_hidden.reshape(tok_rows, outer, group, block)
     hidden_split = jnp.transpose(hidden_split, (2, 0, 1, 3)).reshape(group, tok_rows, outer * block)
+    attention, hidden_split = teacher_attention(context, w_out, tok_rows, hidden_split)
     me = lax.axis_index(GROUP)
     pieces = [hidden_split[me]]
     for k in range(1, group):

time: 141 us -> 140 us (level)
  waiting for transfers between devices: 65.3 us -> 59.9 us
  local copies, waits for them, and re-layouts: 16.1 us -> 17.9 us
    all_gather x1, waiting for transfers between devices: 17.7 us -> 10.3 us  [local(): lax.all_gather(down_weight, TOKS, axis=0, tiled=True)]
    ppermute x1, waiting for transfers between devices: 15.1 us -> 17.6 us  [teacher_attention(): got = lax.ppermute(theirs, 'tensor', perm=[(0, 1), (1, 0)])]
    ppermute x5, waiting for transfers between devices: 15.7 us -> 13.9 us  [butterfly_sum(): lax.ppermute(value, axis, perm=[(i, i ^ step) for i in range(size)])]
    unnamed x53 -> x49, local copies, waits for them, and re-layouts: 5.67 us -> 5.55 us
  transfers between devices with their start and end apart: 19 -> 19, of which waited for: 13 -> 14; matrix products, arithmetic and copies ran while one was open for 22% -> 26% of each run, Pallas kernels for 0% -> 0%
where the time goes in v15:
time: 140 us; the launch traced here: 139 us
  waiting for transfers between devices  59.9 us (43%)
  starting transfers between devices  19.3 us (14%)
  local copies, waits for them, and re-layouts  17.9 us (13%)
  between operations  17.1 us (12%)
  matrix products  16.3 us (12%)
  other arithmetic  8.61 us (6%)
    ppermute x1, waiting for transfers between devices, teacher_attention(): got = lax.ppermute(theirs, 'tensor', perm=[(0, 1), (1, 0)])  17.6 us
    ppermute x5, waiting for transfers between devices, butterfly_sum(): lax.ppermute(value, axis, perm=[(i, i ^ step) for i in range(size)])  13.9 us
    all_gather x1, waiting for transfers between devices, local(): lax.all_gather(down_weight, TOKS, axis=0, tiled=True)  10.3 us
    ppermute x3, waiting for transfers between devices, group_gather(): lax.ppermute(value, chips, perm=[(i, (i - k) % n) for i in range(n)])  9.02 us
    ppermute x7, starting transfers between devices, local(): lax.ppermute(send, GROUP, perm=[(i, (i - k) % group) for i in range(group)])  8.68 us
    dot_general x1, matrix products, teacher_attention(): jnp.dot(context, w_out, preferred_element_type=jnp.float32)  8.41 us
    unnamed x49, local copies, waits for them, and re-layouts  5.55 us
    gather x2, local copies, waits for them, and re-layouts, local(): jnp.take(jnp.roll(jnp.stack(pieces), me, axis=0), group_order(), axis=0)  5.03 us
  transfers between devices with their start and end apart: 19, of which 14 were waited for; matrix products, arithmetic and copies ran while one was open for 26% of the time, Pallas kernels for 0%

profile of v15, /device:TPU:0, one launch (start us, length us, event | category | flops | bytes accessed | tf_op | source)
XLA Modules:
  0.0 139.1 jit_solution(7053121046915104228)
XLA Ops:
  8.1 1.5 %copy.25 = bf16[128,3072]{0,1:T(8,128)(2,1)S(1)} copy(bf16[128,3072]{1,0:T(8,128)(2,1)} %param.20) | data formatting | bytes 1572864 | tf_op args[6]
  10.6 8.4 %convolution_convert_fusion = bf16[256,4096]{1,0:T(8,128)(2,1)S(1)} fusion(bf16[256,2048]{1,0:T(8,128)(2,1)S(1)} %copy-done, bf16[2048,4096]{1,0:T(8,128)(2,1)} %param.15), kind=kOutput, calls=%fused_computation.1 | convolution fusion | flops 4296015872 | bytes 19922944 | tf_op jit(solution)/shard_map/dot_general | solution.py:33
  19.1 2.1 %dynamic-slice_bitcast_fusion = (bf16[128,384]{0,1:T(8,128)(2,1)}, bf16[16,128,384]{1,2,0:T(8,128)(2,1)}, bf16[128,384]{0,1:T(8,128)(2,1)}, bf16[128,384]{0,1:T(...) fusion(bf16[8,128,384]{1,2,0:T(8,128)(2,1)} %bitcast.63, ...), kind=kLoop, calls=%fused_computation.34 | loop fusion | bytes 1572896 | tf_op jit(solution)/shard_map/jit(dynamic_index_in_dim)/squeeze | solution.py:110
  21.2 3.3 %collective-permute-start = (bf16[128,384]{0,1:T(8,128)(2,1)}, bf16[128,384]{0,1:T(8,128)(2,1)S(1)}, u32[]{:S(2)}, u32[]{:S(2)}) collective-permute-start(bf16[128,384]{0,1:T(8,128)(2,1)} %get-tuple-element.37), channel_id=1, source_target_pairs={{0,7},{1,0},{2,1},{3,2},{4,3},{5,4},{6,5},{7,6},{8,15},{9,8},{10,9... | collective-permute-start | bytes 294920 | tf_op jit(solution)/shard_map/ppermute | solution.py:112
  40.1 2.7 %gather_fusion = bf16[8,128,384]{1,2,0:T(8,128)(2,1)} fusion(bf16[8,128,384]{1,2,0:T(8,128)(2,1)} %constant_dynamic-slice_fusion, s32[1024]{0:T(1024)S(1)} %pad_clamp_fusion), kind=kCustom, calls=%fused_computation | custom fusion | bytes 1572896 | tf_op jit(solution)/shard_map/jit(_take)/gather | solution.py:114
  42.8 2.4 %copy.27 = bf16[8,128,384]{2,1,0:T(8,128)(2,1)} copy(bf16[8,128,384]{1,2,0:T(8,128)(2,1)} %gather_fusion) | data formatting | bytes 1572864 | tf_op jit(solution)/shard_map/jit(_take)/gather | solution.py:114
  45.1 2.2 %bitcast_select_fusion = bf16[1024,384]{1,0:T(8,128)(2,1)} fusion(bf16[8,128,384]{2,1,0:T(8,128)(2,1)} %copy.27, pred[1024]{0:T(1024)(128)(4,1)S(1)} %broadcast_bitcast_fusion), kind=kLoop, calls=%fused_computation.14 | loop fusion | flops 393216 | bytes 1573888 | tf_op jit(solution)/shard_map/jit(_take)/select_n | solution.py:114
  47.4 17.6 %collective-permute-done.7 = bf16[128,4096]{1,0:T(8,128)(2,1)} collective-permute-done((bf16[128,4096]{1,0:T(8,128)(2,1)}, bf16[128,4096]{1,0:T(8,128)(2,1)}, u32[]{:S(2)}, u32[]{:S(2)}) %collective-permute-start.7) | collective-permute-done | bytes 1048608 | tf_op jit(solution)/shard_map/ppermute | solution.py:43
  64.9 1.6 %convert_add_fusion.1 = f32[128,4096]{1,0:T(8,128)S(1)} fusion(bf16[128,4096]{1,0:T(8,128)(2,1)} %collective-permute-done.7, pred[]{:T(512)S(6)} %eq.46, bf16[256,4096]{1,0:T(8,128)(2,1)S(1)} %convolution_convert_fusion), kind=kLoop, calls=%fused_computation.7 | loop fusion | flops 2097152 | bytes 5242881 | tf_op jit(solution)/shard_map/add | solution.py:44
  67.7 2.1 %fusion.14 = (f32[128]{0:T(128)S(1)}, f32[128,4]{0,1:T(4,128)S(1)}) fusion(bf16[4096,4]{0,1:T(4,128)(2,1)S(1)} %copy-done.14, bf16[128,4096]{1,0:T(8,128)(2,1)S(1)} %copy-done.1, f32[128,4096]{1,0:T(8,128)S(1)} %convert_add_fusion.1, f32[4096]{0:T(1024)S(1)} %copy-done.9, f32[128]{0:T(128)S(1)} %add_rsqrt_fusion, f32[128]{0:T(128)S(1)} %broadcast_multiply_fusion, ...), kind=kOutput, calls=%fused_computation.96 | convolution fusion | flops 8913280 | bytes 3198472 | tf_op jit(solution)/shard_map/dot_general | solution.py:120
  69.9 10.3 %all-gather.2.cloned.1.call-done = bf16[3072,768]{1,0:T(8,128)(2,1)} async-done(((bf16[96,768]{1,0:T(8,128)(2,1)}), bf16[3072,768]{1,0:T(8,128)(2,1)}) %all-gather.2.cloned.1.call-update) | async-done | bytes 4718608 | tf_op jit(solution)/shard_map/all_gather | solution.py:123
  80.2 3.2 %fusion.13 = (f32[128]{0:T(128)S(1)}, f32[128,768]{1,0:T(8,128)S(1)}) fusion(bf16[128,3072]{1,0:T(8,128)(2,1)S(1)} %copy-done.2, bf16[3072,768]{1,0:T(8,128)(2,1)} %all-gather.2.cloned.1.call-done, bf16[128,768]{1,0:T(8,128)(2,1)S(1)} %copy-done.5), kind=kOutput, calls=%fused_computation.95 | convolution fusion | flops 604274560 | bytes 6095360 | tf_op jit(solution)/shard_map/dot_general | solution.py:28
  86.0 2.2 %collective-permute-start.8 = (bf16[128,768]{1,0:T(8,128)(2,1)S(1)}, bf16[128,768]{1,0:T(8,128)(2,1)S(1)}, u32[]{:S(2)}, u32[]{:S(2)}) collective-permute-start(bf16[128,768]{1,0:T(8,128)(2,1)S(1)} %get-tuple-element.29), channel_id=1, source_target_pairs={{0,5},{1,0},{4,1},{5,4},{2,7},{3,2},{6,3},{7,6},{8,13},{9,8},{12,9... | collective-permute-start | bytes 589832 | tf_op jit(solution)/shard_map/ppermute | solution.py:66
  89.5 5.3 %collective-permute-done.10 = bf16[128,768]{1,0:T(8,128)(2,1)S(1)} collective-permute-done((bf16[128,768]{1,0:T(8,128)(2,1)S(1)}, bf16[128,768]{1,0:T(8,128)(2,1)S(1)}, u32[]{:S(2)}, u32[]{:S(2)}) %collective-permute-start.10) | collective-permute-done | bytes 196640 | tf_op jit(solution)/shard_map/ppermute | solution.py:66
  94.8 2.4 %collective-permute-done.8 = bf16[128,768]{1,0:T(8,128)(2,1)S(1)} collective-permute-done((bf16[128,768]{1,0:T(8,128)(2,1)S(1)}, bf16[128,768]{1,0:T(8,128)(2,1)S(1)}, u32[]{:S(2)}, u32[]{:S(2)}) %collective-permute-start.8) | collective-permute-done | bytes 196640 | tf_op jit(solution)/shard_map/ppermute | solution.py:66
  98.7 2.2 %collective-permute-done.11 = bf16[512,768]{1,0:T(8,128)(2,1)S(1)} collective-permute-done((bf16[512,768]{1,0:T(8,128)(2,1)S(1)}, bf16[512,768]{1,0:T(8,128)(2,1)S(1)}, u32[]{:S(2)}, u32[]{:S(2)}) %collective-permute-start.11) | collective-permute-done | bytes 786464 | tf_op jit(solution)/shard_map/ppermute | solution.py:70
  101.0 1.8 %fusion.17 = f32[384,768]{1,0:T(8,128)} fusion(bf16[1024,384]{1,0:T(8,128)(2,1)S(1)} %copy-done.3, bf16[1024,768]{1,0:T(8,128)(2,1)S(1)} %constant_dynamic-update-slice_fusion), kind=kOutput, calls=%fused_computation.99 | convolution fusion | flops 603979776 | bytes 3538944 | tf_op jit(solution)/shard_map/dot_general | solution.py:164
  104.7 3.7 %collective-permute-done.12 = f32[3074]{0:T(1024)S(1)} collective-permute-done((f32[3074]{0:T(1024)S(1)}, f32[3074]{0:T(1024)S(1)}, u32[]{:S(2)}, u32[]{:S(2)}) %collective-permute-start.12) | collective-permute-done | bytes 12328 | tf_op jit(solution)/shard_map/ppermute | solution.py:55
  110.3 3.0 %collective-permute-done.14 = f32[3074]{0:T(1024)S(1)} collective-permute-done((f32[3074]{0:T(1024)S(1)}, f32[3074]{0:T(1024)S(1)}, u32[]{:S(2)}, u32[]{:S(2)}) %collective-permute-start.14) | collective-permute-done | bytes 12328 | tf_op jit(solution)/shard_map/ppermute | solution.py:55
  113.3 2.1 %collective-permute-start.15 = (f32[3074]{0:T(1024)S(1)}, f32[3074]{0:T(1024)S(1)}, u32[]{:S(2)}, u32[]{:S(2)}) collective-permute-start(f32[3074]{0:T(1024)S(1)} %add.393), channel_id=1, source_target_pairs={{0,8},{8,0},{16,24},{24,16},{1,9},{9,1},{17,25},{25,17},{2,10},{10... | collective-permute-start | bytes 36896 | tf_op jit(solution)/shard_map/ppermute | solution.py:55
  115.4 2.3 %collective-permute-done.15 = f32[3074]{0:T(1024)S(1)} collective-permute-done((f32[3074]{0:T(1024)S(1)}, f32[3074]{0:T(1024)S(1)}, u32[]{:S(2)}, u32[]{:S(2)}) %collective-permute-start.15) | collective-permute-done | bytes 12328 | tf_op jit(solution)/shard_map/ppermute | solution.py:55
  117.7 2.2 %collective-permute-start.16 = (f32[3074]{0:T(1024)S(1)}, f32[3074]{0:T(1024)S(1)}, u32[]{:S(2)}, u32[]{:S(2)}) collective-permute-start(f32[3074]{0:T(1024)S(1)} %add.394), channel_id=1, source_target_pairs={{0,16},{8,24},{16,0},{24,8},{1,17},{9,25},{17,1},{25,9},{2,18},{10... | collective-permute-start | bytes 36896 | tf_op jit(solution)/shard_map/ppermute | solution.py:55
  119.9 3.6 %collective-permute-done.16 = f32[3074]{0:T(1024)S(1)} collective-permute-done((f32[3074]{0:T(1024)S(1)}, f32[3074]{0:T(1024)S(1)}, u32[]{:S(2)}, u32[]{:S(2)}) %collective-permute-start.16) | collective-permute-done | bytes 12328 | tf_op jit(solution)/shard_map/ppermute | solution.py:55
  126.6 4.5 %reduce-scatter.2.cloned.1.call-done = f32[96,768]{1,0:T(8,128)} async-done(((f32[384,768]{1,0:T(8,128)}), f32[96,768]{1,0:T(8,128)}) %reduce-scatter.2.cloned.1.call-update) | async-done | bytes 294928 | tf_op jit(solution)/shard_map/reduce_scatter | solution.py:167
  (121 shorter events, 29.1 us)
Async XLA Ops:
  7.2 73.0 %all-gather.2.cloned.1.call-start = ((), (), s32[]{:S(2)}) async-start(), calls=%async_computation.1 | async-start | bytes 4866048 | tf_op jit(solution)/shard_map/all_gather | solution.py:123
  7.9 123.2 %reduce-scatter.2.cloned.1.call-start = ((), (), s32[]{:S(2)}) async-start(), calls=%async_computation.2 | async-start | bytes 1474560 | tf_op jit(solution)/shard_map/reduce_scatter | solution.py:167
  21.2 9.5 %collective-permute-start = (bf16[128,384]{0,1:T(8,128)(2,1)}, bf16[128,384]{0,1:T(8,128)(2,1)S(1)}, u32[]{:S(2)}, u32[]{:S(2)}) collective-permute-start(bf16[128,384]{0,1:T(8,128)(2,1)} %get-tuple-element.37), channel_id=1, source_target_pairs={{0,7},{1,0},{2,1},{3,2},{4,3},{5,4},{6,5},{7,6},{8,15},{9,8},{10,9... | collective-permute-start | bytes 294920 | tf_op jit(solution)/shard_map/ppermute | solution.py:112
  24.5 7.3 %collective-permute-start.1 = (bf16[128,384]{0,1:T(8,128)(2,1)}, bf16[128,384]{0,1:T(8,128)(2,1)S(1)}, u32[]{:S(2)}, u32[]{:S(2)}) collective-permute-start(bf16[128,384]{0,1:T(8,128)(2,1)} %get-tuple-element.36), channel_id=1, source_target_pairs={{0,6},{1,7},{2,0},{3,1},{4,2},{5,3},{6,4},{7,5},{8,14},{9,15},{10,... | collective-permute-start | bytes 294920 | tf_op jit(solution)/shard_map/ppermute | solution.py:112
  25.4 7.9 %collective-permute-start.2 = (bf16[128,384]{0,1:T(8,128)(2,1)}, bf16[128,384]{0,1:T(8,128)(2,1)S(1)}, u32[]{:S(2)}, u32[]{:S(2)}) collective-permute-start(bf16[128,384]{0,1:T(8,128)(2,1)} %get-tuple-element.35), channel_id=1, source_target_pairs={{0,5},{1,6},{2,7},{3,0},{4,1},{5,2},{6,3},{7,4},{8,13},{9,14},{10,... | collective-permute-start | bytes 294920 | tf_op jit(solution)/shard_map/ppermute | solution.py:112
  25.6 8.9 %collective-permute-start.3 = (bf16[128,384]{0,1:T(8,128)(2,1)}, bf16[128,384]{0,1:T(8,128)(2,1)S(1)}, u32[]{:S(2)}, u32[]{:S(2)}) collective-permute-start(bf16[128,384]{0,1:T(8,128)(2,1)} %get-tuple-element.34), channel_id=1, source_target_pairs={{0,4},{1,5},{2,6},{3,7},{4,0},{5,1},{6,2},{7,3},{8,12},{9,13},{10,... | collective-permute-start | bytes 294920 | tf_op jit(solution)/shard_map/ppermute | solution.py:112
  26.8 7.9 %collective-permute-start.4 = (bf16[128,384]{0,1:T(8,128)(2,1)}, bf16[128,384]{0,1:T(8,128)(2,1)}, u32[]{:S(2)}, u32[]{:S(2)}) collective-permute-start(bf16[128,384]{0,1:T(8,128)(2,1)} %get-tuple-element.33), channel_id=1, source_target_pairs={{0,3},{1,4},{2,5},{3,6},{4,7},{5,0},{6,1},{7,2},{8,11},{9,12},{10,... | collective-permute-start | bytes 294920 | tf_op jit(solution)/shard_map/ppermute | solution.py:112
  30.7 4.9 %collective-permute-start.5 = (bf16[128,384]{0,1:T(8,128)(2,1)S(1)}, bf16[128,384]{0,1:T(8,128)(2,1)S(1)}, u32[]{:S(2)}, u32[]{:S(2)}) collective-permute-start(bf16[128,384]{0,1:T(8,128)(2,1)S(1)} %copy-done.7), channel_id=1, source_target_pairs={{0,2},{1,3},{2,4},{3,5},{4,6},{5,7},{6,0},{7,1},{8,10},{9,11},{10,... | collective-permute-start | bytes 294920 | tf_op jit(solution)/shard_map/ppermute | solution.py:112
  31.8 5.3 %collective-permute-start.6 = (bf16[128,384]{0,1:T(8,128)(2,1)S(1)}, bf16[128,384]{0,1:T(8,128)(2,1)S(1)}, u32[]{:S(2)}, u32[]{:S(2)}) collective-permute-start(bf16[128,384]{0,1:T(8,128)(2,1)S(1)} %copy-done.6), channel_id=1, source_target_pairs={{0,1},{1,2},{2,3},{3,4},{4,5},{5,6},{6,7},{7,0},{8,9},{9,10},{10,1... | collective-permute-start | bytes 294920 | tf_op jit(solution)/shard_map/ppermute | solution.py:112
  33.3 31.7 %collective-permute-start.7 = (bf16[128,4096]{1,0:T(8,128)(2,1)}, bf16[128,4096]{1,0:T(8,128)(2,1)}, u32[]{:S(2)}, u32[]{:S(2)}) collective-permute-start(bf16[128,4096]{1,0:T(8,128)(2,1)} %broadcast_select_fusion), channel_id=1, source_target_pairs={{0,1},{1,0},{2,3},{3,2},{4,5},{5,4},{6,7},{7,6},{8,9},{9,8},{10,11... | collective-permute-start | bytes 3145736 | tf_op jit(solution)/shard_map/ppermute | solution.py:43
  47.4 19.2 %copy-start.1 = (bf16[128,4096]{1,0:T(8,128)(2,1)S(1)}, bf16[128,4096]{1,0:T(8,128)(2,1)}, u32[]{:S(2)}) copy-start(bf16[128,4096]{1,0:T(8,128)(2,1)} %param.16) | copy-start | bytes 3145732
  67.7 12.5 %copy-start.2 = (bf16[128,3072]{1,0:T(8,128)(2,1)S(1)}, bf16[128,3072]{1,0:T(8,128)(2,1)}, u32[]{:S(2)}) copy-start(bf16[128,3072]{1,0:T(8,128)(2,1)} %param.20) | copy-start | bytes 2359300
  67.7 12.5 %copy-start.5 = (bf16[128,768]{1,0:T(8,128)(2,1)S(1)}, bf16[128,768]{1,0:T(8,128)(2,1)}, u32[]{:S(2)}) copy-start(bf16[128,768]{1,0:T(8,128)(2,1)} %param.21) | copy-start | bytes 589828
  69.9 13.9 %copy-start.8 = (bf16[768,4]{0,1:T(4,128)(2,1)S(1)}, bf16[768,4]{0,1:T(4,128)(2,1)}, u32[]{:S(2)}) copy-start(bf16[768,4]{0,1:T(4,128)(2,1)} %param.24) | copy-start | bytes 18436
  69.9 14.1 %copy-start.11 = (s32[128]{0:T(128)S(1)}, s32[128]{0:T(128)}, u32[]{:S(2)}) copy-start(s32[128]{0:T(128)} %param.25) | copy-start | bytes 1540
  85.2 9.6 %collective-permute-start.10 = (bf16[128,768]{1,0:T(8,128)(2,1)S(1)}, bf16[128,768]{1,0:T(8,128)(2,1)S(1)}, u32[]{:S(2)}, u32[]{:S(2)}) collective-permute-start(bf16[128,768]{1,0:T(8,128)(2,1)S(1)} %get-tuple-element.29), channel_id=1, source_target_pairs={{0,1},{1,4},{4,5},{5,0},{2,3},{3,6},{6,7},{7,2},{8,9},{9,12},{12,1... | collective-permute-start | bytes 589832 | tf_op jit(solution)/shard_map/ppermute | solution.py:66
  86.0 11.3 %collective-permute-start.8 = (bf16[128,768]{1,0:T(8,128)(2,1)S(1)}, bf16[128,768]{1,0:T(8,128)(2,1)S(1)}, u32[]{:S(2)}, u32[]{:S(2)}) collective-permute-start(bf16[128,768]{1,0:T(8,128)(2,1)S(1)} %get-tuple-element.29), channel_id=1, source_target_pairs={{0,5},{1,0},{4,1},{5,4},{2,7},{3,2},{6,3},{7,6},{8,13},{9,8},{12,9... | collective-permute-start | bytes 589832 | tf_op jit(solution)/shard_map/ppermute | solution.py:66
  88.2 10.3 %collective-permute-start.9 = (bf16[128,768]{1,0:T(8,128)(2,1)S(1)}, bf16[128,768]{1,0:T(8,128)(2,1)S(1)}, u32[]{:S(2)}, u32[]{:S(2)}) collective-permute-start(bf16[128,768]{1,0:T(8,128)(2,1)S(1)} %get-tuple-element.29), channel_id=1, source_target_pairs={{0,4},{1,5},{4,0},{5,1},{2,6},{3,7},{6,2},{7,3},{8,12},{9,13},{12,... | collective-permute-start | bytes 589832 | tf_op jit(solution)/shard_map/ppermute | solution.py:66
  98.6 2.4 %collective-permute-start.11 = (bf16[512,768]{1,0:T(8,128)(2,1)S(1)}, bf16[512,768]{1,0:T(8,128)(2,1)S(1)}, u32[]{:S(2)}, u32[]{:S(2)}) collective-permute-start(bf16[512,768]{1,0:T(8,128)(2,1)S(1)} %pad_maximum_fusion), channel_id=1, source_target_pairs={{0,2},{2,0},{1,3},{3,1},{4,6},{6,4},{5,7},{7,5},{8,10},{10,8},{9,1... | collective-permute-start | bytes 2359304 | tf_op jit(solution)/shard_map/ppermute | solution.py:70
  104.7 3.7 %collective-permute-start.12 = (f32[3074]{0:T(1024)S(1)}, f32[3074]{0:T(1024)S(1)}, u32[]{:S(2)}, u32[]{:S(2)}) collective-permute-start(f32[3074]{0:T(1024)S(1)} %concatenate.52), channel_id=1, source_target_pairs={{0,1},{1,0},{2,3},{3,2},{4,5},{5,4},{6,7},{7,6},{8,9},{9,8},{10,11... | collective-permute-start | bytes 36896 | tf_op jit(solution)/shard_map/ppermute | solution.py:55
  108.4 1.2 collective-permute-start.13
  109.6 3.7 %collective-permute-start.14 = (f32[3074]{0:T(1024)S(1)}, f32[3074]{0:T(1024)S(1)}, u32[]{:S(2)}, u32[]{:S(2)}) collective-permute-start(f32[3074]{0:T(1024)S(1)} %add.392), channel_id=1, source_target_pairs={{0,4},{4,0},{1,5},{5,1},{2,6},{6,2},{3,7},{7,3},{8,12},{12,8},{9,1... | collective-permute-start | bytes 36896 | tf_op jit(solution)/shard_map/ppermute | solution.py:55
  113.3 4.4 %collective-permute-start.15 = (f32[3074]{0:T(1024)S(1)}, f32[3074]{0:T(1024)S(1)}, u32[]{:S(2)}, u32[]{:S(2)}) collective-permute-start(f32[3074]{0:T(1024)S(1)} %add.393), channel_id=1, source_target_pairs={{0,8},{8,0},{16,24},{24,16},{1,9},{9,1},{17,25},{25,17},{2,10},{10... | collective-permute-start | bytes 36896 | tf_op jit(solution)/shard_map/ppermute | solution.py:55
  117.7 5.8 %collective-permute-start.16 = (f32[3074]{0:T(1024)S(1)}, f32[3074]{0:T(1024)S(1)}, u32[]{:S(2)}, u32[]{:S(2)}) collective-permute-start(f32[3074]{0:T(1024)S(1)} %add.394), channel_id=1, source_target_pairs={{0,16},{8,24},{16,0},{24,8},{1,17},{9,25},{17,1},{25,9},{2,18},{10... | collective-permute-start | bytes 36896 | tf_op jit(solution)/shard_map/ppermute | solution.py:55
  (10 other events, 39.4 us)
Sparse Core Ops, SparseCore 0:
  10.9 69.1 all-gather.1
  103.0 28.1 reduce-scatter.1

commit v16 on v15

--- a/solution.py
+++ b/solution.py
@@ -31,17 +31,16 @@
 def teacher_attention(context, w_out, tok_rows, ride):
     tensor_size = lax.axis_size("tensor")
     partial = jnp.dot(context, w_out, preferred_element_type=jnp.float32).astype(jnp.bfloat16)
-    partial, ride = lax.optimization_barrier((partial, ride))
     if tensor_size != 2:
-        return lax.psum_scatter(
+        return lax.optimization_barrier((lax.psum_scatter(
             partial, "tensor", scatter_dimension=0, tiled=True
-        ).astype(jnp.float32), ride
+        ).astype(jnp.float32), ride))
     me = lax.axis_index("tensor")
     halves = partial.reshape(2, tok_rows, partial.shape[1])
     mine = jnp.where(me == 0, halves[0], halves[1])
     theirs = jnp.where(me == 0, halves[1], halves[0])
     got = lax.ppermute(theirs, "tensor", perm=[(0, 1), (1, 0)])
-    return mine.astype(jnp.float32) + got.astype(jnp.float32), ride
+    return lax.optimization_barrier((mine.astype(jnp.float32) + got.astype(jnp.float32), ride))
 
 
 def butterfly_sum(value, axes):

time: 140 us -> 141 us (level)
  waiting for transfers between devices: 59.9 us -> 65.9 us
  local copies, waits for them, and re-layouts: 17.9 us -> 13.1 us
    all_gather x1, waiting for transfers between devices: 10.3 us -> 1.58 us  [local(): lax.all_gather(down_weight, TOKS, axis=0, tiled=True)]
    ppermute x7, waiting for transfers between devices: 1.67 us -> 9.76 us  [local(): lax.ppermute(send, GROUP, perm=[(i, (i - k) % group) for i in range(group)])]
    ppermute x1, waiting for transfers between devices: 17.6 us -> 24.2 us  [teacher_attention(): got = lax.ppermute(theirs, 'tensor', perm=[(0, 1), (1, 0)])]
    unnamed x49 -> x47, local copies, waits for them, and re-layouts: 5.55 us -> 2.64 us
    squeeze x1, local copies, waits for them, and re-layouts: 2.1 us -> 0.07 us  [local(): lax.dynamic_index_in_dim(hidden_split, (me - k) % group, 0, keepdims=False)]
    ppermute x1, starting transfers between devices: 1.19 us -> 2.97 us  [teacher_attention(): got = lax.ppermute(theirs, 'tensor', perm=[(0, 1), (1, 0)])]
  transfers between devices with their start and end apart: 19 -> 19, of which waited for: 14 -> 17; matrix products, arithmetic and copies ran while one was open for 26% -> 21% of each run, Pallas kernels for 0% -> 0%
where the time goes in v16:
time: 141 us
  waiting for transfers between devices  65.9 us (47%)
  starting transfers between devices  20.2 us (14%)
  between operations  17 us (12%)
  matrix products  16.5 us (12%)
  local copies, waits for them, and re-layouts  13.1 us (9%)
  other arithmetic  8.27 us (6%)
    ppermute x1, waiting for transfers between devices, teacher_attention(): got = lax.ppermute(theirs, 'tensor', perm=[(0, 1), (1, 0)])  24.2 us
    ppermute x5, waiting for transfers between devices, butterfly_sum(): lax.ppermute(value, axis, perm=[(i, i ^ step) for i in range(size)])  13.7 us
    ppermute x7, waiting for transfers between devices, local(): lax.ppermute(send, GROUP, perm=[(i, (i - k) % group) for i in range(group)])  9.76 us
    ppermute x3, waiting for transfers between devices, group_gather(): lax.ppermute(value, chips, perm=[(i, (i - k) % n) for i in range(n)])  9.02 us
    dot_general x1, matrix products, teacher_attention(): jnp.dot(context, w_out, preferred_element_type=jnp.float32)  8.4 us
    ppermute x7, starting transfers between devices, local(): lax.ppermute(send, GROUP, perm=[(i, (i - k) % group) for i in range(group)])  7.96 us
    gather x2, local copies, waits for them, and re-layouts, local(): jnp.take(jnp.roll(jnp.stack(pieces), me, axis=0), group_order(), axis=0)  5.03 us
    ppermute x5, starting transfers between devices, butterfly_sum(): lax.ppermute(value, axis, perm=[(i, i ^ step) for i in range(size)])  4.9 us
  transfers between devices with their start and end apart: 19, of which 17 were waited for; matrix products, arithmetic and copies ran while one was open for 21% of the time, Pallas kernels for 0%

profile of v16, /device:TPU:0, one launch (start us, length us, event | category | flops | bytes accessed | tf_op | source)
XLA Modules:
  0.0 140.9 jit_solution(14645698843667348551)
XLA Ops:
  8.4 8.4 %convolution_convert_fusion = bf16[256,4096]{1,0:T(8,128)(2,1)S(1)} fusion(bf16[256,2048]{1,0:T(8,128)(2,1)S(1)} %copy-done, bf16[2048,4096]{1,0:T(8,128)(2,1)} %param.15), kind=kOutput, calls=%fused_computation.1 | convolution fusion | flops 4296015872 | bytes 19922944 | tf_op jit(solution)/shard_map/dot_general | solution.py:33
  18.5 3.0 %collective-permute-start = (bf16[128,4096]{1,0:T(8,128)(2,1)}, bf16[128,4096]{1,0:T(8,128)(2,1)}, u32[]{:S(2)}, u32[]{:S(2)}) collective-permute-start(bf16[128,4096]{1,0:T(8,128)(2,1)} %broadcast_select_fusion), channel_id=1, source_target_pairs={{0,1},{1,0},{2,3},{3,2},{4,5},{5,4},{6,7},{7,6},{8,9},{9,8},{10,11... | collective-permute-start | bytes 3145736 | tf_op jit(solution)/shard_map/ppermute | solution.py:42
  23.9 24.2 %collective-permute-done = bf16[128,4096]{1,0:T(8,128)(2,1)} collective-permute-done((bf16[128,4096]{1,0:T(8,128)(2,1)}, bf16[128,4096]{1,0:T(8,128)(2,1)}, u32[]{:S(2)}, u32[]{:S(2)}) %collective-permute-start) | collective-permute-done | bytes 1048608 | tf_op jit(solution)/shard_map/ppermute | solution.py:42
  48.1 2.3 %convert_add_fusion.1 = f32[128,4096]{1,0:T(8,128)S(1)} fusion(bf16[128,4096]{1,0:T(8,128)(2,1)} %collective-permute-done, pred[]{:T(512)S(6)} %eq.46, bf16[256,4096]{1,0:T(8,128)(2,1)} %copy-done.1), kind=kLoop, calls=%fused_computation.7 | loop fusion | flops 2097152 | bytes 5242881 | tf_op jit(solution)/shard_map/add | solution.py:43
  56.7 1.8 %collective-permute-start.7 = (bf16[128,384]{0,1:T(8,128)(2,1)S(1)}, bf16[128,384]{0,1:T(8,128)(2,1)S(1)}, u32[]{:S(2)}, u32[]{:S(2)}) collective-permute-start(bf16[128,384]{0,1:T(8,128)(2,1)S(1)} %get-tuple-element.30), channel_id=1, source_target_pairs={{0,1},{1,2},{2,3},{3,4},{4,5},{5,6},{6,7},{7,0},{8,9},{9,10},{10,1... | collective-permute-start | bytes 294920 | tf_op jit(solution)/shard_map/ppermute | solution.py:111
  59.2 4.2 %collective-permute-done.4 = bf16[128,384]{0,1:T(8,128)(2,1)S(1)} collective-permute-done((bf16[128,384]{0,1:T(8,128)(2,1)S(1)}, bf16[128,384]{0,1:T(8,128)(2,1)S(1)}, u32[]{:S(2)}, u32[]{:S(2)}) %collective-permute-start.4) | collective-permute-done | bytes 98336 | tf_op jit(solution)/shard_map/ppermute | solution.py:111
  65.1 3.2 %collective-permute-done.7 = bf16[128,384]{0,1:T(8,128)(2,1)S(1)} collective-permute-done((bf16[128,384]{0,1:T(8,128)(2,1)S(1)}, bf16[128,384]{0,1:T(8,128)(2,1)S(1)}, u32[]{:S(2)}, u32[]{:S(2)}) %collective-permute-start.7) | collective-permute-done | bytes 98336 | tf_op jit(solution)/shard_map/ppermute | solution.py:111
  69.5 2.7 %gather_fusion = bf16[8,128,384]{1,2,0:T(8,128)(2,1)} fusion(bf16[8,128,384]{1,2,0:T(8,128)(2,1)} %constant_dynamic-slice_fusion, s32[1024]{0:T(1024)S(1)} %pad_clamp_fusion), kind=kCustom, calls=%fused_computation | custom fusion | bytes 1572896 | tf_op jit(solution)/shard_map/jit(_take)/gather | solution.py:113
  72.2 2.3 %copy.27 = bf16[8,128,384]{2,1,0:T(8,128)(2,1)} copy(bf16[8,128,384]{1,2,0:T(8,128)(2,1)} %gather_fusion) | data formatting | bytes 1572864 | tf_op jit(solution)/shard_map/jit(_take)/gather | solution.py:113
  74.6 2.3 %bitcast_select_fusion = bf16[1024,384]{1,0:T(8,128)(2,1)} fusion(bf16[8,128,384]{2,1,0:T(8,128)(2,1)} %copy.27, pred[1024]{0:T(1024)(128)(4,1)S(1)} %broadcast_bitcast_fusion), kind=kLoop, calls=%fused_computation.14 | loop fusion | flops 393216 | bytes 1573888 | tf_op jit(solution)/shard_map/jit(_take)/select_n | solution.py:113
  78.0 2.1 %fusion.14 = (f32[128]{0:T(128)S(1)}, f32[128,4]{0,1:T(4,128)S(1)}) fusion(bf16[4096,4]{0,1:T(4,128)(2,1)S(1)} %copy-done.12, bf16[128,4096]{1,0:T(8,128)(2,1)S(1)} %copy-done.2, f32[128,4096]{1,0:T(8,128)S(1)} %convert_add_fusion.1, f32[4096]{0:T(1024)S(1)} %convert_element_type.49, f32[128]{0:T(128)S(1)} %add_rsqrt_fusion, ...), kind=kOutput, calls=%fused_computation.96 | convolution fusion | flops 8913280 | bytes 3198472 | tf_op jit(solution)/shard_map/dot_general | solution.py:119
  81.8 3.5 %fusion.13 = (f32[128]{0:T(128)S(1)}, f32[128,768]{1,0:T(8,128)S(1)}) fusion(bf16[128,3072]{1,0:T(8,128)(2,1)} %param.20, bf16[3072,768]{1,0:T(8,128)(2,1)} %all-gather.2.cloned.1.call-done, bf16[128,768]{1,0:T(8,128)(2,1)S(1)} %copy-done.6), kind=kOutput, calls=%fused_computation.95 | convolution fusion | flops 604274560 | bytes 6095360 | tf_op jit(solution)/shard_map/dot_general | solution.py:28
  87.7 2.3 %collective-permute-start.8 = (bf16[128,768]{1,0:T(8,128)(2,1)S(1)}, bf16[128,768]{1,0:T(8,128)(2,1)S(1)}, u32[]{:S(2)}, u32[]{:S(2)}) collective-permute-start(bf16[128,768]{1,0:T(8,128)(2,1)S(1)} %get-tuple-element.29), channel_id=1, source_target_pairs={{0,5},{1,0},{4,1},{5,4},{2,7},{3,2},{6,3},{7,6},{8,13},{9,8},{12,9... | collective-permute-start | bytes 589832 | tf_op jit(solution)/shard_map/ppermute | solution.py:65
  91.3 5.3 %collective-permute-done.10 = bf16[128,768]{1,0:T(8,128)(2,1)S(1)} collective-permute-done((bf16[128,768]{1,0:T(8,128)(2,1)S(1)}, bf16[128,768]{1,0:T(8,128)(2,1)S(1)}, u32[]{:S(2)}, u32[]{:S(2)}) %collective-permute-start.10) | collective-permute-done | bytes 196640 | tf_op jit(solution)/shard_map/ppermute | solution.py:65
  96.5 2.5 %collective-permute-done.8 = bf16[128,768]{1,0:T(8,128)(2,1)S(1)} collective-permute-done((bf16[128,768]{1,0:T(8,128)(2,1)S(1)}, bf16[128,768]{1,0:T(8,128)(2,1)S(1)}, u32[]{:S(2)}, u32[]{:S(2)}) %collective-permute-start.8) | collective-permute-done | bytes 196640 | tf_op jit(solution)/shard_map/ppermute | solution.py:65
  100.5 2.2 %collective-permute-done.11 = bf16[512,768]{1,0:T(8,128)(2,1)S(1)} collective-permute-done((bf16[512,768]{1,0:T(8,128)(2,1)S(1)}, bf16[512,768]{1,0:T(8,128)(2,1)S(1)}, u32[]{:S(2)}, u32[]{:S(2)}) %collective-permute-start.11) | collective-permute-done | bytes 786464 | tf_op jit(solution)/shard_map/ppermute | solution.py:69
  102.8 1.8 %fusion.17 = f32[384,768]{1,0:T(8,128)} fusion(bf16[1024,384]{1,0:T(8,128)(2,1)S(1)} %copy-done.5, bf16[1024,768]{1,0:T(8,128)(2,1)S(1)} %constant_dynamic-update-slice_fusion), kind=kOutput, calls=%fused_computation.99 | convolution fusion | flops 603979776 | bytes 3538944 | tf_op jit(solution)/shard_map/dot_general | solution.py:163
  106.5 3.7 %collective-permute-done.12 = f32[3074]{0:T(1024)S(1)} collective-permute-done((f32[3074]{0:T(1024)S(1)}, f32[3074]{0:T(1024)S(1)}, u32[]{:S(2)}, u32[]{:S(2)}) %collective-permute-start.12) | collective-permute-done | bytes 12328 | tf_op jit(solution)/shard_map/ppermute | solution.py:54
  112.2 2.9 %collective-permute-done.14 = f32[3074]{0:T(1024)S(1)} collective-permute-done((f32[3074]{0:T(1024)S(1)}, f32[3074]{0:T(1024)S(1)}, u32[]{:S(2)}, u32[]{:S(2)}) %collective-permute-start.14) | collective-permute-done | bytes 12328 | tf_op jit(solution)/shard_map/ppermute | solution.py:54
  115.1 1.9 %collective-permute-start.15 = (f32[3074]{0:T(1024)S(1)}, f32[3074]{0:T(1024)S(1)}, u32[]{:S(2)}, u32[]{:S(2)}) collective-permute-start(f32[3074]{0:T(1024)S(1)} %add.393), channel_id=1, source_target_pairs={{0,8},{8,0},{16,24},{24,16},{1,9},{9,1},{17,25},{25,17},{2,10},{10... | collective-permute-start | bytes 36896 | tf_op jit(solution)/shard_map/ppermute | solution.py:54
  117.1 2.3 %collective-permute-done.15 = f32[3074]{0:T(1024)S(1)} collective-permute-done((f32[3074]{0:T(1024)S(1)}, f32[3074]{0:T(1024)S(1)}, u32[]{:S(2)}, u32[]{:S(2)}) %collective-permute-start.15) | collective-permute-done | bytes 12328 | tf_op jit(solution)/shard_map/ppermute | solution.py:54
  119.4 2.2 %collective-permute-start.16 = (f32[3074]{0:T(1024)S(1)}, f32[3074]{0:T(1024)S(1)}, u32[]{:S(2)}, u32[]{:S(2)}) collective-permute-start(f32[3074]{0:T(1024)S(1)} %add.394), channel_id=1, source_target_pairs={{0,16},{8,24},{16,0},{24,8},{1,17},{9,25},{17,1},{25,9},{2,18},{10... | collective-permute-start | bytes 36896 | tf_op jit(solution)/shard_map/ppermute | solution.py:54
  121.6 3.6 %collective-permute-done.16 = f32[3074]{0:T(1024)S(1)} collective-permute-done((f32[3074]{0:T(1024)S(1)}, f32[3074]{0:T(1024)S(1)}, u32[]{:S(2)}, u32[]{:S(2)}) %collective-permute-start.16) | collective-permute-done | bytes 12328 | tf_op jit(solution)/shard_map/ppermute | solution.py:54
  128.2 4.7 %reduce-scatter.2.cloned.1.call-done = f32[96,768]{1,0:T(8,128)} async-done(((f32[384,768]{1,0:T(8,128)}), f32[96,768]{1,0:T(8,128)}) %reduce-scatter.2.cloned.1.call-update) | async-done | bytes 294928 | tf_op jit(solution)/shard_map/reduce_scatter | solution.py:166
  (119 shorter events, 28.4 us)
Async XLA Ops:
  7.2 74.6 %all-gather.2.cloned.1.call-start = ((), (), s32[]{:S(2)}) async-start(), calls=%async_computation.1 | async-start | bytes 4866048 | tf_op jit(solution)/shard_map/all_gather | solution.py:122
  7.9 125.0 %reduce-scatter.2.cloned.1.call-start = ((), (), s32[]{:S(2)}) async-start(), calls=%async_computation.2 | async-start | bytes 1474560 | tf_op jit(solution)/shard_map/reduce_scatter | solution.py:166
  16.8 4.7 %copy-start.4 = (bf16[128,3072]{1,0:T(8,128)(2,1)S(1)}, bf16[128,3072]{1,0:T(8,128)(2,1)}, u32[]{:S(2)}) copy-start(bf16[128,3072]{1,0:T(8,128)(2,1)} %param.20) | copy-start | bytes 2359300
  18.5 29.6 %collective-permute-start = (bf16[128,4096]{1,0:T(8,128)(2,1)}, bf16[128,4096]{1,0:T(8,128)(2,1)}, u32[]{:S(2)}, u32[]{:S(2)}) collective-permute-start(bf16[128,4096]{1,0:T(8,128)(2,1)} %broadcast_select_fusion), channel_id=1, source_target_pairs={{0,1},{1,0},{2,3},{3,2},{4,5},{5,4},{6,7},{7,6},{8,9},{9,8},{10,11... | collective-permute-start | bytes 3145736 | tf_op jit(solution)/shard_map/ppermute | solution.py:42
  23.9 26.4 %copy-start.3 = (bf16[8,128,4,96]{1,3,2,0:T(8,128)(2,1)S(1)}, bf16[8,128,4,96]{1,3,2,0:T(8,128)(2,1)}, u32[]{:S(2)}) copy-start(bf16[8,128,4,96]{1,3,2,0:T(8,128)(2,1)} %copy.26) | copy-start | bytes 2359300
  50.5 5.0 %collective-permute-start.1 = (bf16[128,384]{0,1:T(8,128)(2,1)S(1)}, bf16[128,384]{0,1:T(8,128)(2,1)S(1)}, u32[]{:S(2)}, u32[]{:S(2)}) collective-permute-start(bf16[128,384]{0,1:T(8,128)(2,1)S(1)} %get-tuple-element.37), channel_id=1, source_target_pairs={{0,7},{1,0},{2,1},{3,2},{4,3},{5,4},{6,5},{7,6},{8,15},{9,8},{10,9... | collective-permute-start | bytes 294920 | tf_op jit(solution)/shard_map/ppermute | solution.py:111
  51.8 4.9 %collective-permute-start.2 = (bf16[128,384]{0,1:T(8,128)(2,1)S(1)}, bf16[128,384]{0,1:T(8,128)(2,1)S(1)}, u32[]{:S(2)}, u32[]{:S(2)}) collective-permute-start(bf16[128,384]{0,1:T(8,128)(2,1)S(1)} %get-tuple-element.36), channel_id=1, source_target_pairs={{0,6},{1,7},{2,0},{3,1},{4,2},{5,3},{6,4},{7,5},{8,14},{9,15},{10,... | collective-permute-start | bytes 294920 | tf_op jit(solution)/shard_map/ppermute | solution.py:111
  53.5 5.7 %collective-permute-start.3 = (bf16[128,384]{0,1:T(8,128)(2,1)S(1)}, bf16[128,384]{0,1:T(8,128)(2,1)S(1)}, u32[]{:S(2)}, u32[]{:S(2)}) collective-permute-start(bf16[128,384]{0,1:T(8,128)(2,1)S(1)} %get-tuple-element.35), channel_id=1, source_target_pairs={{0,5},{1,6},{2,7},{3,0},{4,1},{5,2},{6,3},{7,4},{8,13},{9,14},{10,... | collective-permute-start | bytes 294920 | tf_op jit(solution)/shard_map/ppermute | solution.py:111
  53.8 9.6 %collective-permute-start.4 = (bf16[128,384]{0,1:T(8,128)(2,1)S(1)}, bf16[128,384]{0,1:T(8,128)(2,1)S(1)}, u32[]{:S(2)}, u32[]{:S(2)}) collective-permute-start(bf16[128,384]{0,1:T(8,128)(2,1)S(1)} %get-tuple-element.34), channel_id=1, source_target_pairs={{0,4},{1,5},{2,6},{3,7},{4,0},{5,1},{6,2},{7,3},{8,12},{9,13},{10,... | collective-permute-start | bytes 294920 | tf_op jit(solution)/shard_map/ppermute | solution.py:111
  54.1 9.3 %collective-permute-start.5 = (bf16[128,384]{0,1:T(8,128)(2,1)S(1)}, bf16[128,384]{0,1:T(8,128)(2,1)S(1)}, u32[]{:S(2)}, u32[]{:S(2)}) collective-permute-start(bf16[128,384]{0,1:T(8,128)(2,1)S(1)} %get-tuple-element.33), channel_id=1, source_target_pairs={{0,3},{1,4},{2,5},{3,6},{4,7},{5,0},{6,1},{7,2},{8,11},{9,12},{10,... | collective-permute-start | bytes 294920 | tf_op jit(solution)/shard_map/ppermute | solution.py:111
  55.5 9.6 %collective-permute-start.6 = (bf16[128,384]{0,1:T(8,128)(2,1)S(1)}, bf16[128,384]{0,1:T(8,128)(2,1)S(1)}, u32[]{:S(2)}, u32[]{:S(2)}) collective-permute-start(bf16[128,384]{0,1:T(8,128)(2,1)S(1)} %get-tuple-element.32), channel_id=1, source_target_pairs={{0,2},{1,3},{2,4},{3,5},{4,6},{5,7},{6,0},{7,1},{8,10},{9,11},{10,... | collective-permute-start | bytes 294920 | tf_op jit(solution)/shard_map/ppermute | solution.py:111
  56.7 11.6 %collective-permute-start.7 = (bf16[128,384]{0,1:T(8,128)(2,1)S(1)}, bf16[128,384]{0,1:T(8,128)(2,1)S(1)}, u32[]{:S(2)}, u32[]{:S(2)}) collective-permute-start(bf16[128,384]{0,1:T(8,128)(2,1)S(1)} %get-tuple-element.30), channel_id=1, source_target_pairs={{0,1},{1,2},{2,3},{3,4},{4,5},{5,6},{6,7},{7,0},{8,9},{9,10},{10,1... | collective-permute-start | bytes 294920 | tf_op jit(solution)/shard_map/ppermute | solution.py:111
  78.0 3.7 %copy-start.6 = (bf16[128,768]{1,0:T(8,128)(2,1)S(1)}, bf16[128,768]{1,0:T(8,128)(2,1)}, u32[]{:S(2)}) copy-start(bf16[128,768]{1,0:T(8,128)(2,1)} %param.21) | copy-start | bytes 589828
  80.2 5.4 %copy-start.7 = (bf16[768,4]{0,1:T(4,128)(2,1)S(1)}, bf16[768,4]{0,1:T(4,128)(2,1)}, u32[]{:S(2)}) copy-start(bf16[768,4]{0,1:T(4,128)(2,1)} %param.24) | copy-start | bytes 18436
  80.2 5.7 %copy-start.9 = (s32[128]{0:T(128)S(1)}, s32[128]{0:T(128)}, u32[]{:S(2)}) copy-start(s32[128]{0:T(128)} %param.25) | copy-start | bytes 1540
  87.1 9.5 %collective-permute-start.10 = (bf16[128,768]{1,0:T(8,128)(2,1)S(1)}, bf16[128,768]{1,0:T(8,128)(2,1)S(1)}, u32[]{:S(2)}, u32[]{:S(2)}) collective-permute-start(bf16[128,768]{1,0:T(8,128)(2,1)S(1)} %get-tuple-element.29), channel_id=1, source_target_pairs={{0,1},{1,4},{4,5},{5,0},{2,3},{3,6},{6,7},{7,2},{8,9},{9,12},{12,1... | collective-permute-start | bytes 589832 | tf_op jit(solution)/shard_map/ppermute | solution.py:65
  87.7 11.4 %collective-permute-start.8 = (bf16[128,768]{1,0:T(8,128)(2,1)S(1)}, bf16[128,768]{1,0:T(8,128)(2,1)S(1)}, u32[]{:S(2)}, u32[]{:S(2)}) collective-permute-start(bf16[128,768]{1,0:T(8,128)(2,1)S(1)} %get-tuple-element.29), channel_id=1, source_target_pairs={{0,5},{1,0},{4,1},{5,4},{2,7},{3,2},{6,3},{7,6},{8,13},{9,8},{12,9... | collective-permute-start | bytes 589832 | tf_op jit(solution)/shard_map/ppermute | solution.py:65
  90.0 10.3 %collective-permute-start.9 = (bf16[128,768]{1,0:T(8,128)(2,1)S(1)}, bf16[128,768]{1,0:T(8,128)(2,1)S(1)}, u32[]{:S(2)}, u32[]{:S(2)}) collective-permute-start(bf16[128,768]{1,0:T(8,128)(2,1)S(1)} %get-tuple-element.29), channel_id=1, source_target_pairs={{0,4},{1,5},{4,0},{5,1},{2,6},{3,7},{6,2},{7,3},{8,12},{9,13},{12,... | collective-permute-start | bytes 589832 | tf_op jit(solution)/shard_map/ppermute | solution.py:65
  100.4 2.4 %collective-permute-start.11 = (bf16[512,768]{1,0:T(8,128)(2,1)S(1)}, bf16[512,768]{1,0:T(8,128)(2,1)S(1)}, u32[]{:S(2)}, u32[]{:S(2)}) collective-permute-start(bf16[512,768]{1,0:T(8,128)(2,1)S(1)} %pad_maximum_fusion), channel_id=1, source_target_pairs={{0,2},{2,0},{1,3},{3,1},{4,6},{6,4},{5,7},{7,5},{8,10},{10,8},{9,1... | collective-permute-start | bytes 2359304 | tf_op jit(solution)/shard_map/ppermute | solution.py:69
  106.5 3.7 %collective-permute-start.12 = (f32[3074]{0:T(1024)S(1)}, f32[3074]{0:T(1024)S(1)}, u32[]{:S(2)}, u32[]{:S(2)}) collective-permute-start(f32[3074]{0:T(1024)S(1)} %concatenate.52), channel_id=1, source_target_pairs={{0,1},{1,0},{2,3},{3,2},{4,5},{5,4},{6,7},{7,6},{8,9},{9,8},{10,11... | collective-permute-start | bytes 36896 | tf_op jit(solution)/shard_map/ppermute | solution.py:54
  110.2 1.2 collective-permute-start.13
  111.4 3.7 %collective-permute-start.14 = (f32[3074]{0:T(1024)S(1)}, f32[3074]{0:T(1024)S(1)}, u32[]{:S(2)}, u32[]{:S(2)}) collective-permute-start(f32[3074]{0:T(1024)S(1)} %add.392), channel_id=1, source_target_pairs={{0,4},{4,0},{1,5},{5,1},{2,6},{6,2},{3,7},{7,3},{8,12},{12,8},{9,1... | collective-permute-start | bytes 36896 | tf_op jit(solution)/shard_map/ppermute | solution.py:54
  115.1 4.3 %collective-permute-start.15 = (f32[3074]{0:T(1024)S(1)}, f32[3074]{0:T(1024)S(1)}, u32[]{:S(2)}, u32[]{:S(2)}) collective-permute-start(f32[3074]{0:T(1024)S(1)} %add.393), channel_id=1, source_target_pairs={{0,8},{8,0},{16,24},{24,16},{1,9},{9,1},{17,25},{25,17},{2,10},{10... | collective-permute-start | bytes 36896 | tf_op jit(solution)/shard_map/ppermute | solution.py:54
  119.4 5.7 %collective-permute-start.16 = (f32[3074]{0:T(1024)S(1)}, f32[3074]{0:T(1024)S(1)}, u32[]{:S(2)}, u32[]{:S(2)}) collective-permute-start(f32[3074]{0:T(1024)S(1)} %add.394), channel_id=1, source_target_pairs={{0,16},{8,24},{16,0},{24,8},{1,17},{9,25},{17,1},{25,9},{2,18},{10... | collective-permute-start | bytes 36896 | tf_op jit(solution)/shard_map/ppermute | solution.py:54
  (9 other events, 15.3 us)
Sparse Core Ops, SparseCore 0:
  10.9 70.8 all-gather.1
  104.8 28.1 reduce-scatter.1
